TPU v7x, 256 devices: a whole 4x4x8 slice. The times are simulated.
256 devices in a mesh: tm: 128 (over z, y_lo, x, core), net: 2 (over y_hi).
Axes of the slice: x: 4, y: 4 (y_hi: 2, y_lo: 2; y = y_hi * 2 + y_lo), z: 8, core: 2. Of those that a mesh axis runs over, the one named last changes fastest.
Arguments:
- direction_nodal: float32 [1, 128, 2, 8192], P(None, 'tm', None, 'net'), may hold values from -27 to 27
- direction_capacity: float32 [1, 128, 65536], P(None, 'tm', 'net'), may hold values from -27 to 27
- residual_nodal: float32 [1, 128, 2, 8192], P(None, 'tm', None, 'net'), may hold values from -27 to 27
- residual_capacity: float32 [1, 128, 65536], P(None, 'tm', 'net'), may hold values from -27 to 27
- scale_flow: float32 [128, 12288], P('tm', 'net'), may hold values from 0.25 to 4
- scale_dispatch: float32 [128, 65536], P('tm', 'net'), may hold values from 0.25 to 4
- scale_storage: float32 [128, 2, 8192], P('tm', None, 'net'), may hold values from 0.25 to 4
- scale_capacity: float32 [65536], P('net'), may hold values from 0.02 to 0.3
- availability: float32 [128, 65536], P('tm', 'net'), may hold values from 0.05 to 1
- retention: float32 [8192], P('net'), may hold values from 0.5 to 1
- line_anchor: int32 [96], P('net'), may hold values from 0 to 63
- line_target: int32 [96], P('net'), may hold values from 0 to 63
- anchor_rows: int32 [12288], P('net'), may hold values from 0 to 127
- target_rows: int32 [12288], P('net'), may hold values from 0 to 127
- column_block: int32 [512], P('net'), may hold values from 0 to 63
- column_rows: int32 [65536], P('net'), may hold values from 0 to 127
Outputs:
- updated_nodal: float32 [1, 128, 2, 8192], P(None, 'tm', None, 'net')
- updated_capacity: float32 [1, 128, 65536], P(None, 'tm', 'net')
All inputs are finite; a program needn't handle non-finite values.
Results may differ from a plain program's by a relative error of at most 0.00002.
Values sent between devices are 32-bit elements; how exact they have to be, the bound alone decides.
No kernel may reach another device: no remote copies, remote signals or barrier semaphores. Data moves between devices by JAX's collectives and lax.ppermute only.
A program may use at most 64 MiB of HBM per device.

v0:
```python
import jax
import jax.numpy as jnp
from jax import lax
from jax.sharding import PartitionSpec as P

BLOCK = 128


DAMPING = 0.5


def passed_along(value, axis, steps):
    count = lax.axis_size(axis)
    pairs = [(source, (source + steps) % count) for source in range(count)]
    return lax.ppermute(value, axis, pairs)


def body(
    direction_nodal,
    direction_capacity,
    residual_nodal,
    residual_capacity,
    scale_flow,
    scale_dispatch,
    scale_storage,
    scale_capacity,
    availability,
    retention,
    line_anchor,
    line_target,
    anchor_rows,
    target_rows,
    column_block,
    column_rows,
):
    anchor = jnp.repeat(line_anchor, BLOCK) * BLOCK + anchor_rows
    target = jnp.repeat(line_target, BLOCK) * BLOCK + target_rows
    column_bus = jnp.repeat(column_block, BLOCK) * BLOCK + column_rows
    balance = direction_nodal[:, :, 0, :]
    storage = direction_nodal[:, :, 1, :]
    network = lax.all_gather(balance, "net", axis=2, tiled=True)
    next_first = passed_along(storage, "tm", -1)
    storage_next = jnp.concatenate([storage[:, 1:, :], next_first], axis=1)
    flow_value = jnp.take(network, anchor, axis=2) - jnp.take(network, target, axis=2)
    dispatch_value = jnp.take(network, column_bus, axis=2) + direction_capacity
    partial_sums = -jnp.sum(availability[None] * direction_capacity, axis=1)
    level_value = storage - retention * storage_next
    charge_value = balance - storage
    flow_scaled = scale_flow[None] * flow_value
    dispatch_scaled = scale_dispatch[None] * dispatch_value
    level_scaled = scale_storage[None, :, 0, :] * level_value
    charge_scaled = scale_storage[None, :, 1, :] * charge_value
    capacity_value = lax.psum(partial_sums, "tm")
    capacity_scaled = scale_capacity[None] * capacity_value
    squares_local = jnp.sum(residual_nodal * residual_nodal, axis=(1, 2, 3)) + jnp.sum(
        residual_capacity * residual_capacity, axis=(1, 2)
    )
    bus_terms = jnp.zeros(network.shape, jnp.float32).at[:, :, anchor].add(flow_scaled)
    bus_terms = (
        bus_terms.at[:, :, target].add(-flow_scaled).at[:, :, column_bus].add(dispatch_scaled)
    )
    own_terms = lax.psum_scatter(bus_terms, "net", scatter_dimension=2, tiled=True)
    image_balance = own_terms + charge_scaled + DAMPING * balance
    behind = passed_along(level_scaled, "tm", 1)
    level_before = jnp.concatenate([behind, level_scaled[:, :-1, :]], axis=1)
    image_storage = level_scaled - retention * level_before - charge_scaled + DAMPING * storage
    image_limit = (
        dispatch_scaled
        - availability[None] * capacity_scaled[:, None, :]
        + DAMPING * direction_capacity
    )
    image_nodal = jnp.stack([image_balance, image_storage], axis=2)
    curvature_local = jnp.sum(direction_nodal * image_nodal, axis=(1, 2, 3)) + jnp.sum(
        direction_capacity * image_limit, axis=(1, 2)
    )
    squares, curvature = lax.psum((squares_local, curvature_local), ("tm", "net"))
    step_size = squares / curvature
    updated_nodal = residual_nodal - step_size[:, None, None, None] * image_nodal
    updated_capacity = residual_capacity - step_size[:, None, None] * image_limit
    return (updated_nodal, updated_capacity)


def solution(mesh):
    in_specs = (
        P(None, "tm", None, "net"),
        P(None, "tm", "net"),
        P(None, "tm", None, "net"),
        P(None, "tm", "net"),
        P("tm", "net"),
        P("tm", "net"),
        P("tm", None, "net"),
        P("net"),
        P("tm", "net"),
        P("net"),
        P("net"),
        P("net"),
        P("net"),
        P("net"),
        P("net"),
        P("net"),
    )
    out_specs = (P(None, "tm", None, "net"), P(None, "tm", "net"))
    return jax.shard_map(body, mesh=mesh, in_specs=in_specs, out_specs=out_specs, check_vma=False)
```

profile of v0, /device:TPU:2, one launch (start us, length us, event | category | flops | bytes accessed | tf_op | source)
XLA Modules:
  0.0 1335.8 jit_solution(10901547301141026485)
XLA Ops:
  7.2 0.0 all-reduce.3.cloned.1.call-start
  7.2 1.8 fusion.3
  9.0 0.0 all-reduce.3.cloned.1.call-update
  9.0 0.0 reduce-scatter.4.cloned.1.call-start
  9.1 0.9 fusion.11
  9.9 0.1 collective-permute-start
  10.0 5.9 all-gather
  16.0 0.7 broadcast_multiply_fusion.1
  16.6 0.7 broadcast_multiply_fusion.2
  17.3 0.8 broadcast_clamp_fusion.1
  18.1 34.3 %gather_fusion.2 = f32[6144]{0:T(1024)S(1)} fusion(f32[8192]{0:T(1024)S(1)} %bitcast.85, s32[6144]{0:T(1024)S(1)} %get-tuple-element.12), kind=kCustom, calls=%fused_computation.1.clone | custom fusion | bytes 73728 | tf_op jit(solution)/shard_map/jit(_take)/gather | solution.py:44
  52.4 0.1 broadcast_clamp_fusion.2
  52.5 34.3 %gather_fusion.1 = f32[6144]{0:T(1024)S(1)} fusion(f32[8192]{0:T(1024)S(1)} %bitcast.86, s32[6144]{0:T(1024)S(1)} %get-tuple-element.14), kind=kCustom, calls=%fused_computation.clone | custom fusion | bytes 73728 | tf_op jit(solution)/shard_map/jit(_take)/gather | solution.py:44
  86.8 0.1 broadcast_clamp_fusion
  87.0 180.5 %gather_fusion = f32[32768]{0:T(1024)S(1)} fusion(f32[8192]{0:T(1024)S(1)} %bitcast.87, s32[32768]{0:T(1024)S(1)} %get-tuple-element.8), kind=kCustom, calls=%fused_computation.2 | custom fusion | bytes 393216 | tf_op jit(solution)/shard_map/jit(_take)/gather | solution.py:45
  267.6 0.1 fusion.10
  267.7 0.9 multiply_reduce_fusion.1
  268.5 42.8 %scatter_custom_fusion = f32[8192]{0:T(1024)S(1)} fusion(s32[6144]{0:T(1024)S(1)} %get-tuple-element.15, f32[6144]{0:T(1024)S(1)} %bitcast.99, f32[]{:T(128)} %constant.15.clone.1), kind=kCustom, calls=%fused_computation.36 | custom fusion | flops 6144 | bytes 32772 | tf_op jit(solution)/shard_map/scatter-add | solution.py:58
  311.4 42.9 %scatter_fusion = f32[8192]{0:T(1024)S(1)} fusion(f32[8192]{0:T(1024)S(1)} %scatter_custom_fusion, s32[6144]{0:T(1024)S(1)} %get-tuple-element.13, f32[6144]{0:T(1024)S(1)} %bitcast.94), kind=kCustom, calls=%fused_computation.4 | custom fusion | flops 6144 | bytes 98304 | tf_op jit(solution)/shard_map/scatter-add | solution.py:60
  354.4 0.1 collective-permute-start.1
  354.5 591.5 %all-reduce.3.cloned.1.call-done = f32[1,32768]{1,0:T(1,128)} async-done(((f32[1,32768]{1,0:T(1,128)}), f32[1,32768]{1,0:T(1,128)}) %all-reduce.3.cloned.1.call-update) | async-done | bytes 131088 | tf_op jit(solution)/shard_map/psum | solution.py:53
  946.1 1.9 multiply_reduce_fusion
  948.0 225.9 %scatter_fusion.1 = f32[8192]{0:T(1024)S(1)} fusion(f32[8192]{0:T(1024)S(1)} %scatter_fusion, s32[32768]{0:T(1024)S(1)} %get-tuple-element.9, f32[32768]{0:T(1024)S(1)} %bitcast.91), kind=kCustom, calls=%fused_computation.5 | custom fusion | flops 32768 | bytes 524288 | tf_op jit(solution)/shard_map/scatter-add | solution.py:60
  1173.9 6.4 copy.18
  1180.3 0.6 multiply_reduce_fusion.3
  1182.2 60.7 %reduce-scatter.4.cloned.1.call-done = f32[4096,1]{1,0:T(8,128)} async-done(((f32[8192,1]{1,0:T(8,128)}), f32[4096,1]{1,0:T(8,128)}) %reduce-scatter.4.cloned.1.call-update) | async-done | bytes 16400
  1242.9 4.4 copy.19
  1247.4 0.1 fusion.5
  1247.4 0.7 multiply_reduce_fusion.2
  1249.5 76.6 %all-reduce = (f32[1]{0:T(128)}, f32[1]{0:T(128)}) all-reduce(f32[1]{0:T(128)} %bitcast.2, f32[1]{0:T(128)} %bitcast.31), channel_id=1, replica_groups=mesh['tm'=128,'net'=2] {'tm','net'}, use_global_device_ids=true, to_apply=%region_2.3 | all-reduce | flops 2 | bytes 16 | tf_op jit(solution)/shard_map/psum | solution.py:76
  1327.5 0.7 multiply_subtract_fusion.1
  1328.1 0.8 multiply_subtract_fusion
  (34 shorter events, 0.2 us)
Async XLA Ops:
  7.2 938.9 %all-reduce.3.cloned.1.call-start = ((), (), s32[]{:S(2)}) async-start(), calls=%async_computation.1 | async-start | bytes 262144 | tf_op jit(solution)/shard_map/psum | solution.py:53
  9.0 1233.9 %reduce-scatter.4.cloned.1.call-start = ((), (), s32[]{:S(2)}) async-start(), calls=%async_computation.2 | async-start | bytes 6291456
  9.9 344.4 %collective-permute-start = (f32[1,1,4096]{2,1,0:T(1,128)S(1)}, f32[1,1,4096]{2,1,0:T(1,128)S(1)}, u32[]{:S(2)}, u32[]{:S(2)}) collective-permute-start(f32[1,1,4096]{2,1,0:T(1,128)S(1)} %get-tuple-element.19), channel_id=1, source_target_pairs={{0,254},{2,0},{4,2},{6,4},{8,6},{10,8},{12,10},{14,12},{16,14},{18... | collective-permute-start | bytes 49160 | tf_op jit(solution)/shard_map/ppermute | solution.py:15
  18.1 34.3 %copy-start.10 = (s32[6144]{0:T(1024)S(1)}, s32[6144]{0:T(1024)}, u32[]{:S(2)}) copy-start(s32[6144]{0:T(1024)} %param.30) | copy-start | bytes 73732
  52.5 34.3 %copy-start.12 = (s32[256]{0:T(256)S(1)}, s32[256]{0:T(256)}, u32[]{:S(2)}) copy-start(s32[256]{0:T(256)} %param.32) | copy-start | bytes 3076
  52.5 34.3 %copy-start.4 = (s32[32768]{0:T(1024)S(1)}, s32[32768]{0:T(1024)}, u32[]{:S(2)}) copy-start(s32[32768]{0:T(1024)} %param.33) | copy-start | bytes 393220
  86.9 180.6 %copy-start.11 = (f32[1,6144]{1,0:T(1,128)S(1)}, f32[1,6144]{1,0:T(1,128)}, u32[]{:S(2)}) copy-start(f32[1,6144]{1,0:T(1,128)} %param.22) | copy-start | bytes 73732
  87.0 180.7 %copy-start = (f32[1,1,32768]{2,1,0:T(1,128)S(1)}, f32[1,1,32768]{2,1,0:T(1,128)}, u32[]{:S(2)}) copy-start(f32[1,1,32768]{2,1,0:T(1,128)} %param.21) | copy-start | bytes 393220
  311.4 43.0 %copy-start.3 = (f32[1,1,2,4096]{3,2,1,0:T(2,128)S(1)}, f32[1,1,2,4096]{3,2,1,0:T(2,128)}, u32[]{:S(2)}) copy-start(f32[1,1,2,4096]{3,2,1,0:T(2,128)} %param.18) | copy-start | bytes 98308
  311.4 43.0 %copy-start.8 = (f32[4096]{0:T(1024)S(1)}, f32[4096]{0:T(1024)}, u32[]{:S(2)}) copy-start(f32[4096]{0:T(1024)} %param.27) | copy-start | bytes 49156
  311.4 43.0 %copy-start.9 = (f32[1,2,4096]{2,1,0:T(2,128)S(1)}, f32[1,2,4096]{2,1,0:T(2,128)}, u32[]{:S(2)}) copy-start(f32[1,2,4096]{2,1,0:T(2,128)} %param.24) | copy-start | bytes 98308
  311.4 634.7 %copy-start.1 = (f32[1,1,32768]{2,1,0:T(1,128)S(1)}, f32[1,1,32768]{2,1,0:T(1,128)}, u32[]{:S(2)}) copy-start(f32[1,1,32768]{2,1,0:T(1,128)} %param.19) | copy-start | bytes 393220
  311.4 634.6 %copy-start.2 = (f32[1,32768]{1,0:T(1,128)S(1)}, f32[1,32768]{1,0:T(1,128)}, u32[]{:S(2)}) copy-start(f32[1,32768]{1,0:T(1,128)} %param.26) | copy-start | bytes 393220
  311.4 634.6 %copy-start.6 = (f32[32768]{0:T(1024)S(1)}, f32[32768]{0:T(1024)}, u32[]{:S(2)}) copy-start(f32[32768]{0:T(1024)} %param.25) | copy-start | bytes 393220
  311.4 634.6 %copy-start.7 = (f32[1,32768]{1,0:T(1,128)S(1)}, f32[1,32768]{1,0:T(1,128)}, u32[]{:S(2)}) copy-start(f32[1,32768]{1,0:T(1,128)} %param.23) | copy-start | bytes 393220
  354.4 892.9 %collective-permute-start.1 = (f32[1,1,4096]{2,1,0:T(1,128)S(1)}, f32[1,1,4096]{2,1,0:T(1,128)S(1)}, u32[]{:S(2)}, u32[]{:S(2)}) collective-permute-start(f32[1,1,4096]{2,1,0:T(1,128)S(1)} %subtract_multiply_fusion), channel_id=1, source_target_pairs={{0,2},{2,4},{4,6},{6,8},{8,10},{10,12},{12,14},{14,16},{16,18},{18... | collective-permute-start | bytes 49160 | tf_op jit(solution)/shard_map/ppermute | solution.py:15
  1173.9 6.4 copy-start.5
Sparse Core Ops, SparseCore 0:
  11.2 934.8 all-reduce.2
  1180.5 62.4 reduce-scatter.3
where the time goes:
time: 1340 us
  waiting for transfers between devices  652 us (49%)
  other arithmetic  322 us (24%)
  local copies, waits for them, and re-layouts  261 us (19%)
  blocking collectives  82.6 us (6%)
  between operations  18.3 us (1%)
    psum x1, waiting for transfers between devices, body(): capacity_value = lax.psum(partial_sums, 'tm')  592 us
    scatter-add x2, other arithmetic, body(): bus_terms.at[:, :, target].add(-flow_scaled).at[:, :, column_bus]  269 us
    gather x1, local copies, waits for them, and re-layouts, body(): dispatch_value = jnp.take(network, column_bus, axis=2) + direction_capacity  181 us
    psum x1, blocking collectives, body(): lax.psum((squares_local, curvature_local), ('tm', 'net'))  76.6 us
    unnamed x3, waiting for transfers between devices  60.8 us
    scatter-add x1, other arithmetic, body(): jnp.zeros(network.shape, jnp.float32).at[:, :, anchor].add(flow_scaled)  42.8 us
    gather x1, local copies, waits for them, and re-layouts, body(): jnp.take(network, target, axis=2)  34.3 us
    gather x1, local copies, waits for them, and re-layouts, body(): jnp.take(network, anchor, axis=2) - jnp.take(network, target, axis=2)  34.3 us
  transfers between devices with their start and end apart: 4, of which 2 were waited for; matrix products, arithmetic and copies ran while one was open for 43% of the time, Pallas kernels for 0%

commit v1 on v0

v1 whole, which is shorter than its diff:
```python
import jax
import jax.numpy as jnp
from jax import lax
from jax.sharding import PartitionSpec as P

BLOCK = 128


DAMPING = 0.5


def passed_along(value, axis, steps):
    count = lax.axis_size(axis)
    pairs = [(source, (source + steps) % count) for source in range(count)]
    return lax.ppermute(value, axis, pairs)


def butterfly_sum(value, axis):
    count = lax.axis_size(axis)
    if count & (count - 1):
        return lax.psum(value, axis)
    step = 1
    while step < count:
        pairs = [(source, source ^ step) for source in range(count)]
        value = value + lax.ppermute(value, axis, pairs)
        step *= 2
    return value


def within_block_onehot(rows):
    picked = rows.reshape(-1, BLOCK)
    return picked[:, :, None] == jnp.arange(BLOCK, dtype=rows.dtype)[None, None, :]


def gather_blocks(table, blocks, onehot):
    lead = table.shape[:-1]
    tiled = table.reshape(lead + (-1, BLOCK))
    picked = jnp.take(tiled, blocks, axis=-2)
    values = jnp.sum(jnp.where(onehot, picked[..., :, None, :], 0.0), axis=-1)
    return values.reshape(lead + (-1,))


def scatter_blocks(values, blocks, onehot, count):
    lead = values.shape[:-1]
    tiled = values.reshape(lead + (-1, BLOCK))
    within = jnp.sum(jnp.where(onehot, tiled[..., :, :, None], 0.0), axis=-2)
    out = jnp.zeros(lead + (count, BLOCK), values.dtype)
    out = out.at[..., blocks, :].add(within)
    return out.reshape(lead + (-1,))


def body(
    direction_nodal,
    direction_capacity,
    residual_nodal,
    residual_capacity,
    scale_flow,
    scale_dispatch,
    scale_storage,
    scale_capacity,
    availability,
    retention,
    line_anchor,
    line_target,
    anchor_rows,
    target_rows,
    column_block,
    column_rows,
):
    net_count = lax.axis_size("net")
    net_index = lax.axis_index("net")
    lines = anchor_rows.shape[0]

    partial_sums = -jnp.sum(availability[None] * direction_capacity, axis=1)
    capacity_value = butterfly_sum(partial_sums, "tm")

    balance = direction_nodal[:, :, 0, :]
    storage = direction_nodal[:, :, 1, :]
    buses = balance.shape[-1] * net_count
    if net_count == 2:
        other = lax.ppermute(balance, "net", [(0, 1), (1, 0)])
        network = jnp.where(
            net_index == 0,
            jnp.concatenate([balance, other], axis=-1),
            jnp.concatenate([other, balance], axis=-1),
        )
    else:
        network = lax.all_gather(balance, "net", axis=2, tiled=True)

    blocks = jnp.concatenate([line_anchor, line_target, column_block])
    onehot = within_block_onehot(jnp.concatenate([anchor_rows, target_rows, column_rows]))
    gathered = gather_blocks(network, blocks, onehot)
    flow_value = gathered[..., :lines] - gathered[..., lines : 2 * lines]
    dispatch_value = gathered[..., 2 * lines :] + direction_capacity

    next_first = passed_along(storage[:, :1], "tm", -1)
    storage_next = jnp.concatenate([storage[:, 1:, :], next_first], axis=1)
    level_value = storage - retention * storage_next
    charge_value = balance - storage
    flow_scaled = scale_flow[None] * flow_value
    dispatch_scaled = scale_dispatch[None] * dispatch_value
    level_scaled = scale_storage[None, :, 0, :] * level_value
    charge_scaled = scale_storage[None, :, 1, :] * charge_value
    capacity_scaled = scale_capacity[None] * capacity_value
    squares_local = jnp.sum(residual_nodal * residual_nodal, axis=(1, 2, 3)) + jnp.sum(
        residual_capacity * residual_capacity, axis=(1, 2)
    )

    bus_terms = scatter_blocks(
        jnp.concatenate([flow_scaled, -flow_scaled, dispatch_scaled], axis=-1),
        blocks,
        onehot,
        buses // BLOCK,
    )
    if net_count == 2:
        half = buses // 2
        mine = lax.dynamic_slice_in_dim(bus_terms, net_index * half, half, axis=-1)
        theirs = lax.dynamic_slice_in_dim(bus_terms, (1 - net_index) * half, half, axis=-1)
        own_terms = mine + lax.ppermute(theirs, "net", [(0, 1), (1, 0)])
    else:
        own_terms = lax.psum_scatter(bus_terms, "net", scatter_dimension=2, tiled=True)
    image_balance = own_terms + charge_scaled + DAMPING * balance
    behind = passed_along(level_scaled[:, -1:], "tm", 1)
    level_before = jnp.concatenate([behind, level_scaled[:, :-1, :]], axis=1)
    image_storage = level_scaled - retention * level_before - charge_scaled + DAMPING * storage
    image_limit = (
        dispatch_scaled
        - availability[None] * capacity_scaled[:, None, :]
        + DAMPING * direction_capacity
    )
    image_nodal = jnp.stack([image_balance, image_storage], axis=2)
    curvature_local = jnp.sum(direction_nodal * image_nodal, axis=(1, 2, 3)) + jnp.sum(
        direction_capacity * image_limit, axis=(1, 2)
    )
    totals = butterfly_sum(jnp.stack([squares_local, curvature_local]), "tm")
    totals = butterfly_sum(totals, "net")
    step_size = totals[0] / totals[1]
    updated_nodal = residual_nodal - step_size[:, None, None, None] * image_nodal
    updated_capacity = residual_capacity - step_size[:, None, None] * image_limit
    return (updated_nodal, updated_capacity)


def solution(mesh):
    in_specs = (
        P(None, "tm", None, "net"),
        P(None, "tm", "net"),
        P(None, "tm", None, "net"),
        P(None, "tm", "net"),
        P("tm", "net"),
        P("tm", "net"),
        P("tm", None, "net"),
        P("net"),
        P("tm", "net"),
        P("net"),
        P("net"),
        P("net"),
        P("net"),
        P("net"),
        P("net"),
        P("net"),
    )
    out_specs = (P(None, "tm", None, "net"), P(None, "tm", "net"))
    return jax.shard_map(body, mesh=mesh, in_specs=in_specs, out_specs=out_specs, check_vma=False)
```

time: 1340 us -> 127 us (0.09)
  waiting for transfers between devices: 652 us -> 60.1 us
  other arithmetic: 322 us -> 40.5 us
  local copies, waits for them, and re-layouts: 261 us -> 1.75 us
  blocking collectives: 82.6 us -> 0 us
  starting transfers between devices: 0.25 us -> 19.7 us
    psum x1 -> x0, waiting for transfers between devices: 592 us -> none  [body(): capacity_value = lax.psum(partial_sums, 'tm')]
    scatter-add x3 -> x1, other arithmetic: 312 us -> 1.75 us  [scatter_blocks(): out = out.at[..., blocks, :].add(within)]
    gather x3 -> x1, local copies, waits for them, and re-layouts: 249 us -> 1.1 us  [gather_blocks(): picked = jnp.take(tiled, blocks, axis=-2)]
    psum x1 -> x0, blocking collectives: 76.6 us -> none  [body(): lax.psum((squares_local, curvature_local), ('tm', 'net'))]
    unnamed x3 -> x0, waiting for transfers between devices: 60.8 us -> none
    ppermute x0 -> x17, waiting for transfers between devices: none -> 60.1 us  [the longest x15 57.1 us: butterfly_sum(): value = value + lax.ppermute(value, axis, pairs)]
    reduce_sum x0 -> x2, other arithmetic: none -> 31.4 us  [the longest x1 16.3 us: gather_blocks(): values = jnp.sum(jnp.where(onehot, picked[..., :, None, :], 0.0), axis=-1)]
    ppermute x0 -> x17, starting transfers between devices: none -> 19.3 us  [the longest x15 15.6 us: butterfly_sum(): value = value + lax.ppermute(value, axis, pairs)]
  transfers between devices with their start and end apart: 4 -> 19, of which waited for: 2 -> 14; matrix products, arithmetic and copies ran while one was open for 43% -> 30% of each run, Pallas kernels for 0% -> 0%
where the time goes in v1:
time: 127 us
  waiting for transfers between devices  60.1 us (47%)
  other arithmetic  40.5 us (32%)
  starting transfers between devices  19.7 us (16%)
  between operations  4.95 us (4%)
  local copies, waits for them, and re-layouts  1.75 us (1%)
    ppermute x15, waiting for transfers between devices, butterfly_sum(): value = value + lax.ppermute(value, axis, pairs)  57.1 us
    reduce_sum x1, other arithmetic, gather_blocks(): values = jnp.sum(jnp.where(onehot, picked[..., :, None, :], 0.0), axis=-1)  16.3 us
    ppermute x15, starting transfers between devices, butterfly_sum(): value = value + lax.ppermute(value, axis, pairs)  15.6 us
    reduce_sum x1, other arithmetic, scatter_blocks(): within = jnp.sum(jnp.where(onehot, tiled[..., :, :, None], 0.0), axis=-2)  15.1 us
    ppermute x1, starting transfers between devices, body(): other = lax.ppermute(balance, 'net', [(0, 1), (1, 0)])  3.28 us
    ppermute x1, waiting for transfers between devices, body(): own_terms = mine + lax.ppermute(theirs, 'net', [(0, 1), (1, 0)])  2.99 us
  transfers between devices with their start and end apart: 19, of which 14 were waited for; matrix products, arithmetic and copies ran while one was open for 30% of the time, Pallas kernels for 0%

profile of v1, /device:TPU:2, one launch (start us, length us, event | category | flops | bytes accessed | tf_op | source)
XLA Modules:
  0.0 127.0 jit_solution(10438033500902192087)
XLA Ops:
  0.6 1.1 fusion.4
  1.9 3.3 %collective-permute-start = (f32[1,1,4096]{2,1,0:T(1,128)S(1)}, f32[1,1,4096]{2,1,0:T(1,128)S(1)}, u32[]{:S(2)}, u32[]{:S(2)}) collective-permute-start(f32[1,1,4096]{2,1,0:T(1,128)S(1)} %get-tuple-element.10), channel_id=1, source_target_pairs={{0,1},{1,0},{2,3},{3,2},{4,5},{5,4},{6,7},{7,6},{8,9},{9,8},{10,11... | collective-permute-start | bytes 49160 | tf_op jit(solution)/shard_map/ppermute | solution.py:81
  5.8 8.3 %collective-permute-start.5 = (f32[1,32768]{1,0:T(1,128)S(1)}, f32[1,32768]{1,0:T(1,128)S(1)}, u32[]{:S(2)}, u32[]{:S(2)}) collective-permute-start(f32[1,32768]{1,0:T(1,128)S(1)} %add.114), channel_id=1, source_target_pairs={{0,4},{2,6},{4,0},{6,2},{8,12},{10,14},{12,8},{14,10},{16,20},{18,... | collective-permute-start | bytes 393224 | tf_op jit(solution)/shard_map/ppermute | solution.py:25
  14.2 0.9 multiply_reduce_fusion.1
  15.1 3.2 %collective-permute-done.5 = f32[1,32768]{1,0:T(1,128)S(1)} collective-permute-done((f32[1,32768]{1,0:T(1,128)S(1)}, f32[1,32768]{1,0:T(1,128)S(1)}, u32[]{:S(2)}, u32[]{:S(2)}) %collective-permute-start.5) | collective-permute-done | bytes 131104 | tf_op jit(solution)/shard_map/ppermute | solution.py:25
  18.6 6.4 %collective-permute-done.6 = f32[1,32768]{1,0:T(1,128)S(1)} collective-permute-done((f32[1,32768]{1,0:T(1,128)S(1)}, f32[1,32768]{1,0:T(1,128)S(1)}, u32[]{:S(2)}, u32[]{:S(2)}) %collective-permute-start.6) | collective-permute-done | bytes 131104 | tf_op jit(solution)/shard_map/ppermute | solution.py:25
  25.4 1.1 gather_fusion
  26.5 3.6 %collective-permute-done.7 = f32[1,32768]{1,0:T(1,128)S(1)} collective-permute-done((f32[1,32768]{1,0:T(1,128)S(1)}, f32[1,32768]{1,0:T(1,128)S(1)}, u32[]{:S(2)}, u32[]{:S(2)}) %collective-permute-start.7) | collective-permute-done | bytes 131104 | tf_op jit(solution)/shard_map/ppermute | solution.py:25
  30.5 6.2 %collective-permute-done.8 = f32[1,32768]{1,0:T(1,128)S(1)} collective-permute-done((f32[1,32768]{1,0:T(1,128)S(1)}, f32[1,32768]{1,0:T(1,128)S(1)}, u32[]{:S(2)}, u32[]{:S(2)}) %collective-permute-start.8) | collective-permute-done | bytes 131104 | tf_op jit(solution)/shard_map/ppermute | solution.py:25
  36.9 16.3 %select_reduce_fusion.1 = f32[352,128]{1,0:T(8,128)S(1)} fusion(f32[352,128]{1,0:T(8,128)S(1)} %broadcast_select_fusion, s32[352,128]{1,0:T(8,128)S(1)} %add_bitcast_fusion), kind=kLoop, calls=%fused_computation.3 | loop fusion | flops 17256448 | bytes 540672 | tf_op jit(solution)/shard_map/reduce_sum | solution.py:39
  53.4 1.2 collective-permute-start.10
  54.7 8.5 %collective-permute-done.10 = f32[1,32768]{1,0:T(1,128)S(1)} collective-permute-done((f32[1,32768]{1,0:T(1,128)S(1)}, f32[1,32768]{1,0:T(1,128)S(1)}, u32[]{:S(2)}, u32[]{:S(2)}) %collective-permute-start.10) | collective-permute-done | bytes 131104 | tf_op jit(solution)/shard_map/ppermute | solution.py:25
  63.2 1.1 multiply_reduce_fusion
  64.4 15.1 %select_reduce_fusion = f32[352,128]{1,0:T(8,128)S(1)} fusion(f32[352,128]{1,0:T(8,128)S(1)} %bitcast.62, s32[352,128]{1,0:T(8,128)S(1)} %add_bitcast_fusion), kind=kLoop, calls=%fused_computation.2 | loop fusion | flops 17256448 | bytes 540672 | tf_op jit(solution)/shard_map/reduce_sum | solution.py:46
  79.5 1.7 %scatter_custom_fusion = f32[64,128]{1,0:T(8,128)S(1)} fusion(s32[352]{0:T(512)S(1)} %fusion.9, f32[352,128]{1,0:T(8,128)S(1)} %select_reduce_fusion, f32[]{:T(128)} %constant.10.clone.1), kind=kCustom, calls=%fused_computation.27 | custom fusion | flops 45056 | bytes 32772 | tf_op jit(solution)/shard_map/scatter-add | solution.py:48
  81.7 0.6 multiply_reduce_fusion.3
  83.7 3.0 %collective-permute-done.1 = f32[1,1,4096]{2,1,0:T(1,128)S(1)} collective-permute-done((f32[1,1,4096]{2,1,0:T(1,128)S(1)}, f32[1,1,4096]{2,1,0:T(1,128)S(1)}, u32[]{:S(2)}, u32[]{:S(2)}) %collective-permute-start.1) | collective-permute-done | bytes 16416 | tf_op jit(solution)/shard_map/ppermute | solution.py:119
  86.7 0.6 multiply_reduce_fusion.2
  89.0 1.1 collective-permute-done.11
  90.1 0.4 collective-permute-start.12
  90.5 3.2 %collective-permute-done.12 = f32[2,1]{1,0:T(2,128)S(1)} collective-permute-done((f32[2,1]{1,0:T(2,128)S(1)}, f32[2,1]{1,0:T(2,128)S(1)}, u32[]{:S(2)}, u32[]{:S(2)}) %collective-permute-start.12) | collective-permute-done | bytes 40 | tf_op jit(solution)/shard_map/ppermute | solution.py:25
  93.8 1.0 collective-permute-start.13
  94.8 4.2 %collective-permute-done.13 = f32[2,1]{1,0:T(2,128)S(1)} collective-permute-done((f32[2,1]{1,0:T(2,128)S(1)}, f32[2,1]{1,0:T(2,128)S(1)}, u32[]{:S(2)}, u32[]{:S(2)}) %collective-permute-start.13) | collective-permute-done | bytes 40 | tf_op jit(solution)/shard_map/ppermute | solution.py:25
  98.9 3.6 %collective-permute-done.14 = f32[2,1]{1,0:T(2,128)S(1)} collective-permute-done((f32[2,1]{1,0:T(2,128)S(1)}, f32[2,1]{1,0:T(2,128)S(1)}, u32[]{:S(2)}, u32[]{:S(2)}) %collective-permute-start.14) | collective-permute-done | bytes 40 | tf_op jit(solution)/shard_map/ppermute | solution.py:25
  102.5 3.6 %collective-permute-done.15 = f32[2,1]{1,0:T(2,128)S(1)} collective-permute-done((f32[2,1]{1,0:T(2,128)S(1)}, f32[2,1]{1,0:T(2,128)S(1)}, u32[]{:S(2)}, u32[]{:S(2)}) %collective-permute-start.15) | collective-permute-done | bytes 40 | tf_op jit(solution)/shard_map/ppermute | solution.py:25
  106.1 3.5 %collective-permute-start.16 = (f32[2,1]{1,0:T(2,128)S(1)}, f32[2,1]{1,0:T(2,128)S(1)}, u32[]{:S(2)}, u32[]{:S(2)}) collective-permute-start(f32[2,1]{1,0:T(2,128)S(1)} %add.127), channel_id=1, source_target_pairs={{0,64},{2,66},{4,68},{6,70},{8,72},{10,74},{12,76},{14,78},{16,80}... | collective-permute-start | bytes 32 | tf_op jit(solution)/shard_map/ppermute | solution.py:25
  109.5 1.5 %collective-permute-done.16 = f32[2,1]{1,0:T(2,128)S(1)} collective-permute-done((f32[2,1]{1,0:T(2,128)S(1)}, f32[2,1]{1,0:T(2,128)S(1)}, u32[]{:S(2)}, u32[]{:S(2)}) %collective-permute-start.16) | collective-permute-done | bytes 40 | tf_op jit(solution)/shard_map/ppermute | solution.py:25
  111.3 7.3 %collective-permute-done.17 = f32[2,1]{1,0:T(2,128)S(1)} collective-permute-done((f32[2,1]{1,0:T(2,128)S(1)}, f32[2,1]{1,0:T(2,128)S(1)}, u32[]{:S(2)}, u32[]{:S(2)}) %collective-permute-start.17) | collective-permute-done | bytes 40 | tf_op jit(solution)/shard_map/ppermute | solution.py:25
  118.8 4.8 %collective-permute-done.18 = f32[2,1]{1,0:T(2,128)S(1)} collective-permute-done((f32[2,1]{1,0:T(2,128)S(1)}, f32[2,1]{1,0:T(2,128)S(1)}, u32[]{:S(2)}, u32[]{:S(2)}) %collective-permute-start.18) | collective-permute-done | bytes 40 | tf_op jit(solution)/shard_map/ppermute | solution.py:25
  123.6 0.5 fusion.16
  125.5 0.7 multiply_subtract_fusion.1
  126.2 0.8 multiply_subtract_fusion
  (77 shorter events, 3.7 us)
Async XLA Ops:
  1.8 3.8 %collective-permute-start.4 = (f32[1,32768]{1,0:T(1,128)S(1)}, f32[1,32768]{1,0:T(1,128)S(1)}, u32[]{:S(2)}, u32[]{:S(2)}) collective-permute-start(f32[1,32768]{1,0:T(1,128)S(1)} %fusion.4), channel_id=1, source_target_pairs={{0,2},{2,0},{4,6},{6,4},{8,10},{10,8},{12,14},{14,12},{16,18},{18,... | collective-permute-start | bytes 393224 | tf_op jit(solution)/shard_map/ppermute | solution.py:25
  1.9 23.4 %collective-permute-start = (f32[1,1,4096]{2,1,0:T(1,128)S(1)}, f32[1,1,4096]{2,1,0:T(1,128)S(1)}, u32[]{:S(2)}, u32[]{:S(2)}) collective-permute-start(f32[1,1,4096]{2,1,0:T(1,128)S(1)} %get-tuple-element.10), channel_id=1, source_target_pairs={{0,1},{1,0},{2,3},{3,2},{4,5},{5,4},{6,7},{7,6},{8,9},{9,8},{10,11... | collective-permute-start | bytes 49160 | tf_op jit(solution)/shard_map/ppermute | solution.py:81
  5.2 8.8 %copy-start.7 = (s32[32768]{0:T(1024)S(1)}, s32[32768]{0:T(1024)}, u32[]{:S(2)}) copy-start(s32[32768]{0:T(1024)} %param.31) | copy-start | bytes 393220
  5.2 8.8 %copy-start.10 = (s32[6144]{0:T(1024)S(1)}, s32[6144]{0:T(1024)}, u32[]{:S(2)}) copy-start(s32[6144]{0:T(1024)} %param.29) | copy-start | bytes 73732
  5.2 8.8 %copy-start.11 = (s32[6144]{0:T(1024)S(1)}, s32[6144]{0:T(1024)}, u32[]{:S(2)}) copy-start(s32[6144]{0:T(1024)} %param.28) | copy-start | bytes 73732
  5.2 20.0 %collective-permute-start.2 = (f32[1,1,4096]{2,1,0:T(1,128)S(1)}, f32[1,1,4096]{2,1,0:T(1,128)S(1)}, u32[]{:S(2)}, u32[]{:S(2)}) collective-permute-start(f32[1,1,4096]{2,1,0:T(1,128)S(1)} %get-tuple-element.11), channel_id=1, source_target_pairs={{0,254},{2,0},{4,2},{6,4},{8,6},{10,8},{12,10},{14,12},{16,14},{18... | collective-permute-start | bytes 49160 | tf_op jit(solution)/shard_map/ppermute | solution.py:15
  5.7 8.3 %copy-start.13 = (s32[256]{0:T(256)S(1)}, s32[256]{0:T(256)}, u32[]{:S(2)}) copy-start(s32[256]{0:T(256)} %param.30) | copy-start | bytes 3076
  5.7 8.3 %copy-start.14 = (s32[48]{0:T(128)S(1)}, s32[48]{0:T(128)}, u32[]{:S(2)}) copy-start(s32[48]{0:T(128)} %param.27) | copy-start | bytes 580
  5.7 8.3 %copy-start.15 = (s32[48]{0:T(128)S(1)}, s32[48]{0:T(128)}, u32[]{:S(2)}) copy-start(s32[48]{0:T(128)} %param.26) | copy-start | bytes 580
  5.7 8.4 %copy-start.2 = (f32[1,1,32768]{2,1,0:T(1,128)S(1)}, f32[1,1,32768]{2,1,0:T(1,128)}, u32[]{:S(2)}) copy-start(f32[1,1,32768]{2,1,0:T(1,128)} %param.19) | copy-start | bytes 393220
  5.8 12.5 %collective-permute-start.5 = (f32[1,32768]{1,0:T(1,128)S(1)}, f32[1,32768]{1,0:T(1,128)S(1)}, u32[]{:S(2)}, u32[]{:S(2)}) collective-permute-start(f32[1,32768]{1,0:T(1,128)S(1)} %add.114), channel_id=1, source_target_pairs={{0,4},{2,6},{4,0},{6,2},{8,12},{10,14},{12,8},{14,10},{16,20},{18,... | collective-permute-start | bytes 393224 | tf_op jit(solution)/shard_map/ppermute | solution.py:25
  18.4 6.6 %collective-permute-start.6 = (f32[1,32768]{1,0:T(1,128)S(1)}, f32[1,32768]{1,0:T(1,128)S(1)}, u32[]{:S(2)}, u32[]{:S(2)}) collective-permute-start(f32[1,32768]{1,0:T(1,128)S(1)} %add.115), channel_id=1, source_target_pairs={{0,8},{2,10},{4,12},{6,14},{8,0},{10,2},{12,4},{14,6},{16,24},{18,... | collective-permute-start | bytes 393224 | tf_op jit(solution)/shard_map/ppermute | solution.py:25
  25.1 5.1 %collective-permute-start.7 = (f32[1,32768]{1,0:T(1,128)S(1)}, f32[1,32768]{1,0:T(1,128)S(1)}, u32[]{:S(2)}, u32[]{:S(2)}) collective-permute-start(f32[1,32768]{1,0:T(1,128)S(1)} %add.116), channel_id=1, source_target_pairs={{0,16},{2,18},{4,20},{6,22},{8,24},{10,26},{12,28},{14,30},{16,0},... | collective-permute-start | bytes 393224 | tf_op jit(solution)/shard_map/ppermute | solution.py:25
  25.3 58.4 %collective-permute-start.3 = (f32[1,1,4096]{2,1,0:T(1,128)S(1)}, f32[1,1,4096]{2,1,0:T(1,128)S(1)}, u32[]{:S(2)}, u32[]{:S(2)}) collective-permute-start(f32[1,1,4096]{2,1,0:T(1,128)S(1)} %subtract_multiply_fusion), channel_id=1, source_target_pairs={{0,2},{2,4},{4,6},{6,8},{8,10},{10,12},{12,14},{14,16},{16,18},{18... | collective-permute-start | bytes 49160 | tf_op jit(solution)/shard_map/ppermute | solution.py:15
  30.3 6.4 %collective-permute-start.8 = (f32[1,32768]{1,0:T(1,128)S(1)}, f32[1,32768]{1,0:T(1,128)S(1)}, u32[]{:S(2)}, u32[]{:S(2)}) collective-permute-start(f32[1,32768]{1,0:T(1,128)S(1)} %add.117), channel_id=1, source_target_pairs={{0,32},{2,34},{4,36},{6,38},{8,40},{10,42},{12,44},{14,46},{16,48}... | collective-permute-start | bytes 393224 | tf_op jit(solution)/shard_map/ppermute | solution.py:25
  36.8 16.5 %collective-permute-start.9 = (f32[1,32768]{1,0:T(1,128)S(1)}, f32[1,32768]{1,0:T(1,128)S(1)}, u32[]{:S(2)}, u32[]{:S(2)}) collective-permute-start(f32[1,32768]{1,0:T(1,128)S(1)} %add.118), channel_id=1, source_target_pairs={{0,64},{2,66},{4,68},{6,70},{8,72},{10,74},{12,76},{14,78},{16,80}... | collective-permute-start | bytes 393224 | tf_op jit(solution)/shard_map/ppermute | solution.py:25
  36.9 17.7 %copy-start.12 = (f32[1,6144]{1,0:T(1,128)S(1)}, f32[1,6144]{1,0:T(1,128)}, u32[]{:S(2)}) copy-start(f32[1,6144]{1,0:T(1,128)} %param.20) | copy-start | bytes 73732
  36.9 26.2 %copy-start.5 = (f32[1,32768]{1,0:T(1,128)S(1)}, f32[1,32768]{1,0:T(1,128)}, u32[]{:S(2)}) copy-start(f32[1,32768]{1,0:T(1,128)} %param.21) | copy-start | bytes 393220
  53.2 9.9 %copy-start = (f32[1,1,32768]{2,1,0:T(1,128)S(1)}, f32[1,1,32768]{2,1,0:T(1,128)}, u32[]{:S(2)}) copy-start(f32[1,1,32768]{2,1,0:T(1,128)} %param.17) | copy-start | bytes 393220
  53.3 9.9 %copy-start.1 = (f32[1,32768]{1,0:T(1,128)S(1)}, f32[1,32768]{1,0:T(1,128)}, u32[]{:S(2)}) copy-start(f32[1,32768]{1,0:T(1,128)} %param.24) | copy-start | bytes 393220
  53.3 9.9 %copy-start.4 = (f32[32768]{0:T(1024)S(1)}, f32[32768]{0:T(1024)}, u32[]{:S(2)}) copy-start(f32[32768]{0:T(1024)} %param.23) | copy-start | bytes 393220
  53.4 9.7 %collective-permute-start.10 = (f32[1,32768]{1,0:T(1,128)S(1)}, f32[1,32768]{1,0:T(1,128)S(1)}, u32[]{:S(2)}, u32[]{:S(2)}) collective-permute-start(f32[1,32768]{1,0:T(1,128)S(1)} %add.119), channel_id=1, source_target_pairs={{0,128},{2,130},{4,132},{6,134},{8,136},{10,138},{12,140},{14,142}... | collective-permute-start | bytes 393224 | tf_op jit(solution)/shard_map/ppermute | solution.py:25
  64.4 17.3 %copy-start.6 = (f32[1,1,2,4096]{3,2,1,0:T(2,128)S(1)}, f32[1,1,2,4096]{3,2,1,0:T(2,128)}, u32[]{:S(2)}) copy-start(f32[1,1,2,4096]{3,2,1,0:T(2,128)} %param.18) | copy-start | bytes 98308
  81.3 5.3 %collective-permute-start.1 = (f32[1,1,4096]{2,1,0:T(1,128)S(1)}, f32[1,1,4096]{2,1,0:T(1,128)S(1)}, u32[]{:S(2)}, u32[]{:S(2)}) collective-permute-start(f32[1,1,4096]{2,1,0:T(1,128)S(1)} %constant_dynamic-slice_fusion), channel_id=1, source_target_pairs={{0,1},{1,0},{2,3},{3,2},{4,5},{5,4},{6,7},{7,6},{8,9},{9,8},{10,11... | collective-permute-start | bytes 49160 | tf_op jit(solution)/shard_map/ppermute | solution.py:119
  88.7 1.4 %collective-permute-start.11 = (f32[2,1]{1,0:T(2,128)S(1)}, f32[2,1]{1,0:T(2,128)S(1)}, u32[]{:S(2)}, u32[]{:S(2)}) collective-permute-start(f32[2,1]{1,0:T(2,128)S(1)} %pad_maximum_fusion.2), channel_id=1, source_target_pairs={{0,2},{2,0},{4,6},{6,4},{8,10},{10,8},{12,14},{14,12},{16,18},{18,... | collective-permute-start | bytes 32 | tf_op jit(solution)/shard_map/ppermute | solution.py:25
  90.1 3.7 %collective-permute-start.12 = (f32[2,1]{1,0:T(2,128)S(1)}, f32[2,1]{1,0:T(2,128)S(1)}, u32[]{:S(2)}, u32[]{:S(2)}) collective-permute-start(f32[2,1]{1,0:T(2,128)S(1)} %fusion.10), channel_id=1, source_target_pairs={{0,4},{2,6},{4,0},{6,2},{8,12},{10,14},{12,8},{14,10},{16,20},{18,... | collective-permute-start | bytes 32 | tf_op jit(solution)/shard_map/ppermute | solution.py:25
  93.8 5.2 %collective-permute-start.13 = (f32[2,1]{1,0:T(2,128)S(1)}, f32[2,1]{1,0:T(2,128)S(1)}, u32[]{:S(2)}, u32[]{:S(2)}) collective-permute-start(f32[2,1]{1,0:T(2,128)S(1)} %fusion.17), channel_id=1, source_target_pairs={{0,8},{2,10},{4,12},{6,14},{8,0},{10,2},{12,4},{14,6},{16,24},{18,... | collective-permute-start | bytes 32 | tf_op jit(solution)/shard_map/ppermute | solution.py:25
  98.9 3.6 %collective-permute-start.14 = (f32[2,1]{1,0:T(2,128)S(1)}, f32[2,1]{1,0:T(2,128)S(1)}, u32[]{:S(2)}, u32[]{:S(2)}) collective-permute-start(f32[2,1]{1,0:T(2,128)S(1)} %add.125), channel_id=1, source_target_pairs={{0,16},{2,18},{4,20},{6,22},{8,24},{10,26},{12,28},{14,30},{16,0},... | collective-permute-start | bytes 32 | tf_op jit(solution)/shard_map/ppermute | solution.py:25
  102.5 3.6 %collective-permute-start.15 = (f32[2,1]{1,0:T(2,128)S(1)}, f32[2,1]{1,0:T(2,128)S(1)}, u32[]{:S(2)}, u32[]{:S(2)}) collective-permute-start(f32[2,1]{1,0:T(2,128)S(1)} %add.126), channel_id=1, source_target_pairs={{0,32},{2,34},{4,36},{6,38},{8,40},{10,42},{12,44},{14,46},{16,48}... | collective-permute-start | bytes 32 | tf_op jit(solution)/shard_map/ppermute | solution.py:25
  106.1 5.0 %collective-permute-start.16 = (f32[2,1]{1,0:T(2,128)S(1)}, f32[2,1]{1,0:T(2,128)S(1)}, u32[]{:S(2)}, u32[]{:S(2)}) collective-permute-start(f32[2,1]{1,0:T(2,128)S(1)} %add.127), channel_id=1, source_target_pairs={{0,64},{2,66},{4,68},{6,70},{8,72},{10,74},{12,76},{14,78},{16,80}... | collective-permute-start | bytes 32 | tf_op jit(solution)/shard_map/ppermute | solution.py:25
  111.1 7.5 %collective-permute-start.17 = (f32[2,1]{1,0:T(2,128)S(1)}, f32[2,1]{1,0:T(2,128)S(1)}, u32[]{:S(2)}, u32[]{:S(2)}) collective-permute-start(f32[2,1]{1,0:T(2,128)S(1)} %add.128), channel_id=1, source_target_pairs={{0,128},{2,130},{4,132},{6,134},{8,136},{10,138},{12,140},{14,142}... | collective-permute-start | bytes 32 | tf_op jit(solution)/shard_map/ppermute | solution.py:25
  118.6 5.1 %collective-permute-start.18 = (f32[2,1]{1,0:T(2,128)S(1)}, f32[2,1]{1,0:T(2,128)S(1)}, u32[]{:S(2)}, u32[]{:S(2)}) collective-permute-start(f32[2,1]{1,0:T(2,128)S(1)} %add.129), channel_id=1, source_target_pairs={{0,1},{1,0},{2,3},{3,2},{4,5},{5,4},{6,7},{7,6},{8,9},{9,8},{10,11... | collective-permute-start | bytes 32 | tf_op jit(solution)/shard_map/ppermute | solution.py:25
  (3 other events, 14.5 us)

commit v2 on v1

--- a/solution.py
+++ b/solution.py
@@ -1,6 +1,7 @@
 import jax
 import jax.numpy as jnp
 from jax import lax
+from jax.experimental import pallas as pl
 from jax.sharding import PartitionSpec as P
 
 BLOCK = 128
@@ -27,16 +28,53 @@
     return value
 
 
+def pairwise_total(items):
+    while len(items) > 1:
+        items = [items[i] + items[i + 1] for i in range(0, len(items), 2)]
+    return items[0]
+
+
+def group_sum(value, axis, bits_per_step):
+    count = lax.axis_size(axis)
+    if count & (count - 1):
+        return lax.psum(value, axis)
+    total_bits = count.bit_length() - 1
+    offset = 0
+    while offset < total_bits:
+        bits = min(bits_per_step, total_bits - offset)
+        items = [value]
+        for digit in range(1, 1 << bits):
+            pairs = [(source, source ^ (digit << offset)) for source in range(count)]
+            items.append(lax.ppermute(value, axis, pairs))
+        value = pairwise_total(items)
+        offset += bits
+    return value
+
+
+def lane_gather_kernel(table_ref, index_ref, out_ref):
+    out_ref[...] = jnp.take_along_axis(
+        table_ref[...], index_ref[...], axis=1, mode="promise_in_bounds"
+    )
+
+
+def lane_gather(table, index):
+    return pl.pallas_call(
+        lane_gather_kernel,
+        out_shape=jax.ShapeDtypeStruct(table.shape, table.dtype),
+    )(table, index)
+
+
 def within_block_onehot(rows):
     picked = rows.reshape(-1, BLOCK)
     return picked[:, :, None] == jnp.arange(BLOCK, dtype=rows.dtype)[None, None, :]
 
 
-def gather_blocks(table, blocks, onehot):
+def gather_blocks(table, blocks, rows):
     lead = table.shape[:-1]
     tiled = table.reshape(lead + (-1, BLOCK))
     picked = jnp.take(tiled, blocks, axis=-2)
-    values = jnp.sum(jnp.where(onehot, picked[..., :, None, :], 0.0), axis=-1)
+    index = jnp.broadcast_to(rows.reshape(-1, BLOCK), picked.shape)
+    values = lane_gather(picked.reshape(-1, BLOCK), index.reshape(-1, BLOCK))
     return values.reshape(lead + (-1,))
 
 
@@ -88,8 +126,9 @@
         network = lax.all_gather(balance, "net", axis=2, tiled=True)
 
     blocks = jnp.concatenate([line_anchor, line_target, column_block])
-    onehot = within_block_onehot(jnp.concatenate([anchor_rows, target_rows, column_rows]))
-    gathered = gather_blocks(network, blocks, onehot)
+    rows = jnp.concatenate([anchor_rows, target_rows, column_rows])
+    onehot = within_block_onehot(rows)
+    gathered = gather_blocks(network, blocks, rows)
     flow_value = gathered[..., :lines] - gathered[..., lines : 2 * lines]
     dispatch_value = gathered[..., 2 * lines :] + direction_capacity
 
@@ -130,10 +169,12 @@
     )
     image_nodal = jnp.stack([image_balance, image_storage], axis=2)
     curvature_local = jnp.sum(direction_nodal * image_nodal, axis=(1, 2, 3)) + jnp.sum(
-        direction_capacity * image_limit, axis=(1, 2)
-    )
-    totals = butterfly_sum(jnp.stack([squares_local, curvature_local]), "tm")
-    totals = butterfly_sum(totals, "net")
+        direction_capacity * (dispatch_scaled + DAMPING * direction_capacity), axis=(1, 2)
+    )
+    sums = group_sum(jnp.stack([squares_local, curvature_local]), "tm", 4)
+    capacity_part = jnp.sum(capacity_scaled * capacity_value, axis=1)
+    sums = sums + jnp.stack([jnp.zeros_like(capacity_part), capacity_part])
+    totals = butterfly_sum(sums, "net")
     step_size = totals[0] / totals[1]
     updated_nodal = residual_nodal - step_size[:, None, None, None] * image_nodal
     updated_capacity = residual_capacity - step_size[:, None, None] * image_limit

time: 127 us -> 116 us (0.913)
  the two profiles are of different devices: /device:TPU:2 before, /device:TPU:32 now
where the time goes in v2:
time: 116 us
  starting transfers between devices  59.2 us (51%)
  other arithmetic  29.3 us (25%)
  waiting for transfers between devices  17.7 us (15%)
  between operations  4.87 us (4%)
  local copies, waits for them, and re-layouts  2.57 us (2%)
  Pallas kernels  1.92 us (2%)
    ppermute x22, starting transfers between devices, group_sum(): items.append(lax.ppermute(value, axis, pairs))  36.4 us
    ppermute x8, starting transfers between devices, butterfly_sum(): value = value + lax.ppermute(value, axis, pairs)  16.1 us
    reduce_sum x1, other arithmetic, scatter_blocks(): within = jnp.sum(jnp.where(onehot, tiled[..., :, :, None], 0.0), axis=-2)  15.1 us
    ppermute x8, waiting for transfers between devices, butterfly_sum(): value = value + lax.ppermute(value, axis, pairs)  12.8 us
    ppermute x22, waiting for transfers between devices, group_sum(): items.append(lax.ppermute(value, axis, pairs))  4.83 us
    ppermute x1, starting transfers between devices, body(): other = lax.ppermute(balance, 'net', [(0, 1), (1, 0)])  3.28 us
  transfers between devices with their start and end apart: 34, of which 8 were waited for; matrix products, arithmetic and copies ran while one was open for 24% of the time, Pallas kernels for 2%

profile of v2, /device:TPU:32, one launch (start us, length us, event | category | flops | bytes accessed | tf_op | source)
XLA Modules:
  0.0 115.6 jit_solution(9057401505402735048)
XLA Ops:
  1.5 3.3 %collective-permute-start = (f32[1,1,4096]{2,1,0:T(1,128)S(1)}, f32[1,1,4096]{2,1,0:T(1,128)S(1)}, u32[]{:S(2)}, u32[]{:S(2)}) collective-permute-start(f32[1,1,4096]{2,1,0:T(1,128)S(1)} %get-tuple-element.10), channel_id=1, source_target_pairs={{0,1},{1,0},{2,3},{3,2},{4,5},{5,4},{6,7},{7,6},{8,9},{9,8},{10,11... | collective-permute-start | bytes 49160 | tf_op jit(solution)/shard_map/ppermute | solution.py:119
  4.8 1.6 %collective-permute-start.2 = (f32[1,1,4096]{2,1,0:T(1,128)S(1)}, f32[1,1,4096]{2,1,0:T(1,128)S(1)}, u32[]{:S(2)}, u32[]{:S(2)}) collective-permute-start(f32[1,1,4096]{2,1,0:T(1,128)S(1)} %get-tuple-element.11), channel_id=1, source_target_pairs={{0,254},{2,0},{4,2},{6,4},{8,6},{10,8},{12,10},{14,12},{16,14},{18... | collective-permute-start | bytes 49160 | tf_op jit(solution)/shard_map/ppermute | solution.py:16
  7.2 1.8 %multiply_reduce_fusion.2 = f32[]{:T(128)} fusion(f32[1,1,32768]{2,1,0:T(1,128)} %param.19), kind=kLoop, calls=%fused_computation.17 | loop fusion | flops 65535 | bytes 131076 | tf_op jit(solution)/shard_map/reduce_sum | solution.py:144
  11.7 1.9 %shard_map.167 = f32[352,128]{1,0:T(8,128)} custom-call(f32[352,128]{1,0:T(8,128)} %broadcast_select_fusion.table_ref, s32[352,128]{1,0:T(8,128)} %add_bitcast_fusion.index_ref), custom_call_target="tpu_custom_call" | custom-call | tf_op jit(solution)/shard_map/pallas_call | solution.py:61
  14.5 1.9 %multiply_reduce_fusion.1 = (f32[]{:T(128)}, f32[1,1,32768]{2,1,0:T(1,128)S(1)}, f32[1,32768]{1,0:T(1,128)S(1)}) fusion(f32[1,1,32768]{2,1,0:T(1,128)S(1)} %copy-done.3, f32[1,1,45056]{2,1,0:T(1,128)} %bitcast.65, f32[1,32768]{1,0:T(1,128)S(1)} %copy-done.8, f32[1,32768]{1,0:T(1,128)S(1)} %copy-done.4), kind=kLoop, calls=%fused_computation.16 | loop fusion | flops 262143 | bytes 786436 | tf_op jit(solution)/shard_map/reduce_sum | solution.py:171
  18.0 15.1 %select_reduce_fusion = f32[352,128]{1,0:T(8,128)S(1)} fusion(f32[352,128]{1,0:T(8,128)S(1)} %bitcast.63, s32[352,128]{1,0:T(8,128)S(1)} %copy-done), kind=kLoop, calls=%fused_computation.2 | loop fusion | flops 17256448 | bytes 540672 | tf_op jit(solution)/shard_map/reduce_sum | solution.py:84
  33.1 1.7 %scatter_custom_fusion = f32[64,128]{1,0:T(8,128)S(1)} fusion(s32[352]{0:T(512)S(1)} %fusion.9, f32[352,128]{1,0:T(8,128)S(1)} %select_reduce_fusion, f32[]{:T(128)} %constant.11.clone.1), kind=kCustom, calls=%fused_computation.27 | custom fusion | flops 45056 | bytes 32772 | tf_op jit(solution)/shard_map/scatter-add | solution.py:86
  35.0 2.8 %collective-permute-start.28 = (f32[1,32768]{1,0:T(1,128)S(1)}, f32[1,32768]{1,0:T(1,128)S(1)}, u32[]{:S(2)}, u32[]{:S(2)}) collective-permute-start(f32[1,32768]{1,0:T(1,128)S(1)} %add.190), channel_id=1, source_target_pairs={{0,8},{2,10},{4,12},{6,14},{8,0},{10,2},{12,4},{14,6},{16,24},{18,... | collective-permute-start | bytes 393224 | tf_op jit(solution)/shard_map/ppermute | solution.py:26
  37.9 1.7 %collective-permute-start.1 = (f32[1,1,4096]{2,1,0:T(1,128)S(1)}, f32[1,1,4096]{2,1,0:T(1,128)S(1)}, u32[]{:S(2)}, u32[]{:S(2)}) collective-permute-start(f32[1,1,4096]{2,1,0:T(1,128)S(1)} %constant_dynamic-slice_fusion), channel_id=1, source_target_pairs={{0,1},{1,0},{2,3},{3,2},{4,5},{5,4},{6,7},{7,6},{8,9},{9,8},{10,11... | collective-permute-start | bytes 49160 | tf_op jit(solution)/shard_map/ppermute | solution.py:158
  39.6 2.5 %collective-permute-done.28 = f32[1,32768]{1,0:T(1,128)S(1)} collective-permute-done((f32[1,32768]{1,0:T(1,128)S(1)}, f32[1,32768]{1,0:T(1,128)S(1)}, u32[]{:S(2)}, u32[]{:S(2)}) %collective-permute-start.28) | collective-permute-done | bytes 131104 | tf_op jit(solution)/shard_map/ppermute | solution.py:26
  42.2 1.9 %collective-permute-start.29 = (f32[1,32768]{1,0:T(1,128)S(1)}, f32[1,32768]{1,0:T(1,128)S(1)}, u32[]{:S(2)}, u32[]{:S(2)}) collective-permute-start(f32[1,32768]{1,0:T(1,128)S(1)} %add.191), channel_id=1, source_target_pairs={{0,16},{2,18},{4,20},{6,22},{8,24},{10,26},{12,28},{14,30},{16,0},... | collective-permute-start | bytes 393224 | tf_op jit(solution)/shard_map/ppermute | solution.py:26
  47.4 5.9 %collective-permute-start.30 = (f32[1,32768]{1,0:T(1,128)S(1)}, f32[1,32768]{1,0:T(1,128)S(1)}, u32[]{:S(2)}, u32[]{:S(2)}) collective-permute-start(f32[1,32768]{1,0:T(1,128)S(1)} %add.192), channel_id=1, source_target_pairs={{0,32},{2,34},{4,36},{6,38},{8,40},{10,42},{12,44},{14,46},{16,48}... | collective-permute-start | bytes 393224 | tf_op jit(solution)/shard_map/ppermute | solution.py:26
  53.5 2.9 %collective-permute-done.30 = f32[1,32768]{1,0:T(1,128)S(1)} collective-permute-done((f32[1,32768]{1,0:T(1,128)S(1)}, f32[1,32768]{1,0:T(1,128)S(1)}, u32[]{:S(2)}, u32[]{:S(2)}) %collective-permute-start.30) | collective-permute-done | bytes 131104 | tf_op jit(solution)/shard_map/ppermute | solution.py:26
  59.1 1.7 %collective-permute-start.10 = (f32[2,1]{1,0:T(2,128)S(1)}, f32[2,1]{1,0:T(2,128)S(1)}, u32[]{:S(2)}, u32[]{:S(2)}) collective-permute-start(f32[2,1]{1,0:T(2,128)S(1)} %pad_maximum_fusion.2), channel_id=1, source_target_pairs={{0,14},{2,12},{4,10},{6,8},{8,6},{10,4},{12,2},{14,0},{16,30},{18,... | collective-permute-start | bytes 32 | tf_op jit(solution)/shard_map/ppermute | solution.py:48
  60.8 1.7 %collective-permute-start.11 = (f32[2,1]{1,0:T(2,128)S(1)}, f32[2,1]{1,0:T(2,128)S(1)}, u32[]{:S(2)}, u32[]{:S(2)}) collective-permute-start(f32[2,1]{1,0:T(2,128)S(1)} %pad_maximum_fusion.2), channel_id=1, source_target_pairs={{0,16},{2,18},{4,20},{6,22},{8,24},{10,26},{12,28},{14,30},{16,0},... | collective-permute-start | bytes 32 | tf_op jit(solution)/shard_map/ppermute | solution.py:48
  62.7 2.5 %collective-permute-start.14 = (f32[2,1]{1,0:T(2,128)S(1)}, f32[2,1]{1,0:T(2,128)S(1)}, u32[]{:S(2)}, u32[]{:S(2)}) collective-permute-start(f32[2,1]{1,0:T(2,128)S(1)} %pad_maximum_fusion.2), channel_id=1, source_target_pairs={{0,22},{2,20},{4,18},{6,16},{8,30},{10,28},{12,26},{14,24},{16,6},... | collective-permute-start | bytes 32 | tf_op jit(solution)/shard_map/ppermute | solution.py:48
  65.3 1.6 %collective-permute-start.15 = (f32[2,1]{1,0:T(2,128)S(1)}, f32[2,1]{1,0:T(2,128)S(1)}, u32[]{:S(2)}, u32[]{:S(2)}) collective-permute-start(f32[2,1]{1,0:T(2,128)S(1)} %pad_maximum_fusion.2), channel_id=1, source_target_pairs={{0,24},{2,26},{4,28},{6,30},{8,16},{10,18},{12,20},{14,22},{16,8},... | collective-permute-start | bytes 32 | tf_op jit(solution)/shard_map/ppermute | solution.py:48
  67.0 2.7 %collective-permute-start.16 = (f32[2,1]{1,0:T(2,128)S(1)}, f32[2,1]{1,0:T(2,128)S(1)}, u32[]{:S(2)}, u32[]{:S(2)}) collective-permute-start(f32[2,1]{1,0:T(2,128)S(1)} %pad_maximum_fusion.2), channel_id=1, source_target_pairs={{0,26},{2,24},{4,30},{6,28},{8,18},{10,16},{12,22},{14,20},{16,10}... | collective-permute-start | bytes 32 | tf_op jit(solution)/shard_map/ppermute | solution.py:48
  69.7 1.4 %collective-permute-start.17 = (f32[2,1]{1,0:T(2,128)S(1)}, f32[2,1]{1,0:T(2,128)S(1)}, u32[]{:S(2)}, u32[]{:S(2)}) collective-permute-start(f32[2,1]{1,0:T(2,128)S(1)} %pad_maximum_fusion.2), channel_id=1, source_target_pairs={{0,28},{2,30},{4,24},{6,26},{8,20},{10,22},{12,16},{14,18},{16,12}... | collective-permute-start | bytes 32 | tf_op jit(solution)/shard_map/ppermute | solution.py:48
  71.0 2.4 %collective-permute-start.18 = (f32[2,1]{1,0:T(2,128)S(1)}, f32[2,1]{1,0:T(2,128)S(1)}, u32[]{:S(2)}, u32[]{:S(2)}) collective-permute-start(f32[2,1]{1,0:T(2,128)S(1)} %pad_maximum_fusion.2), channel_id=1, source_target_pairs={{0,30},{2,28},{4,26},{6,24},{8,22},{10,20},{12,18},{14,16},{16,14}... | collective-permute-start | bytes 32 | tf_op jit(solution)/shard_map/ppermute | solution.py:48
  73.9 1.4 %collective-permute-start.6 = (f32[2,1]{1,0:T(2,128)S(1)}, f32[2,1]{1,0:T(2,128)S(1)}, u32[]{:S(2)}, u32[]{:S(2)}) collective-permute-start(f32[2,1]{1,0:T(2,128)S(1)} %pad_maximum_fusion.2), channel_id=1, source_target_pairs={{0,6},{2,4},{4,2},{6,0},{8,14},{10,12},{12,10},{14,8},{16,22},{18,... | collective-permute-start | bytes 32 | tf_op jit(solution)/shard_map/ppermute | solution.py:48
  75.4 1.4 %collective-permute-start.7 = (f32[2,1]{1,0:T(2,128)S(1)}, f32[2,1]{1,0:T(2,128)S(1)}, u32[]{:S(2)}, u32[]{:S(2)}) collective-permute-start(f32[2,1]{1,0:T(2,128)S(1)} %pad_maximum_fusion.2), channel_id=1, source_target_pairs={{0,8},{2,10},{4,12},{6,14},{8,0},{10,2},{12,4},{14,6},{16,24},{18,... | collective-permute-start | bytes 32 | tf_op jit(solution)/shard_map/ppermute | solution.py:48
  76.8 2.1 %collective-permute-start.8 = (f32[2,1]{1,0:T(2,128)S(1)}, f32[2,1]{1,0:T(2,128)S(1)}, u32[]{:S(2)}, u32[]{:S(2)}) collective-permute-start(f32[2,1]{1,0:T(2,128)S(1)} %pad_maximum_fusion.2), channel_id=1, source_target_pairs={{0,10},{2,8},{4,14},{6,12},{8,2},{10,0},{12,6},{14,4},{16,26},{18,... | collective-permute-start | bytes 32 | tf_op jit(solution)/shard_map/ppermute | solution.py:48
  80.3 4.5 %collective-permute-start.32 = (f32[1,32768]{1,0:T(1,128)S(1)}, f32[1,32768]{1,0:T(1,128)S(1)}, u32[]{:S(2)}, u32[]{:S(2)}) collective-permute-start(f32[1,32768]{1,0:T(1,128)S(1)} %add.194), channel_id=1, source_target_pairs={{0,128},{2,130},{4,132},{6,134},{8,136},{10,138},{12,140},{14,142}... | collective-permute-start | bytes 393224 | tf_op jit(solution)/shard_map/ppermute | solution.py:26
  84.8 1.5 %collective-permute-start.19 = (f32[2,1]{1,0:T(2,128)S(1)}, f32[2,1]{1,0:T(2,128)S(1)}, u32[]{:S(2)}, u32[]{:S(2)}) collective-permute-start(f32[2,1]{1,0:T(2,128)S(1)} %add_add_fusion), channel_id=1, source_target_pairs={{0,32},{2,34},{4,36},{6,38},{8,40},{10,42},{12,44},{14,46},{16,48}... | collective-permute-start | bytes 32 | tf_op jit(solution)/shard_map/ppermute | solution.py:48
  86.3 2.3 %collective-permute-start.20 = (f32[2,1]{1,0:T(2,128)S(1)}, f32[2,1]{1,0:T(2,128)S(1)}, u32[]{:S(2)}, u32[]{:S(2)}) collective-permute-start(f32[2,1]{1,0:T(2,128)S(1)} %add_add_fusion), channel_id=1, source_target_pairs={{0,64},{2,66},{4,68},{6,70},{8,72},{10,74},{12,76},{14,78},{16,80}... | collective-permute-start | bytes 32 | tf_op jit(solution)/shard_map/ppermute | solution.py:48
  88.6 3.4 %collective-permute-start.22 = (f32[2,1]{1,0:T(2,128)S(1)}, f32[2,1]{1,0:T(2,128)S(1)}, u32[]{:S(2)}, u32[]{:S(2)}) collective-permute-start(f32[2,1]{1,0:T(2,128)S(1)} %add_add_fusion), channel_id=1, source_target_pairs={{0,128},{2,130},{4,132},{6,134},{8,136},{10,138},{12,140},{14,142}... | collective-permute-start | bytes 32 | tf_op jit(solution)/shard_map/ppermute | solution.py:48
  92.0 3.2 %collective-permute-start.23 = (f32[2,1]{1,0:T(2,128)S(1)}, f32[2,1]{1,0:T(2,128)S(1)}, u32[]{:S(2)}, u32[]{:S(2)}) collective-permute-start(f32[2,1]{1,0:T(2,128)S(1)} %add_add_fusion), channel_id=1, source_target_pairs={{0,160},{2,162},{4,164},{6,166},{8,168},{10,170},{12,172},{14,174}... | collective-permute-start | bytes 32 | tf_op jit(solution)/shard_map/ppermute | solution.py:48
  96.1 3.5 %collective-permute-start.24 = (f32[2,1]{1,0:T(2,128)S(1)}, f32[2,1]{1,0:T(2,128)S(1)}, u32[]{:S(2)}, u32[]{:S(2)}) collective-permute-start(f32[2,1]{1,0:T(2,128)S(1)} %add_add_fusion), channel_id=1, source_target_pairs={{0,192},{2,194},{4,196},{6,198},{8,200},{10,202},{12,204},{14,206}... | collective-permute-start | bytes 32 | tf_op jit(solution)/shard_map/ppermute | solution.py:48
  99.6 1.8 %collective-permute-start.25 = (f32[2,1]{1,0:T(2,128)S(1)}, f32[2,1]{1,0:T(2,128)S(1)}, u32[]{:S(2)}, u32[]{:S(2)}) collective-permute-start(f32[2,1]{1,0:T(2,128)S(1)} %add_add_fusion), channel_id=1, source_target_pairs={{0,224},{2,226},{4,228},{6,230},{8,232},{10,234},{12,236},{14,238}... | collective-permute-start | bytes 32 | tf_op jit(solution)/shard_map/ppermute | solution.py:48
  101.7 4.4 %collective-permute-done.25 = f32[2,1]{1,0:T(2,128)S(1)} collective-permute-done((f32[2,1]{1,0:T(2,128)S(1)}, f32[2,1]{1,0:T(2,128)S(1)}, u32[]{:S(2)}, u32[]{:S(2)}) %collective-permute-start.25) | collective-permute-done | bytes 40 | tf_op jit(solution)/shard_map/ppermute | solution.py:48
  106.9 5.1 %collective-permute-done.33 = f32[2,1]{1,0:T(2,128)S(1)} collective-permute-done((f32[2,1]{1,0:T(2,128)S(1)}, f32[2,1]{1,0:T(2,128)S(1)}, u32[]{:S(2)}, u32[]{:S(2)}) %collective-permute-start.33) | collective-permute-done | bytes 40 | tf_op jit(solution)/shard_map/ppermute | solution.py:26
  (104 shorter events, 17.1 us)
Async XLA Ops:
  1.5 8.3 %collective-permute-start = (f32[1,1,4096]{2,1,0:T(1,128)S(1)}, f32[1,1,4096]{2,1,0:T(1,128)S(1)}, u32[]{:S(2)}, u32[]{:S(2)}) collective-permute-start(f32[1,1,4096]{2,1,0:T(1,128)S(1)} %get-tuple-element.10), channel_id=1, source_target_pairs={{0,1},{1,0},{2,3},{3,2},{4,5},{5,4},{6,7},{7,6},{8,9},{9,8},{10,11... | collective-permute-start | bytes 49160 | tf_op jit(solution)/shard_map/ppermute | solution.py:119
  4.8 39.3 %collective-permute-start.2 = (f32[1,1,4096]{2,1,0:T(1,128)S(1)}, f32[1,1,4096]{2,1,0:T(1,128)S(1)}, u32[]{:S(2)}, u32[]{:S(2)}) collective-permute-start(f32[1,1,4096]{2,1,0:T(1,128)S(1)} %get-tuple-element.11), channel_id=1, source_target_pairs={{0,254},{2,0},{4,2},{6,4},{8,6},{10,8},{12,10},{14,12},{16,14},{18... | collective-permute-start | bytes 49160 | tf_op jit(solution)/shard_map/ppermute | solution.py:16
  17.8 17.0 %collective-permute-start.27 = (f32[1,32768]{1,0:T(1,128)S(1)}, f32[1,32768]{1,0:T(1,128)S(1)}, u32[]{:S(2)}, u32[]{:S(2)}) collective-permute-start(f32[1,32768]{1,0:T(1,128)S(1)} %add.189), channel_id=1, source_target_pairs={{0,4},{2,6},{4,0},{6,2},{8,12},{10,14},{12,8},{14,10},{16,20},{18,... | collective-permute-start | bytes 393224 | tf_op jit(solution)/shard_map/ppermute | solution.py:26
  35.0 7.1 %collective-permute-start.28 = (f32[1,32768]{1,0:T(1,128)S(1)}, f32[1,32768]{1,0:T(1,128)S(1)}, u32[]{:S(2)}, u32[]{:S(2)}) collective-permute-start(f32[1,32768]{1,0:T(1,128)S(1)} %add.190), channel_id=1, source_target_pairs={{0,8},{2,10},{4,12},{6,14},{8,0},{10,2},{12,4},{14,6},{16,24},{18,... | collective-permute-start | bytes 393224 | tf_op jit(solution)/shard_map/ppermute | solution.py:26
  37.9 15.5 %collective-permute-start.1 = (f32[1,1,4096]{2,1,0:T(1,128)S(1)}, f32[1,1,4096]{2,1,0:T(1,128)S(1)}, u32[]{:S(2)}, u32[]{:S(2)}) collective-permute-start(f32[1,1,4096]{2,1,0:T(1,128)S(1)} %constant_dynamic-slice_fusion), channel_id=1, source_target_pairs={{0,1},{1,0},{2,3},{3,2},{4,5},{5,4},{6,7},{7,6},{8,9},{9,8},{10,11... | collective-permute-start | bytes 49160 | tf_op jit(solution)/shard_map/ppermute | solution.py:158
  44.2 9.2 %collective-permute-start.3 = (f32[1,1,4096]{2,1,0:T(1,128)S(1)}, f32[1,1,4096]{2,1,0:T(1,128)S(1)}, u32[]{:S(2)}, u32[]{:S(2)}) collective-permute-start(f32[1,1,4096]{2,1,0:T(1,128)S(1)} %subtract_multiply_fusion), channel_id=1, source_target_pairs={{0,2},{2,4},{4,6},{6,8},{8,10},{10,12},{12,14},{14,16},{16,18},{18... | collective-permute-start | bytes 49160 | tf_op jit(solution)/shard_map/ppermute | solution.py:16
  47.4 8.9 %collective-permute-start.30 = (f32[1,32768]{1,0:T(1,128)S(1)}, f32[1,32768]{1,0:T(1,128)S(1)}, u32[]{:S(2)}, u32[]{:S(2)}) collective-permute-start(f32[1,32768]{1,0:T(1,128)S(1)} %add.192), channel_id=1, source_target_pairs={{0,32},{2,34},{4,36},{6,38},{8,40},{10,42},{12,44},{14,46},{16,48}... | collective-permute-start | bytes 393224 | tf_op jit(solution)/shard_map/ppermute | solution.py:26
  56.5 6.2 %collective-permute-start.31 = (f32[1,32768]{1,0:T(1,128)S(1)}, f32[1,32768]{1,0:T(1,128)S(1)}, u32[]{:S(2)}, u32[]{:S(2)}) collective-permute-start(f32[1,32768]{1,0:T(1,128)S(1)} %add.193), channel_id=1, source_target_pairs={{0,64},{2,66},{4,68},{6,70},{8,72},{10,74},{12,76},{14,78},{16,80}... | collective-permute-start | bytes 393224 | tf_op jit(solution)/shard_map/ppermute | solution.py:26
  59.1 6.2 %collective-permute-start.10 = (f32[2,1]{1,0:T(2,128)S(1)}, f32[2,1]{1,0:T(2,128)S(1)}, u32[]{:S(2)}, u32[]{:S(2)}) collective-permute-start(f32[2,1]{1,0:T(2,128)S(1)} %pad_maximum_fusion.2), channel_id=1, source_target_pairs={{0,14},{2,12},{4,10},{6,8},{8,6},{10,4},{12,2},{14,0},{16,30},{18,... | collective-permute-start | bytes 32 | tf_op jit(solution)/shard_map/ppermute | solution.py:48
  60.8 6.2 %collective-permute-start.11 = (f32[2,1]{1,0:T(2,128)S(1)}, f32[2,1]{1,0:T(2,128)S(1)}, u32[]{:S(2)}, u32[]{:S(2)}) collective-permute-start(f32[2,1]{1,0:T(2,128)S(1)} %pad_maximum_fusion.2), channel_id=1, source_target_pairs={{0,16},{2,18},{4,20},{6,22},{8,24},{10,26},{12,28},{14,30},{16,0},... | collective-permute-start | bytes 32 | tf_op jit(solution)/shard_map/ppermute | solution.py:48
  62.5 7.1 %collective-permute-start.12 = (f32[2,1]{1,0:T(2,128)S(1)}, f32[2,1]{1,0:T(2,128)S(1)}, u32[]{:S(2)}, u32[]{:S(2)}) collective-permute-start(f32[2,1]{1,0:T(2,128)S(1)} %pad_maximum_fusion.2), channel_id=1, source_target_pairs={{0,18},{2,16},{4,22},{6,20},{8,26},{10,24},{12,30},{14,28},{16,2},... | collective-permute-start | bytes 32 | tf_op jit(solution)/shard_map/ppermute | solution.py:48
  62.6 8.5 %collective-permute-start.13 = (f32[2,1]{1,0:T(2,128)S(1)}, f32[2,1]{1,0:T(2,128)S(1)}, u32[]{:S(2)}, u32[]{:S(2)}) collective-permute-start(f32[2,1]{1,0:T(2,128)S(1)} %pad_maximum_fusion.2), channel_id=1, source_target_pairs={{0,20},{2,22},{4,16},{6,18},{8,28},{10,30},{12,24},{14,26},{16,4},... | collective-permute-start | bytes 32 | tf_op jit(solution)/shard_map/ppermute | solution.py:48
  62.7 10.7 %collective-permute-start.14 = (f32[2,1]{1,0:T(2,128)S(1)}, f32[2,1]{1,0:T(2,128)S(1)}, u32[]{:S(2)}, u32[]{:S(2)}) collective-permute-start(f32[2,1]{1,0:T(2,128)S(1)} %pad_maximum_fusion.2), channel_id=1, source_target_pairs={{0,22},{2,20},{4,18},{6,16},{8,30},{10,28},{12,26},{14,24},{16,6},... | collective-permute-start | bytes 32 | tf_op jit(solution)/shard_map/ppermute | solution.py:48
  65.3 8.6 %collective-permute-start.15 = (f32[2,1]{1,0:T(2,128)S(1)}, f32[2,1]{1,0:T(2,128)S(1)}, u32[]{:S(2)}, u32[]{:S(2)}) collective-permute-start(f32[2,1]{1,0:T(2,128)S(1)} %pad_maximum_fusion.2), channel_id=1, source_target_pairs={{0,24},{2,26},{4,28},{6,30},{8,16},{10,18},{12,20},{14,22},{16,8},... | collective-permute-start | bytes 32 | tf_op jit(solution)/shard_map/ppermute | solution.py:48
  67.0 7.0 %collective-permute-start.16 = (f32[2,1]{1,0:T(2,128)S(1)}, f32[2,1]{1,0:T(2,128)S(1)}, u32[]{:S(2)}, u32[]{:S(2)}) collective-permute-start(f32[2,1]{1,0:T(2,128)S(1)} %pad_maximum_fusion.2), channel_id=1, source_target_pairs={{0,26},{2,24},{4,30},{6,28},{8,18},{10,16},{12,22},{14,20},{16,10}... | collective-permute-start | bytes 32 | tf_op jit(solution)/shard_map/ppermute | solution.py:48
  69.7 5.7 %collective-permute-start.17 = (f32[2,1]{1,0:T(2,128)S(1)}, f32[2,1]{1,0:T(2,128)S(1)}, u32[]{:S(2)}, u32[]{:S(2)}) collective-permute-start(f32[2,1]{1,0:T(2,128)S(1)} %pad_maximum_fusion.2), channel_id=1, source_target_pairs={{0,28},{2,30},{4,24},{6,26},{8,20},{10,22},{12,16},{14,18},{16,12}... | collective-permute-start | bytes 32 | tf_op jit(solution)/shard_map/ppermute | solution.py:48
  71.0 5.8 %collective-permute-start.18 = (f32[2,1]{1,0:T(2,128)S(1)}, f32[2,1]{1,0:T(2,128)S(1)}, u32[]{:S(2)}, u32[]{:S(2)}) collective-permute-start(f32[2,1]{1,0:T(2,128)S(1)} %pad_maximum_fusion.2), channel_id=1, source_target_pairs={{0,30},{2,28},{4,26},{6,24},{8,22},{10,20},{12,18},{14,16},{16,14}... | collective-permute-start | bytes 32 | tf_op jit(solution)/shard_map/ppermute | solution.py:48
  73.5 5.5 %collective-permute-start.4 = (f32[2,1]{1,0:T(2,128)S(1)}, f32[2,1]{1,0:T(2,128)S(1)}, u32[]{:S(2)}, u32[]{:S(2)}) collective-permute-start(f32[2,1]{1,0:T(2,128)S(1)} %pad_maximum_fusion.2), channel_id=1, source_target_pairs={{0,2},{2,0},{4,6},{6,4},{8,10},{10,8},{12,14},{14,12},{16,18},{18,... | collective-permute-start | bytes 32 | tf_op jit(solution)/shard_map/ppermute | solution.py:48
  73.9 6.4 %collective-permute-start.5 = (f32[2,1]{1,0:T(2,128)S(1)}, f32[2,1]{1,0:T(2,128)S(1)}, u32[]{:S(2)}, u32[]{:S(2)}) collective-permute-start(f32[2,1]{1,0:T(2,128)S(1)} %pad_maximum_fusion.2), channel_id=1, source_target_pairs={{0,4},{2,6},{4,0},{6,2},{8,12},{10,14},{12,8},{14,10},{16,20},{18,... | collective-permute-start | bytes 32 | tf_op jit(solution)/shard_map/ppermute | solution.py:48
  73.9 10.9 %collective-permute-start.6 = (f32[2,1]{1,0:T(2,128)S(1)}, f32[2,1]{1,0:T(2,128)S(1)}, u32[]{:S(2)}, u32[]{:S(2)}) collective-permute-start(f32[2,1]{1,0:T(2,128)S(1)} %pad_maximum_fusion.2), channel_id=1, source_target_pairs={{0,6},{2,4},{4,2},{6,0},{8,14},{10,12},{12,10},{14,8},{16,22},{18,... | collective-permute-start | bytes 32 | tf_op jit(solution)/shard_map/ppermute | solution.py:48
  75.4 9.4 %collective-permute-start.7 = (f32[2,1]{1,0:T(2,128)S(1)}, f32[2,1]{1,0:T(2,128)S(1)}, u32[]{:S(2)}, u32[]{:S(2)}) collective-permute-start(f32[2,1]{1,0:T(2,128)S(1)} %pad_maximum_fusion.2), channel_id=1, source_target_pairs={{0,8},{2,10},{4,12},{6,14},{8,0},{10,2},{12,4},{14,6},{16,24},{18,... | collective-permute-start | bytes 32 | tf_op jit(solution)/shard_map/ppermute | solution.py:48
  76.8 8.0 %collective-permute-start.8 = (f32[2,1]{1,0:T(2,128)S(1)}, f32[2,1]{1,0:T(2,128)S(1)}, u32[]{:S(2)}, u32[]{:S(2)}) collective-permute-start(f32[2,1]{1,0:T(2,128)S(1)} %pad_maximum_fusion.2), channel_id=1, source_target_pairs={{0,10},{2,8},{4,14},{6,12},{8,2},{10,0},{12,6},{14,4},{16,26},{18,... | collective-permute-start | bytes 32 | tf_op jit(solution)/shard_map/ppermute | solution.py:48
  78.9 5.9 %collective-permute-start.9 = (f32[2,1]{1,0:T(2,128)S(1)}, f32[2,1]{1,0:T(2,128)S(1)}, u32[]{:S(2)}, u32[]{:S(2)}) collective-permute-start(f32[2,1]{1,0:T(2,128)S(1)} %pad_maximum_fusion.2), channel_id=1, source_target_pairs={{0,12},{2,14},{4,8},{6,10},{8,4},{10,6},{12,0},{14,2},{16,28},{18,... | collective-permute-start | bytes 32 | tf_op jit(solution)/shard_map/ppermute | solution.py:48
  80.3 11.7 %collective-permute-start.32 = (f32[1,32768]{1,0:T(1,128)S(1)}, f32[1,32768]{1,0:T(1,128)S(1)}, u32[]{:S(2)}, u32[]{:S(2)}) collective-permute-start(f32[1,32768]{1,0:T(1,128)S(1)} %add.194), channel_id=1, source_target_pairs={{0,128},{2,130},{4,132},{6,134},{8,136},{10,138},{12,140},{14,142}... | collective-permute-start | bytes 393224 | tf_op jit(solution)/shard_map/ppermute | solution.py:26
  84.8 11.2 %collective-permute-start.19 = (f32[2,1]{1,0:T(2,128)S(1)}, f32[2,1]{1,0:T(2,128)S(1)}, u32[]{:S(2)}, u32[]{:S(2)}) collective-permute-start(f32[2,1]{1,0:T(2,128)S(1)} %add_add_fusion), channel_id=1, source_target_pairs={{0,32},{2,34},{4,36},{6,38},{8,40},{10,42},{12,44},{14,46},{16,48}... | collective-permute-start | bytes 32 | tf_op jit(solution)/shard_map/ppermute | solution.py:48
  86.3 13.3 %collective-permute-start.20 = (f32[2,1]{1,0:T(2,128)S(1)}, f32[2,1]{1,0:T(2,128)S(1)}, u32[]{:S(2)}, u32[]{:S(2)}) collective-permute-start(f32[2,1]{1,0:T(2,128)S(1)} %add_add_fusion), channel_id=1, source_target_pairs={{0,64},{2,66},{4,68},{6,70},{8,72},{10,74},{12,76},{14,78},{16,80}... | collective-permute-start | bytes 32 | tf_op jit(solution)/shard_map/ppermute | solution.py:48
  88.6 12.7 %collective-permute-start.21 = (f32[2,1]{1,0:T(2,128)S(1)}, f32[2,1]{1,0:T(2,128)S(1)}, u32[]{:S(2)}, u32[]{:S(2)}) collective-permute-start(f32[2,1]{1,0:T(2,128)S(1)} %add_add_fusion), channel_id=1, source_target_pairs={{0,96},{2,98},{4,100},{6,102},{8,104},{10,106},{12,108},{14,110},{... | collective-permute-start | bytes 32 | tf_op jit(solution)/shard_map/ppermute | solution.py:48
  88.6 12.7 %collective-permute-start.22 = (f32[2,1]{1,0:T(2,128)S(1)}, f32[2,1]{1,0:T(2,128)S(1)}, u32[]{:S(2)}, u32[]{:S(2)}) collective-permute-start(f32[2,1]{1,0:T(2,128)S(1)} %add_add_fusion), channel_id=1, source_target_pairs={{0,128},{2,130},{4,132},{6,134},{8,136},{10,138},{12,140},{14,142}... | collective-permute-start | bytes 32 | tf_op jit(solution)/shard_map/ppermute | solution.py:48
  92.0 9.4 %collective-permute-start.23 = (f32[2,1]{1,0:T(2,128)S(1)}, f32[2,1]{1,0:T(2,128)S(1)}, u32[]{:S(2)}, u32[]{:S(2)}) collective-permute-start(f32[2,1]{1,0:T(2,128)S(1)} %add_add_fusion), channel_id=1, source_target_pairs={{0,160},{2,162},{4,164},{6,166},{8,168},{10,170},{12,172},{14,174}... | collective-permute-start | bytes 32 | tf_op jit(solution)/shard_map/ppermute | solution.py:48
  96.1 5.7 %collective-permute-start.24 = (f32[2,1]{1,0:T(2,128)S(1)}, f32[2,1]{1,0:T(2,128)S(1)}, u32[]{:S(2)}, u32[]{:S(2)}) collective-permute-start(f32[2,1]{1,0:T(2,128)S(1)} %add_add_fusion), channel_id=1, source_target_pairs={{0,192},{2,194},{4,196},{6,198},{8,200},{10,202},{12,204},{14,206}... | collective-permute-start | bytes 32 | tf_op jit(solution)/shard_map/ppermute | solution.py:48
  99.6 6.6 %collective-permute-start.25 = (f32[2,1]{1,0:T(2,128)S(1)}, f32[2,1]{1,0:T(2,128)S(1)}, u32[]{:S(2)}, u32[]{:S(2)}) collective-permute-start(f32[2,1]{1,0:T(2,128)S(1)} %add_add_fusion), channel_id=1, source_target_pairs={{0,224},{2,226},{4,228},{6,230},{8,232},{10,234},{12,236},{14,238}... | collective-permute-start | bytes 32 | tf_op jit(solution)/shard_map/ppermute | solution.py:48
  106.8 5.2 %collective-permute-start.33 = (f32[2,1]{1,0:T(2,128)S(1)}, f32[2,1]{1,0:T(2,128)S(1)}, u32[]{:S(2)}, u32[]{:S(2)}) collective-permute-start(f32[2,1]{1,0:T(2,128)S(1)} %maximum_add_fusion), channel_id=1, source_target_pairs={{0,1},{1,0},{2,3},{3,2},{4,5},{5,4},{6,7},{7,6},{8,9},{9,8},{10,11... | collective-permute-start | bytes 32 | tf_op jit(solution)/shard_map/ppermute | solution.py:26
  (19 other events, 126.0 us)

commit v3 on v2

--- a/solution.py
+++ b/solution.py
@@ -64,9 +64,45 @@
     )(table, index)
 
 
-def within_block_onehot(rows):
-    picked = rows.reshape(-1, BLOCK)
-    return picked[:, :, None] == jnp.arange(BLOCK, dtype=rows.dtype)[None, None, :]
+def lane_scatter_kernel(value_ref, index_ref, out_ref):
+    tiles = BLOCK // 8
+    for lane_tile in range(out_ref.shape[1] // BLOCK):
+        lanes = pl.ds(lane_tile * BLOCK, BLOCK)
+
+        def step(group, sums):
+            start = pl.multiple_of(group * 8, 8)
+            values = value_ref[pl.ds(start, 8), lanes]
+            indices = index_ref[pl.ds(start, 8), lanes]
+            for sub in range(8):
+                value = jnp.broadcast_to(values[sub : sub + 1, :], (8, BLOCK))
+                index = jnp.broadcast_to(indices[sub : sub + 1, :], (8, BLOCK))
+                sums = tuple(
+                    sums[tile]
+                    + jnp.where(
+                        index == lax.broadcasted_iota(jnp.int32, (8, BLOCK), 0) + 8 * tile,
+                        value,
+                        0.0,
+                    )
+                    for tile in range(tiles)
+                )
+            return sums
+
+        zero = jnp.zeros((8, BLOCK), jnp.float32)
+        sums = lax.fori_loop(0, tiles, step, (zero,) * tiles)
+        for tile in range(tiles):
+            out_ref[pl.ds(tile * 8, 8), lanes] = sums[tile]
+
+
+def lane_scatter(values, index):
+    count = values.shape[0]
+    padded = -(-count // BLOCK) * BLOCK
+    values_t = jnp.pad(values, ((0, padded - count), (0, 0))).T
+    index_t = jnp.pad(index, ((0, padded - count), (0, 0))).T
+    out = pl.pallas_call(
+        lane_scatter_kernel,
+        out_shape=jax.ShapeDtypeStruct((BLOCK, padded), values.dtype),
+    )(values_t, index_t)
+    return out.T[:count]
 
 
 def gather_blocks(table, blocks, rows):
@@ -78,10 +114,12 @@
     return values.reshape(lead + (-1,))
 
 
-def scatter_blocks(values, blocks, onehot, count):
+def scatter_blocks(values, blocks, rows, count):
     lead = values.shape[:-1]
     tiled = values.reshape(lead + (-1, BLOCK))
-    within = jnp.sum(jnp.where(onehot, tiled[..., :, :, None], 0.0), axis=-2)
+    index = jnp.broadcast_to(rows.reshape(-1, BLOCK), tiled.shape)
+    within = lane_scatter(tiled.reshape(-1, BLOCK), index.reshape(-1, BLOCK))
+    within = within.reshape(tiled.shape)
     out = jnp.zeros(lead + (count, BLOCK), values.dtype)
     out = out.at[..., blocks, :].add(within)
     return out.reshape(lead + (-1,))
@@ -127,7 +165,6 @@
 
     blocks = jnp.concatenate([line_anchor, line_target, column_block])
     rows = jnp.concatenate([anchor_rows, target_rows, column_rows])
-    onehot = within_block_onehot(rows)
     gathered = gather_blocks(network, blocks, rows)
     flow_value = gathered[..., :lines] - gathered[..., lines : 2 * lines]
     dispatch_value = gathered[..., 2 * lines :] + direction_capacity
@@ -148,7 +185,7 @@
     bus_terms = scatter_blocks(
         jnp.concatenate([flow_scaled, -flow_scaled, dispatch_scaled], axis=-1),
         blocks,
-        onehot,
+        rows,
         buses // BLOCK,
     )
     if net_count == 2:
@@ -171,7 +208,7 @@
     curvature_local = jnp.sum(direction_nodal * image_nodal, axis=(1, 2, 3)) + jnp.sum(
         direction_capacity * (dispatch_scaled + DAMPING * direction_capacity), axis=(1, 2)
     )
-    sums = group_sum(jnp.stack([squares_local, curvature_local]), "tm", 4)
+    sums = butterfly_sum(jnp.stack([squares_local, curvature_local]), "tm")
     capacity_part = jnp.sum(capacity_scaled * capacity_value, axis=1)
     sums = sums + jnp.stack([jnp.zeros_like(capacity_part), capacity_part])
     totals = butterfly_sum(sums, "net")

time: 116 us -> 99.2 us (0.86)
  the two profiles are of different devices: /device:TPU:32 before, /device:TPU:2 now
where the time goes in v3:
time: 99.2 us; the launch traced here: 97.4 us
  waiting for transfers between devices  38.7 us (39%)
  starting transfers between devices  27.4 us (28%)
  other arithmetic  12.8 us (13%)
  local copies, waits for them, and re-layouts  7.34 us (7%)
  Pallas kernels  6.35 us (6%)
  between operations  4.82 us (5%)
    ppermute x15, waiting for transfers between devices, butterfly_sum(): value = value + lax.ppermute(value, axis, pairs)  38.7 us
    ppermute x15, starting transfers between devices, butterfly_sum(): value = value + lax.ppermute(value, axis, pairs)  22.1 us
    pallas_call x1, Pallas kernels, lane_scatter(): pl.pallas_call(lane_scatter_kernel, out_shape=jax.ShapeDtypeStruct((BLOCK...  4.43 us
    ppermute x1, starting transfers between devices, body(): other = lax.ppermute(balance, 'net', [(0, 1), (1, 0)])  3.28 us
    unnamed x32, local copies, waits for them, and re-layouts  2.16 us
  transfers between devices with their start and end apart: 19, of which 11 were waited for; matrix products, arithmetic and copies ran while one was open for 14% of the time, Pallas kernels for 7%

profile of v3, /device:TPU:2, one launch (start us, length us, event | category | flops | bytes accessed | tf_op | source)
XLA Modules:
  0.0 97.4 jit_solution(9146114735330078055)
XLA Ops:
  0.6 0.9 fusion.14
  1.5 3.3 %collective-permute-start = (f32[1,1,4096]{2,1,0:T(1,128)S(1)}, f32[1,1,4096]{2,1,0:T(1,128)S(1)}, u32[]{:S(2)}, u32[]{:S(2)}) collective-permute-start(f32[1,1,4096]{2,1,0:T(1,128)S(1)} %get-tuple-element.10), channel_id=1, source_target_pairs={{0,1},{1,0},{2,3},{3,2},{4,5},{5,4},{6,7},{7,6},{8,9},{9,8},{10,11... | collective-permute-start | bytes 49160 | tf_op jit(solution)/shard_map/ppermute | solution.py:157
  5.6 0.9 add_bitcast_fusion.index_ref
  8.2 0.9 multiply_reduce_fusion.2
  9.2 1.1 %gather_fusion = f32[352,128]{1,0:T(8,128)S(1)} fusion(f32[64,128]{1,0:T(8,128)S(1)} %fusion.5, s32[1024]{0:T(1024)S(1)} %pad_clamp_fusion), kind=kCustom, calls=%fused_computation | custom fusion | bytes 361856 | tf_op jit(solution)/shard_map/jit(_take)/gather | solution.py:111
  11.1 1.9 %shard_map.167 = f32[352,128]{1,0:T(8,128)} custom-call(f32[352,128]{1,0:T(8,128)} %broadcast_select_fusion.table_ref, s32[352,128]{1,0:T(8,128)} %copy-done), custom_call_target="tpu_custom_call" | custom-call | tf_op jit(solution)/shard_map/pallas_call | solution.py:61
  13.8 1.9 %multiply_reduce_fusion.1 = (f32[]{:T(128)}, f32[1,1,32768]{2,1,0:T(1,128)S(1)}, f32[1,32768]{1,0:T(1,128)S(1)}) fusion(f32[1,1,32768]{2,1,0:T(1,128)S(1)} %copy-done.3, f32[1,1,45056]{2,1,0:T(1,128)} %bitcast.72, f32[1,32768]{1,0:T(1,128)S(1)} %copy-done.7, f32[1,32768]{1,0:T(1,128)S(1)} %copy-done.4), kind=kLoop, calls=%fused_computation.16 | loop fusion | flops 262143 | bytes 786436 | tf_op jit(solution)/shard_map/reduce_sum | solution.py:208
  17.2 4.4 %shard_map.168 = f32[128,384]{1,0:T(8,128)} custom-call(f32[128,384]{1,0:T(8,128)} %pad_bitcast_fusion.1.value_ref, s32[128,384]{1,0:T(8,128)} %pad_bitcast_fusion.index_ref), custom_call_target="tpu_custom_call" | custom-call | tf_op jit(solution)/shard_map/pallas_call | solution.py:101
  21.6 1.0 %copy.26 = f32[352,128]{1,0:T(8,128)S(1)} copy(f32[352,128]{0,1:T(8,128)} %bitcast.69) | data formatting | bytes 360448 | tf_op jit(solution)/shard_map/slice | solution.py:105
  22.6 1.8 %scatter_custom_fusion = f32[64,128]{1,0:T(8,128)S(1)} fusion(s32[352]{0:T(512)S(1)} %fusion.9, f32[352,128]{1,0:T(8,128)S(1)} %copy.26, f32[]{:T(128)} %constant.11.clone.1), kind=kCustom, calls=%fused_computation.27 | custom fusion | flops 45056 | bytes 32772 | tf_op jit(solution)/shard_map/scatter-add | solution.py:124
  24.6 7.4 %collective-permute-start.12 = (f32[1,32768]{1,0:T(1,128)S(1)}, f32[1,32768]{1,0:T(1,128)S(1)}, u32[]{:S(2)}, u32[]{:S(2)}) collective-permute-start(f32[1,32768]{1,0:T(1,128)S(1)} %add.133), channel_id=1, source_target_pairs={{0,4},{2,6},{4,0},{6,2},{8,12},{10,14},{12,8},{14,10},{16,20},{18,... | collective-permute-start | bytes 393224 | tf_op jit(solution)/shard_map/ppermute | solution.py:26
  32.0 1.9 %collective-permute-start.1 = (f32[1,1,4096]{2,1,0:T(1,128)S(1)}, f32[1,1,4096]{2,1,0:T(1,128)S(1)}, u32[]{:S(2)}, u32[]{:S(2)}) collective-permute-start(f32[1,1,4096]{2,1,0:T(1,128)S(1)} %constant_dynamic-slice_fusion), channel_id=1, source_target_pairs={{0,1},{1,0},{2,3},{3,2},{4,5},{5,4},{6,7},{7,6},{8,9},{9,8},{10,11... | collective-permute-start | bytes 49160 | tf_op jit(solution)/shard_map/ppermute | solution.py:195
  33.9 2.2 %collective-permute-done.12 = f32[1,32768]{1,0:T(1,128)S(1)} collective-permute-done((f32[1,32768]{1,0:T(1,128)S(1)}, f32[1,32768]{1,0:T(1,128)S(1)}, u32[]{:S(2)}, u32[]{:S(2)}) %collective-permute-start.12) | collective-permute-done | bytes 131104 | tf_op jit(solution)/shard_map/ppermute | solution.py:26
  39.1 4.2 %collective-permute-done.13 = f32[1,32768]{1,0:T(1,128)S(1)} collective-permute-done((f32[1,32768]{1,0:T(1,128)S(1)}, f32[1,32768]{1,0:T(1,128)S(1)}, u32[]{:S(2)}, u32[]{:S(2)}) %collective-permute-start.13) | collective-permute-done | bytes 131104 | tf_op jit(solution)/shard_map/ppermute | solution.py:26
  43.6 4.8 %collective-permute-done.14 = f32[1,32768]{1,0:T(1,128)S(1)} collective-permute-done((f32[1,32768]{1,0:T(1,128)S(1)}, f32[1,32768]{1,0:T(1,128)S(1)}, u32[]{:S(2)}, u32[]{:S(2)}) %collective-permute-start.14) | collective-permute-done | bytes 131104 | tf_op jit(solution)/shard_map/ppermute | solution.py:26
  50.7 2.9 %collective-permute-done.15 = f32[1,32768]{1,0:T(1,128)S(1)} collective-permute-done((f32[1,32768]{1,0:T(1,128)S(1)}, f32[1,32768]{1,0:T(1,128)S(1)}, u32[]{:S(2)}, u32[]{:S(2)}) %collective-permute-start.15) | collective-permute-done | bytes 131104 | tf_op jit(solution)/shard_map/ppermute | solution.py:26
  53.9 1.8 %collective-permute-start.5 = (f32[2,1]{1,0:T(2,128)S(1)}, f32[2,1]{1,0:T(2,128)S(1)}, u32[]{:S(2)}, u32[]{:S(2)}) collective-permute-start(f32[2,1]{1,0:T(2,128)S(1)} %fusion.10), channel_id=1, source_target_pairs={{0,4},{2,6},{4,0},{6,2},{8,12},{10,14},{12,8},{14,10},{16,20},{18,... | collective-permute-start | bytes 32 | tf_op jit(solution)/shard_map/ppermute | solution.py:26
  55.7 4.9 %collective-permute-done.16 = f32[1,32768]{1,0:T(1,128)S(1)} collective-permute-done((f32[1,32768]{1,0:T(1,128)S(1)}, f32[1,32768]{1,0:T(1,128)S(1)}, u32[]{:S(2)}, u32[]{:S(2)}) %collective-permute-start.16) | collective-permute-done | bytes 131104 | tf_op jit(solution)/shard_map/ppermute | solution.py:26
  60.7 2.8 %collective-permute-start.17 = (f32[1,32768]{1,0:T(1,128)S(1)}, f32[1,32768]{1,0:T(1,128)S(1)}, u32[]{:S(2)}, u32[]{:S(2)}) collective-permute-start(f32[1,32768]{1,0:T(1,128)S(1)} %add.138), channel_id=1, source_target_pairs={{0,128},{2,130},{4,132},{6,134},{8,136},{10,138},{12,140},{14,142}... | collective-permute-start | bytes 393224 | tf_op jit(solution)/shard_map/ppermute | solution.py:26
  63.6 1.3 %collective-permute-start.6 = (f32[2,1]{1,0:T(2,128)S(1)}, f32[2,1]{1,0:T(2,128)S(1)}, u32[]{:S(2)}, u32[]{:S(2)}) collective-permute-start(f32[2,1]{1,0:T(2,128)S(1)} %fusion.16), channel_id=1, source_target_pairs={{0,8},{2,10},{4,12},{6,14},{8,0},{10,2},{12,4},{14,6},{16,24},{18,... | collective-permute-start | bytes 32 | tf_op jit(solution)/shard_map/ppermute | solution.py:26
  64.9 4.0 %collective-permute-done.6 = f32[2,1]{1,0:T(2,128)S(1)} collective-permute-done((f32[2,1]{1,0:T(2,128)S(1)}, f32[2,1]{1,0:T(2,128)S(1)}, u32[]{:S(2)}, u32[]{:S(2)}) %collective-permute-start.6) | collective-permute-done | bytes 40 | tf_op jit(solution)/shard_map/ppermute | solution.py:26
  68.9 1.5 %collective-permute-start.7 = (f32[2,1]{1,0:T(2,128)S(1)}, f32[2,1]{1,0:T(2,128)S(1)}, u32[]{:S(2)}, u32[]{:S(2)}) collective-permute-start(f32[2,1]{1,0:T(2,128)S(1)} %add.128), channel_id=1, source_target_pairs={{0,16},{2,18},{4,20},{6,22},{8,24},{10,26},{12,28},{14,30},{16,0},... | collective-permute-start | bytes 32 | tf_op jit(solution)/shard_map/ppermute | solution.py:26
  70.4 2.1 %collective-permute-done.7 = f32[2,1]{1,0:T(2,128)S(1)} collective-permute-done((f32[2,1]{1,0:T(2,128)S(1)}, f32[2,1]{1,0:T(2,128)S(1)}, u32[]{:S(2)}, u32[]{:S(2)}) %collective-permute-start.7) | collective-permute-done | bytes 40 | tf_op jit(solution)/shard_map/ppermute | solution.py:26
  72.5 3.6 %collective-permute-done.8 = f32[2,1]{1,0:T(2,128)S(1)} collective-permute-done((f32[2,1]{1,0:T(2,128)S(1)}, f32[2,1]{1,0:T(2,128)S(1)}, u32[]{:S(2)}, u32[]{:S(2)}) %collective-permute-start.8) | collective-permute-done | bytes 40 | tf_op jit(solution)/shard_map/ppermute | solution.py:26
  76.1 1.1 %collective-permute-start.9 = (f32[2,1]{1,0:T(2,128)S(1)}, f32[2,1]{1,0:T(2,128)S(1)}, u32[]{:S(2)}, u32[]{:S(2)}) collective-permute-start(f32[2,1]{1,0:T(2,128)S(1)} %add.130), channel_id=1, source_target_pairs={{0,64},{2,66},{4,68},{6,70},{8,72},{10,74},{12,76},{14,78},{16,80}... | collective-permute-start | bytes 32 | tf_op jit(solution)/shard_map/ppermute | solution.py:26
  77.2 3.4 %collective-permute-done.9 = f32[2,1]{1,0:T(2,128)S(1)} collective-permute-done((f32[2,1]{1,0:T(2,128)S(1)}, f32[2,1]{1,0:T(2,128)S(1)}, u32[]{:S(2)}, u32[]{:S(2)}) %collective-permute-start.9) | collective-permute-done | bytes 40 | tf_op jit(solution)/shard_map/ppermute | solution.py:26
  80.6 3.2 %collective-permute-start.10 = (f32[2,1]{1,0:T(2,128)S(1)}, f32[2,1]{1,0:T(2,128)S(1)}, u32[]{:S(2)}, u32[]{:S(2)}) collective-permute-start(f32[2,1]{1,0:T(2,128)S(1)} %add.131), channel_id=1, source_target_pairs={{0,128},{2,130},{4,132},{6,134},{8,136},{10,138},{12,140},{14,142}... | collective-permute-start | bytes 32 | tf_op jit(solution)/shard_map/ppermute | solution.py:26
  83.7 0.9 multiply_reduce_fusion
  84.6 3.4 %collective-permute-done.10 = f32[2,1]{1,0:T(2,128)S(1)} collective-permute-done((f32[2,1]{1,0:T(2,128)S(1)}, f32[2,1]{1,0:T(2,128)S(1)}, u32[]{:S(2)}, u32[]{:S(2)}) %collective-permute-start.10) | collective-permute-done | bytes 40 | tf_op jit(solution)/shard_map/ppermute | solution.py:26
  88.7 2.0 %collective-permute-start.18 = (f32[2,1]{1,0:T(2,128)S(1)}, f32[2,1]{1,0:T(2,128)S(1)}, u32[]{:S(2)}, u32[]{:S(2)}) collective-permute-start(f32[2,1]{1,0:T(2,128)S(1)} %maximum_add_fusion), channel_id=1, source_target_pairs={{0,1},{1,0},{2,3},{3,2},{4,5},{5,4},{6,7},{7,6},{8,9},{9,8},{10,11... | collective-permute-start | bytes 32 | tf_op jit(solution)/shard_map/ppermute | solution.py:26
  90.7 3.1 %collective-permute-done.18 = f32[2,1]{1,0:T(2,128)S(1)} collective-permute-done((f32[2,1]{1,0:T(2,128)S(1)}, f32[2,1]{1,0:T(2,128)S(1)}, u32[]{:S(2)}, u32[]{:S(2)}) %collective-permute-start.18) | collective-permute-done | bytes 40 | tf_op jit(solution)/shard_map/ppermute | solution.py:26
  96.4 1.1 %multiply_subtract_fusion = f32[1,1,32768]{2,1,0:T(1,128)} fusion(f32[1,1,32768]{2,1,0:T(1,128)S(1)} %copy-done.2, f32[1,1,32768]{2,1,0:T(1,128)S(1)} %get-tuple-element.3, f32[1,32768]{1,0:T(1,128)S(1)} %copy-done.4, f32[1,32768]{1,0:T(1,128)S(1)} %bitcast.74, f32[1,1,32768]{2,1,0:T(1,128)S(1)} %copy-done.3, f32[]{:T(128)} %bitcast.26, ...), kind=kLoop, calls=%fused_computation.14 | loop fusion | flops 262144 | bytes 1048580 | tf_op jit(solution)/shard_map/sub | solution.py:217
  (82 shorter events, 10.9 us)
Async XLA Ops:
  0.6 5.0 %copy-start.10 = (s32[6144]{0:T(1024)S(1)}, s32[6144]{0:T(1024)}, u32[]{:S(2)}) copy-start(s32[6144]{0:T(1024)} %param.29) | copy-start | bytes 73732
  0.6 5.0 %copy-start.11 = (s32[6144]{0:T(1024)S(1)}, s32[6144]{0:T(1024)}, u32[]{:S(2)}) copy-start(s32[6144]{0:T(1024)} %param.28) | copy-start | bytes 73732
  1.5 7.6 %collective-permute-start = (f32[1,1,4096]{2,1,0:T(1,128)S(1)}, f32[1,1,4096]{2,1,0:T(1,128)S(1)}, u32[]{:S(2)}, u32[]{:S(2)}) collective-permute-start(f32[1,1,4096]{2,1,0:T(1,128)S(1)} %get-tuple-element.10), channel_id=1, source_target_pairs={{0,1},{1,0},{2,3},{3,2},{4,5},{5,4},{6,7},{7,6},{8,9},{9,8},{10,11... | collective-permute-start | bytes 49160 | tf_op jit(solution)/shard_map/ppermute | solution.py:157
  4.8 31.6 %collective-permute-start.2 = (f32[1,1,4096]{2,1,0:T(1,128)S(1)}, f32[1,1,4096]{2,1,0:T(1,128)S(1)}, u32[]{:S(2)}, u32[]{:S(2)}) collective-permute-start(f32[1,1,4096]{2,1,0:T(1,128)S(1)} %get-tuple-element.11), channel_id=1, source_target_pairs={{0,254},{2,0},{4,2},{6,4},{8,6},{10,8},{12,10},{14,12},{16,14},{18... | collective-permute-start | bytes 49160 | tf_op jit(solution)/shard_map/ppermute | solution.py:16
  4.8 0.7 copy-start.14
  7.2 1.0 %copy-start.2 = (f32[1,1,32768]{2,1,0:T(1,128)S(1)}, f32[1,1,32768]{2,1,0:T(1,128)}, u32[]{:S(2)}) copy-start(f32[1,1,32768]{2,1,0:T(1,128)} %param.19) | copy-start | bytes 393220
  11.0 1.9 %copy-start.12 = (f32[1,6144]{1,0:T(1,128)S(1)}, f32[1,6144]{1,0:T(1,128)}, u32[]{:S(2)}) copy-start(f32[1,6144]{1,0:T(1,128)} %param.20) | copy-start | bytes 73732
  11.0 2.7 %copy-start.3 = (f32[1,1,32768]{2,1,0:T(1,128)S(1)}, f32[1,1,32768]{2,1,0:T(1,128)}, u32[]{:S(2)}) copy-start(f32[1,1,32768]{2,1,0:T(1,128)} %param.17) | copy-start | bytes 393220
  11.1 2.8 %copy-start.4 = (f32[1,32768]{1,0:T(1,128)S(1)}, f32[1,32768]{1,0:T(1,128)}, u32[]{:S(2)}) copy-start(f32[1,32768]{1,0:T(1,128)} %param.24) | copy-start | bytes 393220
  11.1 2.8 %copy-start.7 = (f32[1,32768]{1,0:T(1,128)S(1)}, f32[1,32768]{1,0:T(1,128)}, u32[]{:S(2)}) copy-start(f32[1,32768]{1,0:T(1,128)} %param.21) | copy-start | bytes 393220
  15.7 8.7 %collective-permute-start.11 = (f32[1,32768]{1,0:T(1,128)S(1)}, f32[1,32768]{1,0:T(1,128)S(1)}, u32[]{:S(2)}, u32[]{:S(2)}) collective-permute-start(f32[1,32768]{1,0:T(1,128)S(1)} %get-tuple-element.6), channel_id=1, source_target_pairs={{0,2},{2,0},{4,6},{6,4},{8,10},{10,8},{12,14},{14,12},{16,18},{18,... | collective-permute-start | bytes 393224 | tf_op jit(solution)/shard_map/ppermute | solution.py:26
  24.6 11.6 %collective-permute-start.12 = (f32[1,32768]{1,0:T(1,128)S(1)}, f32[1,32768]{1,0:T(1,128)S(1)}, u32[]{:S(2)}, u32[]{:S(2)}) collective-permute-start(f32[1,32768]{1,0:T(1,128)S(1)} %add.133), channel_id=1, source_target_pairs={{0,4},{2,6},{4,0},{6,2},{8,12},{10,14},{12,8},{14,10},{16,20},{18,... | collective-permute-start | bytes 393224 | tf_op jit(solution)/shard_map/ppermute | solution.py:26
  32.0 4.4 %copy-start.5 = (f32[1,1,2,4096]{3,2,1,0:T(2,128)S(1)}, f32[1,1,2,4096]{3,2,1,0:T(2,128)}, u32[]{:S(2)}) copy-start(f32[1,1,2,4096]{3,2,1,0:T(2,128)} %param.16) | copy-start | bytes 98308
  32.0 4.4 %copy-start.8 = (f32[4096]{0:T(1024)S(1)}, f32[4096]{0:T(1024)}, u32[]{:S(2)}) copy-start(f32[4096]{0:T(1024)} %param.25) | copy-start | bytes 49156
  32.0 4.4 %copy-start.9 = (f32[1,2,4096]{2,1,0:T(2,128)S(1)}, f32[1,2,4096]{2,1,0:T(2,128)}, u32[]{:S(2)}) copy-start(f32[1,2,4096]{2,1,0:T(2,128)} %param.22) | copy-start | bytes 98308
  32.0 11.5 %collective-permute-start.1 = (f32[1,1,4096]{2,1,0:T(1,128)S(1)}, f32[1,1,4096]{2,1,0:T(1,128)S(1)}, u32[]{:S(2)}, u32[]{:S(2)}) collective-permute-start(f32[1,1,4096]{2,1,0:T(1,128)S(1)} %constant_dynamic-slice_fusion), channel_id=1, source_target_pairs={{0,1},{1,0},{2,3},{3,2},{4,5},{5,4},{6,7},{7,6},{8,9},{9,8},{10,11... | collective-permute-start | bytes 49160 | tf_op jit(solution)/shard_map/ppermute | solution.py:195
  36.3 6.9 %collective-permute-start.13 = (f32[1,32768]{1,0:T(1,128)S(1)}, f32[1,32768]{1,0:T(1,128)S(1)}, u32[]{:S(2)}, u32[]{:S(2)}) collective-permute-start(f32[1,32768]{1,0:T(1,128)S(1)} %add.134), channel_id=1, source_target_pairs={{0,8},{2,10},{4,12},{6,14},{8,0},{10,2},{12,4},{14,6},{16,24},{18,... | collective-permute-start | bytes 393224 | tf_op jit(solution)/shard_map/ppermute | solution.py:26
  36.4 0.8 copy-start.6
  36.5 7.0 %collective-permute-start.3 = (f32[1,1,4096]{2,1,0:T(1,128)S(1)}, f32[1,1,4096]{2,1,0:T(1,128)S(1)}, u32[]{:S(2)}, u32[]{:S(2)}) collective-permute-start(f32[1,1,4096]{2,1,0:T(1,128)S(1)} %subtract_multiply_fusion), channel_id=1, source_target_pairs={{0,2},{2,4},{4,6},{6,8},{8,10},{10,12},{12,14},{14,16},{16,18},{18... | collective-permute-start | bytes 49160 | tf_op jit(solution)/shard_map/ppermute | solution.py:16
  43.4 5.1 %collective-permute-start.14 = (f32[1,32768]{1,0:T(1,128)S(1)}, f32[1,32768]{1,0:T(1,128)S(1)}, u32[]{:S(2)}, u32[]{:S(2)}) collective-permute-start(f32[1,32768]{1,0:T(1,128)S(1)} %add.135), channel_id=1, source_target_pairs={{0,16},{2,18},{4,20},{6,22},{8,24},{10,26},{12,28},{14,30},{16,0},... | collective-permute-start | bytes 393224 | tf_op jit(solution)/shard_map/ppermute | solution.py:26
  48.6 5.1 %collective-permute-start.15 = (f32[1,32768]{1,0:T(1,128)S(1)}, f32[1,32768]{1,0:T(1,128)S(1)}, u32[]{:S(2)}, u32[]{:S(2)}) collective-permute-start(f32[1,32768]{1,0:T(1,128)S(1)} %add.136), channel_id=1, source_target_pairs={{0,32},{2,34},{4,36},{6,38},{8,40},{10,42},{12,44},{14,46},{16,48}... | collective-permute-start | bytes 393224 | tf_op jit(solution)/shard_map/ppermute | solution.py:26
  50.6 3.2 %collective-permute-start.4 = (f32[2,1]{1,0:T(2,128)S(1)}, f32[2,1]{1,0:T(2,128)S(1)}, u32[]{:S(2)}, u32[]{:S(2)}) collective-permute-start(f32[2,1]{1,0:T(2,128)S(1)} %pad_maximum_fusion.2), channel_id=1, source_target_pairs={{0,2},{2,0},{4,6},{6,4},{8,10},{10,8},{12,14},{14,12},{16,18},{18,... | collective-permute-start | bytes 32 | tf_op jit(solution)/shard_map/ppermute | solution.py:26
  53.8 6.8 %collective-permute-start.16 = (f32[1,32768]{1,0:T(1,128)S(1)}, f32[1,32768]{1,0:T(1,128)S(1)}, u32[]{:S(2)}, u32[]{:S(2)}) collective-permute-start(f32[1,32768]{1,0:T(1,128)S(1)} %add.137), channel_id=1, source_target_pairs={{0,64},{2,66},{4,68},{6,70},{8,72},{10,74},{12,76},{14,78},{16,80}... | collective-permute-start | bytes 393224 | tf_op jit(solution)/shard_map/ppermute | solution.py:26
  53.9 29.9 %copy-start.1 = (f32[32768]{0:T(1024)S(1)}, f32[32768]{0:T(1024)}, u32[]{:S(2)}) copy-start(f32[32768]{0:T(1024)} %param.23) | copy-start | bytes 393220
  53.9 9.7 %collective-permute-start.5 = (f32[2,1]{1,0:T(2,128)S(1)}, f32[2,1]{1,0:T(2,128)S(1)}, u32[]{:S(2)}, u32[]{:S(2)}) collective-permute-start(f32[2,1]{1,0:T(2,128)S(1)} %fusion.10), channel_id=1, source_target_pairs={{0,4},{2,6},{4,0},{6,2},{8,12},{10,14},{12,8},{14,10},{16,20},{18,... | collective-permute-start | bytes 32 | tf_op jit(solution)/shard_map/ppermute | solution.py:26
  60.7 23.0 %collective-permute-start.17 = (f32[1,32768]{1,0:T(1,128)S(1)}, f32[1,32768]{1,0:T(1,128)S(1)}, u32[]{:S(2)}, u32[]{:S(2)}) collective-permute-start(f32[1,32768]{1,0:T(1,128)S(1)} %add.138), channel_id=1, source_target_pairs={{0,128},{2,130},{4,132},{6,134},{8,136},{10,138},{12,140},{14,142}... | collective-permute-start | bytes 393224 | tf_op jit(solution)/shard_map/ppermute | solution.py:26
  63.6 5.3 %collective-permute-start.6 = (f32[2,1]{1,0:T(2,128)S(1)}, f32[2,1]{1,0:T(2,128)S(1)}, u32[]{:S(2)}, u32[]{:S(2)}) collective-permute-start(f32[2,1]{1,0:T(2,128)S(1)} %fusion.16), channel_id=1, source_target_pairs={{0,8},{2,10},{4,12},{6,14},{8,0},{10,2},{12,4},{14,6},{16,24},{18,... | collective-permute-start | bytes 32 | tf_op jit(solution)/shard_map/ppermute | solution.py:26
  68.9 3.6 %collective-permute-start.7 = (f32[2,1]{1,0:T(2,128)S(1)}, f32[2,1]{1,0:T(2,128)S(1)}, u32[]{:S(2)}, u32[]{:S(2)}) collective-permute-start(f32[2,1]{1,0:T(2,128)S(1)} %add.128), channel_id=1, source_target_pairs={{0,16},{2,18},{4,20},{6,22},{8,24},{10,26},{12,28},{14,30},{16,0},... | collective-permute-start | bytes 32 | tf_op jit(solution)/shard_map/ppermute | solution.py:26
  72.5 3.6 %collective-permute-start.8 = (f32[2,1]{1,0:T(2,128)S(1)}, f32[2,1]{1,0:T(2,128)S(1)}, u32[]{:S(2)}, u32[]{:S(2)}) collective-permute-start(f32[2,1]{1,0:T(2,128)S(1)} %add.129), channel_id=1, source_target_pairs={{0,32},{2,34},{4,36},{6,38},{8,40},{10,42},{12,44},{14,46},{16,48}... | collective-permute-start | bytes 32 | tf_op jit(solution)/shard_map/ppermute | solution.py:26
  76.1 4.5 %collective-permute-start.9 = (f32[2,1]{1,0:T(2,128)S(1)}, f32[2,1]{1,0:T(2,128)S(1)}, u32[]{:S(2)}, u32[]{:S(2)}) collective-permute-start(f32[2,1]{1,0:T(2,128)S(1)} %add.130), channel_id=1, source_target_pairs={{0,64},{2,66},{4,68},{6,70},{8,72},{10,74},{12,76},{14,78},{16,80}... | collective-permute-start | bytes 32 | tf_op jit(solution)/shard_map/ppermute | solution.py:26
  80.6 7.5 %collective-permute-start.10 = (f32[2,1]{1,0:T(2,128)S(1)}, f32[2,1]{1,0:T(2,128)S(1)}, u32[]{:S(2)}, u32[]{:S(2)}) collective-permute-start(f32[2,1]{1,0:T(2,128)S(1)} %add.131), channel_id=1, source_target_pairs={{0,128},{2,130},{4,132},{6,134},{8,136},{10,138},{12,140},{14,142}... | collective-permute-start | bytes 32 | tf_op jit(solution)/shard_map/ppermute | solution.py:26
  88.7 5.2 %collective-permute-start.18 = (f32[2,1]{1,0:T(2,128)S(1)}, f32[2,1]{1,0:T(2,128)S(1)}, u32[]{:S(2)}, u32[]{:S(2)}) collective-permute-start(f32[2,1]{1,0:T(2,128)S(1)} %maximum_add_fusion), channel_id=1, source_target_pairs={{0,1},{1,0},{2,3},{3,2},{4,5},{5,4},{6,7},{7,6},{8,9},{9,8},{10,11... | collective-permute-start | bytes 32 | tf_op jit(solution)/shard_map/ppermute | solution.py:26
  (3 other events, 2.0 us)

commit v4 on v3

--- a/solution.py
+++ b/solution.py
@@ -148,7 +148,6 @@
     lines = anchor_rows.shape[0]
 
     partial_sums = -jnp.sum(availability[None] * direction_capacity, axis=1)
-    capacity_value = butterfly_sum(partial_sums, "tm")
 
     balance = direction_nodal[:, :, 0, :]
     storage = direction_nodal[:, :, 1, :]
@@ -177,10 +176,34 @@
     dispatch_scaled = scale_dispatch[None] * dispatch_value
     level_scaled = scale_storage[None, :, 0, :] * level_value
     charge_scaled = scale_storage[None, :, 1, :] * charge_value
-    capacity_scaled = scale_capacity[None] * capacity_value
     squares_local = jnp.sum(residual_nodal * residual_nodal, axis=(1, 2, 3)) + jnp.sum(
         residual_capacity * residual_capacity, axis=(1, 2)
     )
+
+    curvature_local = (
+        jnp.sum(flow_scaled * flow_value, axis=(1, 2))
+        + jnp.sum(dispatch_scaled * dispatch_value, axis=(1, 2))
+        + jnp.sum(charge_scaled * charge_value, axis=(1, 2))
+        + jnp.sum(level_scaled * level_value, axis=(1, 2))
+        + DAMPING
+        * (
+            jnp.sum(direction_nodal * direction_nodal, axis=(1, 2, 3))
+            + jnp.sum(direction_capacity * direction_capacity, axis=(1, 2))
+        )
+    )
+    columns = partial_sums.shape[-1]
+    scalars = jnp.stack([squares_local, curvature_local], axis=-1)
+    packed = jnp.concatenate(
+        [partial_sums, jnp.pad(scalars, ((0, 0), (0, BLOCK - 2)))], axis=-1
+    )
+    packed = butterfly_sum(packed, "tm")
+    capacity_value = packed[:, :columns]
+    capacity_scaled = scale_capacity[None] * capacity_value
+    capacity_part = jnp.sum(capacity_scaled * capacity_value, axis=1)
+    sums = packed[:, columns : columns + 2] + jnp.stack(
+        [jnp.zeros_like(capacity_part), capacity_part], axis=-1
+    )
+    totals = butterfly_sum(sums, "net")
 
     bus_terms = scatter_blocks(
         jnp.concatenate([flow_scaled, -flow_scaled, dispatch_scaled], axis=-1),
@@ -205,14 +228,7 @@
         + DAMPING * direction_capacity
     )
     image_nodal = jnp.stack([image_balance, image_storage], axis=2)
-    curvature_local = jnp.sum(direction_nodal * image_nodal, axis=(1, 2, 3)) + jnp.sum(
-        direction_capacity * (dispatch_scaled + DAMPING * direction_capacity), axis=(1, 2)
-    )
-    sums = butterfly_sum(jnp.stack([squares_local, curvature_local]), "tm")
-    capacity_part = jnp.sum(capacity_scaled * capacity_value, axis=1)
-    sums = sums + jnp.stack([jnp.zeros_like(capacity_part), capacity_part])
-    totals = butterfly_sum(sums, "net")
-    step_size = totals[0] / totals[1]
+    step_size = totals[:, 0] / totals[:, 1]
     updated_nodal = residual_nodal - step_size[:, None, None, None] * image_nodal
     updated_capacity = residual_capacity - step_size[:, None, None] * image_limit
     return (updated_nodal, updated_capacity)

time: 99.2 us -> 85.8 us (0.86)
  waiting for transfers between devices: 38.7 us -> 27.3 us
  starting transfers between devices: 27.4 us -> 20.3 us
  other arithmetic: 12.8 us -> 17.4 us
  between operations: 4.82 us -> 7.4 us
  local copies, waits for them, and re-layouts: 7.34 us -> 5.32 us
    ppermute x15 -> x8, waiting for transfers between devices: 38.7 us -> 27.3 us  [butterfly_sum(): value = value + lax.ppermute(value, axis, pairs)]
    ppermute x15 -> x8, starting transfers between devices: 22.1 us -> 15 us  [butterfly_sum(): value = value + lax.ppermute(value, axis, pairs)]
    reduce_sum x2 -> x4, other arithmetic: 2.49 us -> 5.62 us  [the longest x1 1.95 us: body(): jnp.sum(direction_capacity * direction_capacity, axis=(1, 2))]
    unnamed x32 -> x30, local copies, waits for them, and re-layouts: 2.16 us -> 0.07 us
  transfers between devices with their start and end apart: 19 -> 12, of which waited for: 11 -> 7; matrix products, arithmetic and copies ran while one was open for 14% -> 18% of each run, Pallas kernels for 7% -> 8%
where the time goes in v4:
time: 85.8 us; the launch traced here: 84.1 us
  waiting for transfers between devices  27.3 us (32%)
  starting transfers between devices  20.3 us (24%)
  other arithmetic  17.4 us (20%)
  between operations  7.4 us (9%)
  Pallas kernels  6.36 us (7%)
  local copies, waits for them, and re-layouts  5.32 us (6%)
    ppermute x8, waiting for transfers between devices, butterfly_sum(): value = value + lax.ppermute(value, axis, pairs)  27.3 us
    ppermute x8, starting transfers between devices, butterfly_sum(): value = value + lax.ppermute(value, axis, pairs)  15 us
    pallas_call x1, Pallas kernels, lane_scatter(): pl.pallas_call(lane_scatter_kernel, out_shape=jax.ShapeDtypeStruct((BLOCK...  4.44 us
    ppermute x1, starting transfers between devices, body(): other = lax.ppermute(balance, 'net', [(0, 1), (1, 0)])  3.28 us
    reduce_sum x1, other arithmetic, body(): jnp.sum(direction_capacity * direction_capacity, axis=(1, 2))  1.95 us
    ppermute x1, starting transfers between devices, body(): own_terms = mine + lax.ppermute(theirs, 'net', [(0, 1), (1, 0)])  1.93 us
    pallas_call x1, Pallas kernels, lane_gather(): pl.pallas_call(lane_gather_kernel, out_shape=jax.ShapeDtypeStruct(table.s...  1.92 us
    scatter-add x1, other arithmetic, scatter_blocks(): out = out.at[..., blocks, :].add(within)  1.75 us
  transfers between devices with their start and end apart: 12, of which 7 were waited for; matrix products, arithmetic and copies ran while one was open for 18% of the time, Pallas kernels for 8%

profile of v4, /device:TPU:2, one launch (start us, length us, event | category | flops | bytes accessed | tf_op | source)
XLA Modules:
  0.0 84.1 jit_solution(4800487368594203302)
XLA Ops:
  0.6 0.9 %fusion.11 = (f32[1,1,1,4096]{3,2,1,0:T(1,128)S(1)}, f32[1,1,4096]{2,1,0:T(1,128)S(1)}, f32[1,1,4096]{2,1,0:T(1,128)S(1)}) fusion(f32[1,1,2,4096]{3,2,1,0:T(2,128)} %param.16), kind=kLoop, calls=%fused_computation.53 | loop fusion | bytes 81920 | tf_op jit(solution)/shard_map/slice | solution.py:152
  1.5 3.3 %collective-permute-start = (f32[1,1,4096]{2,1,0:T(1,128)S(1)}, f32[1,1,4096]{2,1,0:T(1,128)S(1)}, u32[]{:S(2)}, u32[]{:S(2)}) collective-permute-start(f32[1,1,4096]{2,1,0:T(1,128)S(1)} %get-tuple-element.14), channel_id=1, source_target_pairs={{0,1},{1,0},{2,3},{3,2},{4,5},{5,4},{6,7},{7,6},{8,9},{9,8},{10,11... | collective-permute-start | bytes 49160 | tf_op jit(solution)/shard_map/ppermute | solution.py:156
  4.8 1.5 %multiply_reduce_fusion.4 = f32[]{:T(128)} fusion(f32[1,1,2,4096]{3,2,1,0:T(2,128)} %param.16), kind=kLoop, calls=%fused_computation.26 | loop fusion | flops 16383 | bytes 32772 | tf_op jit(solution)/shard_map/reduce_sum | solution.py:190
  6.3 0.8 fusion.8
  7.1 0.9 %multiply_reduce_fusion.3 = f32[]{:T(128)} fusion(f32[1,1,32768]{2,1,0:T(1,128)S(1)} %copy-done.1), kind=kLoop, calls=%fused_computation.19 | loop fusion | flops 65535 | bytes 131076 | tf_op jit(solution)/shard_map/reduce_sum | solution.py:179
  8.6 1.5 %add_bitcast_fusion.index_ref = s32[352,128]{1,0:T(8,128)} fusion(s32[32768]{0:T(1024)S(1)} %copy-done.7, s32[6144]{0:T(1024)} %param.29, s32[6144]{0:T(1024)} %param.28), kind=kLoop, calls=%fused_computation.4 | loop fusion | flops 90112 | bytes 360448 | tf_op jit(solution)/shard_map/reshape;broadcast_in_dim;reshape | solution.py:113
  11.5 1.1 %gather_fusion = f32[352,128]{1,0:T(8,128)S(1)} fusion(f32[64,128]{1,0:T(8,128)S(1)} %fusion.4, s32[1024]{0:T(1024)S(1)} %pad_clamp_fusion), kind=kCustom, calls=%fused_computation | custom fusion | bytes 361856 | tf_op jit(solution)/shard_map/jit(_take)/gather | solution.py:111
  12.6 0.8 broadcast_select_fusion.table_ref
  13.4 1.9 %shard_map.167 = f32[352,128]{1,0:T(8,128)} custom-call(f32[352,128]{1,0:T(8,128)} %broadcast_select_fusion.table_ref, s32[352,128]{1,0:T(8,128)} %add_bitcast_fusion.index_ref), custom_call_target="tpu_custom_call" | custom-call | tf_op jit(solution)/shard_map/pallas_call | solution.py:61
  15.3 1.9 %multiply_reduce_fusion.1 = (f32[]{:T(128)}, f32[]{:T(128)}, f32[1,1,32768]{2,1,0:T(1,128)S(1)}, f32[1,32768]{1,0:T(1,128)S(1)}) fusion(f32[1,1,32768]{2,1,0:T(1,128)S(1)} %copy-done.4, f32[1,1,45056]{2,1,0:T(1,128)} %bitcast.79, f32[1,32768]{1,0:T(1,128)S(1)} %copy-done.8, f32[1,32768]{1,0:T(1,128)S(1)} %copy-done.5), kind=kLoop, calls=%fused_computation.17 | loop fusion | flops 262142 | bytes 786440 | tf_op jit(solution)/shard_map/reduce_sum | solution.py:191
  17.3 1.5 %multiply_reduce_fusion.6 = (f32[]{:T(128)}, f32[1,1,6144]{2,1,0:T(1,128)S(1)}) fusion(f32[1,1,45056]{2,1,0:T(1,128)} %bitcast.80, f32[1,6144]{1,0:T(1,128)S(1)} %copy-done.11), kind=kLoop, calls=%fused_computation.30 | loop fusion | flops 24575 | bytes 98308 | tf_op jit(solution)/shard_map/reduce_sum | solution.py:184
  20.1 0.7 multiply_reduce_fusion.7
  24.2 1.0 %collective-permute-done.2 = f32[1,32896]{1,0:T(1,128)S(1)} collective-permute-done((f32[1,32896]{1,0:T(1,128)S(1)}, f32[1,32896]{1,0:T(1,128)S(1)}, u32[]{:S(2)}, u32[]{:S(2)}) %collective-permute-start.2) | collective-permute-done | bytes 131616 | tf_op jit(solution)/shard_map/ppermute | solution.py:26
  25.3 7.8 %collective-permute-start.3 = (f32[1,32896]{1,0:T(1,128)S(1)}, f32[1,32896]{1,0:T(1,128)S(1)}, u32[]{:S(2)}, u32[]{:S(2)}) collective-permute-start(f32[1,32896]{1,0:T(1,128)S(1)} %fusion.10), channel_id=1, source_target_pairs={{0,4},{2,6},{4,0},{6,2},{8,12},{10,14},{12,8},{14,10},{16,20},{18,... | collective-permute-start | bytes 394760 | tf_op jit(solution)/shard_map/ppermute | solution.py:26
  33.1 3.8 %collective-permute-done.3 = f32[1,32896]{1,0:T(1,128)S(1)} collective-permute-done((f32[1,32896]{1,0:T(1,128)S(1)}, f32[1,32896]{1,0:T(1,128)S(1)}, u32[]{:S(2)}, u32[]{:S(2)}) %collective-permute-start.3) | collective-permute-done | bytes 131616 | tf_op jit(solution)/shard_map/ppermute | solution.py:26
  37.2 6.5 %collective-permute-done.4 = f32[1,32896]{1,0:T(1,128)S(1)} collective-permute-done((f32[1,32896]{1,0:T(1,128)S(1)}, f32[1,32896]{1,0:T(1,128)S(1)}, u32[]{:S(2)}, u32[]{:S(2)}) %collective-permute-start.4) | collective-permute-done | bytes 131616 | tf_op jit(solution)/shard_map/ppermute | solution.py:26
  44.1 0.7 pad_bitcast_fusion.index_ref
  44.9 4.1 %collective-permute-done.5 = f32[1,32896]{1,0:T(1,128)S(1)} collective-permute-done((f32[1,32896]{1,0:T(1,128)S(1)}, f32[1,32896]{1,0:T(1,128)S(1)}, u32[]{:S(2)}, u32[]{:S(2)}) %collective-permute-start.5) | collective-permute-done | bytes 131616 | tf_op jit(solution)/shard_map/ppermute | solution.py:26
  49.5 0.7 pad_bitcast_fusion.1.value_ref
  50.2 4.4 %shard_map.168 = f32[128,384]{1,0:T(8,128)} custom-call(f32[128,384]{1,0:T(8,128)} %pad_bitcast_fusion.1.value_ref, s32[128,384]{1,0:T(8,128)} %pad_bitcast_fusion.index_ref), custom_call_target="tpu_custom_call" | custom-call | tf_op jit(solution)/shard_map/pallas_call | solution.py:101
  54.6 1.0 %copy.26 = f32[352,128]{1,0:T(8,128)S(1)} copy(f32[352,128]{0,1:T(8,128)} %bitcast.77) | data formatting | bytes 360448 | tf_op jit(solution)/shard_map/slice | solution.py:105
  55.7 1.8 %scatter_custom_fusion = f32[64,128]{1,0:T(8,128)S(1)} fusion(s32[352]{0:T(512)S(1)} %fusion.8, f32[352,128]{1,0:T(8,128)S(1)} %copy.26, f32[]{:T(128)} %constant.11.clone.1), kind=kCustom, calls=%fused_computation.31 | custom fusion | flops 45056 | bytes 32772 | tf_op jit(solution)/shard_map/scatter-add | solution.py:124
  57.7 1.9 %collective-permute-start.10 = (f32[1,1,4096]{2,1,0:T(1,128)S(1)}, f32[1,1,4096]{2,1,0:T(1,128)S(1)}, u32[]{:S(2)}, u32[]{:S(2)}) collective-permute-start(f32[1,1,4096]{2,1,0:T(1,128)S(1)} %constant_dynamic-slice_fusion), channel_id=1, source_target_pairs={{0,1},{1,0},{2,3},{3,2},{4,5},{5,4},{6,7},{7,6},{8,9},{9,8},{10,11... | collective-permute-start | bytes 49160 | tf_op jit(solution)/shard_map/ppermute | solution.py:218
  59.6 3.9 %collective-permute-done.7 = f32[1,32896]{1,0:T(1,128)S(1)} collective-permute-done((f32[1,32896]{1,0:T(1,128)S(1)}, f32[1,32896]{1,0:T(1,128)S(1)}, u32[]{:S(2)}, u32[]{:S(2)}) %collective-permute-start.7) | collective-permute-done | bytes 131616 | tf_op jit(solution)/shard_map/ppermute | solution.py:26
  63.7 4.3 %collective-permute-start.8 = (f32[1,32896]{1,0:T(1,128)S(1)}, f32[1,32896]{1,0:T(1,128)S(1)}, u32[]{:S(2)}, u32[]{:S(2)}) collective-permute-start(f32[1,32896]{1,0:T(1,128)S(1)} %add.122), channel_id=1, source_target_pairs={{0,128},{2,130},{4,132},{6,134},{8,136},{10,138},{12,140},{14,142}... | collective-permute-start | bytes 394760 | tf_op jit(solution)/shard_map/ppermute | solution.py:26
  68.1 4.9 %collective-permute-done.8 = f32[1,32896]{1,0:T(1,128)S(1)} collective-permute-done((f32[1,32896]{1,0:T(1,128)S(1)}, f32[1,32896]{1,0:T(1,128)S(1)}, u32[]{:S(2)}, u32[]{:S(2)}) %collective-permute-start.8) | collective-permute-done | bytes 131616 | tf_op jit(solution)/shard_map/ppermute | solution.py:26
  73.1 0.9 %multiply_reduce_fusion = f32[]{:T(128)} fusion(f32[1,32896]{1,0:T(1,128)S(1)} %add.123, f32[1,32768]{1,0:T(1,128)S(1)} %bitcast.81), kind=kLoop, calls=%fused_computation.16 | loop fusion | flops 98303 | bytes 262148 | tf_op jit(solution)/shard_map/reduce_sum | solution.py:202
  74.0 0.7 slice_add_fusion.1
  74.7 2.0 %collective-permute-start.9 = (f32[1,2]{1,0:T(1,128)S(1)}, f32[1,2]{1,0:T(1,128)S(1)}, u32[]{:S(2)}, u32[]{:S(2)}) collective-permute-start(f32[1,2]{1,0:T(1,128)S(1)} %slice_add_fusion.1), channel_id=1, source_target_pairs={{0,1},{1,0},{2,3},{3,2},{4,5},{5,4},{6,7},{7,6},{8,9},{9,8},{10,11... | collective-permute-start | bytes 32 | tf_op jit(solution)/shard_map/ppermute | solution.py:26
  76.7 3.1 %collective-permute-done.9 = f32[1,2]{1,0:T(1,128)S(1)} collective-permute-done((f32[1,2]{1,0:T(1,128)S(1)}, f32[1,2]{1,0:T(1,128)S(1)}, u32[]{:S(2)}, u32[]{:S(2)}) %collective-permute-start.9) | collective-permute-done | bytes 40 | tf_op jit(solution)/shard_map/ppermute | solution.py:26
  79.8 0.7 fusion.13
  82.4 1.0 %multiply_subtract_fusion = f32[1,1,32768]{2,1,0:T(1,128)} fusion(f32[1,1,32768]{2,1,0:T(1,128)S(1)} %copy-done.1, f32[1,1,32768]{2,1,0:T(1,128)S(1)} %copy-done.4, f32[1,1,32768]{2,1,0:T(1,128)S(1)} %get-tuple-element.7, f32[1,32768]{1,0:T(1,128)S(1)} %copy-done.5, f32[]{:T(128)} %bitcast.19, f32[1,32768]{1,0:T(1,128)S(1)} %bitcast.82, f32[1,32896]{1,0:T(1,128)S(1)} %add.123), kind=kLoop, calls=%fused_computation.15 | loop fusion | flops 229376 | bytes 917508 | tf_op jit(solution)/shard_map/sub | solution.py:233
  (63 shorter events, 4.7 us)
Async XLA Ops:
  0.6 6.4 %copy-start.1 = (f32[1,1,32768]{2,1,0:T(1,128)S(1)}, f32[1,1,32768]{2,1,0:T(1,128)}, u32[]{:S(2)}) copy-start(f32[1,1,32768]{2,1,0:T(1,128)} %param.19) | copy-start | bytes 393220
  1.5 10.0 %collective-permute-start = (f32[1,1,4096]{2,1,0:T(1,128)S(1)}, f32[1,1,4096]{2,1,0:T(1,128)S(1)}, u32[]{:S(2)}, u32[]{:S(2)}) collective-permute-start(f32[1,1,4096]{2,1,0:T(1,128)S(1)} %get-tuple-element.14), channel_id=1, source_target_pairs={{0,1},{1,0},{2,3},{3,2},{4,5},{5,4},{6,7},{7,6},{8,9},{9,8},{10,11... | collective-permute-start | bytes 49160 | tf_op jit(solution)/shard_map/ppermute | solution.py:156
  4.8 15.3 %collective-permute-start.1 = (f32[1,1,4096]{2,1,0:T(1,128)S(1)}, f32[1,1,4096]{2,1,0:T(1,128)S(1)}, u32[]{:S(2)}, u32[]{:S(2)}) collective-permute-start(f32[1,1,4096]{2,1,0:T(1,128)S(1)} %get-tuple-element.15), channel_id=1, source_target_pairs={{0,254},{2,0},{4,2},{6,4},{8,6},{10,8},{12,10},{14,12},{16,14},{18... | collective-permute-start | bytes 49160 | tf_op jit(solution)/shard_map/ppermute | solution.py:16
  7.1 0.9 %copy-start.6 = (f32[1,1,2,4096]{3,2,1,0:T(2,128)S(1)}, f32[1,1,2,4096]{3,2,1,0:T(2,128)}, u32[]{:S(2)}) copy-start(f32[1,1,2,4096]{3,2,1,0:T(2,128)} %param.18) | copy-start | bytes 98308
  7.1 1.5 %copy-start.7 = (s32[32768]{0:T(1024)S(1)}, s32[32768]{0:T(1024)}, u32[]{:S(2)}) copy-start(s32[32768]{0:T(1024)} %param.31) | copy-start | bytes 393220
  8.6 1.5 %copy-start.12 = (s32[256]{0:T(256)S(1)}, s32[256]{0:T(256)}, u32[]{:S(2)}) copy-start(s32[256]{0:T(256)} %param.30) | copy-start | bytes 3076
  8.6 1.5 %copy-start.13 = (s32[48]{0:T(128)S(1)}, s32[48]{0:T(128)}, u32[]{:S(2)}) copy-start(s32[48]{0:T(128)} %param.27) | copy-start | bytes 580
  8.6 1.5 %copy-start.14 = (s32[48]{0:T(128)S(1)}, s32[48]{0:T(128)}, u32[]{:S(2)}) copy-start(s32[48]{0:T(128)} %param.26) | copy-start | bytes 580
  13.4 1.9 %copy-start.4 = (f32[1,1,32768]{2,1,0:T(1,128)S(1)}, f32[1,1,32768]{2,1,0:T(1,128)}, u32[]{:S(2)}) copy-start(f32[1,1,32768]{2,1,0:T(1,128)} %param.17) | copy-start | bytes 393220
  13.4 1.9 %copy-start.5 = (f32[1,32768]{1,0:T(1,128)S(1)}, f32[1,32768]{1,0:T(1,128)}, u32[]{:S(2)}) copy-start(f32[1,32768]{1,0:T(1,128)} %param.24) | copy-start | bytes 393220
  13.4 1.9 %copy-start.8 = (f32[1,32768]{1,0:T(1,128)S(1)}, f32[1,32768]{1,0:T(1,128)}, u32[]{:S(2)}) copy-start(f32[1,32768]{1,0:T(1,128)} %param.21) | copy-start | bytes 393220
  15.3 2.0 %copy-start.11 = (f32[1,6144]{1,0:T(1,128)S(1)}, f32[1,6144]{1,0:T(1,128)}, u32[]{:S(2)}) copy-start(f32[1,6144]{1,0:T(1,128)} %param.20) | copy-start | bytes 73732
  17.3 2.8 %copy-start.3 = (f32[1,1,2,4096]{3,2,1,0:T(2,128)S(1)}, f32[1,1,2,4096]{3,2,1,0:T(2,128)}, u32[]{:S(2)}) copy-start(f32[1,1,2,4096]{3,2,1,0:T(2,128)} %param.16) | copy-start | bytes 98308
  17.3 2.8 %copy-start.9 = (f32[1,2,4096]{2,1,0:T(2,128)S(1)}, f32[1,2,4096]{2,1,0:T(2,128)}, u32[]{:S(2)}) copy-start(f32[1,2,4096]{2,1,0:T(2,128)} %param.22) | copy-start | bytes 98308
  17.3 2.8 %copy-start.10 = (f32[4096]{0:T(1024)S(1)}, f32[4096]{0:T(1024)}, u32[]{:S(2)}) copy-start(f32[4096]{0:T(1024)} %param.25) | copy-start | bytes 49156
  23.6 1.6 %collective-permute-start.2 = (f32[1,32896]{1,0:T(1,128)S(1)}, f32[1,32896]{1,0:T(1,128)S(1)}, u32[]{:S(2)}, u32[]{:S(2)}) collective-permute-start(f32[1,32896]{1,0:T(1,128)S(1)} %pad_maximum_fusion.1), channel_id=1, source_target_pairs={{0,2},{2,0},{4,6},{6,4},{8,10},{10,8},{12,14},{14,12},{16,18},{18,... | collective-permute-start | bytes 394760 | tf_op jit(solution)/shard_map/ppermute | solution.py:26
  25.3 11.6 %collective-permute-start.3 = (f32[1,32896]{1,0:T(1,128)S(1)}, f32[1,32896]{1,0:T(1,128)S(1)}, u32[]{:S(2)}, u32[]{:S(2)}) collective-permute-start(f32[1,32896]{1,0:T(1,128)S(1)} %fusion.10), channel_id=1, source_target_pairs={{0,4},{2,6},{4,0},{6,2},{8,12},{10,14},{12,8},{14,10},{16,20},{18,... | collective-permute-start | bytes 394760 | tf_op jit(solution)/shard_map/ppermute | solution.py:26
  37.1 6.9 %copy-start = (s32[352,128]{1,0:T(8,128)S(1)}, s32[352,128]{1,0:T(8,128)}, u32[]{:S(2)}) copy-start(s32[352,128]{1,0:T(8,128)} %add_bitcast_fusion.index_ref) | copy-start | bytes 540676
  37.1 6.6 %collective-permute-start.4 = (f32[1,32896]{1,0:T(1,128)S(1)}, f32[1,32896]{1,0:T(1,128)S(1)}, u32[]{:S(2)}, u32[]{:S(2)}) collective-permute-start(f32[1,32896]{1,0:T(1,128)S(1)} %add.118), channel_id=1, source_target_pairs={{0,8},{2,10},{4,12},{6,14},{8,0},{10,2},{12,4},{14,6},{16,24},{18,... | collective-permute-start | bytes 394760 | tf_op jit(solution)/shard_map/ppermute | solution.py:26
  43.9 5.1 %collective-permute-start.5 = (f32[1,32896]{1,0:T(1,128)S(1)}, f32[1,32896]{1,0:T(1,128)S(1)}, u32[]{:S(2)}, u32[]{:S(2)}) collective-permute-start(f32[1,32896]{1,0:T(1,128)S(1)} %add.119), channel_id=1, source_target_pairs={{0,16},{2,18},{4,20},{6,22},{8,24},{10,26},{12,28},{14,30},{16,0},... | collective-permute-start | bytes 394760 | tf_op jit(solution)/shard_map/ppermute | solution.py:26
  49.1 8.3 %collective-permute-start.6 = (f32[1,32896]{1,0:T(1,128)S(1)}, f32[1,32896]{1,0:T(1,128)S(1)}, u32[]{:S(2)}, u32[]{:S(2)}) collective-permute-start(f32[1,32896]{1,0:T(1,128)S(1)} %add.120), channel_id=1, source_target_pairs={{0,32},{2,34},{4,36},{6,38},{8,40},{10,42},{12,44},{14,46},{16,48}... | collective-permute-start | bytes 394760 | tf_op jit(solution)/shard_map/ppermute | solution.py:26
  57.6 6.0 %collective-permute-start.7 = (f32[1,32896]{1,0:T(1,128)S(1)}, f32[1,32896]{1,0:T(1,128)S(1)}, u32[]{:S(2)}, u32[]{:S(2)}) collective-permute-start(f32[1,32896]{1,0:T(1,128)S(1)} %add.121), channel_id=1, source_target_pairs={{0,64},{2,66},{4,68},{6,70},{8,72},{10,74},{12,76},{14,78},{16,80}... | collective-permute-start | bytes 394760 | tf_op jit(solution)/shard_map/ppermute | solution.py:26
  57.7 10.3 %collective-permute-start.10 = (f32[1,1,4096]{2,1,0:T(1,128)S(1)}, f32[1,1,4096]{2,1,0:T(1,128)S(1)}, u32[]{:S(2)}, u32[]{:S(2)}) collective-permute-start(f32[1,1,4096]{2,1,0:T(1,128)S(1)} %constant_dynamic-slice_fusion), channel_id=1, source_target_pairs={{0,1},{1,0},{2,3},{3,2},{4,5},{5,4},{6,7},{7,6},{8,9},{9,8},{10,11... | collective-permute-start | bytes 49160 | tf_op jit(solution)/shard_map/ppermute | solution.py:218
  59.6 8.4 %collective-permute-start.11 = (f32[1,1,4096]{2,1,0:T(1,128)S(1)}, f32[1,1,4096]{2,1,0:T(1,128)S(1)}, u32[]{:S(2)}, u32[]{:S(2)}) collective-permute-start(f32[1,1,4096]{2,1,0:T(1,128)S(1)} %get-tuple-element.6), channel_id=1, source_target_pairs={{0,2},{2,4},{4,6},{6,8},{8,10},{10,12},{12,14},{14,16},{16,18},{18... | collective-permute-start | bytes 49160 | tf_op jit(solution)/shard_map/ppermute | solution.py:16
  63.7 9.3 %collective-permute-start.8 = (f32[1,32896]{1,0:T(1,128)S(1)}, f32[1,32896]{1,0:T(1,128)S(1)}, u32[]{:S(2)}, u32[]{:S(2)}) collective-permute-start(f32[1,32896]{1,0:T(1,128)S(1)} %add.122), channel_id=1, source_target_pairs={{0,128},{2,130},{4,132},{6,134},{8,136},{10,138},{12,140},{14,142}... | collective-permute-start | bytes 394760 | tf_op jit(solution)/shard_map/ppermute | solution.py:26
  68.1 5.0 %copy-start.2 = (f32[32768]{0:T(1024)S(1)}, f32[32768]{0:T(1024)}, u32[]{:S(2)}) copy-start(f32[32768]{0:T(1024)} %param.23) | copy-start | bytes 393220
  74.7 5.1 %collective-permute-start.9 = (f32[1,2]{1,0:T(1,128)S(1)}, f32[1,2]{1,0:T(1,128)S(1)}, u32[]{:S(2)}, u32[]{:S(2)}) collective-permute-start(f32[1,2]{1,0:T(1,128)S(1)} %slice_add_fusion.1), channel_id=1, source_target_pairs={{0,1},{1,0},{2,3},{3,2},{4,5},{5,4},{6,7},{7,6},{8,9},{9,8},{10,11... | collective-permute-start | bytes 32 | tf_op jit(solution)/shard_map/ppermute | solution.py:26

commit v5 on v4

--- a/solution.py
+++ b/solution.py
@@ -16,16 +16,19 @@
     return lax.ppermute(value, axis, pairs)
 
 
-def butterfly_sum(value, axis):
+def butterfly_sum(value, axis, first=0, last=None):
     count = lax.axis_size(axis)
-    if count & (count - 1):
-        return lax.psum(value, axis)
-    step = 1
-    while step < count:
+    bits = count.bit_length() - 1
+    last = bits if last is None else min(last, bits)
+    for bit in range(first, last):
+        step = 1 << bit
         pairs = [(source, source ^ step) for source in range(count)]
         value = value + lax.ppermute(value, axis, pairs)
-        step *= 2
     return value
+
+
+def is_power_of_two(count):
+    return count & (count - 1) == 0
 
 
 def pairwise_total(items):
@@ -147,13 +150,20 @@
     net_index = lax.axis_index("net")
     lines = anchor_rows.shape[0]
 
+    tm_count = lax.axis_size("tm")
     partial_sums = -jnp.sum(availability[None] * direction_capacity, axis=1)
 
     balance = direction_nodal[:, :, 0, :]
     storage = direction_nodal[:, :, 1, :]
     buses = balance.shape[-1] * net_count
+    next_first = passed_along(storage[:, :1], "tm", -1)
+    if is_power_of_two(tm_count):
+        early = butterfly_sum(partial_sums, "tm", 0, 4)
+    else:
+        early = lax.psum(partial_sums, "tm")
     if net_count == 2:
         other = lax.ppermute(balance, "net", [(0, 1), (1, 0)])
+        early, other, next_first = lax.optimization_barrier((early, other, next_first))
         network = jnp.where(
             net_index == 0,
             jnp.concatenate([balance, other], axis=-1),
@@ -161,6 +171,8 @@
         )
     else:
         network = lax.all_gather(balance, "net", axis=2, tiled=True)
+        early, network, next_first = lax.optimization_barrier((early, network, next_first))
+    capacity_value = butterfly_sum(early, "tm", 4) if is_power_of_two(tm_count) else early
 
     blocks = jnp.concatenate([line_anchor, line_target, column_block])
     rows = jnp.concatenate([anchor_rows, target_rows, column_rows])
@@ -168,7 +180,6 @@
     flow_value = gathered[..., :lines] - gathered[..., lines : 2 * lines]
     dispatch_value = gathered[..., 2 * lines :] + direction_capacity
 
-    next_first = passed_along(storage[:, :1], "tm", -1)
     storage_next = jnp.concatenate([storage[:, 1:, :], next_first], axis=1)
     level_value = storage - retention * storage_next
     charge_value = balance - storage
@@ -191,19 +202,15 @@
             + jnp.sum(direction_capacity * direction_capacity, axis=(1, 2))
         )
     )
-    columns = partial_sums.shape[-1]
     scalars = jnp.stack([squares_local, curvature_local], axis=-1)
-    packed = jnp.concatenate(
-        [partial_sums, jnp.pad(scalars, ((0, 0), (0, BLOCK - 2)))], axis=-1
-    )
-    packed = butterfly_sum(packed, "tm")
-    capacity_value = packed[:, :columns]
+    if is_power_of_two(tm_count):
+        scalars = butterfly_sum(scalars, "tm")
+    else:
+        scalars = lax.psum(scalars, "tm")
     capacity_scaled = scale_capacity[None] * capacity_value
     capacity_part = jnp.sum(capacity_scaled * capacity_value, axis=1)
-    sums = packed[:, columns : columns + 2] + jnp.stack(
-        [jnp.zeros_like(capacity_part), capacity_part], axis=-1
-    )
-    totals = butterfly_sum(sums, "net")
+    sums = scalars + jnp.stack([jnp.zeros_like(capacity_part), capacity_part], axis=-1)
+    totals = butterfly_sum(sums, "net") if is_power_of_two(net_count) else lax.psum(sums, "net")
 
     bus_terms = scatter_blocks(
         jnp.concatenate([flow_scaled, -flow_scaled, dispatch_scaled], axis=-1),

time: 85.8 us -> 96.1 us (1.12)
  waiting for transfers between devices: 27.3 us -> 34.7 us
  starting transfers between devices: 20.3 us -> 27.1 us
  other arithmetic: 17.4 us -> 14.6 us
    ppermute x8 -> x15, starting transfers between devices: 15 us -> 22.7 us  [butterfly_sum(): value = value + lax.ppermute(value, axis, pairs)]
    ppermute x8 -> x15, waiting for transfers between devices: 27.3 us -> 34.7 us  [butterfly_sum(): value = value + lax.ppermute(value, axis, pairs)]
    another operation x1, other arithmetic: 1.47 us -> 0.01 us  [gather_blocks(): values = lane_gather(picked.reshape(-1, BLOCK), index.reshape(-1, BLOCK))]
    ppermute x1, starting transfers between devices: 1.93 us -> 0.67 us  [body(): own_terms = mine + lax.ppermute(theirs, 'net', [(0, 1), (1, 0)])]
    neg x0 -> x1, other arithmetic: none -> 1.18 us  [body(): partial_sums = -jnp.sum(availability[None] * direction_capacity, axis=1)]
  transfers between devices with their start and end apart: 12 -> 19, of which waited for: 7 -> 10; matrix products, arithmetic and copies ran while one was open for 18% -> 9% of each run, Pallas kernels for 8% -> 5%
where the time goes in v5:
time: 96.1 us; the launch traced here: 95.3 us
  waiting for transfers between devices  34.7 us (36%)
  starting transfers between devices  27.1 us (28%)
  other arithmetic  14.6 us (15%)
  between operations  7.4 us (8%)
  Pallas kernels  6.34 us (7%)
  local copies, waits for them, and re-layouts  5.15 us (5%)
    ppermute x15, waiting for transfers between devices, butterfly_sum(): value = value + lax.ppermute(value, axis, pairs)  34.7 us
    ppermute x15, starting transfers between devices, butterfly_sum(): value = value + lax.ppermute(value, axis, pairs)  22.7 us
    pallas_call x1, Pallas kernels, lane_scatter(): pl.pallas_call(lane_scatter_kernel, out_shape=jax.ShapeDtypeStruct((BLOCK...  4.43 us
    ppermute x1, starting transfers between devices, body(): other = lax.ppermute(balance, 'net', [(0, 1), (1, 0)])  3.28 us
  transfers between devices with their start and end apart: 19, of which 10 were waited for; matrix products, arithmetic and copies ran while one was open for 9% of the time, Pallas kernels for 5%

profile of v5, /device:TPU:2, one launch (start us, length us, event | category | flops | bytes accessed | tf_op | source)
XLA Modules:
  0.0 95.3 jit_solution(16874771946756656923)
XLA Ops:
  0.6 1.2 %fusion.3 = f32[1,32768]{1,0:T(1,128)S(1)} fusion(f32[1,1,32768]{2,1,0:T(1,128)} %param.17, f32[1,32768]{1,0:T(1,128)} %param.24), kind=kLoop, calls=%fused_computation.13 | loop fusion | flops 65536 | bytes 393216 | tf_op jit(solution)/shard_map/neg | solution.py:154
  2.0 3.3 %collective-permute-start.4 = (f32[1,1,4096]{2,1,0:T(1,128)S(1)}, f32[1,1,4096]{2,1,0:T(1,128)S(1)}, u32[]{:S(2)}, u32[]{:S(2)}) collective-permute-start(f32[1,1,4096]{2,1,0:T(1,128)S(1)} %get-tuple-element.19), channel_id=1, source_target_pairs={{0,1},{1,0},{2,3},{3,2},{4,5},{5,4},{6,7},{7,6},{8,9},{9,8},{10,11... | collective-permute-start | bytes 49160 | tf_op jit(solution)/shard_map/ppermute | solution.py:165
  5.8 8.3 %collective-permute-start.1 = (f32[1,32768]{1,0:T(1,128)S(1)}, f32[1,32768]{1,0:T(1,128)S(1)}, u32[]{:S(2)}, u32[]{:S(2)}) collective-permute-start(f32[1,32768]{1,0:T(1,128)S(1)} %add.128), channel_id=1, source_target_pairs={{0,4},{2,6},{4,0},{6,2},{8,12},{10,14},{12,8},{14,10},{16,20},{18,... | collective-permute-start | bytes 393224 | tf_op jit(solution)/shard_map/ppermute | solution.py:26
  14.9 0.7 pad_bitcast_fusion.index_ref
  15.6 2.7 %collective-permute-done.1 = f32[1,32768]{1,0:T(1,128)S(1)} collective-permute-done((f32[1,32768]{1,0:T(1,128)S(1)}, f32[1,32768]{1,0:T(1,128)S(1)}, u32[]{:S(2)}, u32[]{:S(2)}) %collective-permute-start.1) | collective-permute-done | bytes 131104 | tf_op jit(solution)/shard_map/ppermute | solution.py:26
  20.0 0.9 multiply_reduce_fusion.3
  20.9 4.1 %collective-permute-done.2 = f32[1,32768]{1,0:T(1,128)S(1)} collective-permute-done((f32[1,32768]{1,0:T(1,128)S(1)}, f32[1,32768]{1,0:T(1,128)S(1)}, u32[]{:S(2)}, u32[]{:S(2)}) %collective-permute-start.2) | collective-permute-done | bytes 131104 | tf_op jit(solution)/shard_map/ppermute | solution.py:26
  26.6 3.6 %collective-permute-done.3 = f32[1,32768]{1,0:T(1,128)S(1)} collective-permute-done((f32[1,32768]{1,0:T(1,128)S(1)}, f32[1,32768]{1,0:T(1,128)S(1)}, u32[]{:S(2)}, u32[]{:S(2)}) %collective-permute-start.3) | collective-permute-done | bytes 131104 | tf_op jit(solution)/shard_map/ppermute | solution.py:26
  30.4 1.1 %gather_fusion = f32[352,128]{1,0:T(8,128)S(1)} fusion(f32[64,128]{1,0:T(8,128)S(1)} %fusion.4, s32[1024]{0:T(1024)S(1)} %pad_clamp_fusion), kind=kCustom, calls=%fused_computation | custom fusion | bytes 361856 | tf_op jit(solution)/shard_map/jit(_take)/gather | solution.py:114
  31.5 0.8 broadcast_select_fusion.table_ref
  32.3 1.9 %shard_map.167 = f32[352,128]{1,0:T(8,128)} custom-call(f32[352,128]{1,0:T(8,128)} %broadcast_select_fusion.table_ref, s32[352,128]{1,0:T(8,128)} %copy-done), custom_call_target="tpu_custom_call" | custom-call | tf_op jit(solution)/shard_map/pallas_call | solution.py:64
  34.2 1.8 %multiply_reduce_fusion.1 = (f32[]{:T(128)}, f32[]{:T(128)}, f32[1,1,32768]{2,1,0:T(1,128)S(1)}) fusion(f32[1,1,32768]{2,1,0:T(1,128)S(1)} %copy-done.1, f32[1,1,45056]{2,1,0:T(1,128)} %bitcast.79, f32[1,32768]{1,0:T(1,128)S(1)} %copy-done.8), kind=kLoop, calls=%fused_computation.16 | loop fusion | flops 196606 | bytes 524296 | tf_op jit(solution)/shard_map/reduce_sum | solution.py:202
  36.0 1.4 %multiply_reduce_fusion.6 = (f32[]{:T(128)}, f32[1,1,6144]{2,1,0:T(1,128)S(1)}) fusion(f32[1,1,45056]{2,1,0:T(1,128)} %bitcast.80, f32[1,6144]{1,0:T(1,128)S(1)} %copy-done.13), kind=kLoop, calls=%fused_computation.28 | loop fusion | flops 24575 | bytes 98308 | tf_op jit(solution)/shard_map/reduce_sum | solution.py:195
  43.2 4.4 %shard_map.168 = f32[128,384]{1,0:T(8,128)} custom-call(f32[128,384]{1,0:T(8,128)} %pad_bitcast_fusion.1.value_ref, s32[128,384]{1,0:T(8,128)} %pad_bitcast_fusion.index_ref), custom_call_target="tpu_custom_call" | custom-call | tf_op jit(solution)/shard_map/pallas_call | solution.py:104
  47.6 1.0 %copy.26 = f32[352,128]{1,0:T(8,128)S(1)} copy(f32[352,128]{0,1:T(8,128)} %bitcast.77) | data formatting | bytes 360448 | tf_op jit(solution)/shard_map/slice | solution.py:108
  48.7 1.8 %scatter_custom_fusion = f32[64,128]{1,0:T(8,128)S(1)} fusion(s32[352]{0:T(512)S(1)} %fusion.8, f32[352,128]{1,0:T(8,128)S(1)} %copy.26, f32[]{:T(128)} %constant.11.clone.1), kind=kCustom, calls=%fused_computation.29 | custom fusion | flops 45056 | bytes 32772 | tf_op jit(solution)/shard_map/scatter-add | solution.py:127
  51.3 2.0 %collective-permute-start.7 = (f32[1,2]{1,0:T(1,128)S(1)}, f32[1,2]{1,0:T(1,128)S(1)}, u32[]{:S(2)}, u32[]{:S(2)}) collective-permute-start(f32[1,2]{1,0:T(1,128)S(1)} %fusion.11), channel_id=1, source_target_pairs={{0,4},{2,6},{4,0},{6,2},{8,12},{10,14},{12,8},{14,10},{16,20},{18,... | collective-permute-start | bytes 32 | tf_op jit(solution)/shard_map/ppermute | solution.py:26
  53.6 1.3 %collective-permute-done.7 = f32[1,2]{1,0:T(1,128)S(1)} collective-permute-done((f32[1,2]{1,0:T(1,128)S(1)}, f32[1,2]{1,0:T(1,128)S(1)}, u32[]{:S(2)}, u32[]{:S(2)}) %collective-permute-start.7) | collective-permute-done | bytes 40 | tf_op jit(solution)/shard_map/ppermute | solution.py:26
  54.9 5.0 %collective-permute-done.8 = f32[1,2]{1,0:T(1,128)S(1)} collective-permute-done((f32[1,2]{1,0:T(1,128)S(1)}, f32[1,2]{1,0:T(1,128)S(1)}, u32[]{:S(2)}, u32[]{:S(2)}) %collective-permute-start.8) | collective-permute-done | bytes 40 | tf_op jit(solution)/shard_map/ppermute | solution.py:26
  60.0 3.5 %collective-permute-done.9 = f32[1,2]{1,0:T(1,128)S(1)} collective-permute-done((f32[1,2]{1,0:T(1,128)S(1)}, f32[1,2]{1,0:T(1,128)S(1)}, u32[]{:S(2)}, u32[]{:S(2)}) %collective-permute-start.9) | collective-permute-done | bytes 40 | tf_op jit(solution)/shard_map/ppermute | solution.py:26
  63.5 1.9 %collective-permute-start.10 = (f32[1,2]{1,0:T(1,128)S(1)}, f32[1,2]{1,0:T(1,128)S(1)}, u32[]{:S(2)}, u32[]{:S(2)}) collective-permute-start(f32[1,2]{1,0:T(1,128)S(1)} %add.143), channel_id=1, source_target_pairs={{0,32},{2,34},{4,36},{6,38},{8,40},{10,42},{12,44},{14,46},{16,48}... | collective-permute-start | bytes 32 | tf_op jit(solution)/shard_map/ppermute | solution.py:26
  65.4 1.6 %collective-permute-done.10 = f32[1,2]{1,0:T(1,128)S(1)} collective-permute-done((f32[1,2]{1,0:T(1,128)S(1)}, f32[1,2]{1,0:T(1,128)S(1)}, u32[]{:S(2)}, u32[]{:S(2)}) %collective-permute-start.10) | collective-permute-done | bytes 40 | tf_op jit(solution)/shard_map/ppermute | solution.py:26
  67.1 1.6 %collective-permute-start.11 = (f32[1,2]{1,0:T(1,128)S(1)}, f32[1,2]{1,0:T(1,128)S(1)}, u32[]{:S(2)}, u32[]{:S(2)}) collective-permute-start(f32[1,2]{1,0:T(1,128)S(1)} %add.144), channel_id=1, source_target_pairs={{0,64},{2,66},{4,68},{6,70},{8,72},{10,74},{12,76},{14,78},{16,80}... | collective-permute-start | bytes 32 | tf_op jit(solution)/shard_map/ppermute | solution.py:26
  68.7 2.8 %collective-permute-done.11 = f32[1,2]{1,0:T(1,128)S(1)} collective-permute-done((f32[1,2]{1,0:T(1,128)S(1)}, f32[1,2]{1,0:T(1,128)S(1)}, u32[]{:S(2)}, u32[]{:S(2)}) %collective-permute-start.11) | collective-permute-done | bytes 40 | tf_op jit(solution)/shard_map/ppermute | solution.py:26
  71.5 3.4 %collective-permute-start.12 = (f32[1,2]{1,0:T(1,128)S(1)}, f32[1,2]{1,0:T(1,128)S(1)}, u32[]{:S(2)}, u32[]{:S(2)}) collective-permute-start(f32[1,2]{1,0:T(1,128)S(1)} %add.145), channel_id=1, source_target_pairs={{0,128},{2,130},{4,132},{6,134},{8,136},{10,138},{12,140},{14,142}... | collective-permute-start | bytes 32 | tf_op jit(solution)/shard_map/ppermute | solution.py:26
  75.1 2.6 %collective-permute-start.15 = (f32[1,32768]{1,0:T(1,128)S(1)}, f32[1,32768]{1,0:T(1,128)S(1)}, u32[]{:S(2)}, u32[]{:S(2)}) collective-permute-start(f32[1,32768]{1,0:T(1,128)S(1)} %add.148), channel_id=1, source_target_pairs={{0,128},{2,130},{4,132},{6,134},{8,136},{10,138},{12,140},{14,142}... | collective-permute-start | bytes 393224 | tf_op jit(solution)/shard_map/ppermute | solution.py:26
  77.8 7.1 %collective-permute-done.15 = f32[1,32768]{1,0:T(1,128)S(1)} collective-permute-done((f32[1,32768]{1,0:T(1,128)S(1)}, f32[1,32768]{1,0:T(1,128)S(1)}, u32[]{:S(2)}, u32[]{:S(2)}) %collective-permute-start.15) | collective-permute-done | bytes 131104 | tf_op jit(solution)/shard_map/ppermute | solution.py:26
  84.9 0.9 multiply_reduce_fusion
  85.8 0.7 maximum_add_fusion
  86.5 2.3 %collective-permute-start.16 = (f32[1,2]{1,0:T(1,128)S(1)}, f32[1,2]{1,0:T(1,128)S(1)}, u32[]{:S(2)}, u32[]{:S(2)}) collective-permute-start(f32[1,2]{1,0:T(1,128)S(1)} %maximum_add_fusion), channel_id=1, source_target_pairs={{0,1},{1,0},{2,3},{3,2},{4,5},{5,4},{6,7},{7,6},{8,9},{9,8},{10,11... | collective-permute-start | bytes 32 | tf_op jit(solution)/shard_map/ppermute | solution.py:26
  88.8 2.8 %collective-permute-done.16 = f32[1,2]{1,0:T(1,128)S(1)} collective-permute-done((f32[1,2]{1,0:T(1,128)S(1)}, f32[1,2]{1,0:T(1,128)S(1)}, u32[]{:S(2)}, u32[]{:S(2)}) %collective-permute-start.16) | collective-permute-done | bytes 40 | tf_op jit(solution)/shard_map/ppermute | solution.py:26
  94.2 1.1 %multiply_subtract_fusion = f32[1,1,32768]{2,1,0:T(1,128)} fusion(f32[1,1,32768]{2,1,0:T(1,128)S(1)} %copy-done.5, f32[1,1,32768]{2,1,0:T(1,128)S(1)} %copy-done.1, f32[1,1,32768]{2,1,0:T(1,128)S(1)} %get-tuple-element.13, f32[1,32768]{1,0:T(1,128)S(1)} %copy-done.3, f32[1,32768]{1,0:T(1,128)S(1)} %bitcast.82, f32[]{:T(128)} %bitcast.19, ...), kind=kLoop, calls=%fused_computation.14 | loop fusion | flops 262144 | bytes 1048580 | tf_op jit(solution)/shard_map/sub | solution.py:240
  (86 shorter events, 8.1 us)
Async XLA Ops:
  0.6 5.0 %copy-start.7 = (s32[32768]{0:T(1024)S(1)}, s32[32768]{0:T(1024)}, u32[]{:S(2)}) copy-start(s32[32768]{0:T(1024)} %param.31) | copy-start | bytes 393220
  1.8 3.8 %copy-start.11 = (s32[6144]{0:T(1024)S(1)}, s32[6144]{0:T(1024)}, u32[]{:S(2)}) copy-start(s32[6144]{0:T(1024)} %param.29) | copy-start | bytes 73732
  1.8 3.8 %copy-start.12 = (s32[6144]{0:T(1024)S(1)}, s32[6144]{0:T(1024)}, u32[]{:S(2)}) copy-start(s32[6144]{0:T(1024)} %param.28) | copy-start | bytes 73732
  1.9 3.8 %collective-permute-start = (f32[1,32768]{1,0:T(1,128)S(1)}, f32[1,32768]{1,0:T(1,128)S(1)}, u32[]{:S(2)}, u32[]{:S(2)}) collective-permute-start(f32[1,32768]{1,0:T(1,128)S(1)} %fusion.3), channel_id=1, source_target_pairs={{0,2},{2,0},{4,6},{6,4},{8,10},{10,8},{12,14},{14,12},{16,18},{18,... | collective-permute-start | bytes 393224 | tf_op jit(solution)/shard_map/ppermute | solution.py:26
  2.0 28.3 %collective-permute-start.4 = (f32[1,1,4096]{2,1,0:T(1,128)S(1)}, f32[1,1,4096]{2,1,0:T(1,128)S(1)}, u32[]{:S(2)}, u32[]{:S(2)}) collective-permute-start(f32[1,1,4096]{2,1,0:T(1,128)S(1)} %get-tuple-element.19), channel_id=1, source_target_pairs={{0,1},{1,0},{2,3},{3,2},{4,5},{5,4},{6,7},{7,6},{8,9},{9,8},{10,11... | collective-permute-start | bytes 49160 | tf_op jit(solution)/shard_map/ppermute | solution.py:165
  5.3 25.1 %collective-permute-start.5 = (f32[1,1,4096]{2,1,0:T(1,128)S(1)}, f32[1,1,4096]{2,1,0:T(1,128)S(1)}, u32[]{:S(2)}, u32[]{:S(2)}) collective-permute-start(f32[1,1,4096]{2,1,0:T(1,128)S(1)} %get-tuple-element.20), channel_id=1, source_target_pairs={{0,254},{2,0},{4,2},{6,4},{8,6},{10,8},{12,10},{14,12},{16,14},{18... | collective-permute-start | bytes 49160 | tf_op jit(solution)/shard_map/ppermute | solution.py:16
  5.7 9.1 %copy-start = (s32[352,128]{1,0:T(8,128)}, s32[352,128]{1,0:T(8,128)S(1)}, u32[]{:S(2)}) copy-start(s32[352,128]{1,0:T(8,128)S(1)} %add_bitcast_fusion.index_ref) | copy-start | bytes 540676
  5.8 12.5 %collective-permute-start.1 = (f32[1,32768]{1,0:T(1,128)S(1)}, f32[1,32768]{1,0:T(1,128)S(1)}, u32[]{:S(2)}, u32[]{:S(2)}) collective-permute-start(f32[1,32768]{1,0:T(1,128)S(1)} %add.128), channel_id=1, source_target_pairs={{0,4},{2,6},{4,0},{6,2},{8,12},{10,14},{12,8},{14,10},{16,20},{18,... | collective-permute-start | bytes 393224 | tf_op jit(solution)/shard_map/ppermute | solution.py:26
  15.6 3.0 %copy-start.6 = (f32[1,1,2,4096]{3,2,1,0:T(2,128)S(1)}, f32[1,1,2,4096]{3,2,1,0:T(2,128)}, u32[]{:S(2)}) copy-start(f32[1,1,2,4096]{3,2,1,0:T(2,128)} %param.18) | copy-start | bytes 98308
  15.6 4.4 %copy-start.5 = (f32[1,1,32768]{2,1,0:T(1,128)S(1)}, f32[1,1,32768]{2,1,0:T(1,128)}, u32[]{:S(2)}) copy-start(f32[1,1,32768]{2,1,0:T(1,128)} %param.19) | copy-start | bytes 393220
  18.4 6.6 %collective-permute-start.2 = (f32[1,32768]{1,0:T(1,128)S(1)}, f32[1,32768]{1,0:T(1,128)S(1)}, u32[]{:S(2)}, u32[]{:S(2)}) collective-permute-start(f32[1,32768]{1,0:T(1,128)S(1)} %add.129), channel_id=1, source_target_pairs={{0,8},{2,10},{4,12},{6,14},{8,0},{10,2},{12,4},{14,6},{16,24},{18,... | collective-permute-start | bytes 393224 | tf_op jit(solution)/shard_map/ppermute | solution.py:26
  25.1 5.1 %collective-permute-start.3 = (f32[1,32768]{1,0:T(1,128)S(1)}, f32[1,32768]{1,0:T(1,128)S(1)}, u32[]{:S(2)}, u32[]{:S(2)}) collective-permute-start(f32[1,32768]{1,0:T(1,128)S(1)} %add.130), channel_id=1, source_target_pairs={{0,16},{2,18},{4,20},{6,22},{8,24},{10,26},{12,28},{14,30},{16,0},... | collective-permute-start | bytes 393224 | tf_op jit(solution)/shard_map/ppermute | solution.py:26
  32.3 1.9 %copy-start.1 = (f32[1,1,32768]{2,1,0:T(1,128)S(1)}, f32[1,1,32768]{2,1,0:T(1,128)}, u32[]{:S(2)}) copy-start(f32[1,1,32768]{2,1,0:T(1,128)} %param.17) | copy-start | bytes 393220
  32.3 1.9 %copy-start.8 = (f32[1,32768]{1,0:T(1,128)S(1)}, f32[1,32768]{1,0:T(1,128)}, u32[]{:S(2)}) copy-start(f32[1,32768]{1,0:T(1,128)} %param.21) | copy-start | bytes 393220
  34.2 1.8 %copy-start.13 = (f32[1,6144]{1,0:T(1,128)S(1)}, f32[1,6144]{1,0:T(1,128)}, u32[]{:S(2)}) copy-start(f32[1,6144]{1,0:T(1,128)} %param.20) | copy-start | bytes 73732
  36.0 2.7 %copy-start.9 = (f32[1,2,4096]{2,1,0:T(2,128)S(1)}, f32[1,2,4096]{2,1,0:T(2,128)}, u32[]{:S(2)}) copy-start(f32[1,2,4096]{2,1,0:T(2,128)} %param.22) | copy-start | bytes 98308
  36.0 2.7 %copy-start.10 = (f32[4096]{0:T(1024)S(1)}, f32[4096]{0:T(1024)}, u32[]{:S(2)}) copy-start(f32[4096]{0:T(1024)} %param.25) | copy-start | bytes 49156
  42.0 9.2 %collective-permute-start.6 = (f32[1,2]{1,0:T(1,128)S(1)}, f32[1,2]{1,0:T(1,128)S(1)}, u32[]{:S(2)}, u32[]{:S(2)}) collective-permute-start(f32[1,2]{1,0:T(1,128)S(1)} %pad_maximum_fusion.1), channel_id=1, source_target_pairs={{0,2},{2,0},{4,6},{6,4},{8,10},{10,8},{12,14},{14,12},{16,18},{18,... | collective-permute-start | bytes 32 | tf_op jit(solution)/shard_map/ppermute | solution.py:26
  42.1 11.2 %collective-permute-start.13 = (f32[1,32768]{1,0:T(1,128)S(1)}, f32[1,32768]{1,0:T(1,128)S(1)}, u32[]{:S(2)}, u32[]{:S(2)}) collective-permute-start(f32[1,32768]{1,0:T(1,128)S(1)} %add.131), channel_id=1, source_target_pairs={{0,32},{2,34},{4,36},{6,38},{8,40},{10,42},{12,44},{14,46},{16,48}... | collective-permute-start | bytes 393224 | tf_op jit(solution)/shard_map/ppermute | solution.py:26
  50.4 27.3 %collective-permute-start.17 = (f32[1,1,4096]{2,1,0:T(1,128)S(1)}, f32[1,1,4096]{2,1,0:T(1,128)S(1)}, u32[]{:S(2)}, u32[]{:S(2)}) collective-permute-start(f32[1,1,4096]{2,1,0:T(1,128)S(1)} %constant_dynamic-slice_fusion), channel_id=1, source_target_pairs={{0,1},{1,0},{2,3},{3,2},{4,5},{5,4},{6,7},{7,6},{8,9},{9,8},{10,11... | collective-permute-start | bytes 49160 | tf_op jit(solution)/shard_map/ppermute | solution.py:225
  51.1 26.6 %collective-permute-start.18 = (f32[1,1,4096]{2,1,0:T(1,128)S(1)}, f32[1,1,4096]{2,1,0:T(1,128)S(1)}, u32[]{:S(2)}, u32[]{:S(2)}) collective-permute-start(f32[1,1,4096]{2,1,0:T(1,128)S(1)} %get-tuple-element.12), channel_id=1, source_target_pairs={{0,2},{2,4},{4,6},{6,8},{8,10},{10,12},{12,14},{14,16},{16,18},{18... | collective-permute-start | bytes 49160 | tf_op jit(solution)/shard_map/ppermute | solution.py:16
  51.3 3.6 %collective-permute-start.7 = (f32[1,2]{1,0:T(1,128)S(1)}, f32[1,2]{1,0:T(1,128)S(1)}, u32[]{:S(2)}, u32[]{:S(2)}) collective-permute-start(f32[1,2]{1,0:T(1,128)S(1)} %fusion.11), channel_id=1, source_target_pairs={{0,4},{2,6},{4,0},{6,2},{8,12},{10,14},{12,8},{14,10},{16,20},{18,... | collective-permute-start | bytes 32 | tf_op jit(solution)/shard_map/ppermute | solution.py:26
  53.5 21.5 %collective-permute-start.14 = (f32[1,32768]{1,0:T(1,128)S(1)}, f32[1,32768]{1,0:T(1,128)S(1)}, u32[]{:S(2)}, u32[]{:S(2)}) collective-permute-start(f32[1,32768]{1,0:T(1,128)S(1)} %add.147), channel_id=1, source_target_pairs={{0,64},{2,66},{4,68},{6,70},{8,72},{10,74},{12,76},{14,78},{16,80}... | collective-permute-start | bytes 393224 | tf_op jit(solution)/shard_map/ppermute | solution.py:26
  54.9 5.1 %collective-permute-start.8 = (f32[1,2]{1,0:T(1,128)S(1)}, f32[1,2]{1,0:T(1,128)S(1)}, u32[]{:S(2)}, u32[]{:S(2)}) collective-permute-start(f32[1,2]{1,0:T(1,128)S(1)} %fusion.12), channel_id=1, source_target_pairs={{0,8},{2,10},{4,12},{6,14},{8,0},{10,2},{12,4},{14,6},{16,24},{18,... | collective-permute-start | bytes 32 | tf_op jit(solution)/shard_map/ppermute | solution.py:26
  60.0 3.5 %collective-permute-start.9 = (f32[1,2]{1,0:T(1,128)S(1)}, f32[1,2]{1,0:T(1,128)S(1)}, u32[]{:S(2)}, u32[]{:S(2)}) collective-permute-start(f32[1,2]{1,0:T(1,128)S(1)} %add.142), channel_id=1, source_target_pairs={{0,16},{2,18},{4,20},{6,22},{8,24},{10,26},{12,28},{14,30},{16,0},... | collective-permute-start | bytes 32 | tf_op jit(solution)/shard_map/ppermute | solution.py:26
  63.5 3.5 %collective-permute-start.10 = (f32[1,2]{1,0:T(1,128)S(1)}, f32[1,2]{1,0:T(1,128)S(1)}, u32[]{:S(2)}, u32[]{:S(2)}) collective-permute-start(f32[1,2]{1,0:T(1,128)S(1)} %add.143), channel_id=1, source_target_pairs={{0,32},{2,34},{4,36},{6,38},{8,40},{10,42},{12,44},{14,46},{16,48}... | collective-permute-start | bytes 32 | tf_op jit(solution)/shard_map/ppermute | solution.py:26
  67.1 4.4 %collective-permute-start.11 = (f32[1,2]{1,0:T(1,128)S(1)}, f32[1,2]{1,0:T(1,128)S(1)}, u32[]{:S(2)}, u32[]{:S(2)}) collective-permute-start(f32[1,2]{1,0:T(1,128)S(1)} %add.144), channel_id=1, source_target_pairs={{0,64},{2,66},{4,68},{6,70},{8,72},{10,74},{12,76},{14,78},{16,80}... | collective-permute-start | bytes 32 | tf_op jit(solution)/shard_map/ppermute | solution.py:26
  71.5 14.3 %collective-permute-start.12 = (f32[1,2]{1,0:T(1,128)S(1)}, f32[1,2]{1,0:T(1,128)S(1)}, u32[]{:S(2)}, u32[]{:S(2)}) collective-permute-start(f32[1,2]{1,0:T(1,128)S(1)} %add.145), channel_id=1, source_target_pairs={{0,128},{2,130},{4,132},{6,134},{8,136},{10,138},{12,140},{14,142}... | collective-permute-start | bytes 32 | tf_op jit(solution)/shard_map/ppermute | solution.py:26
  75.1 9.8 %copy-start.4 = (f32[32768]{0:T(1024)S(1)}, f32[32768]{0:T(1024)}, u32[]{:S(2)}) copy-start(f32[32768]{0:T(1024)} %param.23) | copy-start | bytes 393220
  75.1 9.8 %collective-permute-start.15 = (f32[1,32768]{1,0:T(1,128)S(1)}, f32[1,32768]{1,0:T(1,128)S(1)}, u32[]{:S(2)}, u32[]{:S(2)}) collective-permute-start(f32[1,32768]{1,0:T(1,128)S(1)} %add.148), channel_id=1, source_target_pairs={{0,128},{2,130},{4,132},{6,134},{8,136},{10,138},{12,140},{14,142}... | collective-permute-start | bytes 393224 | tf_op jit(solution)/shard_map/ppermute | solution.py:26
  84.9 9.3 %copy-start.3 = (f32[1,32768]{1,0:T(1,128)S(1)}, f32[1,32768]{1,0:T(1,128)}, u32[]{:S(2)}) copy-start(f32[1,32768]{1,0:T(1,128)} %param.24) | copy-start | bytes 393220
  86.5 5.1 %collective-permute-start.16 = (f32[1,2]{1,0:T(1,128)S(1)}, f32[1,2]{1,0:T(1,128)S(1)}, u32[]{:S(2)}, u32[]{:S(2)}) collective-permute-start(f32[1,2]{1,0:T(1,128)S(1)} %maximum_add_fusion), channel_id=1, source_target_pairs={{0,1},{1,0},{2,3},{3,2},{4,5},{5,4},{6,7},{7,6},{8,9},{9,8},{10,11... | collective-permute-start | bytes 32 | tf_op jit(solution)/shard_map/ppermute | solution.py:26
  (4 other events, 3.3 us)

commit v6 on v4

--- a/solution.py
+++ b/solution.py
@@ -168,7 +168,8 @@
     flow_value = gathered[..., :lines] - gathered[..., lines : 2 * lines]
     dispatch_value = gathered[..., 2 * lines :] + direction_capacity
 
-    next_first = passed_along(storage[:, :1], "tm", -1)
+    first_hour, gathered = lax.optimization_barrier((storage[:, :1], gathered))
+    next_first = passed_along(first_hour, "tm", -1)
     storage_next = jnp.concatenate([storage[:, 1:, :], next_first], axis=1)
     level_value = storage - retention * storage_next
     charge_value = balance - storage
@@ -203,6 +204,12 @@
     sums = packed[:, columns : columns + 2] + jnp.stack(
         [jnp.zeros_like(capacity_part), capacity_part], axis=-1
     )
+    image_limit = (
+        dispatch_scaled
+        - availability[None] * capacity_scaled[:, None, :]
+        + DAMPING * direction_capacity
+    )
+    sums, image_limit = lax.optimization_barrier((sums, image_limit))
     totals = butterfly_sum(sums, "net")
 
     bus_terms = scatter_blocks(
@@ -222,11 +229,6 @@
     behind = passed_along(level_scaled[:, -1:], "tm", 1)
     level_before = jnp.concatenate([behind, level_scaled[:, :-1, :]], axis=1)
     image_storage = level_scaled - retention * level_before - charge_scaled + DAMPING * storage
-    image_limit = (
-        dispatch_scaled
-        - availability[None] * capacity_scaled[:, None, :]
-        + DAMPING * direction_capacity
-    )
     image_nodal = jnp.stack([image_balance, image_storage], axis=2)
     step_size = totals[:, 0] / totals[:, 1]
     updated_nodal = residual_nodal - step_size[:, None, None, None] * image_nodal

time: 85.8 us -> 84.4 us (0.984)
  other arithmetic: 17.4 us -> 16 us
    reduce_sum x1, other arithmetic: 0.87 us -> 1.8 us  [body(): jnp.sum(residual_capacity * residual_capacity, axis=(1, 2))]
  transfers between devices with their start and end apart: 12 -> 12, of which waited for: 7 -> 7; matrix products, arithmetic and copies ran while one was open for 18% -> 15% of each run, Pallas kernels for 8% -> 5%
where the time goes in v6:
time: 84.4 us; the launch traced here: 82.8 us
  waiting for transfers between devices  27.3 us (32%)
  starting transfers between devices  20.2 us (24%)
  other arithmetic  16 us (19%)
  between operations  7.36 us (9%)
  Pallas kernels  6.35 us (8%)
  local copies, waits for them, and re-layouts  5.5 us (7%)
    ppermute x8, waiting for transfers between devices, butterfly_sum(): value = value + lax.ppermute(value, axis, pairs)  27.3 us
    ppermute x8, starting transfers between devices, butterfly_sum(): value = value + lax.ppermute(value, axis, pairs)  15 us
    pallas_call x1, Pallas kernels, lane_scatter(): pl.pallas_call(lane_scatter_kernel, out_shape=jax.ShapeDtypeStruct((BLOCK...  4.44 us
    ppermute x1, starting transfers between devices, body(): other = lax.ppermute(balance, 'net', [(0, 1), (1, 0)])  3.28 us
    reduce_sum x1, other arithmetic, body(): jnp.sum(direction_capacity * direction_capacity, axis=(1, 2))  1.94 us
    ppermute x1, starting transfers between devices, body(): own_terms = mine + lax.ppermute(theirs, 'net', [(0, 1), (1, 0)])  1.93 us
    pallas_call x1, Pallas kernels, lane_gather(): pl.pallas_call(lane_gather_kernel, out_shape=jax.ShapeDtypeStruct(table.s...  1.92 us
    reduce_sum x1, other arithmetic, body(): jnp.sum(residual_capacity * residual_capacity, axis=(1, 2))  1.8 us
  transfers between devices with their start and end apart: 12, of which 7 were waited for; matrix products, arithmetic and copies ran while one was open for 15% of the time, Pallas kernels for 5%

profile of v6, /device:TPU:2, one launch (start us, length us, event | category | flops | bytes accessed | tf_op | source)
XLA Modules:
  0.0 82.8 jit_solution(9353758062679415190)
XLA Ops:
  0.6 0.9 %fusion.11 = (f32[1,1,1,4096]{3,2,1,0:T(1,128)S(1)}, f32[1,1,4096]{2,1,0:T(1,128)S(1)}, f32[1,1,4096]{2,1,0:T(1,128)S(1)}) fusion(f32[1,1,2,4096]{3,2,1,0:T(2,128)} %param.16), kind=kLoop, calls=%fused_computation.53 | loop fusion | bytes 81920 | tf_op jit(solution)/shard_map/slice | solution.py:152
  1.6 3.3 %collective-permute-start = (f32[1,1,4096]{2,1,0:T(1,128)S(1)}, f32[1,1,4096]{2,1,0:T(1,128)S(1)}, u32[]{:S(2)}, u32[]{:S(2)}) collective-permute-start(f32[1,1,4096]{2,1,0:T(1,128)S(1)} %get-tuple-element.20), channel_id=1, source_target_pairs={{0,1},{1,0},{2,3},{3,2},{4,5},{5,4},{6,7},{7,6},{8,9},{9,8},{10,11... | collective-permute-start | bytes 49160 | tf_op jit(solution)/shard_map/ppermute | solution.py:156
  5.5 0.8 fusion.8
  6.3 1.8 %multiply_reduce_fusion.3 = f32[]{:T(128)} fusion(f32[1,1,32768]{2,1,0:T(1,128)} %param.19), kind=kLoop, calls=%fused_computation.19 | loop fusion | flops 65535 | bytes 131076 | tf_op jit(solution)/shard_map/reduce_sum | solution.py:180
  8.1 0.6 multiply_reduce_fusion.5
  8.9 0.7 add_bitcast_fusion.index_ref
  11.0 1.1 %gather_fusion = f32[352,128]{1,0:T(8,128)S(1)} fusion(f32[64,128]{1,0:T(8,128)S(1)} %fusion.4, s32[1024]{0:T(1024)S(1)} %pad_clamp_fusion), kind=kCustom, calls=%fused_computation | custom fusion | bytes 361856 | tf_op jit(solution)/shard_map/jit(_take)/gather | solution.py:111
  12.1 0.8 broadcast_select_fusion.table_ref
  12.9 1.9 %shard_map.167 = f32[352,128]{1,0:T(8,128)} custom-call(f32[352,128]{1,0:T(8,128)} %broadcast_select_fusion.table_ref, s32[352,128]{1,0:T(8,128)} %add_bitcast_fusion.index_ref), custom_call_target="tpu_custom_call" | custom-call | tf_op jit(solution)/shard_map/pallas_call | solution.py:61
  14.8 1.9 %multiply_reduce_fusion.1 = (f32[]{:T(128)}, f32[]{:T(128)}, f32[1,1,32768]{2,1,0:T(1,128)S(1)}, f32[1,32768]{1,0:T(1,128)S(1)}) fusion(f32[1,1,32768]{2,1,0:T(1,128)S(1)} %copy-done.4, f32[1,1,45056]{2,1,0:T(1,128)} %bitcast.75, f32[1,32768]{1,0:T(1,128)S(1)} %copy-done.8, f32[1,32768]{1,0:T(1,128)S(1)} %copy-done.5), kind=kLoop, calls=%fused_computation.17 | loop fusion | flops 262142 | bytes 786440 | tf_op jit(solution)/shard_map/reduce_sum | solution.py:192
  16.8 1.4 %multiply_reduce_fusion.6 = (f32[]{:T(128)}, f32[1,1,6144]{2,1,0:T(1,128)S(1)}) fusion(f32[1,1,45056]{2,1,0:T(1,128)} %bitcast.76, f32[1,6144]{1,0:T(1,128)S(1)} %copy-done.13), kind=kLoop, calls=%fused_computation.30 | loop fusion | flops 24575 | bytes 98308 | tf_op jit(solution)/shard_map/reduce_sum | solution.py:185
  20.7 0.7 multiply_reduce_fusion.7
  23.5 1.0 %collective-permute-done.2 = f32[1,32896]{1,0:T(1,128)S(1)} collective-permute-done((f32[1,32896]{1,0:T(1,128)S(1)}, f32[1,32896]{1,0:T(1,128)S(1)}, u32[]{:S(2)}, u32[]{:S(2)}) %collective-permute-start.2) | collective-permute-done | bytes 131616 | tf_op jit(solution)/shard_map/ppermute | solution.py:26
  24.6 7.8 %collective-permute-start.3 = (f32[1,32896]{1,0:T(1,128)S(1)}, f32[1,32896]{1,0:T(1,128)S(1)}, u32[]{:S(2)}, u32[]{:S(2)}) collective-permute-start(f32[1,32896]{1,0:T(1,128)S(1)} %fusion.10), channel_id=1, source_target_pairs={{0,4},{2,6},{4,0},{6,2},{8,12},{10,14},{12,8},{14,10},{16,20},{18,... | collective-permute-start | bytes 394760 | tf_op jit(solution)/shard_map/ppermute | solution.py:26
  32.4 3.8 %collective-permute-done.3 = f32[1,32896]{1,0:T(1,128)S(1)} collective-permute-done((f32[1,32896]{1,0:T(1,128)S(1)}, f32[1,32896]{1,0:T(1,128)S(1)}, u32[]{:S(2)}, u32[]{:S(2)}) %collective-permute-start.3) | collective-permute-done | bytes 131616 | tf_op jit(solution)/shard_map/ppermute | solution.py:26
  36.5 6.5 %collective-permute-done.4 = f32[1,32896]{1,0:T(1,128)S(1)} collective-permute-done((f32[1,32896]{1,0:T(1,128)S(1)}, f32[1,32896]{1,0:T(1,128)S(1)}, u32[]{:S(2)}, u32[]{:S(2)}) %collective-permute-start.4) | collective-permute-done | bytes 131616 | tf_op jit(solution)/shard_map/ppermute | solution.py:26
  43.4 0.7 pad_bitcast_fusion.index_ref
  44.1 4.1 %collective-permute-done.5 = f32[1,32896]{1,0:T(1,128)S(1)} collective-permute-done((f32[1,32896]{1,0:T(1,128)S(1)}, f32[1,32896]{1,0:T(1,128)S(1)}, u32[]{:S(2)}, u32[]{:S(2)}) %collective-permute-start.5) | collective-permute-done | bytes 131616 | tf_op jit(solution)/shard_map/ppermute | solution.py:26
  48.8 0.7 pad_bitcast_fusion.1.value_ref
  49.5 4.4 %shard_map.168 = f32[128,384]{1,0:T(8,128)} custom-call(f32[128,384]{1,0:T(8,128)} %pad_bitcast_fusion.1.value_ref, s32[128,384]{1,0:T(8,128)} %pad_bitcast_fusion.index_ref), custom_call_target="tpu_custom_call" | custom-call | tf_op jit(solution)/shard_map/pallas_call | solution.py:101
  53.9 1.0 %copy.26 = f32[352,128]{1,0:T(8,128)S(1)} copy(f32[352,128]{0,1:T(8,128)} %bitcast.73) | data formatting | bytes 360448 | tf_op jit(solution)/shard_map/slice | solution.py:105
  54.9 1.8 %scatter_custom_fusion = f32[64,128]{1,0:T(8,128)S(1)} fusion(s32[352]{0:T(512)S(1)} %fusion.8, f32[352,128]{1,0:T(8,128)S(1)} %copy.26, f32[]{:T(128)} %constant.11.clone.1), kind=kCustom, calls=%fused_computation.31 | custom fusion | flops 45056 | bytes 32772 | tf_op jit(solution)/shard_map/scatter-add | solution.py:124
  57.0 1.9 %collective-permute-start.10 = (f32[1,1,4096]{2,1,0:T(1,128)S(1)}, f32[1,1,4096]{2,1,0:T(1,128)S(1)}, u32[]{:S(2)}, u32[]{:S(2)}) collective-permute-start(f32[1,1,4096]{2,1,0:T(1,128)S(1)} %constant_dynamic-slice_fusion), channel_id=1, source_target_pairs={{0,1},{1,0},{2,3},{3,2},{4,5},{5,4},{6,7},{7,6},{8,9},{9,8},{10,11... | collective-permute-start | bytes 49160 | tf_op jit(solution)/shard_map/ppermute | solution.py:225
  58.9 3.9 %collective-permute-done.7 = f32[1,32896]{1,0:T(1,128)S(1)} collective-permute-done((f32[1,32896]{1,0:T(1,128)S(1)}, f32[1,32896]{1,0:T(1,128)S(1)}, u32[]{:S(2)}, u32[]{:S(2)}) %collective-permute-start.7) | collective-permute-done | bytes 131616 | tf_op jit(solution)/shard_map/ppermute | solution.py:26
  63.0 4.3 %collective-permute-start.8 = (f32[1,32896]{1,0:T(1,128)S(1)}, f32[1,32896]{1,0:T(1,128)S(1)}, u32[]{:S(2)}, u32[]{:S(2)}) collective-permute-start(f32[1,32896]{1,0:T(1,128)S(1)} %add.122), channel_id=1, source_target_pairs={{0,128},{2,130},{4,132},{6,134},{8,136},{10,138},{12,140},{14,142}... | collective-permute-start | bytes 394760 | tf_op jit(solution)/shard_map/ppermute | solution.py:26
  67.4 4.9 %collective-permute-done.8 = f32[1,32896]{1,0:T(1,128)S(1)} collective-permute-done((f32[1,32896]{1,0:T(1,128)S(1)}, f32[1,32896]{1,0:T(1,128)S(1)}, u32[]{:S(2)}, u32[]{:S(2)}) %collective-permute-start.8) | collective-permute-done | bytes 131616 | tf_op jit(solution)/shard_map/ppermute | solution.py:26
  72.7 0.9 %multiply_reduce_fusion = f32[]{:T(128)} fusion(f32[1,32896]{1,0:T(1,128)S(1)} %add.123, f32[1,32768]{1,0:T(1,128)S(1)} %bitcast.78), kind=kLoop, calls=%fused_computation.16 | loop fusion | flops 98303 | bytes 262148 | tf_op jit(solution)/shard_map/reduce_sum | solution.py:203
  73.6 0.7 slice_add_fusion.1
  74.3 2.0 %collective-permute-start.9 = (f32[1,2]{1,0:T(1,128)S(1)}, f32[1,2]{1,0:T(1,128)S(1)}, u32[]{:S(2)}, u32[]{:S(2)}) collective-permute-start(f32[1,2]{1,0:T(1,128)S(1)} %slice_add_fusion.1), channel_id=1, source_target_pairs={{0,1},{1,0},{2,3},{3,2},{4,5},{5,4},{6,7},{7,6},{8,9},{9,8},{10,11... | collective-permute-start | bytes 32 | tf_op jit(solution)/shard_map/ppermute | solution.py:26
  76.3 3.1 %collective-permute-done.9 = f32[1,2]{1,0:T(1,128)S(1)} collective-permute-done((f32[1,2]{1,0:T(1,128)S(1)}, f32[1,2]{1,0:T(1,128)S(1)}, u32[]{:S(2)}, u32[]{:S(2)}) %collective-permute-start.9) | collective-permute-done | bytes 40 | tf_op jit(solution)/shard_map/ppermute | solution.py:26
  81.3 0.8 multiply_subtract_fusion
  82.1 0.7 fusion.5
  (68 shorter events, 4.5 us)
Async XLA Ops:
  0.6 4.2 %copy-start.1 = (f32[1,1,2,4096]{3,2,1,0:T(2,128)S(1)}, f32[1,1,2,4096]{3,2,1,0:T(2,128)}, u32[]{:S(2)}) copy-start(f32[1,1,2,4096]{3,2,1,0:T(2,128)} %param.16) | copy-start | bytes 98308
  0.6 8.1 %copy-start.7 = (s32[32768]{0:T(1024)S(1)}, s32[32768]{0:T(1024)}, u32[]{:S(2)}) copy-start(s32[32768]{0:T(1024)} %param.31) | copy-start | bytes 393220
  1.6 9.4 %collective-permute-start = (f32[1,1,4096]{2,1,0:T(1,128)S(1)}, f32[1,1,4096]{2,1,0:T(1,128)S(1)}, u32[]{:S(2)}, u32[]{:S(2)}) collective-permute-start(f32[1,1,4096]{2,1,0:T(1,128)S(1)} %get-tuple-element.20), channel_id=1, source_target_pairs={{0,1},{1,0},{2,3},{3,2},{4,5},{5,4},{6,7},{7,6},{8,9},{9,8},{10,11... | collective-permute-start | bytes 49160 | tf_op jit(solution)/shard_map/ppermute | solution.py:156
  6.3 1.8 %copy-start.6 = (f32[1,1,2,4096]{3,2,1,0:T(2,128)S(1)}, f32[1,1,2,4096]{3,2,1,0:T(2,128)}, u32[]{:S(2)}) copy-start(f32[1,1,2,4096]{3,2,1,0:T(2,128)} %param.18) | copy-start | bytes 98308
  6.3 2.5 %copy-start.12 = (s32[6144]{0:T(1024)S(1)}, s32[6144]{0:T(1024)}, u32[]{:S(2)}) copy-start(s32[6144]{0:T(1024)} %param.28) | copy-start | bytes 73732
  8.1 0.7 copy-start.11
  8.8 0.7 copy-start.14
  8.9 0.7 copy-start.15
  8.9 0.7 copy-start.16
  12.9 1.9 %copy-start.4 = (f32[1,1,32768]{2,1,0:T(1,128)S(1)}, f32[1,1,32768]{2,1,0:T(1,128)}, u32[]{:S(2)}) copy-start(f32[1,1,32768]{2,1,0:T(1,128)} %param.17) | copy-start | bytes 393220
  12.9 1.9 %copy-start.5 = (f32[1,32768]{1,0:T(1,128)S(1)}, f32[1,32768]{1,0:T(1,128)}, u32[]{:S(2)}) copy-start(f32[1,32768]{1,0:T(1,128)} %param.24) | copy-start | bytes 393220
  12.9 1.9 %copy-start.8 = (f32[1,32768]{1,0:T(1,128)S(1)}, f32[1,32768]{1,0:T(1,128)}, u32[]{:S(2)}) copy-start(f32[1,32768]{1,0:T(1,128)} %param.21) | copy-start | bytes 393220
  14.8 2.0 %copy-start.13 = (f32[1,6144]{1,0:T(1,128)S(1)}, f32[1,6144]{1,0:T(1,128)}, u32[]{:S(2)}) copy-start(f32[1,6144]{1,0:T(1,128)} %param.20) | copy-start | bytes 73732
  14.8 5.9 %collective-permute-start.1 = (f32[1,1,4096]{2,1,0:T(1,128)S(1)}, f32[1,1,4096]{2,1,0:T(1,128)S(1)}, u32[]{:S(2)}, u32[]{:S(2)}) collective-permute-start(f32[1,1,4096]{2,1,0:T(1,128)S(1)} %get-tuple-element.5), channel_id=1, source_target_pairs={{0,254},{2,0},{4,2},{6,4},{8,6},{10,8},{12,10},{14,12},{16,14},{18... | collective-permute-start | bytes 49160 | tf_op jit(solution)/shard_map/ppermute | solution.py:16
  16.8 3.9 %copy-start.9 = (f32[1,2,4096]{2,1,0:T(2,128)S(1)}, f32[1,2,4096]{2,1,0:T(2,128)}, u32[]{:S(2)}) copy-start(f32[1,2,4096]{2,1,0:T(2,128)} %param.22) | copy-start | bytes 98308
  16.8 3.9 %copy-start.10 = (f32[4096]{0:T(1024)S(1)}, f32[4096]{0:T(1024)}, u32[]{:S(2)}) copy-start(f32[4096]{0:T(1024)} %param.25) | copy-start | bytes 49156
  22.9 1.6 %collective-permute-start.2 = (f32[1,32896]{1,0:T(1,128)S(1)}, f32[1,32896]{1,0:T(1,128)S(1)}, u32[]{:S(2)}, u32[]{:S(2)}) collective-permute-start(f32[1,32896]{1,0:T(1,128)S(1)} %pad_maximum_fusion.1), channel_id=1, source_target_pairs={{0,2},{2,0},{4,6},{6,4},{8,10},{10,8},{12,14},{14,12},{16,18},{18,... | collective-permute-start | bytes 394760 | tf_op jit(solution)/shard_map/ppermute | solution.py:26
  24.6 11.6 %collective-permute-start.3 = (f32[1,32896]{1,0:T(1,128)S(1)}, f32[1,32896]{1,0:T(1,128)S(1)}, u32[]{:S(2)}, u32[]{:S(2)}) collective-permute-start(f32[1,32896]{1,0:T(1,128)S(1)} %fusion.10), channel_id=1, source_target_pairs={{0,4},{2,6},{4,0},{6,2},{8,12},{10,14},{12,8},{14,10},{16,20},{18,... | collective-permute-start | bytes 394760 | tf_op jit(solution)/shard_map/ppermute | solution.py:26
  36.4 6.9 %copy-start = (s32[352,128]{1,0:T(8,128)S(1)}, s32[352,128]{1,0:T(8,128)}, u32[]{:S(2)}) copy-start(s32[352,128]{1,0:T(8,128)} %add_bitcast_fusion.index_ref) | copy-start | bytes 540676
  36.4 6.6 %collective-permute-start.4 = (f32[1,32896]{1,0:T(1,128)S(1)}, f32[1,32896]{1,0:T(1,128)S(1)}, u32[]{:S(2)}, u32[]{:S(2)}) collective-permute-start(f32[1,32896]{1,0:T(1,128)S(1)} %add.118), channel_id=1, source_target_pairs={{0,8},{2,10},{4,12},{6,14},{8,0},{10,2},{12,4},{14,6},{16,24},{18,... | collective-permute-start | bytes 394760 | tf_op jit(solution)/shard_map/ppermute | solution.py:26
  43.2 5.1 %collective-permute-start.5 = (f32[1,32896]{1,0:T(1,128)S(1)}, f32[1,32896]{1,0:T(1,128)S(1)}, u32[]{:S(2)}, u32[]{:S(2)}) collective-permute-start(f32[1,32896]{1,0:T(1,128)S(1)} %add.119), channel_id=1, source_target_pairs={{0,16},{2,18},{4,20},{6,22},{8,24},{10,26},{12,28},{14,30},{16,0},... | collective-permute-start | bytes 394760 | tf_op jit(solution)/shard_map/ppermute | solution.py:26
  48.4 8.3 %collective-permute-start.6 = (f32[1,32896]{1,0:T(1,128)S(1)}, f32[1,32896]{1,0:T(1,128)S(1)}, u32[]{:S(2)}, u32[]{:S(2)}) collective-permute-start(f32[1,32896]{1,0:T(1,128)S(1)} %add.120), channel_id=1, source_target_pairs={{0,32},{2,34},{4,36},{6,38},{8,40},{10,42},{12,44},{14,46},{16,48}... | collective-permute-start | bytes 394760 | tf_op jit(solution)/shard_map/ppermute | solution.py:26
  56.9 6.0 %collective-permute-start.7 = (f32[1,32896]{1,0:T(1,128)S(1)}, f32[1,32896]{1,0:T(1,128)S(1)}, u32[]{:S(2)}, u32[]{:S(2)}) collective-permute-start(f32[1,32896]{1,0:T(1,128)S(1)} %add.121), channel_id=1, source_target_pairs={{0,64},{2,66},{4,68},{6,70},{8,72},{10,74},{12,76},{14,78},{16,80}... | collective-permute-start | bytes 394760 | tf_op jit(solution)/shard_map/ppermute | solution.py:26
  57.0 10.3 %collective-permute-start.10 = (f32[1,1,4096]{2,1,0:T(1,128)S(1)}, f32[1,1,4096]{2,1,0:T(1,128)S(1)}, u32[]{:S(2)}, u32[]{:S(2)}) collective-permute-start(f32[1,1,4096]{2,1,0:T(1,128)S(1)} %constant_dynamic-slice_fusion), channel_id=1, source_target_pairs={{0,1},{1,0},{2,3},{3,2},{4,5},{5,4},{6,7},{7,6},{8,9},{9,8},{10,11... | collective-permute-start | bytes 49160 | tf_op jit(solution)/shard_map/ppermute | solution.py:225
  58.9 8.4 %collective-permute-start.11 = (f32[1,1,4096]{2,1,0:T(1,128)S(1)}, f32[1,1,4096]{2,1,0:T(1,128)S(1)}, u32[]{:S(2)}, u32[]{:S(2)}) collective-permute-start(f32[1,1,4096]{2,1,0:T(1,128)S(1)} %get-tuple-element.12), channel_id=1, source_target_pairs={{0,2},{2,4},{4,6},{6,8},{8,10},{10,12},{12,14},{14,16},{16,18},{18... | collective-permute-start | bytes 49160 | tf_op jit(solution)/shard_map/ppermute | solution.py:16
  63.0 9.3 %collective-permute-start.8 = (f32[1,32896]{1,0:T(1,128)S(1)}, f32[1,32896]{1,0:T(1,128)S(1)}, u32[]{:S(2)}, u32[]{:S(2)}) collective-permute-start(f32[1,32896]{1,0:T(1,128)S(1)} %add.122), channel_id=1, source_target_pairs={{0,128},{2,130},{4,132},{6,134},{8,136},{10,138},{12,140},{14,142}... | collective-permute-start | bytes 394760 | tf_op jit(solution)/shard_map/ppermute | solution.py:26
  67.4 5.0 %copy-start.3 = (f32[32768]{0:T(1024)S(1)}, f32[32768]{0:T(1024)}, u32[]{:S(2)}) copy-start(f32[32768]{0:T(1024)} %param.23) | copy-start | bytes 393220
  72.7 8.6 %copy-start.2 = (f32[1,1,32768]{2,1,0:T(1,128)S(1)}, f32[1,1,32768]{2,1,0:T(1,128)}, u32[]{:S(2)}) copy-start(f32[1,1,32768]{2,1,0:T(1,128)} %param.19) | copy-start | bytes 393220
  74.3 5.1 %collective-permute-start.9 = (f32[1,2]{1,0:T(1,128)S(1)}, f32[1,2]{1,0:T(1,128)S(1)}, u32[]{:S(2)}, u32[]{:S(2)}) collective-permute-start(f32[1,2]{1,0:T(1,128)S(1)} %slice_add_fusion.1), channel_id=1, source_target_pairs={{0,1},{1,0},{2,3},{3,2},{4,5},{5,4},{6,7},{7,6},{8,9},{9,8},{10,11... | collective-permute-start | bytes 32 | tf_op jit(solution)/shard_map/ppermute | solution.py:26

commit v7 on v6

--- a/solution.py
+++ b/solution.py
@@ -14,6 +14,19 @@
     count = lax.axis_size(axis)
     pairs = [(source, (source + steps) % count) for source in range(count)]
     return lax.ppermute(value, axis, pairs)
+
+
+def from_next(value, axis):
+    count = lax.axis_size(axis)
+    if count % 2 or count < 4:
+        return passed_along(value, axis, -1)
+    pair = lax.ppermute(value, axis, [(source, source ^ 1) for source in range(count)])
+    swap = lax.ppermute(
+        value,
+        axis,
+        [(source, (source + 1) % count if source % 2 else (source - 1) % count) for source in range(count)],
+    )
+    return jnp.where(lax.axis_index(axis) % 2 == 0, pair, swap)
 
 
 def butterfly_sum(value, axis):
@@ -169,7 +182,7 @@
     dispatch_value = gathered[..., 2 * lines :] + direction_capacity
 
     first_hour, gathered = lax.optimization_barrier((storage[:, :1], gathered))
-    next_first = passed_along(first_hour, "tm", -1)
+    next_first = from_next(first_hour, "tm")
     storage_next = jnp.concatenate([storage[:, 1:, :], next_first], axis=1)
     level_value = storage - retention * storage_next
     charge_value = balance - storage

time: 84.4 us -> 98.1 us (1.16)
  waiting for transfers between devices: 27.3 us -> 39.6 us
  starting transfers between devices: 20.2 us -> 22.4 us
    ppermute x8, waiting for transfers between devices: 27.3 us -> 39.6 us  [butterfly_sum(): value = value + lax.ppermute(value, axis, pairs)]
    ppermute x8, starting transfers between devices: 15 us -> 16.3 us  [butterfly_sum(): value = value + lax.ppermute(value, axis, pairs)]
  transfers between devices with their start and end apart: 12 -> 13, of which waited for: 7 -> 8; matrix products, arithmetic and copies ran while one was open for 15% -> 12% of each run, Pallas kernels for 5% -> 5%
where the time goes in v7:
time: 98.1 us; the launch traced here: 97.1 us
  waiting for transfers between devices  39.6 us (40%)
  starting transfers between devices  22.4 us (23%)
  other arithmetic  15.2 us (15%)
  between operations  7.22 us (7%)
  Pallas kernels  6.35 us (6%)
  local copies, waits for them, and re-layouts  6.26 us (6%)
    ppermute x8, waiting for transfers between devices, butterfly_sum(): value = value + lax.ppermute(value, axis, pairs)  39.6 us
    ppermute x8, starting transfers between devices, butterfly_sum(): value = value + lax.ppermute(value, axis, pairs)  16.3 us
    pallas_call x1, Pallas kernels, lane_scatter(): pl.pallas_call(lane_scatter_kernel, out_shape=jax.ShapeDtypeStruct((BLOCK...  4.44 us
    ppermute x1, starting transfers between devices, body(): other = lax.ppermute(balance, 'net', [(0, 1), (1, 0)])  3.28 us
    ppermute x1, starting transfers between devices, body(): own_terms = mine + lax.ppermute(theirs, 'net', [(0, 1), (1, 0)])  2.16 us
  transfers between devices with their start and end apart: 13, of which 8 were waited for; matrix products, arithmetic and copies ran while one was open for 12% of the time, Pallas kernels for 5%

profile of v7, /device:TPU:2, one launch (start us, length us, event | category | flops | bytes accessed | tf_op | source)
XLA Modules:
  0.0 97.1 jit_solution(2464541039289318913)
XLA Ops:
  0.6 0.9 fusion.13
  1.6 3.3 %collective-permute-start = (f32[1,1,4096]{2,1,0:T(1,128)S(1)}, f32[1,1,4096]{2,1,0:T(1,128)S(1)}, u32[]{:S(2)}, u32[]{:S(2)}) collective-permute-start(f32[1,1,4096]{2,1,0:T(1,128)S(1)} %get-tuple-element.20), channel_id=1, source_target_pairs={{0,1},{1,0},{2,3},{3,2},{4,5},{5,4},{6,7},{7,6},{8,9},{9,8},{10,11... | collective-permute-start | bytes 49160 | tf_op jit(solution)/shard_map/ppermute | solution.py:169
  4.9 0.7 multiply_reduce_fusion.4
  5.7 0.9 add_bitcast_fusion.index_ref
  7.3 0.7 pad_bitcast_fusion.index_ref
  8.3 0.8 multiply_reduce_fusion.3
  9.2 1.1 %gather_fusion = f32[352,128]{1,0:T(8,128)S(1)} fusion(f32[64,128]{1,0:T(8,128)S(1)} %fusion.4, s32[1024]{0:T(1024)S(1)} %pad_clamp_fusion), kind=kCustom, calls=%fused_computation | custom fusion | bytes 361856 | tf_op jit(solution)/shard_map/jit(_take)/gather | solution.py:124
  10.3 0.8 broadcast_select_fusion.table_ref
  11.1 1.9 %shard_map.167 = f32[352,128]{1,0:T(8,128)} custom-call(f32[352,128]{1,0:T(8,128)} %broadcast_select_fusion.table_ref, s32[352,128]{1,0:T(8,128)} %copy-done), custom_call_target="tpu_custom_call" | custom-call | tf_op jit(solution)/shard_map/pallas_call | solution.py:74
  13.7 1.4 %multiply_reduce_fusion.6 = (f32[]{:T(128)}, f32[1,1,6144]{2,1,0:T(1,128)S(1)}) fusion(f32[1,1,45056]{2,1,0:T(1,128)} %bitcast.72, f32[1,6144]{1,0:T(1,128)S(1)} %copy-done.12), kind=kLoop, calls=%fused_computation.31 | loop fusion | flops 24575 | bytes 98308 | tf_op jit(solution)/shard_map/reduce_sum | solution.py:198
  15.2 1.9 %multiply_reduce_fusion.1 = (f32[]{:T(128)}, f32[]{:T(128)}, f32[1,1,32768]{2,1,0:T(1,128)S(1)}, f32[1,32768]{1,0:T(1,128)S(1)}) fusion(f32[1,1,32768]{2,1,0:T(1,128)S(1)} %copy-done.3, f32[1,1,45056]{2,1,0:T(1,128)} %bitcast.73, f32[1,32768]{1,0:T(1,128)S(1)} %copy-done.7, f32[1,32768]{1,0:T(1,128)S(1)} %copy-done.4), kind=kLoop, calls=%fused_computation.17 | loop fusion | flops 262142 | bytes 786440 | tf_op jit(solution)/shard_map/reduce_sum | solution.py:205
  17.3 0.7 pad_bitcast_fusion.1.value_ref
  18.0 4.4 %shard_map.168 = f32[128,384]{1,0:T(8,128)} custom-call(f32[128,384]{1,0:T(8,128)} %pad_bitcast_fusion.1.value_ref, s32[128,384]{1,0:T(8,128)} %pad_bitcast_fusion.index_ref), custom_call_target="tpu_custom_call" | custom-call | tf_op jit(solution)/shard_map/pallas_call | solution.py:114
  22.5 1.0 %copy.26 = f32[352,128]{1,0:T(8,128)S(1)} copy(f32[352,128]{0,1:T(8,128)} %bitcast.70) | data formatting | bytes 360448 | tf_op jit(solution)/shard_map/slice | solution.py:118
  23.5 1.7 %scatter_custom_fusion = f32[64,128]{1,0:T(8,128)S(1)} fusion(s32[352]{0:T(512)S(1)} %fusion.10, f32[352,128]{1,0:T(8,128)S(1)} %copy.26, f32[]{:T(128)} %constant.18.clone.1), kind=kCustom, calls=%fused_computation.34 | custom fusion | flops 45056 | bytes 32772 | tf_op jit(solution)/shard_map/scatter-add | solution.py:137
  25.3 2.2 %collective-permute-start.11 = (f32[1,1,4096]{2,1,0:T(1,128)S(1)}, f32[1,1,4096]{2,1,0:T(1,128)S(1)}, u32[]{:S(2)}, u32[]{:S(2)}) collective-permute-start(f32[1,1,4096]{2,1,0:T(1,128)S(1)} %constant_dynamic-slice_fusion), channel_id=1, source_target_pairs={{0,1},{1,0},{2,3},{3,2},{4,5},{5,4},{6,7},{7,6},{8,9},{9,8},{10,11... | collective-permute-start | bytes 49160 | tf_op jit(solution)/shard_map/ppermute | solution.py:238
  28.2 0.7 multiply_reduce_fusion.5
  32.6 0.7 multiply_reduce_fusion.8
  35.2 1.0 %collective-permute-done.3 = f32[1,32896]{1,0:T(1,128)S(1)} collective-permute-done((f32[1,32896]{1,0:T(1,128)S(1)}, f32[1,32896]{1,0:T(1,128)S(1)}, u32[]{:S(2)}, u32[]{:S(2)}) %collective-permute-start.3) | collective-permute-done | bytes 131616 | tf_op jit(solution)/shard_map/ppermute | solution.py:39
  36.4 10.9 %collective-permute-start.4 = (f32[1,32896]{1,0:T(1,128)S(1)}, f32[1,32896]{1,0:T(1,128)S(1)}, u32[]{:S(2)}, u32[]{:S(2)}) collective-permute-start(f32[1,32896]{1,0:T(1,128)S(1)} %fusion.12), channel_id=1, source_target_pairs={{0,4},{2,6},{4,0},{6,2},{8,12},{10,14},{12,8},{14,10},{16,20},{18,... | collective-permute-start | bytes 394760 | tf_op jit(solution)/shard_map/ppermute | solution.py:39
  47.3 3.8 %collective-permute-done.4 = f32[1,32896]{1,0:T(1,128)S(1)} collective-permute-done((f32[1,32896]{1,0:T(1,128)S(1)}, f32[1,32896]{1,0:T(1,128)S(1)}, u32[]{:S(2)}, u32[]{:S(2)}) %collective-permute-start.4) | collective-permute-done | bytes 131616 | tf_op jit(solution)/shard_map/ppermute | solution.py:39
  51.4 6.5 %collective-permute-done.5 = f32[1,32896]{1,0:T(1,128)S(1)} collective-permute-done((f32[1,32896]{1,0:T(1,128)S(1)}, f32[1,32896]{1,0:T(1,128)S(1)}, u32[]{:S(2)}, u32[]{:S(2)}) %collective-permute-start.5) | collective-permute-done | bytes 131616 | tf_op jit(solution)/shard_map/ppermute | solution.py:39
  58.2 5.0 %collective-permute-done.6 = f32[1,32896]{1,0:T(1,128)S(1)} collective-permute-done((f32[1,32896]{1,0:T(1,128)S(1)}, f32[1,32896]{1,0:T(1,128)S(1)}, u32[]{:S(2)}, u32[]{:S(2)}) %collective-permute-start.6) | collective-permute-done | bytes 131616 | tf_op jit(solution)/shard_map/ppermute | solution.py:39
  63.4 5.0 %collective-permute-done.7 = f32[1,32896]{1,0:T(1,128)S(1)} collective-permute-done((f32[1,32896]{1,0:T(1,128)S(1)}, f32[1,32896]{1,0:T(1,128)S(1)}, u32[]{:S(2)}, u32[]{:S(2)}) %collective-permute-start.7) | collective-permute-done | bytes 131616 | tf_op jit(solution)/shard_map/ppermute | solution.py:39
  68.6 8.7 %collective-permute-done.8 = f32[1,32896]{1,0:T(1,128)S(1)} collective-permute-done((f32[1,32896]{1,0:T(1,128)S(1)}, f32[1,32896]{1,0:T(1,128)S(1)}, u32[]{:S(2)}, u32[]{:S(2)}) %collective-permute-start.8) | collective-permute-done | bytes 131616 | tf_op jit(solution)/shard_map/ppermute | solution.py:39
  77.5 2.9 %collective-permute-start.9 = (f32[1,32896]{1,0:T(1,128)S(1)}, f32[1,32896]{1,0:T(1,128)S(1)}, u32[]{:S(2)}, u32[]{:S(2)}) collective-permute-start(f32[1,32896]{1,0:T(1,128)S(1)} %add.127), channel_id=1, source_target_pairs={{0,128},{2,130},{4,132},{6,134},{8,136},{10,138},{12,140},{14,142}... | collective-permute-start | bytes 394760 | tf_op jit(solution)/shard_map/ppermute | solution.py:39
  80.3 6.3 %collective-permute-done.9 = f32[1,32896]{1,0:T(1,128)S(1)} collective-permute-done((f32[1,32896]{1,0:T(1,128)S(1)}, f32[1,32896]{1,0:T(1,128)S(1)}, u32[]{:S(2)}, u32[]{:S(2)}) %collective-permute-start.9) | collective-permute-done | bytes 131616 | tf_op jit(solution)/shard_map/ppermute | solution.py:39
  87.1 0.9 multiply_reduce_fusion
  87.9 0.7 slice_add_fusion.1
  88.7 1.7 %collective-permute-start.10 = (f32[1,2]{1,0:T(1,128)S(1)}, f32[1,2]{1,0:T(1,128)S(1)}, u32[]{:S(2)}, u32[]{:S(2)}) collective-permute-start(f32[1,2]{1,0:T(1,128)S(1)} %slice_add_fusion.1), channel_id=1, source_target_pairs={{0,1},{1,0},{2,3},{3,2},{4,5},{5,4},{6,7},{7,6},{8,9},{9,8},{10,11... | collective-permute-start | bytes 32 | tf_op jit(solution)/shard_map/ppermute | solution.py:39
  90.4 3.4 %collective-permute-done.10 = f32[1,2]{1,0:T(1,128)S(1)} collective-permute-done((f32[1,2]{1,0:T(1,128)S(1)}, f32[1,2]{1,0:T(1,128)S(1)}, u32[]{:S(2)}, u32[]{:S(2)}) %collective-permute-start.10) | collective-permute-done | bytes 40 | tf_op jit(solution)/shard_map/ppermute | solution.py:39
  95.7 0.8 multiply_subtract_fusion
  (68 shorter events, 6.5 us)
Async XLA Ops:
  0.6 4.3 %copy-start.5 = (f32[1,1,2,4096]{3,2,1,0:T(2,128)S(1)}, f32[1,1,2,4096]{3,2,1,0:T(2,128)}, u32[]{:S(2)}) copy-start(f32[1,1,2,4096]{3,2,1,0:T(2,128)} %param.16) | copy-start | bytes 98308
  1.5 4.0 %copy-start.13 = (s32[256]{0:T(256)S(1)}, s32[256]{0:T(256)}, u32[]{:S(2)}) copy-start(s32[256]{0:T(256)} %param.30) | copy-start | bytes 3076
  1.5 4.0 %copy-start.14 = (s32[48]{0:T(128)S(1)}, s32[48]{0:T(128)}, u32[]{:S(2)}) copy-start(s32[48]{0:T(128)} %param.27) | copy-start | bytes 580
  1.6 4.0 %copy-start.15 = (s32[48]{0:T(128)S(1)}, s32[48]{0:T(128)}, u32[]{:S(2)}) copy-start(s32[48]{0:T(128)} %param.26) | copy-start | bytes 580
  1.6 4.1 %copy-start.10 = (s32[6144]{0:T(1024)S(1)}, s32[6144]{0:T(1024)}, u32[]{:S(2)}) copy-start(s32[6144]{0:T(1024)} %param.29) | copy-start | bytes 73732
  1.6 4.1 %copy-start.11 = (s32[6144]{0:T(1024)S(1)}, s32[6144]{0:T(1024)}, u32[]{:S(2)}) copy-start(s32[6144]{0:T(1024)} %param.28) | copy-start | bytes 73732
  1.6 7.6 %collective-permute-start = (f32[1,1,4096]{2,1,0:T(1,128)S(1)}, f32[1,1,4096]{2,1,0:T(1,128)S(1)}, u32[]{:S(2)}, u32[]{:S(2)}) collective-permute-start(f32[1,1,4096]{2,1,0:T(1,128)S(1)} %get-tuple-element.20), channel_id=1, source_target_pairs={{0,1},{1,0},{2,3},{3,2},{4,5},{5,4},{6,7},{7,6},{8,9},{9,8},{10,11... | collective-permute-start | bytes 49160 | tf_op jit(solution)/shard_map/ppermute | solution.py:169
  6.6 0.7 copy-start
  7.3 1.0 %copy-start.1 = (f32[1,1,32768]{2,1,0:T(1,128)S(1)}, f32[1,1,32768]{2,1,0:T(1,128)}, u32[]{:S(2)}) copy-start(f32[1,1,32768]{2,1,0:T(1,128)} %param.19) | copy-start | bytes 393220
  11.1 2.6 %copy-start.12 = (f32[1,6144]{1,0:T(1,128)S(1)}, f32[1,6144]{1,0:T(1,128)}, u32[]{:S(2)}) copy-start(f32[1,6144]{1,0:T(1,128)} %param.20) | copy-start | bytes 73732
  11.1 4.0 %copy-start.4 = (f32[1,32768]{1,0:T(1,128)S(1)}, f32[1,32768]{1,0:T(1,128)}, u32[]{:S(2)}) copy-start(f32[1,32768]{1,0:T(1,128)} %param.24) | copy-start | bytes 393220
  11.1 4.0 %copy-start.7 = (f32[1,32768]{1,0:T(1,128)S(1)}, f32[1,32768]{1,0:T(1,128)}, u32[]{:S(2)}) copy-start(f32[1,32768]{1,0:T(1,128)} %param.21) | copy-start | bytes 393220
  13.0 2.1 %copy-start.3 = (f32[1,1,32768]{2,1,0:T(1,128)S(1)}, f32[1,1,32768]{2,1,0:T(1,128)}, u32[]{:S(2)}) copy-start(f32[1,1,32768]{2,1,0:T(1,128)} %param.17) | copy-start | bytes 393220
  13.0 14.4 %collective-permute-start.1 = (f32[1,1,4096]{2,1,0:T(1,128)S(1)}, f32[1,1,4096]{2,1,0:T(1,128)S(1)}, u32[]{:S(2)}, u32[]{:S(2)}) collective-permute-start(f32[1,1,4096]{2,1,0:T(1,128)S(1)} %get-tuple-element.5), channel_id=1, source_target_pairs={{0,2},{2,0},{4,6},{6,4},{8,10},{10,8},{12,14},{14,12},{16,18},{18,... | collective-permute-start | bytes 49160 | tf_op jit(solution)/shard_map/ppermute | solution.py:23
  13.0 14.4 %collective-permute-start.2 = (f32[1,1,4096]{2,1,0:T(1,128)S(1)}, f32[1,1,4096]{2,1,0:T(1,128)S(1)}, u32[]{:S(2)}, u32[]{:S(2)}) collective-permute-start(f32[1,1,4096]{2,1,0:T(1,128)S(1)} %get-tuple-element.5), channel_id=1, source_target_pairs={{0,254},{2,4},{4,2},{6,8},{8,6},{10,12},{12,10},{14,16},{16,14},{1... | collective-permute-start | bytes 49160 | tf_op jit(solution)/shard_map/ppermute | solution.py:24
  23.5 4.0 %copy-start.9 = (f32[1,2,4096]{2,1,0:T(2,128)S(1)}, f32[1,2,4096]{2,1,0:T(2,128)}, u32[]{:S(2)}) copy-start(f32[1,2,4096]{2,1,0:T(2,128)} %param.22) | copy-start | bytes 98308
  25.3 2.2 %copy-start.8 = (f32[4096]{0:T(1024)S(1)}, f32[4096]{0:T(1024)}, u32[]{:S(2)}) copy-start(f32[4096]{0:T(1024)} %param.25) | copy-start | bytes 49156
  25.3 7.3 %collective-permute-start.11 = (f32[1,1,4096]{2,1,0:T(1,128)S(1)}, f32[1,1,4096]{2,1,0:T(1,128)S(1)}, u32[]{:S(2)}, u32[]{:S(2)}) collective-permute-start(f32[1,1,4096]{2,1,0:T(1,128)S(1)} %constant_dynamic-slice_fusion), channel_id=1, source_target_pairs={{0,1},{1,0},{2,3},{3,2},{4,5},{5,4},{6,7},{7,6},{8,9},{9,8},{10,11... | collective-permute-start | bytes 49160 | tf_op jit(solution)/shard_map/ppermute | solution.py:238
  27.5 0.8 copy-start.6
  28.2 4.5 %collective-permute-start.12 = (f32[1,1,4096]{2,1,0:T(1,128)S(1)}, f32[1,1,4096]{2,1,0:T(1,128)S(1)}, u32[]{:S(2)}, u32[]{:S(2)}) collective-permute-start(f32[1,1,4096]{2,1,0:T(1,128)S(1)} %get-tuple-element.11), channel_id=1, source_target_pairs={{0,2},{2,4},{4,6},{6,8},{8,10},{10,12},{12,14},{14,16},{16,18},{18... | collective-permute-start | bytes 49160 | tf_op jit(solution)/shard_map/ppermute | solution.py:16
  34.8 1.4 %collective-permute-start.3 = (f32[1,32896]{1,0:T(1,128)S(1)}, f32[1,32896]{1,0:T(1,128)S(1)}, u32[]{:S(2)}, u32[]{:S(2)}) collective-permute-start(f32[1,32896]{1,0:T(1,128)S(1)} %pad_maximum_fusion.1), channel_id=1, source_target_pairs={{0,2},{2,0},{4,6},{6,4},{8,10},{10,8},{12,14},{14,12},{16,18},{18,... | collective-permute-start | bytes 394760 | tf_op jit(solution)/shard_map/ppermute | solution.py:39
  36.4 14.8 %collective-permute-start.4 = (f32[1,32896]{1,0:T(1,128)S(1)}, f32[1,32896]{1,0:T(1,128)S(1)}, u32[]{:S(2)}, u32[]{:S(2)}) collective-permute-start(f32[1,32896]{1,0:T(1,128)S(1)} %fusion.12), channel_id=1, source_target_pairs={{0,4},{2,6},{4,0},{6,2},{8,12},{10,14},{12,8},{14,10},{16,20},{18,... | collective-permute-start | bytes 394760 | tf_op jit(solution)/shard_map/ppermute | solution.py:39
  51.3 6.6 %collective-permute-start.5 = (f32[1,32896]{1,0:T(1,128)S(1)}, f32[1,32896]{1,0:T(1,128)S(1)}, u32[]{:S(2)}, u32[]{:S(2)}) collective-permute-start(f32[1,32896]{1,0:T(1,128)S(1)} %add.123), channel_id=1, source_target_pairs={{0,8},{2,10},{4,12},{6,14},{8,0},{10,2},{12,4},{14,6},{16,24},{18,... | collective-permute-start | bytes 394760 | tf_op jit(solution)/shard_map/ppermute | solution.py:39
  58.1 5.1 %collective-permute-start.6 = (f32[1,32896]{1,0:T(1,128)S(1)}, f32[1,32896]{1,0:T(1,128)S(1)}, u32[]{:S(2)}, u32[]{:S(2)}) collective-permute-start(f32[1,32896]{1,0:T(1,128)S(1)} %add.124), channel_id=1, source_target_pairs={{0,16},{2,18},{4,20},{6,22},{8,24},{10,26},{12,28},{14,30},{16,0},... | collective-permute-start | bytes 394760 | tf_op jit(solution)/shard_map/ppermute | solution.py:39
  63.3 5.1 %collective-permute-start.7 = (f32[1,32896]{1,0:T(1,128)S(1)}, f32[1,32896]{1,0:T(1,128)S(1)}, u32[]{:S(2)}, u32[]{:S(2)}) collective-permute-start(f32[1,32896]{1,0:T(1,128)S(1)} %add.125), channel_id=1, source_target_pairs={{0,32},{2,34},{4,36},{6,38},{8,40},{10,42},{12,44},{14,46},{16,48}... | collective-permute-start | bytes 394760 | tf_op jit(solution)/shard_map/ppermute | solution.py:39
  68.5 8.8 %collective-permute-start.8 = (f32[1,32896]{1,0:T(1,128)S(1)}, f32[1,32896]{1,0:T(1,128)S(1)}, u32[]{:S(2)}, u32[]{:S(2)}) collective-permute-start(f32[1,32896]{1,0:T(1,128)S(1)} %add.126), channel_id=1, source_target_pairs={{0,64},{2,66},{4,68},{6,70},{8,72},{10,74},{12,76},{14,78},{16,80}... | collective-permute-start | bytes 394760 | tf_op jit(solution)/shard_map/ppermute | solution.py:39
  77.4 9.3 %copy-start.2 = (f32[32768]{0:T(1024)S(1)}, f32[32768]{0:T(1024)}, u32[]{:S(2)}) copy-start(f32[32768]{0:T(1024)} %param.23) | copy-start | bytes 393220
  77.5 9.1 %collective-permute-start.9 = (f32[1,32896]{1,0:T(1,128)S(1)}, f32[1,32896]{1,0:T(1,128)S(1)}, u32[]{:S(2)}, u32[]{:S(2)}) collective-permute-start(f32[1,32896]{1,0:T(1,128)S(1)} %add.127), channel_id=1, source_target_pairs={{0,128},{2,130},{4,132},{6,134},{8,136},{10,138},{12,140},{14,142}... | collective-permute-start | bytes 394760 | tf_op jit(solution)/shard_map/ppermute | solution.py:39
  88.7 5.1 %collective-permute-start.10 = (f32[1,2]{1,0:T(1,128)S(1)}, f32[1,2]{1,0:T(1,128)S(1)}, u32[]{:S(2)}, u32[]{:S(2)}) collective-permute-start(f32[1,2]{1,0:T(1,128)S(1)} %slice_add_fusion.1), channel_id=1, source_target_pairs={{0,1},{1,0},{2,3},{3,2},{4,5},{5,4},{6,7},{7,6},{8,9},{9,8},{10,11... | collective-permute-start | bytes 32 | tf_op jit(solution)/shard_map/ppermute | solution.py:39

commit v8 on v6

--- a/solution.py
+++ b/solution.py
@@ -168,24 +168,23 @@
     flow_value = gathered[..., :lines] - gathered[..., lines : 2 * lines]
     dispatch_value = gathered[..., 2 * lines :] + direction_capacity
 
-    first_hour, gathered = lax.optimization_barrier((storage[:, :1], gathered))
-    next_first = passed_along(first_hour, "tm", -1)
-    storage_next = jnp.concatenate([storage[:, 1:, :], next_first], axis=1)
-    level_value = storage - retention * storage_next
+    tm_count = lax.axis_size("tm")
+    tm_index = lax.axis_index("tm")
+    level_scale = scale_storage[None, :, 0, :]
     charge_value = balance - storage
     flow_scaled = scale_flow[None] * flow_value
     dispatch_scaled = scale_dispatch[None] * dispatch_value
-    level_scaled = scale_storage[None, :, 0, :] * level_value
     charge_scaled = scale_storage[None, :, 1, :] * charge_value
     squares_local = jnp.sum(residual_nodal * residual_nodal, axis=(1, 2, 3)) + jnp.sum(
         residual_capacity * residual_capacity, axis=(1, 2)
     )
+    inner_level = storage[:, :-1, :] - retention * storage[:, 1:, :]
 
     curvature_local = (
         jnp.sum(flow_scaled * flow_value, axis=(1, 2))
         + jnp.sum(dispatch_scaled * dispatch_value, axis=(1, 2))
         + jnp.sum(charge_scaled * charge_value, axis=(1, 2))
-        + jnp.sum(level_scaled * level_value, axis=(1, 2))
+        + jnp.sum(level_scale[:, :-1] * inner_level * inner_level, axis=(1, 2))
         + DAMPING
         * (
             jnp.sum(direction_nodal * direction_nodal, axis=(1, 2, 3))
@@ -194,10 +193,57 @@
     )
     columns = partial_sums.shape[-1]
     scalars = jnp.stack([squares_local, curvature_local], axis=-1)
-    packed = jnp.concatenate(
-        [partial_sums, jnp.pad(scalars, ((0, 0), (0, BLOCK - 2)))], axis=-1
-    )
-    packed = butterfly_sum(packed, "tm")
+    head = jnp.concatenate([partial_sums, jnp.pad(scalars, ((0, 0), (0, BLOCK - 2)))], axis=-1)
+    first_row = storage[:, 0, :]
+    last_row = storage[:, -1, :]
+    last_scale = jnp.broadcast_to(level_scale[:, -1, :], last_row.shape)
+    width = columns + BLOCK
+    bus_count = first_row.shape[-1]
+    if not tm_count & (tm_count - 1):
+        group_first, group_last, group_scale = first_row, last_row, last_scale
+        step = 1
+        while step < tm_count:
+            pairs = [(source, source ^ step) for source in range(tm_count)]
+            message = jnp.concatenate([head, group_first, group_last, group_scale], axis=-1)
+            received = lax.ppermute(message, "tm", pairs)
+            if step == 1:
+                received, first_row, last_row, last_scale = lax.optimization_barrier(
+                    (received, first_row, last_row, last_scale)
+                )
+                next_first = passed_along(first_row, "tm", -1)
+                before = passed_along(jnp.stack([last_row, last_scale]), "tm", 1)
+            got_first = received[:, width : width + bus_count]
+            got_last = received[:, width + bus_count : width + 2 * bus_count]
+            got_scale = received[:, width + 2 * bus_count :]
+            lower = (tm_index // step) % 2 == 0
+            low_last = jnp.where(lower, group_last, got_last)
+            low_scale = jnp.where(lower, group_scale, got_scale)
+            high_first = jnp.where(lower, got_first, group_first)
+            span = low_last - retention * high_first
+            head = head + received[:, :width]
+            head = head.at[:, columns + 1].add(jnp.sum(low_scale * span * span, axis=-1))
+            group_first = jnp.where(lower, group_first, got_first)
+            group_last = jnp.where(lower, got_last, group_last)
+            group_scale = jnp.where(lower, got_scale, group_scale)
+            step *= 2
+        span = group_last - retention * group_first
+        head = head.at[:, columns + 1].add(jnp.sum(group_scale * span * span, axis=-1))
+        packed = head
+        if tm_count == 1:
+            next_first = first_row
+            before = jnp.stack([last_row, last_scale])
+        behind = before[1] * (before[0] - retention * first_row)
+    else:
+        next_first = passed_along(first_row, "tm", -1)
+        span = last_row - retention * next_first
+        boundary = jnp.sum(last_scale * span * span, axis=-1)
+        packed = lax.psum(head.at[:, columns + 1].add(boundary), "tm")
+        behind = None
+    storage_next = jnp.concatenate([storage[:, 1:, :], next_first[:, None, :]], axis=1)
+    level_value = storage - retention * storage_next
+    level_scaled = level_scale * level_value
+    if behind is None:
+        behind = passed_along(level_scaled[:, -1, :], "tm", 1)
     capacity_value = packed[:, :columns]
     capacity_scaled = scale_capacity[None] * capacity_value
     capacity_part = jnp.sum(capacity_scaled * capacity_value, axis=1)
@@ -226,8 +272,7 @@
     else:
         own_terms = lax.psum_scatter(bus_terms, "net", scatter_dimension=2, tiled=True)
     image_balance = own_terms + charge_scaled + DAMPING * balance
-    behind = passed_along(level_scaled[:, -1:], "tm", 1)
-    level_before = jnp.concatenate([behind, level_scaled[:, :-1, :]], axis=1)
+    level_before = jnp.concatenate([behind[:, None, :], level_scaled[:, :-1, :]], axis=1)
     image_storage = level_scaled - retention * level_before - charge_scaled + DAMPING * storage
     image_nodal = jnp.stack([image_balance, image_storage], axis=2)
     step_size = totals[:, 0] / totals[:, 1]

time: 84.4 us -> 118 us (1.40)
  between operations: 7.36 us -> 26.2 us
  other arithmetic: 16 us -> 21.9 us
  local copies, waits for them, and re-layouts: 5.5 us -> 11.1 us
  waiting for transfers between devices: 27.3 us -> 30 us
  starting transfers between devices: 20.2 us -> 21.9 us
    ppermute x0 -> x7, waiting for transfers between devices: none -> 26.3 us  [body(): received = lax.ppermute(message, 'tm', pairs)]
    ppermute x8 -> x1, waiting for transfers between devices: 27.3 us -> 3.65 us  [butterfly_sum(): value = value + lax.ppermute(value, axis, pairs)]
    ppermute x0 -> x7, starting transfers between devices: none -> 15.2 us  [body(): received = lax.ppermute(message, 'tm', pairs)]
    ppermute x8 -> x1, starting transfers between devices: 15 us -> 1.42 us  [butterfly_sum(): value = value + lax.ppermute(value, axis, pairs)]
    select_n x0 -> x6, other arithmetic: none -> 4.31 us  [body(): group_first = jnp.where(lower, group_first, got_first)]
    another operation x0 -> x7, local copies, waits for them, and re-layouts: none -> 4.12 us
    another operation x1 -> x3, other arithmetic: 0.08 us -> 1.38 us  [the longest x1 0.71 us: body(): last_scale = jnp.broadcast_to(level_scale[:, -1, :], last_row.shape)]
  transfers between devices with their start and end apart: 12 -> 12, of which waited for: 7 -> 7; matrix products, arithmetic and copies ran while one was open for 15% -> 12% of each run, Pallas kernels for 5% -> 4%
where the time goes in v8:
time: 118 us; the launch traced here: 117 us
  waiting for transfers between devices  30 us (25%)
  between operations  26.2 us (22%)
  starting transfers between devices  21.9 us (19%)
  other arithmetic  21.9 us (19%)
  local copies, waits for them, and re-layouts  11.1 us (9%)
  Pallas kernels  6.33 us (5%)
    ppermute x7, waiting for transfers between devices, body(): received = lax.ppermute(message, 'tm', pairs)  26.3 us
    ppermute x7, starting transfers between devices, body(): received = lax.ppermute(message, 'tm', pairs)  15.2 us
    pallas_call x1, Pallas kernels, lane_scatter(): pl.pallas_call(lane_scatter_kernel, out_shape=jax.ShapeDtypeStruct((BLOCK...  4.43 us
    select_n x6, other arithmetic, body(): group_first = jnp.where(lower, group_first, got_first)  4.31 us
    another operation x7, local copies, waits for them, and re-layouts  4.12 us
    ppermute x1, waiting for transfers between devices, butterfly_sum(): value = value + lax.ppermute(value, axis, pairs)  3.65 us
    ppermute x1, starting transfers between devices, body(): other = lax.ppermute(balance, 'net', [(0, 1), (1, 0)])  3.28 us
  transfers between devices with their start and end apart: 12, of which 7 were waited for; matrix products, arithmetic and copies ran while one was open for 12% of the time, Pallas kernels for 4%

profile of v8, /device:TPU:2, one launch (start us, length us, event | category | flops | bytes accessed | tf_op | source)
XLA Modules:
  0.0 117.4 jit_solution(15257995261482138625)
XLA Ops:
  0.7 0.9 fusion.41
  1.5 3.3 %collective-permute-start = (f32[1,1,4096]{2,1,0:T(1,128)S(1)}, f32[1,1,4096]{2,1,0:T(1,128)S(1)}, u32[]{:S(2)}, u32[]{:S(2)}) collective-permute-start(f32[1,1,4096]{2,1,0:T(1,128)S(1)} %get-tuple-element.149), channel_id=1, source_target_pairs={{0,1},{1,0},{2,3},{3,2},{4,5},{5,4},{6,7},{7,6},{8,9},{9,8},{10,11... | collective-permute-start | bytes 49160 | tf_op jit(solution)/shard_map/ppermute | solution.py:156
  5.5 1.8 %multiply_reduce_fusion.3 = f32[]{:T(128)} fusion(f32[1,1,32768]{2,1,0:T(1,128)} %param.35), kind=kLoop, calls=%fused_computation.31 | loop fusion | flops 65535 | bytes 131076 | tf_op jit(solution)/shard_map/reduce_sum | solution.py:178
  11.8 1.1 gather_fusion
  12.9 0.8 broadcast_select_fusion.table_ref
  13.7 1.9 %shard_map.167 = f32[352,128]{1,0:T(8,128)} custom-call(f32[352,128]{1,0:T(8,128)} %broadcast_select_fusion.table_ref, s32[352,128]{1,0:T(8,128)} %add_bitcast_fusion.index_ref), custom_call_target="tpu_custom_call" | custom-call | tf_op jit(solution)/shard_map/pallas_call | solution.py:61
  15.6 0.9 fusion.38
  16.4 1.4 %multiply_reduce_fusion.6 = f32[]{:T(128)} fusion(f32[1,1,6144]{2,1,0:T(1,128)S(1)} %get-tuple-element.115, f32[1,1,45056]{2,1,0:T(1,128)} %bitcast.128), kind=kLoop, calls=%fused_computation.93 | loop fusion | flops 18431 | bytes 73732 | tf_op jit(solution)/shard_map/reduce_sum | solution.py:184
  17.9 0.9 multiply_reduce_fusion.1
  22.9 0.7 collective-permute-done.1
  28.6 6.3 %collective-permute-done.2 = f32[1,45184]{1,0:T(1,128)S(1)} collective-permute-done((f32[1,45184]{1,0:T(1,128)S(1)}, f32[1,45184]{1,0:T(1,128)S(1)}, u32[]{:S(2)}, u32[]{:S(2)}) %collective-permute-start.2) | collective-permute-done | bytes 180768 | tf_op jit(solution)/shard_map/ppermute | solution.py:208
  39.2 2.2 %collective-permute-start.3 = (f32[1,45184]{1,0:T(1,128)S(1)}, f32[1,45184]{1,0:T(1,128)S(1)}, u32[]{:S(2)}, u32[]{:S(2)}) collective-permute-start(f32[1,45184]{1,0:T(1,128)S(1)} %pad_maximum_fusion.1), channel_id=1, source_target_pairs={{0,8},{2,10},{4,12},{6,14},{8,0},{10,2},{12,4},{14,6},{16,24},{18,... | collective-permute-start | bytes 542216 | tf_op jit(solution)/shard_map/ppermute | solution.py:208
  42.3 4.0 %collective-permute-done.3 = f32[1,45184]{1,0:T(1,128)S(1)} collective-permute-done((f32[1,45184]{1,0:T(1,128)S(1)}, f32[1,45184]{1,0:T(1,128)S(1)}, u32[]{:S(2)}, u32[]{:S(2)}) %collective-permute-start.3) | collective-permute-done | bytes 180768 | tf_op jit(solution)/shard_map/ppermute | solution.py:208
  50.6 0.8 collective-permute-start.4
  52.3 4.4 %shard_map.168 = f32[128,384]{1,0:T(8,128)} custom-call(f32[128,384]{1,0:T(8,128)} %pad_bitcast_fusion.1.value_ref, s32[128,384]{1,0:T(8,128)} %pad_bitcast_fusion.index_ref), custom_call_target="tpu_custom_call" | custom-call | tf_op jit(solution)/shard_map/pallas_call | solution.py:101
  56.8 1.0 copy.26
  57.8 1.8 %scatter_custom_fusion = f32[64,128]{1,0:T(8,128)S(1)} fusion(s32[352]{0:T(512)S(1)} %fusion.36, f32[352,128]{1,0:T(8,128)S(1)} %copy.26, f32[]{:T(128)} %constant.296.clone.1), kind=kCustom, calls=%fused_computation.118 | custom fusion | flops 45056 | bytes 32772 | tf_op jit(solution)/shard_map/scatter-add | solution.py:124
  60.3 0.7 broadcast_select_fusion.21
  64.0 2.0 %collective-permute-start.5 = (f32[1,45184]{1,0:T(1,128)S(1)}, f32[1,45184]{1,0:T(1,128)S(1)}, u32[]{:S(2)}, u32[]{:S(2)}) collective-permute-start(f32[1,45184]{1,0:T(1,128)S(1)} %pad_maximum_fusion.3), channel_id=1, source_target_pairs={{0,32},{2,34},{4,36},{6,38},{8,40},{10,42},{12,44},{14,46},{16,48}... | collective-permute-start | bytes 542216 | tf_op jit(solution)/shard_map/ppermute | solution.py:208
  66.0 1.8 %collective-permute-start.9 = (f32[1,1,4096]{2,1,0:T(1,128)S(1)}, f32[1,1,4096]{2,1,0:T(1,128)S(1)}, u32[]{:S(2)}, u32[]{:S(2)}) collective-permute-start(f32[1,1,4096]{2,1,0:T(1,128)S(1)} %constant_dynamic-slice_fusion), channel_id=1, source_target_pairs={{0,1},{1,0},{2,3},{3,2},{4,5},{5,4},{6,7},{7,6},{8,9},{9,8},{10,11... | collective-permute-start | bytes 49160 | tf_op jit(solution)/shard_map/ppermute | solution.py:271
  67.8 1.7 %collective-permute-done.5 = f32[1,45184]{1,0:T(1,128)S(1)} collective-permute-done((f32[1,45184]{1,0:T(1,128)S(1)}, f32[1,45184]{1,0:T(1,128)S(1)}, u32[]{:S(2)}, u32[]{:S(2)}) %collective-permute-start.5) | collective-permute-done | bytes 180768 | tf_op jit(solution)/shard_map/ppermute | solution.py:208
  70.3 0.7 broadcast_select_fusion.15
  73.9 3.4 %collective-permute-start.6 = (f32[1,45184]{1,0:T(1,128)S(1)}, f32[1,45184]{1,0:T(1,128)S(1)}, u32[]{:S(2)}, u32[]{:S(2)}) collective-permute-start(f32[1,45184]{1,0:T(1,128)S(1)} %pad_maximum_fusion.4), channel_id=1, source_target_pairs={{0,64},{2,66},{4,68},{6,70},{8,72},{10,74},{12,76},{14,78},{16,80}... | collective-permute-start | bytes 542216 | tf_op jit(solution)/shard_map/ppermute | solution.py:208
  77.3 6.9 %collective-permute-done.6 = f32[1,45184]{1,0:T(1,128)S(1)} collective-permute-done((f32[1,45184]{1,0:T(1,128)S(1)}, f32[1,45184]{1,0:T(1,128)S(1)}, u32[]{:S(2)}, u32[]{:S(2)}) %collective-permute-start.6) | collective-permute-done | bytes 180768 | tf_op jit(solution)/shard_map/ppermute | solution.py:208
  84.9 0.7 broadcast_select_fusion.9
  88.6 6.2 %collective-permute-start.7 = (f32[1,45184]{1,0:T(1,128)S(1)}, f32[1,45184]{1,0:T(1,128)S(1)}, u32[]{:S(2)}, u32[]{:S(2)}) collective-permute-start(f32[1,45184]{1,0:T(1,128)S(1)} %pad_maximum_fusion.5), channel_id=1, source_target_pairs={{0,128},{2,130},{4,132},{6,134},{8,136},{10,138},{12,140},{14,142}... | collective-permute-start | bytes 542216 | tf_op jit(solution)/shard_map/ppermute | solution.py:208
  94.9 6.6 %collective-permute-done.7 = f32[1,45184]{1,0:T(1,128)S(1)} collective-permute-done((f32[1,45184]{1,0:T(1,128)S(1)}, f32[1,45184]{1,0:T(1,128)S(1)}, u32[]{:S(2)}, u32[]{:S(2)}) %collective-permute-start.7) | collective-permute-done | bytes 180768 | tf_op jit(solution)/shard_map/ppermute | solution.py:208
  102.2 0.7 fusion.35
  107.1 0.9 multiply_reduce_fusion
  109.0 1.4 %collective-permute-start.8 = (f32[1,2]{1,0:T(1,128)S(1)}, f32[1,2]{1,0:T(1,128)S(1)}, u32[]{:S(2)}, u32[]{:S(2)}) collective-permute-start(f32[1,2]{1,0:T(1,128)S(1)} %slice_add_fusion.7), channel_id=1, source_target_pairs={{0,1},{1,0},{2,3},{3,2},{4,5},{5,4},{6,7},{7,6},{8,9},{9,8},{10,11... | collective-permute-start | bytes 32 | tf_op jit(solution)/shard_map/ppermute | solution.py:26
  110.4 3.7 %collective-permute-done.8 = f32[1,2]{1,0:T(1,128)S(1)} collective-permute-done((f32[1,2]{1,0:T(1,128)S(1)}, f32[1,2]{1,0:T(1,128)S(1)}, u32[]{:S(2)}, u32[]{:S(2)}) %collective-permute-start.8) | collective-permute-done | bytes 40 | tf_op jit(solution)/shard_map/ppermute | solution.py:26
  116.0 0.8 multiply_subtract_fusion
  (104 shorter events, 18.6 us)
Async XLA Ops:
  0.6 4.2 %copy-start.3 = (f32[1,1,2,4096]{3,2,1,0:T(2,128)S(1)}, f32[1,1,2,4096]{3,2,1,0:T(2,128)}, u32[]{:S(2)}) copy-start(f32[1,1,2,4096]{3,2,1,0:T(2,128)} %param.32) | copy-start | bytes 98308
  0.6 6.6 %copy-start.9 = (f32[1,1,2,4096]{3,2,1,0:T(2,128)S(1)}, f32[1,1,2,4096]{3,2,1,0:T(2,128)}, u32[]{:S(2)}) copy-start(f32[1,1,2,4096]{3,2,1,0:T(2,128)} %param.34) | copy-start | bytes 98308
  0.6 7.3 %copy-start.17 = (s32[48]{0:T(128)S(1)}, s32[48]{0:T(128)}, u32[]{:S(2)}) copy-start(s32[48]{0:T(128)} %param.42) | copy-start | bytes 580
  1.5 10.2 %collective-permute-start = (f32[1,1,4096]{2,1,0:T(1,128)S(1)}, f32[1,1,4096]{2,1,0:T(1,128)S(1)}, u32[]{:S(2)}, u32[]{:S(2)}) collective-permute-start(f32[1,1,4096]{2,1,0:T(1,128)S(1)} %get-tuple-element.149), channel_id=1, source_target_pairs={{0,1},{1,0},{2,3},{3,2},{4,5},{5,4},{6,7},{7,6},{8,9},{9,8},{10,11... | collective-permute-start | bytes 49160 | tf_op jit(solution)/shard_map/ppermute | solution.py:156
  4.8 3.1 %copy-start.15 = (s32[256]{0:T(256)S(1)}, s32[256]{0:T(256)}, u32[]{:S(2)}) copy-start(s32[256]{0:T(256)} %param.46) | copy-start | bytes 3076
  4.8 3.1 %copy-start.16 = (s32[48]{0:T(128)S(1)}, s32[48]{0:T(128)}, u32[]{:S(2)}) copy-start(s32[48]{0:T(128)} %param.43) | copy-start | bytes 580
  4.8 3.2 %copy-start.8 = (f32[1,2,4096]{2,1,0:T(2,128)S(1)}, f32[1,2,4096]{2,1,0:T(2,128)}, u32[]{:S(2)}) copy-start(f32[1,2,4096]{2,1,0:T(2,128)} %param.38) | copy-start | bytes 98308
  5.5 3.3 %copy-start.1 = (f32[1,1,32768]{2,1,0:T(1,128)S(1)}, f32[1,1,32768]{2,1,0:T(1,128)}, u32[]{:S(2)}) copy-start(f32[1,1,32768]{2,1,0:T(1,128)} %param.33) | copy-start | bytes 393220
  5.5 3.3 %copy-start.7 = (f32[1,32768]{1,0:T(1,128)S(1)}, f32[1,32768]{1,0:T(1,128)}, u32[]{:S(2)}) copy-start(f32[1,32768]{1,0:T(1,128)} %param.40) | copy-start | bytes 393220
  8.8 0.9 copy-start.10
  8.8 0.9 copy-start.12
  8.8 0.9 copy-start.13
  13.6 1.9 %copy-start.14 = (f32[1,6144]{1,0:T(1,128)S(1)}, f32[1,6144]{1,0:T(1,128)}, u32[]{:S(2)}) copy-start(f32[1,6144]{1,0:T(1,128)} %param.36) | copy-start | bytes 73732
  13.6 4.2 %copy-start.11 = (f32[1,32768]{1,0:T(1,128)S(1)}, f32[1,32768]{1,0:T(1,128)}, u32[]{:S(2)}) copy-start(f32[1,32768]{1,0:T(1,128)} %param.37) | copy-start | bytes 393220
  15.6 2.3 %copy-start.4 = (f32[352,128]{1,0:T(8,128)S(1)}, f32[352,128]{1,0:T(8,128)}, u32[]{:S(2)}) copy-start(f32[352,128]{1,0:T(8,128)} %shard_map.167) | copy-start | bytes 540676
  22.1 1.5 %collective-permute-start.1 = (f32[1,45184]{1,0:T(1,128)S(1)}, f32[1,45184]{1,0:T(1,128)S(1)}, u32[]{:S(2)}, u32[]{:S(2)}) collective-permute-start(f32[1,45184]{1,0:T(1,128)S(1)} %constant_dynamic-update-slice_fusion), channel_id=1, source_target_pairs={{0,2},{2,0},{4,6},{6,4},{8,10},{10,8},{12,14},{14,12},{16,18},{18,... | collective-permute-start | bytes 542216 | tf_op jit(solution)/shard_map/ppermute | solution.py:208
  23.6 0.8 copy-start.2
  27.9 7.0 %collective-permute-start.2 = (f32[1,45184]{1,0:T(1,128)S(1)}, f32[1,45184]{1,0:T(1,128)S(1)}, u32[]{:S(2)}, u32[]{:S(2)}) collective-permute-start(f32[1,45184]{1,0:T(1,128)S(1)} %pad_maximum_fusion), channel_id=1, source_target_pairs={{0,4},{2,6},{4,0},{6,2},{8,12},{10,14},{12,8},{14,10},{16,20},{18,... | collective-permute-start | bytes 542216 | tf_op jit(solution)/shard_map/ppermute | solution.py:208
  28.5 7.1 %collective-permute-start.11 = (f32[2,1,4096]{2,1,0:T(1,128)S(1)}, f32[2,1,4096]{2,1,0:T(1,128)S(1)}, u32[]{:S(2)}, u32[]{:S(2)}) collective-permute-start(f32[2,1,4096]{2,1,0:T(1,128)S(1)} %pad_maximum_fusion.7), channel_id=1, source_target_pairs={{0,2},{2,4},{4,6},{6,8},{8,10},{10,12},{12,14},{14,16},{16,18},{18... | collective-permute-start | bytes 98312 | tf_op jit(solution)/shard_map/ppermute | solution.py:16
  39.2 2.2 %copy-start = (s32[352,128]{1,0:T(8,128)S(1)}, s32[352,128]{1,0:T(8,128)}, u32[]{:S(2)}) copy-start(s32[352,128]{1,0:T(8,128)} %add_bitcast_fusion.index_ref) | copy-start | bytes 540676
  39.2 7.1 %collective-permute-start.3 = (f32[1,45184]{1,0:T(1,128)S(1)}, f32[1,45184]{1,0:T(1,128)S(1)}, u32[]{:S(2)}, u32[]{:S(2)}) collective-permute-start(f32[1,45184]{1,0:T(1,128)S(1)} %pad_maximum_fusion.1), channel_id=1, source_target_pairs={{0,8},{2,10},{4,12},{6,14},{8,0},{10,2},{12,4},{14,6},{16,24},{18,... | collective-permute-start | bytes 542216 | tf_op jit(solution)/shard_map/ppermute | solution.py:208
  50.6 9.0 %collective-permute-start.4 = (f32[1,45184]{1,0:T(1,128)S(1)}, f32[1,45184]{1,0:T(1,128)S(1)}, u32[]{:S(2)}, u32[]{:S(2)}) collective-permute-start(f32[1,45184]{1,0:T(1,128)S(1)} %pad_maximum_fusion.2), channel_id=1, source_target_pairs={{0,16},{2,18},{4,20},{6,22},{8,24},{10,26},{12,28},{14,30},{16,0},... | collective-permute-start | bytes 542216 | tf_op jit(solution)/shard_map/ppermute | solution.py:208
  64.0 5.6 %collective-permute-start.5 = (f32[1,45184]{1,0:T(1,128)S(1)}, f32[1,45184]{1,0:T(1,128)S(1)}, u32[]{:S(2)}, u32[]{:S(2)}) collective-permute-start(f32[1,45184]{1,0:T(1,128)S(1)} %pad_maximum_fusion.3), channel_id=1, source_target_pairs={{0,32},{2,34},{4,36},{6,38},{8,40},{10,42},{12,44},{14,46},{16,48}... | collective-permute-start | bytes 542216 | tf_op jit(solution)/shard_map/ppermute | solution.py:208
  66.0 28.8 %collective-permute-start.9 = (f32[1,1,4096]{2,1,0:T(1,128)S(1)}, f32[1,1,4096]{2,1,0:T(1,128)S(1)}, u32[]{:S(2)}, u32[]{:S(2)}) collective-permute-start(f32[1,1,4096]{2,1,0:T(1,128)S(1)} %constant_dynamic-slice_fusion), channel_id=1, source_target_pairs={{0,1},{1,0},{2,3},{3,2},{4,5},{5,4},{6,7},{7,6},{8,9},{9,8},{10,11... | collective-permute-start | bytes 49160 | tf_op jit(solution)/shard_map/ppermute | solution.py:271
  67.8 9.5 %collective-permute-start.10 = (f32[1,4096]{1,0:T(1,128)S(1)}, f32[1,4096]{1,0:T(1,128)S(1)}, u32[]{:S(2)}, u32[]{:S(2)}) collective-permute-start(f32[1,4096]{1,0:T(1,128)S(1)} %get-tuple-element.107), channel_id=1, source_target_pairs={{0,254},{2,0},{4,2},{6,4},{8,6},{10,8},{12,10},{14,12},{16,14},{18... | collective-permute-start | bytes 49160 | tf_op jit(solution)/shard_map/ppermute | solution.py:16
  73.9 10.3 %collective-permute-start.6 = (f32[1,45184]{1,0:T(1,128)S(1)}, f32[1,45184]{1,0:T(1,128)S(1)}, u32[]{:S(2)}, u32[]{:S(2)}) collective-permute-start(f32[1,45184]{1,0:T(1,128)S(1)} %pad_maximum_fusion.4), channel_id=1, source_target_pairs={{0,64},{2,66},{4,68},{6,70},{8,72},{10,74},{12,76},{14,78},{16,80}... | collective-permute-start | bytes 542216 | tf_op jit(solution)/shard_map/ppermute | solution.py:208
  88.6 12.9 %collective-permute-start.7 = (f32[1,45184]{1,0:T(1,128)S(1)}, f32[1,45184]{1,0:T(1,128)S(1)}, u32[]{:S(2)}, u32[]{:S(2)}) collective-permute-start(f32[1,45184]{1,0:T(1,128)S(1)} %pad_maximum_fusion.5), channel_id=1, source_target_pairs={{0,128},{2,130},{4,132},{6,134},{8,136},{10,138},{12,140},{14,142}... | collective-permute-start | bytes 542216 | tf_op jit(solution)/shard_map/ppermute | solution.py:208
  101.6 5.4 %copy-start.6 = (f32[32768]{0:T(1024)S(1)}, f32[32768]{0:T(1024)}, u32[]{:S(2)}) copy-start(f32[32768]{0:T(1024)} %param.39) | copy-start | bytes 393220
  107.9 8.0 %copy-start.5 = (f32[1,1,32768]{2,1,0:T(1,128)S(1)}, f32[1,1,32768]{2,1,0:T(1,128)}, u32[]{:S(2)}) copy-start(f32[1,1,32768]{2,1,0:T(1,128)} %param.35) | copy-start | bytes 393220
  109.0 5.1 %collective-permute-start.8 = (f32[1,2]{1,0:T(1,128)S(1)}, f32[1,2]{1,0:T(1,128)S(1)}, u32[]{:S(2)}, u32[]{:S(2)}) collective-permute-start(f32[1,2]{1,0:T(1,128)S(1)} %slice_add_fusion.7), channel_id=1, source_target_pairs={{0,1},{1,0},{2,3},{3,2},{4,5},{5,4},{6,7},{7,6},{8,9},{9,8},{10,11... | collective-permute-start | bytes 32 | tf_op jit(solution)/shard_map/ppermute | solution.py:26

commit v9 on v6

--- a/solution.py
+++ b/solution.py
@@ -183,13 +183,15 @@
 
     curvature_local = (
         jnp.sum(flow_scaled * flow_value, axis=(1, 2))
-        + jnp.sum(dispatch_scaled * dispatch_value, axis=(1, 2))
-        + jnp.sum(charge_scaled * charge_value, axis=(1, 2))
-        + jnp.sum(level_scaled * level_value, axis=(1, 2))
-        + DAMPING
-        * (
-            jnp.sum(direction_nodal * direction_nodal, axis=(1, 2, 3))
-            + jnp.sum(direction_capacity * direction_capacity, axis=(1, 2))
+        + jnp.sum(
+            dispatch_scaled * dispatch_value + DAMPING * direction_capacity * direction_capacity,
+            axis=(1, 2),
+        )
+        + jnp.sum(
+            charge_scaled * charge_value
+            + level_scaled * level_value
+            + DAMPING * (balance * balance + storage * storage),
+            axis=(1, 2),
         )
     )
     columns = partial_sums.shape[-1]

time: 84.4 us -> 81.8 us (0.969)
  the two profiles are of different devices: /device:TPU:2 before, /device:TPU:34 now
where the time goes in v9:
time: 81.8 us; the launch traced here: 81.4 us
  waiting for transfers between devices  26.9 us (33%)
  starting transfers between devices  21.9 us (27%)
  other arithmetic  15.3 us (19%)
  Pallas kernels  6.35 us (8%)
  between operations  5.5 us (7%)
  local copies, waits for them, and re-layouts  5.43 us (7%)
    ppermute x8, waiting for transfers between devices, butterfly_sum(): value = value + lax.ppermute(value, axis, pairs)  26.9 us
    ppermute x8, starting transfers between devices, butterfly_sum(): value = value + lax.ppermute(value, axis, pairs)  16.7 us
    pallas_call x1, Pallas kernels, lane_scatter(): pl.pallas_call(lane_scatter_kernel, out_shape=jax.ShapeDtypeStruct((BLOCK...  4.43 us
    ppermute x1, starting transfers between devices, body(): other = lax.ppermute(balance, 'net', [(0, 1), (1, 0)])  3.28 us
    ppermute x1, starting transfers between devices, body(): own_terms = mine + lax.ppermute(theirs, 'net', [(0, 1), (1, 0)])  1.93 us
    pallas_call x1, Pallas kernels, lane_gather(): pl.pallas_call(lane_gather_kernel, out_shape=jax.ShapeDtypeStruct(table.s...  1.92 us
    reduce_sum x1, other arithmetic, body(): jnp.sum(dispatch_scaled * dispatch_value + DAMPING * direction_capacity *...  1.87 us
    reduce_sum x1, other arithmetic, body(): jnp.sum(residual_capacity * residual_capacity, axis=(1, 2))  1.8 us
  transfers between devices with their start and end apart: 12, of which 7 were waited for; matrix products, arithmetic and copies ran while one was open for 15% of the time, Pallas kernels for 5%

profile of v9, /device:TPU:34, one launch (start us, length us, event | category | flops | bytes accessed | tf_op | source)
XLA Modules:
  0.0 81.4 jit_solution(6773688107796491872)
XLA Ops:
  0.6 0.9 %fusion.12 = (f32[1,1,1,4096]{3,2,1,0:T(1,128)S(1)}, f32[1,1,4096]{2,1,0:T(1,128)S(1)}, f32[1,1,4096]{2,1,0:T(1,128)S(1)}) fusion(f32[1,1,2,4096]{3,2,1,0:T(2,128)} %param.16), kind=kLoop, calls=%fused_computation.52 | loop fusion | bytes 81920 | tf_op jit(solution)/shard_map/slice | solution.py:152
  1.5 3.3 %collective-permute-start = (f32[1,1,4096]{2,1,0:T(1,128)S(1)}, f32[1,1,4096]{2,1,0:T(1,128)S(1)}, u32[]{:S(2)}, u32[]{:S(2)}) collective-permute-start(f32[1,1,4096]{2,1,0:T(1,128)S(1)} %get-tuple-element.18), channel_id=1, source_target_pairs={{0,1},{1,0},{2,3},{3,2},{4,5},{5,4},{6,7},{7,6},{8,9},{9,8},{10,11... | collective-permute-start | bytes 49160 | tf_op jit(solution)/shard_map/ppermute | solution.py:156
  4.8 0.8 fusion.9
  5.6 1.8 %multiply_reduce_fusion.1 = f32[]{:T(128)} fusion(f32[1,1,32768]{2,1,0:T(1,128)} %param.19), kind=kLoop, calls=%fused_computation.19 | loop fusion | flops 65535 | bytes 131076 | tf_op jit(solution)/shard_map/reduce_sum | solution.py:180
  10.3 1.1 %gather_fusion = f32[352,128]{1,0:T(8,128)S(1)} fusion(f32[64,128]{1,0:T(8,128)S(1)} %fusion.5, s32[1024]{0:T(1024)S(1)} %pad_clamp_fusion), kind=kCustom, calls=%fused_computation | custom fusion | bytes 361856 | tf_op jit(solution)/shard_map/jit(_take)/gather | solution.py:111
  11.4 0.8 broadcast_select_fusion.table_ref
  12.2 1.9 %shard_map.167 = f32[352,128]{1,0:T(8,128)} custom-call(f32[352,128]{1,0:T(8,128)} %broadcast_select_fusion.table_ref, s32[352,128]{1,0:T(8,128)} %add_bitcast_fusion.index_ref), custom_call_target="tpu_custom_call" | custom-call | tf_op jit(solution)/shard_map/pallas_call | solution.py:61
  14.1 1.9 %fusion.4 = (f32[]{:T(128)}, f32[1,1,32768]{2,1,0:T(1,128)S(1)}, f32[1,32768]{1,0:T(1,128)S(1)}) fusion(f32[1,1,32768]{2,1,0:T(1,128)S(1)} %copy-done.3, f32[1,1,45056]{2,1,0:T(1,128)} %bitcast.73, f32[1,32768]{1,0:T(1,128)S(1)} %copy-done.8, f32[1,32768]{1,0:T(1,128)S(1)} %copy-done.4), kind=kLoop, calls=%fused_computation.20 | loop fusion | flops 294911 | bytes 786436 | tf_op jit(solution)/shard_map/reduce_sum | solution.py:186
  16.0 1.4 %multiply_reduce_fusion.3 = (f32[]{:T(128)}, f32[1,1,6144]{2,1,0:T(1,128)S(1)}) fusion(f32[1,1,45056]{2,1,0:T(1,128)} %bitcast.74, f32[1,6144]{1,0:T(1,128)S(1)} %copy-done.13), kind=kLoop, calls=%fused_computation.30 | loop fusion | flops 24575 | bytes 98308 | tf_op jit(solution)/shard_map/reduce_sum | solution.py:185
  18.8 0.7 add_reduce_fusion
  20.9 1.0 %collective-permute-done.2 = f32[1,32896]{1,0:T(1,128)S(1)} collective-permute-done((f32[1,32896]{1,0:T(1,128)S(1)}, f32[1,32896]{1,0:T(1,128)S(1)}, u32[]{:S(2)}, u32[]{:S(2)}) %collective-permute-start.2) | collective-permute-done | bytes 131616 | tf_op jit(solution)/shard_map/ppermute | solution.py:26
  22.1 2.0 %collective-permute-start.3 = (f32[1,32896]{1,0:T(1,128)S(1)}, f32[1,32896]{1,0:T(1,128)S(1)}, u32[]{:S(2)}, u32[]{:S(2)}) collective-permute-start(f32[1,32896]{1,0:T(1,128)S(1)} %fusion.11), channel_id=1, source_target_pairs={{0,4},{2,6},{4,0},{6,2},{8,12},{10,14},{12,8},{14,10},{16,20},{18,... | collective-permute-start | bytes 394760 | tf_op jit(solution)/shard_map/ppermute | solution.py:26
  24.1 3.8 %collective-permute-done.3 = f32[1,32896]{1,0:T(1,128)S(1)} collective-permute-done((f32[1,32896]{1,0:T(1,128)S(1)}, f32[1,32896]{1,0:T(1,128)S(1)}, u32[]{:S(2)}, u32[]{:S(2)}) %collective-permute-start.3) | collective-permute-done | bytes 131616 | tf_op jit(solution)/shard_map/ppermute | solution.py:26
  28.1 2.2 %collective-permute-start.4 = (f32[1,32896]{1,0:T(1,128)S(1)}, f32[1,32896]{1,0:T(1,128)S(1)}, u32[]{:S(2)}, u32[]{:S(2)}) collective-permute-start(f32[1,32896]{1,0:T(1,128)S(1)} %add.127), channel_id=1, source_target_pairs={{0,8},{2,10},{4,12},{6,14},{8,0},{10,2},{12,4},{14,6},{16,24},{18,... | collective-permute-start | bytes 394760 | tf_op jit(solution)/shard_map/ppermute | solution.py:26
  30.3 4.4 %collective-permute-done.4 = f32[1,32896]{1,0:T(1,128)S(1)} collective-permute-done((f32[1,32896]{1,0:T(1,128)S(1)}, f32[1,32896]{1,0:T(1,128)S(1)}, u32[]{:S(2)}, u32[]{:S(2)}) %collective-permute-start.4) | collective-permute-done | bytes 131616 | tf_op jit(solution)/shard_map/ppermute | solution.py:26
  34.8 2.0 %collective-permute-start.5 = (f32[1,32896]{1,0:T(1,128)S(1)}, f32[1,32896]{1,0:T(1,128)S(1)}, u32[]{:S(2)}, u32[]{:S(2)}) collective-permute-start(f32[1,32896]{1,0:T(1,128)S(1)} %add.128), channel_id=1, source_target_pairs={{0,16},{2,18},{4,20},{6,22},{8,24},{10,26},{12,28},{14,30},{16,0},... | collective-permute-start | bytes 394760 | tf_op jit(solution)/shard_map/ppermute | solution.py:26
  36.9 0.7 pad_bitcast_fusion.index_ref
  37.6 2.2 %collective-permute-done.5 = f32[1,32896]{1,0:T(1,128)S(1)} collective-permute-done((f32[1,32896]{1,0:T(1,128)S(1)}, f32[1,32896]{1,0:T(1,128)S(1)}, u32[]{:S(2)}, u32[]{:S(2)}) %collective-permute-start.5) | collective-permute-done | bytes 131616 | tf_op jit(solution)/shard_map/ppermute | solution.py:26
  40.0 6.0 %collective-permute-start.6 = (f32[1,32896]{1,0:T(1,128)S(1)}, f32[1,32896]{1,0:T(1,128)S(1)}, u32[]{:S(2)}, u32[]{:S(2)}) collective-permute-start(f32[1,32896]{1,0:T(1,128)S(1)} %add.129), channel_id=1, source_target_pairs={{0,32},{2,34},{4,36},{6,38},{8,40},{10,42},{12,44},{14,46},{16,48}... | collective-permute-start | bytes 394760 | tf_op jit(solution)/shard_map/ppermute | solution.py:26
  46.3 0.7 pad_bitcast_fusion.1.value_ref
  47.0 4.4 %shard_map.168 = f32[128,384]{1,0:T(8,128)} custom-call(f32[128,384]{1,0:T(8,128)} %pad_bitcast_fusion.1.value_ref, s32[128,384]{1,0:T(8,128)} %pad_bitcast_fusion.index_ref), custom_call_target="tpu_custom_call" | custom-call | tf_op jit(solution)/shard_map/pallas_call | solution.py:101
  51.4 1.0 %copy.26 = f32[352,128]{1,0:T(8,128)S(1)} copy(f32[352,128]{0,1:T(8,128)} %bitcast.71) | data formatting | bytes 360448 | tf_op jit(solution)/shard_map/slice | solution.py:105
  52.5 1.8 %scatter_custom_fusion = f32[64,128]{1,0:T(8,128)S(1)} fusion(s32[352]{0:T(512)S(1)} %fusion.9, f32[352,128]{1,0:T(8,128)S(1)} %copy.26, f32[]{:T(128)} %constant.11.clone.1), kind=kCustom, calls=%fused_computation.31 | custom fusion | flops 45056 | bytes 32772 | tf_op jit(solution)/shard_map/scatter-add | solution.py:124
  54.5 1.9 %collective-permute-start.10 = (f32[1,1,4096]{2,1,0:T(1,128)S(1)}, f32[1,1,4096]{2,1,0:T(1,128)S(1)}, u32[]{:S(2)}, u32[]{:S(2)}) collective-permute-start(f32[1,1,4096]{2,1,0:T(1,128)S(1)} %constant_dynamic-slice_fusion), channel_id=1, source_target_pairs={{0,1},{1,0},{2,3},{3,2},{4,5},{5,4},{6,7},{7,6},{8,9},{9,8},{10,11... | collective-permute-start | bytes 49160 | tf_op jit(solution)/shard_map/ppermute | solution.py:227
  56.4 3.9 %collective-permute-done.7 = f32[1,32896]{1,0:T(1,128)S(1)} collective-permute-done((f32[1,32896]{1,0:T(1,128)S(1)}, f32[1,32896]{1,0:T(1,128)S(1)}, u32[]{:S(2)}, u32[]{:S(2)}) %collective-permute-start.7) | collective-permute-done | bytes 131616 | tf_op jit(solution)/shard_map/ppermute | solution.py:26
  60.5 1.9 %collective-permute-start.8 = (f32[1,32896]{1,0:T(1,128)S(1)}, f32[1,32896]{1,0:T(1,128)S(1)}, u32[]{:S(2)}, u32[]{:S(2)}) collective-permute-start(f32[1,32896]{1,0:T(1,128)S(1)} %add.131), channel_id=1, source_target_pairs={{0,128},{2,130},{4,132},{6,134},{8,136},{10,138},{12,140},{14,142}... | collective-permute-start | bytes 394760 | tf_op jit(solution)/shard_map/ppermute | solution.py:26
  62.5 8.3 %collective-permute-done.8 = f32[1,32896]{1,0:T(1,128)S(1)} collective-permute-done((f32[1,32896]{1,0:T(1,128)S(1)}, f32[1,32896]{1,0:T(1,128)S(1)}, u32[]{:S(2)}, u32[]{:S(2)}) %collective-permute-start.8) | collective-permute-done | bytes 131616 | tf_op jit(solution)/shard_map/ppermute | solution.py:26
  71.3 0.9 %multiply_reduce_fusion = f32[]{:T(128)} fusion(f32[1,32896]{1,0:T(1,128)S(1)} %add.132, f32[1,32768]{1,0:T(1,128)S(1)} %bitcast.76), kind=kLoop, calls=%fused_computation.18 | loop fusion | flops 98303 | bytes 262148 | tf_op jit(solution)/shard_map/reduce_sum | solution.py:205
  72.2 0.7 slice_add_fusion.1
  72.9 1.9 %collective-permute-start.9 = (f32[1,2]{1,0:T(1,128)S(1)}, f32[1,2]{1,0:T(1,128)S(1)}, u32[]{:S(2)}, u32[]{:S(2)}) collective-permute-start(f32[1,2]{1,0:T(1,128)S(1)} %slice_add_fusion.1), channel_id=1, source_target_pairs={{0,1},{1,0},{2,3},{3,2},{4,5},{5,4},{6,7},{7,6},{8,9},{9,8},{10,11... | collective-permute-start | bytes 32 | tf_op jit(solution)/shard_map/ppermute | solution.py:26
  74.8 3.2 %collective-permute-done.9 = f32[1,2]{1,0:T(1,128)S(1)} collective-permute-done((f32[1,2]{1,0:T(1,128)S(1)}, f32[1,2]{1,0:T(1,128)S(1)}, u32[]{:S(2)}, u32[]{:S(2)}) %collective-permute-start.9) | collective-permute-done | bytes 40 | tf_op jit(solution)/shard_map/ppermute | solution.py:26
  80.0 0.8 multiply_subtract_fusion
  (67 shorter events, 5.6 us)
Async XLA Ops:
  0.6 7.4 %copy-start.7 = (s32[32768]{0:T(1024)S(1)}, s32[32768]{0:T(1024)}, u32[]{:S(2)}) copy-start(s32[32768]{0:T(1024)} %param.31) | copy-start | bytes 393220
  1.5 8.7 %collective-permute-start = (f32[1,1,4096]{2,1,0:T(1,128)S(1)}, f32[1,1,4096]{2,1,0:T(1,128)S(1)}, u32[]{:S(2)}, u32[]{:S(2)}) collective-permute-start(f32[1,1,4096]{2,1,0:T(1,128)S(1)} %get-tuple-element.18), channel_id=1, source_target_pairs={{0,1},{1,0},{2,3},{3,2},{4,5},{5,4},{6,7},{7,6},{8,9},{9,8},{10,11... | collective-permute-start | bytes 49160 | tf_op jit(solution)/shard_map/ppermute | solution.py:156
  5.6 1.8 %copy-start.6 = (f32[1,1,2,4096]{3,2,1,0:T(2,128)S(1)}, f32[1,1,2,4096]{3,2,1,0:T(2,128)}, u32[]{:S(2)}) copy-start(f32[1,1,2,4096]{3,2,1,0:T(2,128)} %param.18) | copy-start | bytes 98308
  5.6 2.5 %copy-start.12 = (s32[6144]{0:T(1024)S(1)}, s32[6144]{0:T(1024)}, u32[]{:S(2)}) copy-start(s32[6144]{0:T(1024)} %param.28) | copy-start | bytes 73732
  7.4 0.7 copy-start.11
  8.2 0.7 copy-start.14
  8.2 0.7 copy-start.15
  8.2 0.7 copy-start.16
  12.2 1.9 %copy-start.3 = (f32[1,1,32768]{2,1,0:T(1,128)S(1)}, f32[1,1,32768]{2,1,0:T(1,128)}, u32[]{:S(2)}) copy-start(f32[1,1,32768]{2,1,0:T(1,128)} %param.17) | copy-start | bytes 393220
  12.2 1.9 %copy-start.4 = (f32[1,32768]{1,0:T(1,128)S(1)}, f32[1,32768]{1,0:T(1,128)}, u32[]{:S(2)}) copy-start(f32[1,32768]{1,0:T(1,128)} %param.24) | copy-start | bytes 393220
  12.2 1.9 %copy-start.8 = (f32[1,32768]{1,0:T(1,128)S(1)}, f32[1,32768]{1,0:T(1,128)}, u32[]{:S(2)}) copy-start(f32[1,32768]{1,0:T(1,128)} %param.21) | copy-start | bytes 393220
  14.1 1.9 %copy-start.13 = (f32[1,6144]{1,0:T(1,128)S(1)}, f32[1,6144]{1,0:T(1,128)}, u32[]{:S(2)}) copy-start(f32[1,6144]{1,0:T(1,128)} %param.20) | copy-start | bytes 73732
  14.1 4.6 %collective-permute-start.1 = (f32[1,1,4096]{2,1,0:T(1,128)S(1)}, f32[1,1,4096]{2,1,0:T(1,128)S(1)}, u32[]{:S(2)}, u32[]{:S(2)}) collective-permute-start(f32[1,1,4096]{2,1,0:T(1,128)S(1)} %get-tuple-element.5), channel_id=1, source_target_pairs={{0,254},{2,0},{4,2},{6,4},{8,6},{10,8},{12,10},{14,12},{16,14},{18... | collective-permute-start | bytes 49160 | tf_op jit(solution)/shard_map/ppermute | solution.py:16
  16.0 2.8 %copy-start.5 = (f32[1,1,2,4096]{3,2,1,0:T(2,128)S(1)}, f32[1,1,2,4096]{3,2,1,0:T(2,128)}, u32[]{:S(2)}) copy-start(f32[1,1,2,4096]{3,2,1,0:T(2,128)} %param.16) | copy-start | bytes 98308
  16.0 2.8 %copy-start.9 = (f32[1,2,4096]{2,1,0:T(2,128)S(1)}, f32[1,2,4096]{2,1,0:T(2,128)}, u32[]{:S(2)}) copy-start(f32[1,2,4096]{2,1,0:T(2,128)} %param.22) | copy-start | bytes 98308
  16.0 2.8 %copy-start.10 = (f32[4096]{0:T(1024)S(1)}, f32[4096]{0:T(1024)}, u32[]{:S(2)}) copy-start(f32[4096]{0:T(1024)} %param.25) | copy-start | bytes 49156
  20.3 1.6 %collective-permute-start.2 = (f32[1,32896]{1,0:T(1,128)S(1)}, f32[1,32896]{1,0:T(1,128)S(1)}, u32[]{:S(2)}, u32[]{:S(2)}) collective-permute-start(f32[1,32896]{1,0:T(1,128)S(1)} %pad_maximum_fusion.1), channel_id=1, source_target_pairs={{0,2},{2,0},{4,6},{6,4},{8,10},{10,8},{12,14},{14,12},{16,18},{18,... | collective-permute-start | bytes 394760 | tf_op jit(solution)/shard_map/ppermute | solution.py:26
  22.1 5.9 %collective-permute-start.3 = (f32[1,32896]{1,0:T(1,128)S(1)}, f32[1,32896]{1,0:T(1,128)S(1)}, u32[]{:S(2)}, u32[]{:S(2)}) collective-permute-start(f32[1,32896]{1,0:T(1,128)S(1)} %fusion.11), channel_id=1, source_target_pairs={{0,4},{2,6},{4,0},{6,2},{8,12},{10,14},{12,8},{14,10},{16,20},{18,... | collective-permute-start | bytes 394760 | tf_op jit(solution)/shard_map/ppermute | solution.py:26
  28.1 8.7 %copy-start = (s32[352,128]{1,0:T(8,128)S(1)}, s32[352,128]{1,0:T(8,128)}, u32[]{:S(2)}) copy-start(s32[352,128]{1,0:T(8,128)} %add_bitcast_fusion.index_ref) | copy-start | bytes 540676
  28.1 6.6 %collective-permute-start.4 = (f32[1,32896]{1,0:T(1,128)S(1)}, f32[1,32896]{1,0:T(1,128)S(1)}, u32[]{:S(2)}, u32[]{:S(2)}) collective-permute-start(f32[1,32896]{1,0:T(1,128)S(1)} %add.127), channel_id=1, source_target_pairs={{0,8},{2,10},{4,12},{6,14},{8,0},{10,2},{12,4},{14,6},{16,24},{18,... | collective-permute-start | bytes 394760 | tf_op jit(solution)/shard_map/ppermute | solution.py:26
  34.8 5.1 %collective-permute-start.5 = (f32[1,32896]{1,0:T(1,128)S(1)}, f32[1,32896]{1,0:T(1,128)S(1)}, u32[]{:S(2)}, u32[]{:S(2)}) collective-permute-start(f32[1,32896]{1,0:T(1,128)S(1)} %add.128), channel_id=1, source_target_pairs={{0,16},{2,18},{4,20},{6,22},{8,24},{10,26},{12,28},{14,30},{16,0},... | collective-permute-start | bytes 394760 | tf_op jit(solution)/shard_map/ppermute | solution.py:26
  40.0 14.2 %collective-permute-start.6 = (f32[1,32896]{1,0:T(1,128)S(1)}, f32[1,32896]{1,0:T(1,128)S(1)}, u32[]{:S(2)}, u32[]{:S(2)}) collective-permute-start(f32[1,32896]{1,0:T(1,128)S(1)} %add.129), channel_id=1, source_target_pairs={{0,32},{2,34},{4,36},{6,38},{8,40},{10,42},{12,44},{14,46},{16,48}... | collective-permute-start | bytes 394760 | tf_op jit(solution)/shard_map/ppermute | solution.py:26
  54.4 6.0 %collective-permute-start.7 = (f32[1,32896]{1,0:T(1,128)S(1)}, f32[1,32896]{1,0:T(1,128)S(1)}, u32[]{:S(2)}, u32[]{:S(2)}) collective-permute-start(f32[1,32896]{1,0:T(1,128)S(1)} %add.130), channel_id=1, source_target_pairs={{0,64},{2,66},{4,68},{6,70},{8,72},{10,74},{12,76},{14,78},{16,80}... | collective-permute-start | bytes 394760 | tf_op jit(solution)/shard_map/ppermute | solution.py:26
  54.5 7.9 %collective-permute-start.10 = (f32[1,1,4096]{2,1,0:T(1,128)S(1)}, f32[1,1,4096]{2,1,0:T(1,128)S(1)}, u32[]{:S(2)}, u32[]{:S(2)}) collective-permute-start(f32[1,1,4096]{2,1,0:T(1,128)S(1)} %constant_dynamic-slice_fusion), channel_id=1, source_target_pairs={{0,1},{1,0},{2,3},{3,2},{4,5},{5,4},{6,7},{7,6},{8,9},{9,8},{10,11... | collective-permute-start | bytes 49160 | tf_op jit(solution)/shard_map/ppermute | solution.py:227
  56.4 6.0 %collective-permute-start.11 = (f32[1,1,4096]{2,1,0:T(1,128)S(1)}, f32[1,1,4096]{2,1,0:T(1,128)S(1)}, u32[]{:S(2)}, u32[]{:S(2)}) collective-permute-start(f32[1,1,4096]{2,1,0:T(1,128)S(1)} %get-tuple-element.9), channel_id=1, source_target_pairs={{0,2},{2,4},{4,6},{6,8},{8,10},{10,12},{12,14},{14,16},{16,18},{18... | collective-permute-start | bytes 49160 | tf_op jit(solution)/shard_map/ppermute | solution.py:16
  60.5 10.4 %collective-permute-start.8 = (f32[1,32896]{1,0:T(1,128)S(1)}, f32[1,32896]{1,0:T(1,128)S(1)}, u32[]{:S(2)}, u32[]{:S(2)}) collective-permute-start(f32[1,32896]{1,0:T(1,128)S(1)} %add.131), channel_id=1, source_target_pairs={{0,128},{2,130},{4,132},{6,134},{8,136},{10,138},{12,140},{14,142}... | collective-permute-start | bytes 394760 | tf_op jit(solution)/shard_map/ppermute | solution.py:26
  62.5 8.5 %copy-start.2 = (f32[32768]{0:T(1024)S(1)}, f32[32768]{0:T(1024)}, u32[]{:S(2)}) copy-start(f32[32768]{0:T(1024)} %param.23) | copy-start | bytes 393220
  71.3 8.6 %copy-start.1 = (f32[1,1,32768]{2,1,0:T(1,128)S(1)}, f32[1,1,32768]{2,1,0:T(1,128)}, u32[]{:S(2)}) copy-start(f32[1,1,32768]{2,1,0:T(1,128)} %param.19) | copy-start | bytes 393220
  72.9 5.1 %collective-permute-start.9 = (f32[1,2]{1,0:T(1,128)S(1)}, f32[1,2]{1,0:T(1,128)S(1)}, u32[]{:S(2)}, u32[]{:S(2)}) collective-permute-start(f32[1,2]{1,0:T(1,128)S(1)} %slice_add_fusion.1), channel_id=1, source_target_pairs={{0,1},{1,0},{2,3},{3,2},{4,5},{5,4},{6,7},{7,6},{8,9},{9,8},{10,11... | collective-permute-start | bytes 32 | tf_op jit(solution)/shard_map/ppermute | solution.py:26

commit v10 on v9

--- a/solution.py
+++ b/solution.py
@@ -168,8 +168,7 @@
     flow_value = gathered[..., :lines] - gathered[..., lines : 2 * lines]
     dispatch_value = gathered[..., 2 * lines :] + direction_capacity
 
-    first_hour, gathered = lax.optimization_barrier((storage[:, :1], gathered))
-    next_first = passed_along(first_hour, "tm", -1)
+    next_first = passed_along(storage[:, :1], "tm", -1)
     storage_next = jnp.concatenate([storage[:, 1:, :], next_first], axis=1)
     level_value = storage - retention * storage_next
     charge_value = balance - storage
@@ -211,9 +210,6 @@
         - availability[None] * capacity_scaled[:, None, :]
         + DAMPING * direction_capacity
     )
-    sums, image_limit = lax.optimization_barrier((sums, image_limit))
-    totals = butterfly_sum(sums, "net")
-
     bus_terms = scatter_blocks(
         jnp.concatenate([flow_scaled, -flow_scaled, dispatch_scaled], axis=-1),
         blocks,
@@ -232,6 +228,9 @@
     level_before = jnp.concatenate([behind, level_scaled[:, :-1, :]], axis=1)
     image_storage = level_scaled - retention * level_before - charge_scaled + DAMPING * storage
     image_nodal = jnp.stack([image_balance, image_storage], axis=2)
+    sums, image_limit, image_nodal = lax.optimization_barrier((sums, image_limit, image_nodal))
+    totals = butterfly_sum(sums, "net")
+
     step_size = totals[:, 0] / totals[:, 1]
     updated_nodal = residual_nodal - step_size[:, None, None, None] * image_nodal
     updated_capacity = residual_capacity - step_size[:, None, None] * image_limit

time: 81.8 us -> 86.9 us (1.062)
  the two profiles are of different devices: /device:TPU:34 before, /device:TPU:6 now
where the time goes in v10:
time: 86.9 us; the launch traced here: 86.4 us
  waiting for transfers between devices  32.8 us (38%)
  starting transfers between devices  19.7 us (23%)
  other arithmetic  16.7 us (19%)
  Pallas kernels  6.35 us (7%)
  between operations  5.51 us (6%)
  local copies, waits for them, and re-layouts  5.3 us (6%)
    ppermute x8, waiting for transfers between devices, butterfly_sum(): value = value + lax.ppermute(value, axis, pairs)  32.7 us
    ppermute x8, starting transfers between devices, butterfly_sum(): value = value + lax.ppermute(value, axis, pairs)  14.5 us
    pallas_call x1, Pallas kernels, lane_scatter(): pl.pallas_call(lane_scatter_kernel, out_shape=jax.ShapeDtypeStruct((BLOCK...  4.43 us
    ppermute x1, starting transfers between devices, body(): other = lax.ppermute(balance, 'net', [(0, 1), (1, 0)])  3.28 us
    ppermute x1, starting transfers between devices, body(): own_terms = mine + lax.ppermute(theirs, 'net', [(0, 1), (1, 0)])  1.93 us
    pallas_call x1, Pallas kernels, lane_gather(): pl.pallas_call(lane_gather_kernel, out_shape=jax.ShapeDtypeStruct(table.s...  1.92 us
    reduce_sum x1, other arithmetic, body(): jnp.sum(dispatch_scaled * dispatch_value + DAMPING * direction_capacity *...  1.88 us
    scatter-add x1, other arithmetic, scatter_blocks(): out = out.at[..., blocks, :].add(within)  1.75 us
  transfers between devices with their start and end apart: 12, of which 8 were waited for; matrix products, arithmetic and copies ran while one was open for 18% of the time, Pallas kernels for 7%

profile of v10, /device:TPU:6, one launch (start us, length us, event | category | flops | bytes accessed | tf_op | source)
XLA Modules:
  0.0 86.4 jit_solution(8063296795080838614)
XLA Ops:
  0.6 0.9 %slice_bitcast_fusion = (f32[1,1,4096]{2,1,0:T(1,128)S(1)}, f32[1,1,4096]{2,1,0:T(1,128)S(1)}, f32[1,1,1,4096]{3,2,1,0:T(1,128)S(1)}) fusion(f32[1,1,2,4096]{3,2,1,0:T(2,128)} %param.16), kind=kLoop, calls=%fused_computation.38 | loop fusion | bytes 81920 | tf_op jit(solution)/shard_map/squeeze | solution.py:153
  1.5 3.3 %collective-permute-start = (f32[1,1,4096]{2,1,0:T(1,128)S(1)}, f32[1,1,4096]{2,1,0:T(1,128)S(1)}, u32[]{:S(2)}, u32[]{:S(2)}) collective-permute-start(f32[1,1,4096]{2,1,0:T(1,128)S(1)} %get-tuple-element.18), channel_id=1, source_target_pairs={{0,1},{1,0},{2,3},{3,2},{4,5},{5,4},{6,7},{7,6},{8,9},{9,8},{10,11... | collective-permute-start | bytes 49160 | tf_op jit(solution)/shard_map/ppermute | solution.py:156
  4.8 0.8 fusion.8
  5.6 1.4 %multiply_reduce_fusion.2 = f32[]{:T(128)} fusion(f32[1,1,2,4096]{3,2,1,0:T(2,128)} %param.18), kind=kLoop, calls=%fused_computation.27 | loop fusion | flops 16383 | bytes 32772 | tf_op jit(solution)/shard_map/reduce_sum | solution.py:179
  7.0 0.9 %multiply_reduce_fusion.1 = f32[]{:T(128)} fusion(f32[1,1,32768]{2,1,0:T(1,128)S(1)} %copy-done.1), kind=kLoop, calls=%fused_computation.19 | loop fusion | flops 65535 | bytes 131076 | tf_op jit(solution)/shard_map/reduce_sum | solution.py:179
  7.9 1.5 %add_bitcast_fusion.index_ref = s32[352,128]{1,0:T(8,128)} fusion(s32[32768]{0:T(1024)S(1)} %copy-done.7, s32[6144]{0:T(1024)} %param.29, s32[6144]{0:T(1024)} %param.28), kind=kLoop, calls=%fused_computation.4 | loop fusion | flops 90112 | bytes 360448 | tf_op jit(solution)/shard_map/reshape;broadcast_in_dim;reshape | solution.py:113
  10.8 1.1 %gather_fusion = f32[352,128]{1,0:T(8,128)S(1)} fusion(f32[64,128]{1,0:T(8,128)S(1)} %fusion.5, s32[1024]{0:T(1024)S(1)} %pad_clamp_fusion), kind=kCustom, calls=%fused_computation | custom fusion | bytes 361856 | tf_op jit(solution)/shard_map/jit(_take)/gather | solution.py:111
  11.9 0.8 broadcast_select_fusion.table_ref
  12.7 1.9 %shard_map.167 = f32[352,128]{1,0:T(8,128)} custom-call(f32[352,128]{1,0:T(8,128)} %broadcast_select_fusion.table_ref, s32[352,128]{1,0:T(8,128)} %add_bitcast_fusion.index_ref), custom_call_target="tpu_custom_call" | custom-call | tf_op jit(solution)/shard_map/pallas_call | solution.py:61
  14.6 0.8 fusion.11
  15.5 1.9 %fusion.4 = (f32[]{:T(128)}, f32[1,1,32768]{2,1,0:T(1,128)S(1)}, f32[1,32768]{1,0:T(1,128)S(1)}) fusion(f32[1,1,32768]{2,1,0:T(1,128)S(1)} %copy-done.3, f32[1,1,45056]{2,1,0:T(1,128)} %bitcast.72, f32[1,32768]{1,0:T(1,128)S(1)} %copy-done.8, f32[1,32768]{1,0:T(1,128)S(1)} %copy-done.4), kind=kLoop, calls=%fused_computation.20 | loop fusion | flops 294911 | bytes 786436 | tf_op jit(solution)/shard_map/reduce_sum | solution.py:185
  17.3 1.4 %multiply_reduce_fusion.3 = f32[]{:T(128)} fusion(f32[1,1,6144]{2,1,0:T(1,128)S(1)} %get-tuple-element.9, f32[1,1,45056]{2,1,0:T(1,128)} %bitcast.73), kind=kLoop, calls=%fused_computation.30 | loop fusion | flops 18431 | bytes 73732 | tf_op jit(solution)/shard_map/reduce_sum | solution.py:184
  20.1 0.7 add_reduce_fusion
  22.2 1.0 %collective-permute-done.2 = f32[1,32896]{1,0:T(1,128)S(1)} collective-permute-done((f32[1,32896]{1,0:T(1,128)S(1)}, f32[1,32896]{1,0:T(1,128)S(1)}, u32[]{:S(2)}, u32[]{:S(2)}) %collective-permute-start.2) | collective-permute-done | bytes 131616 | tf_op jit(solution)/shard_map/ppermute | solution.py:26
  23.4 0.9 %collective-permute-start.3 = (f32[1,32896]{1,0:T(1,128)S(1)}, f32[1,32896]{1,0:T(1,128)S(1)}, u32[]{:S(2)}, u32[]{:S(2)}) collective-permute-start(f32[1,32896]{1,0:T(1,128)S(1)} %fusion.10), channel_id=1, source_target_pairs={{0,4},{2,6},{4,0},{6,2},{8,12},{10,14},{12,8},{14,10},{16,20},{18,... | collective-permute-start | bytes 394760 | tf_op jit(solution)/shard_map/ppermute | solution.py:26
  24.3 4.9 %collective-permute-done.3 = f32[1,32896]{1,0:T(1,128)S(1)} collective-permute-done((f32[1,32896]{1,0:T(1,128)S(1)}, f32[1,32896]{1,0:T(1,128)S(1)}, u32[]{:S(2)}, u32[]{:S(2)}) %collective-permute-start.3) | collective-permute-done | bytes 131616 | tf_op jit(solution)/shard_map/ppermute | solution.py:26
  29.4 7.2 %collective-permute-start.4 = (f32[1,32896]{1,0:T(1,128)S(1)}, f32[1,32896]{1,0:T(1,128)S(1)}, u32[]{:S(2)}, u32[]{:S(2)}) collective-permute-start(f32[1,32896]{1,0:T(1,128)S(1)} %add.127), channel_id=1, source_target_pairs={{0,8},{2,10},{4,12},{6,14},{8,0},{10,2},{12,4},{14,6},{16,24},{18,... | collective-permute-start | bytes 394760 | tf_op jit(solution)/shard_map/ppermute | solution.py:26
  37.5 2.5 %collective-permute-done.4 = f32[1,32896]{1,0:T(1,128)S(1)} collective-permute-done((f32[1,32896]{1,0:T(1,128)S(1)}, f32[1,32896]{1,0:T(1,128)S(1)}, u32[]{:S(2)}, u32[]{:S(2)}) %collective-permute-start.4) | collective-permute-done | bytes 131616 | tf_op jit(solution)/shard_map/ppermute | solution.py:26
  40.5 0.7 pad_bitcast_fusion.1.value_ref
  41.2 4.4 %shard_map.168 = f32[128,384]{1,0:T(8,128)} custom-call(f32[128,384]{1,0:T(8,128)} %pad_bitcast_fusion.1.value_ref, s32[128,384]{1,0:T(8,128)} %pad_bitcast_fusion.index_ref), custom_call_target="tpu_custom_call" | custom-call | tf_op jit(solution)/shard_map/pallas_call | solution.py:101
  45.6 1.0 %copy.26 = f32[352,128]{1,0:T(8,128)S(1)} copy(f32[352,128]{0,1:T(8,128)} %bitcast.74) | data formatting | bytes 360448 | tf_op jit(solution)/shard_map/slice | solution.py:105
  46.7 1.8 %scatter_custom_fusion = f32[64,128]{1,0:T(8,128)S(1)} fusion(s32[352]{0:T(512)S(1)} %fusion.8, f32[352,128]{1,0:T(8,128)S(1)} %copy.26, f32[]{:T(128)} %constant.11.clone.1), kind=kCustom, calls=%fused_computation.31 | custom fusion | flops 45056 | bytes 32772 | tf_op jit(solution)/shard_map/scatter-add | solution.py:124
  48.7 1.9 %collective-permute-start.9 = (f32[1,1,4096]{2,1,0:T(1,128)S(1)}, f32[1,1,4096]{2,1,0:T(1,128)S(1)}, u32[]{:S(2)}, u32[]{:S(2)}) collective-permute-start(f32[1,1,4096]{2,1,0:T(1,128)S(1)} %constant_dynamic-slice_fusion), channel_id=1, source_target_pairs={{0,1},{1,0},{2,3},{3,2},{4,5},{5,4},{6,7},{7,6},{8,9},{9,8},{10,11... | collective-permute-start | bytes 49160 | tf_op jit(solution)/shard_map/ppermute | solution.py:223
  50.6 3.0 %collective-permute-done.6 = f32[1,32896]{1,0:T(1,128)S(1)} collective-permute-done((f32[1,32896]{1,0:T(1,128)S(1)}, f32[1,32896]{1,0:T(1,128)S(1)}, u32[]{:S(2)}, u32[]{:S(2)}) %collective-permute-start.6) | collective-permute-done | bytes 131616 | tf_op jit(solution)/shard_map/ppermute | solution.py:26
  54.1 9.3 %collective-permute-done.7 = f32[1,32896]{1,0:T(1,128)S(1)} collective-permute-done((f32[1,32896]{1,0:T(1,128)S(1)}, f32[1,32896]{1,0:T(1,128)S(1)}, u32[]{:S(2)}, u32[]{:S(2)}) %collective-permute-start.7) | collective-permute-done | bytes 131616 | tf_op jit(solution)/shard_map/ppermute | solution.py:26
  63.5 3.9 %collective-permute-start.8 = (f32[1,32896]{1,0:T(1,128)S(1)}, f32[1,32896]{1,0:T(1,128)S(1)}, u32[]{:S(2)}, u32[]{:S(2)}) collective-permute-start(f32[1,32896]{1,0:T(1,128)S(1)} %add.131), channel_id=1, source_target_pairs={{0,128},{2,130},{4,132},{6,134},{8,136},{10,138},{12,140},{14,142}... | collective-permute-start | bytes 394760 | tf_op jit(solution)/shard_map/ppermute | solution.py:26
  67.5 8.4 %collective-permute-done.8 = f32[1,32896]{1,0:T(1,128)S(1)} collective-permute-done((f32[1,32896]{1,0:T(1,128)S(1)}, f32[1,32896]{1,0:T(1,128)S(1)}, u32[]{:S(2)}, u32[]{:S(2)}) %collective-permute-start.8) | collective-permute-done | bytes 131616 | tf_op jit(solution)/shard_map/ppermute | solution.py:26
  76.0 0.9 %multiply_reduce_fusion = f32[]{:T(128)} fusion(f32[1,32896]{1,0:T(1,128)S(1)} %add.132, f32[1,32768]{1,0:T(1,128)S(1)} %bitcast.76), kind=kLoop, calls=%fused_computation.18 | loop fusion | flops 98303 | bytes 262148 | tf_op jit(solution)/shard_map/reduce_sum | solution.py:204
  77.2 0.7 slice_add_fusion.1
  77.9 1.5 %collective-permute-start.11 = (f32[1,2]{1,0:T(1,128)S(1)}, f32[1,2]{1,0:T(1,128)S(1)}, u32[]{:S(2)}, u32[]{:S(2)}) collective-permute-start(f32[1,2]{1,0:T(1,128)S(1)} %slice_add_fusion.1), channel_id=1, source_target_pairs={{0,1},{1,0},{2,3},{3,2},{4,5},{5,4},{6,7},{7,6},{8,9},{9,8},{10,11... | collective-permute-start | bytes 32 | tf_op jit(solution)/shard_map/ppermute | solution.py:26
  79.4 3.6 %collective-permute-done.11 = f32[1,2]{1,0:T(1,128)S(1)} collective-permute-done((f32[1,2]{1,0:T(1,128)S(1)}, f32[1,2]{1,0:T(1,128)S(1)}, u32[]{:S(2)}, u32[]{:S(2)}) %collective-permute-start.11) | collective-permute-done | bytes 40 | tf_op jit(solution)/shard_map/ppermute | solution.py:26
  85.6 0.8 multiply_subtract_fusion
  (64 shorter events, 5.1 us)
Async XLA Ops:
  0.6 6.4 %copy-start.1 = (f32[1,1,32768]{2,1,0:T(1,128)S(1)}, f32[1,1,32768]{2,1,0:T(1,128)}, u32[]{:S(2)}) copy-start(f32[1,1,32768]{2,1,0:T(1,128)} %param.19) | copy-start | bytes 393220
  0.6 7.2 %copy-start.7 = (s32[32768]{0:T(1024)S(1)}, s32[32768]{0:T(1024)}, u32[]{:S(2)}) copy-start(s32[32768]{0:T(1024)} %param.31) | copy-start | bytes 393220
  1.5 9.2 %collective-permute-start = (f32[1,1,4096]{2,1,0:T(1,128)S(1)}, f32[1,1,4096]{2,1,0:T(1,128)S(1)}, u32[]{:S(2)}, u32[]{:S(2)}) collective-permute-start(f32[1,1,4096]{2,1,0:T(1,128)S(1)} %get-tuple-element.18), channel_id=1, source_target_pairs={{0,1},{1,0},{2,3},{3,2},{4,5},{5,4},{6,7},{7,6},{8,9},{9,8},{10,11... | collective-permute-start | bytes 49160 | tf_op jit(solution)/shard_map/ppermute | solution.py:156
  4.8 15.3 %collective-permute-start.1 = (f32[1,1,4096]{2,1,0:T(1,128)S(1)}, f32[1,1,4096]{2,1,0:T(1,128)S(1)}, u32[]{:S(2)}, u32[]{:S(2)}) collective-permute-start(f32[1,1,4096]{2,1,0:T(1,128)S(1)} %get-tuple-element.17), channel_id=1, source_target_pairs={{0,254},{2,0},{4,2},{6,4},{8,6},{10,8},{12,10},{14,12},{16,14},{18... | collective-permute-start | bytes 49160 | tf_op jit(solution)/shard_map/ppermute | solution.py:16
  7.9 1.5 %copy-start.12 = (s32[256]{0:T(256)S(1)}, s32[256]{0:T(256)}, u32[]{:S(2)}) copy-start(s32[256]{0:T(256)} %param.30) | copy-start | bytes 3076
  7.9 1.5 %copy-start.13 = (s32[48]{0:T(128)S(1)}, s32[48]{0:T(128)}, u32[]{:S(2)}) copy-start(s32[48]{0:T(128)} %param.27) | copy-start | bytes 580
  7.9 1.5 %copy-start.14 = (s32[48]{0:T(128)S(1)}, s32[48]{0:T(128)}, u32[]{:S(2)}) copy-start(s32[48]{0:T(128)} %param.26) | copy-start | bytes 580
  12.7 1.9 %copy-start.11 = (f32[1,6144]{1,0:T(1,128)S(1)}, f32[1,6144]{1,0:T(1,128)}, u32[]{:S(2)}) copy-start(f32[1,6144]{1,0:T(1,128)} %param.20) | copy-start | bytes 73732
  12.7 2.7 %copy-start.3 = (f32[1,1,32768]{2,1,0:T(1,128)S(1)}, f32[1,1,32768]{2,1,0:T(1,128)}, u32[]{:S(2)}) copy-start(f32[1,1,32768]{2,1,0:T(1,128)} %param.17) | copy-start | bytes 393220
  12.7 2.8 %copy-start.4 = (f32[1,32768]{1,0:T(1,128)S(1)}, f32[1,32768]{1,0:T(1,128)}, u32[]{:S(2)}) copy-start(f32[1,32768]{1,0:T(1,128)} %param.24) | copy-start | bytes 393220
  12.7 2.8 %copy-start.8 = (f32[1,32768]{1,0:T(1,128)S(1)}, f32[1,32768]{1,0:T(1,128)}, u32[]{:S(2)}) copy-start(f32[1,32768]{1,0:T(1,128)} %param.21) | copy-start | bytes 393220
  15.4 4.6 %copy-start.10 = (f32[4096]{0:T(1024)S(1)}, f32[4096]{0:T(1024)}, u32[]{:S(2)}) copy-start(f32[4096]{0:T(1024)} %param.25) | copy-start | bytes 49156
  17.3 2.7 %copy-start.5 = (f32[1,1,2,4096]{3,2,1,0:T(2,128)S(1)}, f32[1,1,2,4096]{3,2,1,0:T(2,128)}, u32[]{:S(2)}) copy-start(f32[1,1,2,4096]{3,2,1,0:T(2,128)} %param.16) | copy-start | bytes 98308
  17.3 2.8 %copy-start.9 = (f32[1,2,4096]{2,1,0:T(2,128)S(1)}, f32[1,2,4096]{2,1,0:T(2,128)}, u32[]{:S(2)}) copy-start(f32[1,2,4096]{2,1,0:T(2,128)} %param.22) | copy-start | bytes 98308
  21.6 1.6 %collective-permute-start.2 = (f32[1,32896]{1,0:T(1,128)S(1)}, f32[1,32896]{1,0:T(1,128)S(1)}, u32[]{:S(2)}, u32[]{:S(2)}) collective-permute-start(f32[1,32896]{1,0:T(1,128)S(1)} %pad_maximum_fusion.1), channel_id=1, source_target_pairs={{0,2},{2,0},{4,6},{6,4},{8,10},{10,8},{12,14},{14,12},{16,18},{18,... | collective-permute-start | bytes 394760 | tf_op jit(solution)/shard_map/ppermute | solution.py:26
  23.4 13.3 %copy-start = (s32[352,128]{1,0:T(8,128)S(1)}, s32[352,128]{1,0:T(8,128)}, u32[]{:S(2)}) copy-start(s32[352,128]{1,0:T(8,128)} %add_bitcast_fusion.index_ref) | copy-start | bytes 540676
  23.4 5.9 %collective-permute-start.3 = (f32[1,32896]{1,0:T(1,128)S(1)}, f32[1,32896]{1,0:T(1,128)S(1)}, u32[]{:S(2)}, u32[]{:S(2)}) collective-permute-start(f32[1,32896]{1,0:T(1,128)S(1)} %fusion.10), channel_id=1, source_target_pairs={{0,4},{2,6},{4,0},{6,2},{8,12},{10,14},{12,8},{14,10},{16,20},{18,... | collective-permute-start | bytes 394760 | tf_op jit(solution)/shard_map/ppermute | solution.py:26
  29.4 10.6 %collective-permute-start.4 = (f32[1,32896]{1,0:T(1,128)S(1)}, f32[1,32896]{1,0:T(1,128)S(1)}, u32[]{:S(2)}, u32[]{:S(2)}) collective-permute-start(f32[1,32896]{1,0:T(1,128)S(1)} %add.127), channel_id=1, source_target_pairs={{0,8},{2,10},{4,12},{6,14},{8,0},{10,2},{12,4},{14,6},{16,24},{18,... | collective-permute-start | bytes 394760 | tf_op jit(solution)/shard_map/ppermute | solution.py:26
  40.1 8.3 %collective-permute-start.5 = (f32[1,32896]{1,0:T(1,128)S(1)}, f32[1,32896]{1,0:T(1,128)S(1)}, u32[]{:S(2)}, u32[]{:S(2)}) collective-permute-start(f32[1,32896]{1,0:T(1,128)S(1)} %add.128), channel_id=1, source_target_pairs={{0,16},{2,18},{4,20},{6,22},{8,24},{10,26},{12,28},{14,30},{16,0},... | collective-permute-start | bytes 394760 | tf_op jit(solution)/shard_map/ppermute | solution.py:26
  48.6 5.1 %collective-permute-start.6 = (f32[1,32896]{1,0:T(1,128)S(1)}, f32[1,32896]{1,0:T(1,128)S(1)}, u32[]{:S(2)}, u32[]{:S(2)}) collective-permute-start(f32[1,32896]{1,0:T(1,128)S(1)} %add.129), channel_id=1, source_target_pairs={{0,32},{2,34},{4,36},{6,38},{8,40},{10,42},{12,44},{14,46},{16,48}... | collective-permute-start | bytes 394760 | tf_op jit(solution)/shard_map/ppermute | solution.py:26
  48.7 5.3 %collective-permute-start.9 = (f32[1,1,4096]{2,1,0:T(1,128)S(1)}, f32[1,1,4096]{2,1,0:T(1,128)S(1)}, u32[]{:S(2)}, u32[]{:S(2)}) collective-permute-start(f32[1,1,4096]{2,1,0:T(1,128)S(1)} %constant_dynamic-slice_fusion), channel_id=1, source_target_pairs={{0,1},{1,0},{2,3},{3,2},{4,5},{5,4},{6,7},{7,6},{8,9},{9,8},{10,11... | collective-permute-start | bytes 49160 | tf_op jit(solution)/shard_map/ppermute | solution.py:223
  50.6 3.4 %collective-permute-start.10 = (f32[1,1,4096]{2,1,0:T(1,128)S(1)}, f32[1,1,4096]{2,1,0:T(1,128)S(1)}, u32[]{:S(2)}, u32[]{:S(2)}) collective-permute-start(f32[1,1,4096]{2,1,0:T(1,128)S(1)} %get-tuple-element.11), channel_id=1, source_target_pairs={{0,2},{2,4},{4,6},{6,8},{8,10},{10,12},{12,14},{14,16},{16,18},{18... | collective-permute-start | bytes 49160 | tf_op jit(solution)/shard_map/ppermute | solution.py:16
  53.8 9.6 %collective-permute-start.7 = (f32[1,32896]{1,0:T(1,128)S(1)}, f32[1,32896]{1,0:T(1,128)S(1)}, u32[]{:S(2)}, u32[]{:S(2)}) collective-permute-start(f32[1,32896]{1,0:T(1,128)S(1)} %add.130), channel_id=1, source_target_pairs={{0,64},{2,66},{4,68},{6,70},{8,72},{10,74},{12,76},{14,78},{16,80}... | collective-permute-start | bytes 394760 | tf_op jit(solution)/shard_map/ppermute | solution.py:26
  63.5 12.3 %collective-permute-start.8 = (f32[1,32896]{1,0:T(1,128)S(1)}, f32[1,32896]{1,0:T(1,128)S(1)}, u32[]{:S(2)}, u32[]{:S(2)}) collective-permute-start(f32[1,32896]{1,0:T(1,128)S(1)} %add.131), channel_id=1, source_target_pairs={{0,128},{2,130},{4,132},{6,134},{8,136},{10,138},{12,140},{14,142}... | collective-permute-start | bytes 394760 | tf_op jit(solution)/shard_map/ppermute | solution.py:26
  67.4 8.6 %copy-start.2 = (f32[32768]{0:T(1024)S(1)}, f32[32768]{0:T(1024)}, u32[]{:S(2)}) copy-start(f32[32768]{0:T(1024)} %param.23) | copy-start | bytes 393220
  76.9 8.0 %copy-start.6 = (f32[1,1,2,4096]{3,2,1,0:T(2,128)S(1)}, f32[1,1,2,4096]{3,2,1,0:T(2,128)}, u32[]{:S(2)}) copy-start(f32[1,1,2,4096]{3,2,1,0:T(2,128)} %param.18) | copy-start | bytes 98308
  77.9 5.1 %collective-permute-start.11 = (f32[1,2]{1,0:T(1,128)S(1)}, f32[1,2]{1,0:T(1,128)S(1)}, u32[]{:S(2)}, u32[]{:S(2)}) collective-permute-start(f32[1,2]{1,0:T(1,128)S(1)} %slice_add_fusion.1), channel_id=1, source_target_pairs={{0,1},{1,0},{2,3},{3,2},{4,5},{5,4},{6,7},{7,6},{8,9},{9,8},{10,11... | collective-permute-start | bytes 32 | tf_op jit(solution)/shard_map/ppermute | solution.py:26

commit v11 on v9

--- a/solution.py
+++ b/solution.py
@@ -16,15 +16,21 @@
     return lax.ppermute(value, axis, pairs)
 
 
+def butterfly_masks(count):
+    masks = [1 << bit for bit in range(count.bit_length() - 1)]
+    if count == 128:
+        masks[2] = 6
+        masks[6] = 96
+    return masks
+
+
 def butterfly_sum(value, axis):
     count = lax.axis_size(axis)
     if count & (count - 1):
         return lax.psum(value, axis)
-    step = 1
-    while step < count:
-        pairs = [(source, source ^ step) for source in range(count)]
+    for mask in butterfly_masks(count):
+        pairs = [(source, source ^ mask) for source in range(count)]
         value = value + lax.ppermute(value, axis, pairs)
-        step *= 2
     return value
 
 

time: 81.8 us -> 80.3 us (0.982)
  the two profiles are of different devices: /device:TPU:34 before, /device:TPU:32 now
where the time goes in v11:
time: 80.3 us; the launch traced here: 79.9 us
  waiting for transfers between devices  25.8 us (32%)
  starting transfers between devices  21.5 us (27%)
  other arithmetic  15.3 us (19%)
  Pallas kernels  6.35 us (8%)
  between operations  5.49 us (7%)
  local copies, waits for them, and re-layouts  5.43 us (7%)
    ppermute x8, waiting for transfers between devices, butterfly_sum(): value = value + lax.ppermute(value, axis, pairs)  25.8 us
    ppermute x8, starting transfers between devices, butterfly_sum(): value = value + lax.ppermute(value, axis, pairs)  14.7 us
    pallas_call x1, Pallas kernels, lane_scatter(): pl.pallas_call(lane_scatter_kernel, out_shape=jax.ShapeDtypeStruct((BLOCK...  4.43 us
    ppermute x1, starting transfers between devices, body(): other = lax.ppermute(balance, 'net', [(0, 1), (1, 0)])  3.28 us
    ppermute x1, starting transfers between devices, body(): own_terms = mine + lax.ppermute(theirs, 'net', [(0, 1), (1, 0)])  1.93 us
    pallas_call x1, Pallas kernels, lane_gather(): pl.pallas_call(lane_gather_kernel, out_shape=jax.ShapeDtypeStruct(table.s...  1.92 us
    reduce_sum x1, other arithmetic, body(): jnp.sum(dispatch_scaled * dispatch_value + DAMPING * direction_capacity *...  1.87 us
    reduce_sum x1, other arithmetic, body(): jnp.sum(residual_capacity * residual_capacity, axis=(1, 2))  1.8 us
  transfers between devices with their start and end apart: 12, of which 7 were waited for; matrix products, arithmetic and copies ran while one was open for 15% of the time, Pallas kernels for 6%

profile of v11, /device:TPU:32, one launch (start us, length us, event | category | flops | bytes accessed | tf_op | source)
XLA Modules:
  0.0 79.9 jit_solution(7598698322489443379)
XLA Ops:
  0.6 0.9 %fusion.12 = (f32[1,1,1,4096]{3,2,1,0:T(1,128)S(1)}, f32[1,1,4096]{2,1,0:T(1,128)S(1)}, f32[1,1,4096]{2,1,0:T(1,128)S(1)}) fusion(f32[1,1,2,4096]{3,2,1,0:T(2,128)} %param.16), kind=kLoop, calls=%fused_computation.52 | loop fusion | bytes 81920 | tf_op jit(solution)/shard_map/slice | solution.py:158
  1.5 3.3 %collective-permute-start = (f32[1,1,4096]{2,1,0:T(1,128)S(1)}, f32[1,1,4096]{2,1,0:T(1,128)S(1)}, u32[]{:S(2)}, u32[]{:S(2)}) collective-permute-start(f32[1,1,4096]{2,1,0:T(1,128)S(1)} %get-tuple-element.18), channel_id=1, source_target_pairs={{0,1},{1,0},{2,3},{3,2},{4,5},{5,4},{6,7},{7,6},{8,9},{9,8},{10,11... | collective-permute-start | bytes 49160 | tf_op jit(solution)/shard_map/ppermute | solution.py:162
  4.8 0.8 fusion.9
  5.6 1.8 %multiply_reduce_fusion.1 = f32[]{:T(128)} fusion(f32[1,1,32768]{2,1,0:T(1,128)} %param.19), kind=kLoop, calls=%fused_computation.19 | loop fusion | flops 65535 | bytes 131076 | tf_op jit(solution)/shard_map/reduce_sum | solution.py:186
  10.3 1.1 %gather_fusion = f32[352,128]{1,0:T(8,128)S(1)} fusion(f32[64,128]{1,0:T(8,128)S(1)} %fusion.5, s32[1024]{0:T(1024)S(1)} %pad_clamp_fusion), kind=kCustom, calls=%fused_computation | custom fusion | bytes 361856 | tf_op jit(solution)/shard_map/jit(_take)/gather | solution.py:117
  11.4 0.8 broadcast_select_fusion.table_ref
  12.2 1.9 %shard_map.167 = f32[352,128]{1,0:T(8,128)} custom-call(f32[352,128]{1,0:T(8,128)} %broadcast_select_fusion.table_ref, s32[352,128]{1,0:T(8,128)} %add_bitcast_fusion.index_ref), custom_call_target="tpu_custom_call" | custom-call | tf_op jit(solution)/shard_map/pallas_call | solution.py:67
  14.1 1.6 %collective-permute-start.1 = (f32[1,1,4096]{2,1,0:T(1,128)S(1)}, f32[1,1,4096]{2,1,0:T(1,128)S(1)}, u32[]{:S(2)}, u32[]{:S(2)}) collective-permute-start(f32[1,1,4096]{2,1,0:T(1,128)S(1)} %get-tuple-element.5), channel_id=1, source_target_pairs={{0,254},{2,0},{4,2},{6,4},{8,6},{10,8},{12,10},{14,12},{16,14},{18... | collective-permute-start | bytes 49160 | tf_op jit(solution)/shard_map/ppermute | solution.py:16
  15.7 1.9 %fusion.4 = (f32[]{:T(128)}, f32[1,1,32768]{2,1,0:T(1,128)S(1)}, f32[1,32768]{1,0:T(1,128)S(1)}) fusion(f32[1,1,32768]{2,1,0:T(1,128)S(1)} %copy-done.3, f32[1,1,45056]{2,1,0:T(1,128)} %bitcast.73, f32[1,32768]{1,0:T(1,128)S(1)} %copy-done.8, f32[1,32768]{1,0:T(1,128)S(1)} %copy-done.4), kind=kLoop, calls=%fused_computation.20 | loop fusion | flops 294911 | bytes 786436 | tf_op jit(solution)/shard_map/reduce_sum | solution.py:192
  17.6 1.4 %multiply_reduce_fusion.3 = (f32[]{:T(128)}, f32[1,1,6144]{2,1,0:T(1,128)S(1)}) fusion(f32[1,1,45056]{2,1,0:T(1,128)} %bitcast.74, f32[1,6144]{1,0:T(1,128)S(1)} %copy-done.13), kind=kLoop, calls=%fused_computation.30 | loop fusion | flops 24575 | bytes 98308 | tf_op jit(solution)/shard_map/reduce_sum | solution.py:191
  20.3 0.7 add_reduce_fusion
  22.0 1.3 %collective-permute-done.2 = f32[1,32896]{1,0:T(1,128)S(1)} collective-permute-done((f32[1,32896]{1,0:T(1,128)S(1)}, f32[1,32896]{1,0:T(1,128)S(1)}, u32[]{:S(2)}, u32[]{:S(2)}) %collective-permute-start.2) | collective-permute-done | bytes 131616 | tf_op jit(solution)/shard_map/ppermute | solution.py:33
  23.6 5.5 %collective-permute-done.3 = f32[1,32896]{1,0:T(1,128)S(1)} collective-permute-done((f32[1,32896]{1,0:T(1,128)S(1)}, f32[1,32896]{1,0:T(1,128)S(1)}, u32[]{:S(2)}, u32[]{:S(2)}) %collective-permute-start.3) | collective-permute-done | bytes 131616 | tf_op jit(solution)/shard_map/ppermute | solution.py:33
  29.3 1.6 %collective-permute-start.4 = (f32[1,32896]{1,0:T(1,128)S(1)}, f32[1,32896]{1,0:T(1,128)S(1)}, u32[]{:S(2)}, u32[]{:S(2)}) collective-permute-start(f32[1,32896]{1,0:T(1,128)S(1)} %add.127), channel_id=1, source_target_pairs={{0,12},{2,14},{4,8},{6,10},{8,4},{10,6},{12,0},{14,2},{16,28},{18,... | collective-permute-start | bytes 394760 | tf_op jit(solution)/shard_map/ppermute | solution.py:33
  30.9 4.6 %collective-permute-done.4 = f32[1,32896]{1,0:T(1,128)S(1)} collective-permute-done((f32[1,32896]{1,0:T(1,128)S(1)}, f32[1,32896]{1,0:T(1,128)S(1)}, u32[]{:S(2)}, u32[]{:S(2)}) %collective-permute-start.4) | collective-permute-done | bytes 131616 | tf_op jit(solution)/shard_map/ppermute | solution.py:33
  35.7 1.9 %collective-permute-start.5 = (f32[1,32896]{1,0:T(1,128)S(1)}, f32[1,32896]{1,0:T(1,128)S(1)}, u32[]{:S(2)}, u32[]{:S(2)}) collective-permute-start(f32[1,32896]{1,0:T(1,128)S(1)} %add.128), channel_id=1, source_target_pairs={{0,16},{2,18},{4,20},{6,22},{8,24},{10,26},{12,28},{14,30},{16,0},... | collective-permute-start | bytes 394760 | tf_op jit(solution)/shard_map/ppermute | solution.py:33
  37.7 0.7 pad_bitcast_fusion.index_ref
  38.4 2.3 %collective-permute-done.5 = f32[1,32896]{1,0:T(1,128)S(1)} collective-permute-done((f32[1,32896]{1,0:T(1,128)S(1)}, f32[1,32896]{1,0:T(1,128)S(1)}, u32[]{:S(2)}, u32[]{:S(2)}) %collective-permute-start.5) | collective-permute-done | bytes 131616 | tf_op jit(solution)/shard_map/ppermute | solution.py:33
  40.9 5.9 %collective-permute-start.6 = (f32[1,32896]{1,0:T(1,128)S(1)}, f32[1,32896]{1,0:T(1,128)S(1)}, u32[]{:S(2)}, u32[]{:S(2)}) collective-permute-start(f32[1,32896]{1,0:T(1,128)S(1)} %add.129), channel_id=1, source_target_pairs={{0,32},{2,34},{4,36},{6,38},{8,40},{10,42},{12,44},{14,46},{16,48}... | collective-permute-start | bytes 394760 | tf_op jit(solution)/shard_map/ppermute | solution.py:33
  47.1 0.7 pad_bitcast_fusion.1.value_ref
  47.8 4.4 %shard_map.168 = f32[128,384]{1,0:T(8,128)} custom-call(f32[128,384]{1,0:T(8,128)} %pad_bitcast_fusion.1.value_ref, s32[128,384]{1,0:T(8,128)} %pad_bitcast_fusion.index_ref), custom_call_target="tpu_custom_call" | custom-call | tf_op jit(solution)/shard_map/pallas_call | solution.py:107
  52.3 1.0 %copy.26 = f32[352,128]{1,0:T(8,128)S(1)} copy(f32[352,128]{0,1:T(8,128)} %bitcast.71) | data formatting | bytes 360448 | tf_op jit(solution)/shard_map/slice | solution.py:111
  53.3 1.8 %scatter_custom_fusion = f32[64,128]{1,0:T(8,128)S(1)} fusion(s32[352]{0:T(512)S(1)} %fusion.9, f32[352,128]{1,0:T(8,128)S(1)} %copy.26, f32[]{:T(128)} %constant.11.clone.1), kind=kCustom, calls=%fused_computation.31 | custom fusion | flops 45056 | bytes 32772 | tf_op jit(solution)/shard_map/scatter-add | solution.py:130
  55.3 1.9 %collective-permute-start.10 = (f32[1,1,4096]{2,1,0:T(1,128)S(1)}, f32[1,1,4096]{2,1,0:T(1,128)S(1)}, u32[]{:S(2)}, u32[]{:S(2)}) collective-permute-start(f32[1,1,4096]{2,1,0:T(1,128)S(1)} %constant_dynamic-slice_fusion), channel_id=1, source_target_pairs={{0,1},{1,0},{2,3},{3,2},{4,5},{5,4},{6,7},{7,6},{8,9},{9,8},{10,11... | collective-permute-start | bytes 49160 | tf_op jit(solution)/shard_map/ppermute | solution.py:233
  57.3 3.9 %collective-permute-done.7 = f32[1,32896]{1,0:T(1,128)S(1)} collective-permute-done((f32[1,32896]{1,0:T(1,128)S(1)}, f32[1,32896]{1,0:T(1,128)S(1)}, u32[]{:S(2)}, u32[]{:S(2)}) %collective-permute-start.7) | collective-permute-done | bytes 131616 | tf_op jit(solution)/shard_map/ppermute | solution.py:33
  61.3 3.0 %collective-permute-start.8 = (f32[1,32896]{1,0:T(1,128)S(1)}, f32[1,32896]{1,0:T(1,128)S(1)}, u32[]{:S(2)}, u32[]{:S(2)}) collective-permute-start(f32[1,32896]{1,0:T(1,128)S(1)} %add.131), channel_id=1, source_target_pairs={{0,192},{2,194},{4,196},{6,198},{8,200},{10,202},{12,204},{14,206}... | collective-permute-start | bytes 394760 | tf_op jit(solution)/shard_map/ppermute | solution.py:33
  64.4 4.9 %collective-permute-done.8 = f32[1,32896]{1,0:T(1,128)S(1)} collective-permute-done((f32[1,32896]{1,0:T(1,128)S(1)}, f32[1,32896]{1,0:T(1,128)S(1)}, u32[]{:S(2)}, u32[]{:S(2)}) %collective-permute-start.8) | collective-permute-done | bytes 131616 | tf_op jit(solution)/shard_map/ppermute | solution.py:33
  69.8 0.9 %multiply_reduce_fusion = f32[]{:T(128)} fusion(f32[1,32896]{1,0:T(1,128)S(1)} %add.132, f32[1,32768]{1,0:T(1,128)S(1)} %bitcast.76), kind=kLoop, calls=%fused_computation.18 | loop fusion | flops 98303 | bytes 262148 | tf_op jit(solution)/shard_map/reduce_sum | solution.py:211
  70.7 0.7 slice_add_fusion.1
  71.4 1.9 %collective-permute-start.9 = (f32[1,2]{1,0:T(1,128)S(1)}, f32[1,2]{1,0:T(1,128)S(1)}, u32[]{:S(2)}, u32[]{:S(2)}) collective-permute-start(f32[1,2]{1,0:T(1,128)S(1)} %slice_add_fusion.1), channel_id=1, source_target_pairs={{0,1},{1,0},{2,3},{3,2},{4,5},{5,4},{6,7},{7,6},{8,9},{9,8},{10,11... | collective-permute-start | bytes 32 | tf_op jit(solution)/shard_map/ppermute | solution.py:33
  73.3 3.2 %collective-permute-done.9 = f32[1,2]{1,0:T(1,128)S(1)} collective-permute-done((f32[1,2]{1,0:T(1,128)S(1)}, f32[1,2]{1,0:T(1,128)S(1)}, u32[]{:S(2)}, u32[]{:S(2)}) %collective-permute-start.9) | collective-permute-done | bytes 40 | tf_op jit(solution)/shard_map/ppermute | solution.py:33
  78.4 0.8 multiply_subtract_fusion
  (67 shorter events, 5.2 us)
Async XLA Ops:
  0.6 7.4 %copy-start.7 = (s32[32768]{0:T(1024)S(1)}, s32[32768]{0:T(1024)}, u32[]{:S(2)}) copy-start(s32[32768]{0:T(1024)} %param.31) | copy-start | bytes 393220
  1.5 8.7 %collective-permute-start = (f32[1,1,4096]{2,1,0:T(1,128)S(1)}, f32[1,1,4096]{2,1,0:T(1,128)S(1)}, u32[]{:S(2)}, u32[]{:S(2)}) collective-permute-start(f32[1,1,4096]{2,1,0:T(1,128)S(1)} %get-tuple-element.18), channel_id=1, source_target_pairs={{0,1},{1,0},{2,3},{3,2},{4,5},{5,4},{6,7},{7,6},{8,9},{9,8},{10,11... | collective-permute-start | bytes 49160 | tf_op jit(solution)/shard_map/ppermute | solution.py:162
  5.6 1.8 %copy-start.6 = (f32[1,1,2,4096]{3,2,1,0:T(2,128)S(1)}, f32[1,1,2,4096]{3,2,1,0:T(2,128)}, u32[]{:S(2)}) copy-start(f32[1,1,2,4096]{3,2,1,0:T(2,128)} %param.18) | copy-start | bytes 98308
  5.6 2.5 %copy-start.12 = (s32[6144]{0:T(1024)S(1)}, s32[6144]{0:T(1024)}, u32[]{:S(2)}) copy-start(s32[6144]{0:T(1024)} %param.28) | copy-start | bytes 73732
  7.4 0.7 copy-start.11
  8.2 0.7 copy-start.14
  8.2 0.7 copy-start.15
  8.2 0.7 copy-start.16
  12.2 3.5 %copy-start.3 = (f32[1,1,32768]{2,1,0:T(1,128)S(1)}, f32[1,1,32768]{2,1,0:T(1,128)}, u32[]{:S(2)}) copy-start(f32[1,1,32768]{2,1,0:T(1,128)} %param.17) | copy-start | bytes 393220
  12.2 3.5 %copy-start.4 = (f32[1,32768]{1,0:T(1,128)S(1)}, f32[1,32768]{1,0:T(1,128)}, u32[]{:S(2)}) copy-start(f32[1,32768]{1,0:T(1,128)} %param.24) | copy-start | bytes 393220
  12.2 3.5 %copy-start.8 = (f32[1,32768]{1,0:T(1,128)S(1)}, f32[1,32768]{1,0:T(1,128)}, u32[]{:S(2)}) copy-start(f32[1,32768]{1,0:T(1,128)} %param.21) | copy-start | bytes 393220
  14.1 3.5 %copy-start.13 = (f32[1,6144]{1,0:T(1,128)S(1)}, f32[1,6144]{1,0:T(1,128)}, u32[]{:S(2)}) copy-start(f32[1,6144]{1,0:T(1,128)} %param.20) | copy-start | bytes 73732
  14.1 6.2 %collective-permute-start.1 = (f32[1,1,4096]{2,1,0:T(1,128)S(1)}, f32[1,1,4096]{2,1,0:T(1,128)S(1)}, u32[]{:S(2)}, u32[]{:S(2)}) collective-permute-start(f32[1,1,4096]{2,1,0:T(1,128)S(1)} %get-tuple-element.5), channel_id=1, source_target_pairs={{0,254},{2,0},{4,2},{6,4},{8,6},{10,8},{12,10},{14,12},{16,14},{18... | collective-permute-start | bytes 49160 | tf_op jit(solution)/shard_map/ppermute | solution.py:16
  17.5 2.8 %copy-start.5 = (f32[1,1,2,4096]{3,2,1,0:T(2,128)S(1)}, f32[1,1,2,4096]{3,2,1,0:T(2,128)}, u32[]{:S(2)}) copy-start(f32[1,1,2,4096]{3,2,1,0:T(2,128)} %param.16) | copy-start | bytes 98308
  17.6 2.8 %copy-start.9 = (f32[1,2,4096]{2,1,0:T(2,128)S(1)}, f32[1,2,4096]{2,1,0:T(2,128)}, u32[]{:S(2)}) copy-start(f32[1,2,4096]{2,1,0:T(2,128)} %param.22) | copy-start | bytes 98308
  17.6 2.8 %copy-start.10 = (f32[4096]{0:T(1024)S(1)}, f32[4096]{0:T(1024)}, u32[]{:S(2)}) copy-start(f32[4096]{0:T(1024)} %param.25) | copy-start | bytes 49156
  21.9 1.4 %collective-permute-start.2 = (f32[1,32896]{1,0:T(1,128)S(1)}, f32[1,32896]{1,0:T(1,128)S(1)}, u32[]{:S(2)}, u32[]{:S(2)}) collective-permute-start(f32[1,32896]{1,0:T(1,128)S(1)} %pad_maximum_fusion.1), channel_id=1, source_target_pairs={{0,2},{2,0},{4,6},{6,4},{8,10},{10,8},{12,14},{14,12},{16,18},{18,... | collective-permute-start | bytes 394760 | tf_op jit(solution)/shard_map/ppermute | solution.py:33
  23.5 5.6 %collective-permute-start.3 = (f32[1,32896]{1,0:T(1,128)S(1)}, f32[1,32896]{1,0:T(1,128)S(1)}, u32[]{:S(2)}, u32[]{:S(2)}) collective-permute-start(f32[1,32896]{1,0:T(1,128)S(1)} %fusion.11), channel_id=1, source_target_pairs={{0,4},{2,6},{4,0},{6,2},{8,12},{10,14},{12,8},{14,10},{16,20},{18,... | collective-permute-start | bytes 394760 | tf_op jit(solution)/shard_map/ppermute | solution.py:33
  29.3 8.3 %copy-start = (s32[352,128]{1,0:T(8,128)S(1)}, s32[352,128]{1,0:T(8,128)}, u32[]{:S(2)}) copy-start(s32[352,128]{1,0:T(8,128)} %add_bitcast_fusion.index_ref) | copy-start | bytes 540676
  29.3 6.3 %collective-permute-start.4 = (f32[1,32896]{1,0:T(1,128)S(1)}, f32[1,32896]{1,0:T(1,128)S(1)}, u32[]{:S(2)}, u32[]{:S(2)}) collective-permute-start(f32[1,32896]{1,0:T(1,128)S(1)} %add.127), channel_id=1, source_target_pairs={{0,12},{2,14},{4,8},{6,10},{8,4},{10,6},{12,0},{14,2},{16,28},{18,... | collective-permute-start | bytes 394760 | tf_op jit(solution)/shard_map/ppermute | solution.py:33
  35.7 5.1 %collective-permute-start.5 = (f32[1,32896]{1,0:T(1,128)S(1)}, f32[1,32896]{1,0:T(1,128)S(1)}, u32[]{:S(2)}, u32[]{:S(2)}) collective-permute-start(f32[1,32896]{1,0:T(1,128)S(1)} %add.128), channel_id=1, source_target_pairs={{0,16},{2,18},{4,20},{6,22},{8,24},{10,26},{12,28},{14,30},{16,0},... | collective-permute-start | bytes 394760 | tf_op jit(solution)/shard_map/ppermute | solution.py:33
  40.9 14.2 %collective-permute-start.6 = (f32[1,32896]{1,0:T(1,128)S(1)}, f32[1,32896]{1,0:T(1,128)S(1)}, u32[]{:S(2)}, u32[]{:S(2)}) collective-permute-start(f32[1,32896]{1,0:T(1,128)S(1)} %add.129), channel_id=1, source_target_pairs={{0,32},{2,34},{4,36},{6,38},{8,40},{10,42},{12,44},{14,46},{16,48}... | collective-permute-start | bytes 394760 | tf_op jit(solution)/shard_map/ppermute | solution.py:33
  55.2 6.0 %collective-permute-start.7 = (f32[1,32896]{1,0:T(1,128)S(1)}, f32[1,32896]{1,0:T(1,128)S(1)}, u32[]{:S(2)}, u32[]{:S(2)}) collective-permute-start(f32[1,32896]{1,0:T(1,128)S(1)} %add.130), channel_id=1, source_target_pairs={{0,64},{2,66},{4,68},{6,70},{8,72},{10,74},{12,76},{14,78},{16,80}... | collective-permute-start | bytes 394760 | tf_op jit(solution)/shard_map/ppermute | solution.py:33
  55.3 9.0 %collective-permute-start.10 = (f32[1,1,4096]{2,1,0:T(1,128)S(1)}, f32[1,1,4096]{2,1,0:T(1,128)S(1)}, u32[]{:S(2)}, u32[]{:S(2)}) collective-permute-start(f32[1,1,4096]{2,1,0:T(1,128)S(1)} %constant_dynamic-slice_fusion), channel_id=1, source_target_pairs={{0,1},{1,0},{2,3},{3,2},{4,5},{5,4},{6,7},{7,6},{8,9},{9,8},{10,11... | collective-permute-start | bytes 49160 | tf_op jit(solution)/shard_map/ppermute | solution.py:233
  57.3 7.1 %collective-permute-start.11 = (f32[1,1,4096]{2,1,0:T(1,128)S(1)}, f32[1,1,4096]{2,1,0:T(1,128)S(1)}, u32[]{:S(2)}, u32[]{:S(2)}) collective-permute-start(f32[1,1,4096]{2,1,0:T(1,128)S(1)} %get-tuple-element.9), channel_id=1, source_target_pairs={{0,2},{2,4},{4,6},{6,8},{8,10},{10,12},{12,14},{14,16},{16,18},{18... | collective-permute-start | bytes 49160 | tf_op jit(solution)/shard_map/ppermute | solution.py:16
  61.3 8.0 %collective-permute-start.8 = (f32[1,32896]{1,0:T(1,128)S(1)}, f32[1,32896]{1,0:T(1,128)S(1)}, u32[]{:S(2)}, u32[]{:S(2)}) collective-permute-start(f32[1,32896]{1,0:T(1,128)S(1)} %add.131), channel_id=1, source_target_pairs={{0,192},{2,194},{4,196},{6,198},{8,200},{10,202},{12,204},{14,206}... | collective-permute-start | bytes 394760 | tf_op jit(solution)/shard_map/ppermute | solution.py:33
  64.4 5.1 %copy-start.2 = (f32[32768]{0:T(1024)S(1)}, f32[32768]{0:T(1024)}, u32[]{:S(2)}) copy-start(f32[32768]{0:T(1024)} %param.23) | copy-start | bytes 393220
  69.8 8.6 %copy-start.1 = (f32[1,1,32768]{2,1,0:T(1,128)S(1)}, f32[1,1,32768]{2,1,0:T(1,128)}, u32[]{:S(2)}) copy-start(f32[1,1,32768]{2,1,0:T(1,128)} %param.19) | copy-start | bytes 393220
  71.4 5.1 %collective-permute-start.9 = (f32[1,2]{1,0:T(1,128)S(1)}, f32[1,2]{1,0:T(1,128)S(1)}, u32[]{:S(2)}, u32[]{:S(2)}) collective-permute-start(f32[1,2]{1,0:T(1,128)S(1)} %slice_add_fusion.1), channel_id=1, source_target_pairs={{0,1},{1,0},{2,3},{3,2},{4,5},{5,4},{6,7},{7,6},{8,9},{9,8},{10,11... | collective-permute-start | bytes 32 | tf_op jit(solution)/shard_map/ppermute | solution.py:33

commit v12 on v11

--- a/solution.py
+++ b/solution.py
@@ -14,6 +14,10 @@
     count = lax.axis_size(axis)
     pairs = [(source, (source + steps) % count) for source in range(count)]
     return lax.ppermute(value, axis, pairs)
+
+
+def tm_count_is_power(count):
+    return count & (count - 1) == 0
 
 
 def butterfly_masks(count):
@@ -129,6 +133,20 @@
     out = jnp.zeros(lead + (count, BLOCK), values.dtype)
     out = out.at[..., blocks, :].add(within)
     return out.reshape(lead + (-1,))
+
+
+def chain_with_fillers(value, axis, fillers):
+    count = lax.axis_size(axis)
+    state = None
+    for index, mask in enumerate(butterfly_masks(count)):
+        pairs = [(source, source ^ mask) for source in range(count)]
+        if index in fillers:
+            value, state = lax.optimization_barrier((value, state))
+            state = fillers[index](state)
+        value = value + lax.ppermute(value, axis, pairs)
+        if index in fillers:
+            value, state = lax.optimization_barrier((value, state))
+    return value, state
 
 
 def body(
@@ -205,7 +223,27 @@
     packed = jnp.concatenate(
         [partial_sums, jnp.pad(scalars, ((0, 0), (0, BLOCK - 2)))], axis=-1
     )
-    packed = butterfly_sum(packed, "tm")
+    scatter_values = jnp.concatenate([flow_scaled, -flow_scaled, dispatch_scaled], axis=-1)
+    lead = scatter_values.shape[:-1]
+    tiled = scatter_values.reshape(lead + (-1, BLOCK))
+    scatter_index = jnp.broadcast_to(rows.reshape(-1, BLOCK), tiled.shape)
+
+    def within_blocks(state):
+        return lane_scatter(tiled.reshape(-1, BLOCK), scatter_index.reshape(-1, BLOCK))
+
+    def onto_buses(within):
+        out = jnp.zeros(lead + (buses // BLOCK, BLOCK), tiled.dtype)
+        return out.at[..., blocks, :].add(within.reshape(tiled.shape)).reshape(lead + (-1,))
+
+    steps = lax.axis_size("tm").bit_length() - 1
+    if tm_count_is_power(lax.axis_size("tm")) and steps >= 3:
+        first = min(2, steps - 2)
+        packed, bus_terms = chain_with_fillers(
+            packed, "tm", {first: within_blocks, first + 1: onto_buses}
+        )
+    else:
+        packed = butterfly_sum(packed, "tm")
+        bus_terms = onto_buses(within_blocks(None))
     capacity_value = packed[:, :columns]
     capacity_scaled = scale_capacity[None] * capacity_value
     capacity_part = jnp.sum(capacity_scaled * capacity_value, axis=1)
@@ -220,12 +258,6 @@
     sums, image_limit = lax.optimization_barrier((sums, image_limit))
     totals = butterfly_sum(sums, "net")
 
-    bus_terms = scatter_blocks(
-        jnp.concatenate([flow_scaled, -flow_scaled, dispatch_scaled], axis=-1),
-        blocks,
-        rows,
-        buses // BLOCK,
-    )
     if net_count == 2:
         half = buses // 2
         mine = lax.dynamic_slice_in_dim(bus_terms, net_index * half, half, axis=-1)

time: 80.3 us -> 77.7 us (0.968)
  the two profiles are of different devices: /device:TPU:32 before, /device:TPU:6 now
where the time goes in v12:
time: 77.7 us; the launch traced here: 77.2 us
  waiting for transfers between devices  26.8 us (34%)
  starting transfers between devices  17.2 us (22%)
  other arithmetic  16.1 us (21%)
  Pallas kernels  6.34 us (8%)
  between operations  5.53 us (7%)
  local copies, waits for them, and re-layouts  5.2 us (7%)
    ppermute x7, waiting for transfers between devices, chain_with_fillers(): value = value + lax.ppermute(value, axis, pairs)  23.6 us
    ppermute x7, starting transfers between devices, chain_with_fillers(): value = value + lax.ppermute(value, axis, pairs)  9.98 us
    pallas_call x1, Pallas kernels, lane_scatter(): pl.pallas_call(lane_scatter_kernel, out_shape=jax.ShapeDtypeStruct((BLOCK...  4.43 us
    ppermute x1, starting transfers between devices, body(): other = lax.ppermute(balance, 'net', [(0, 1), (1, 0)])  3.28 us
    ppermute x1, waiting for transfers between devices, butterfly_sum(): value = value + lax.ppermute(value, axis, pairs)  3.2 us
    ppermute x1, starting transfers between devices, body(): own_terms = mine + lax.ppermute(theirs, 'net', [(0, 1), (1, 0)])  1.93 us
    pallas_call x1, Pallas kernels, lane_gather(): pl.pallas_call(lane_gather_kernel, out_shape=jax.ShapeDtypeStruct(table.s...  1.91 us
    reduce_sum x1, other arithmetic, body(): jnp.sum(dispatch_scaled * dispatch_value + DAMPING * direction_capacity *...  1.88 us
  transfers between devices with their start and end apart: 12, of which 7 were waited for; matrix products, arithmetic and copies ran while one was open for 15% of the time, Pallas kernels for 6%

profile of v12, /device:TPU:6, one launch (start us, length us, event | category | flops | bytes accessed | tf_op | source)
XLA Modules:
  0.0 77.2 jit_solution(539308753632508861)
XLA Ops:
  0.6 0.9 %fusion.13 = (f32[1,1,1,4096]{3,2,1,0:T(1,128)S(1)}, f32[1,1,4096]{2,1,0:T(1,128)S(1)}, f32[1,1,4096]{2,1,0:T(1,128)S(1)}) fusion(f32[1,1,2,4096]{3,2,1,0:T(2,128)} %param.16), kind=kLoop, calls=%fused_computation.54 | loop fusion | bytes 81920 | tf_op jit(solution)/shard_map/slice | solution.py:176
  1.5 3.3 %collective-permute-start = (f32[1,1,4096]{2,1,0:T(1,128)S(1)}, f32[1,1,4096]{2,1,0:T(1,128)S(1)}, u32[]{:S(2)}, u32[]{:S(2)}) collective-permute-start(f32[1,1,4096]{2,1,0:T(1,128)S(1)} %get-tuple-element.26), channel_id=1, source_target_pairs={{0,1},{1,0},{2,3},{3,2},{4,5},{5,4},{6,7},{7,6},{8,9},{9,8},{10,11... | collective-permute-start | bytes 49160 | tf_op jit(solution)/shard_map/ppermute | solution.py:180
  4.8 0.8 %fusion.9 = s32[352]{0:T(512)S(1)} fusion(s32[256,1]{0,1:T(1,128)} %bitcast.88, s32[48,1]{0,1:T(1,128)} %bitcast.89, s32[48,1]{0,1:T(1,128)} %bitcast.90), kind=kLoop, calls=%fused_computation.44 | loop fusion | flops 1760 | bytes 2816 | tf_op jit(solution)/shard_map/jit(_take)/jit(_where)/select_n | solution.py:121
  5.6 1.8 %multiply_reduce_fusion.1 = f32[]{:T(128)} fusion(f32[1,1,32768]{2,1,0:T(1,128)} %param.19), kind=kLoop, calls=%fused_computation.19 | loop fusion | flops 65535 | bytes 131076 | tf_op jit(solution)/shard_map/reduce_sum | solution.py:204
  8.2 0.7 add_bitcast_fusion.index_ref
  10.3 1.1 %gather_fusion = f32[352,128]{1,0:T(8,128)S(1)} fusion(f32[64,128]{1,0:T(8,128)S(1)} %fusion.5, s32[1024]{0:T(1024)S(1)} %pad_clamp_fusion), kind=kCustom, calls=%fused_computation | custom fusion | bytes 361856 | tf_op jit(solution)/shard_map/jit(_take)/gather | solution.py:121
  11.4 0.8 %broadcast_select_fusion.table_ref = f32[352,128]{1,0:T(8,128)} fusion(f32[352,128]{1,0:T(8,128)S(1)} %gather_fusion, pred[352]{0:T(512)(128)(4,1)S(1)} %compare_and_fusion), kind=kLoop, calls=%fused_computation.21 | loop fusion | flops 45056 | bytes 360800 | tf_op jit(solution)/shard_map/jit(_take)/select_n | solution.py:121
  12.2 1.9 %shard_map.167 = f32[352,128]{1,0:T(8,128)} custom-call(f32[352,128]{1,0:T(8,128)} %broadcast_select_fusion.table_ref, s32[352,128]{1,0:T(8,128)} %add_bitcast_fusion.index_ref), custom_call_target="tpu_custom_call" | custom-call | tf_op jit(solution)/shard_map/pallas_call | solution.py:71
  14.1 0.8 %fusion.12 = (f32[1,1,6144]{2,1,0:T(1,128)S(1)}, f32[1,1,6144]{2,1,0:T(1,128)S(1)}) fusion(f32[1,1,45056]{2,1,0:T(1,128)} %bitcast.75, f32[1,6144]{1,0:T(1,128)S(1)} %copy-done.14), kind=kLoop, calls=%fused_computation.53 | loop fusion | flops 18432 | bytes 122880 | tf_op jit(solution)/shard_map/neg | solution.py:226
  15.0 1.9 %fusion.4 = (f32[]{:T(128)}, f32[1,1,32768]{2,1,0:T(1,128)S(1)}, f32[1,32768]{1,0:T(1,128)S(1)}) fusion(f32[1,1,32768]{2,1,0:T(1,128)S(1)} %copy-done.4, f32[1,1,45056]{2,1,0:T(1,128)} %bitcast.76, f32[1,32768]{1,0:T(1,128)S(1)} %copy-done.9, f32[1,32768]{1,0:T(1,128)S(1)} %copy-done.5), kind=kLoop, calls=%fused_computation.20 | loop fusion | flops 294911 | bytes 786436 | tf_op jit(solution)/shard_map/reduce_sum | solution.py:210
  16.9 1.4 %multiply_reduce_fusion.3 = f32[]{:T(128)} fusion(f32[1,1,6144]{2,1,0:T(1,128)S(1)} %get-tuple-element.17, f32[1,1,45056]{2,1,0:T(1,128)} %bitcast.77), kind=kLoop, calls=%fused_computation.30 | loop fusion | flops 18431 | bytes 73732 | tf_op jit(solution)/shard_map/reduce_sum | solution.py:209
  19.7 0.7 add_reduce_fusion
  21.8 1.0 %collective-permute-done.2 = f32[1,32896]{1,0:T(1,128)S(1)} collective-permute-done((f32[1,32896]{1,0:T(1,128)S(1)}, f32[1,32896]{1,0:T(1,128)S(1)}, u32[]{:S(2)}, u32[]{:S(2)}) %collective-permute-start.2) | collective-permute-done | bytes 131616 | tf_op jit(solution)/shard_map/ppermute | solution.py:146
  23.0 0.9 %collective-permute-start.3 = (f32[1,32896]{1,0:T(1,128)S(1)}, f32[1,32896]{1,0:T(1,128)S(1)}, u32[]{:S(2)}, u32[]{:S(2)}) collective-permute-start(f32[1,32896]{1,0:T(1,128)S(1)} %fusion.11), channel_id=1, source_target_pairs={{0,4},{2,6},{4,0},{6,2},{8,12},{10,14},{12,8},{14,10},{16,20},{18,... | collective-permute-start | bytes 394760 | tf_op jit(solution)/shard_map/ppermute | solution.py:146
  24.0 0.7 pad_bitcast_fusion.index_ref
  24.7 4.1 %collective-permute-done.3 = f32[1,32896]{1,0:T(1,128)S(1)} collective-permute-done((f32[1,32896]{1,0:T(1,128)S(1)}, f32[1,32896]{1,0:T(1,128)S(1)}, u32[]{:S(2)}, u32[]{:S(2)}) %collective-permute-start.3) | collective-permute-done | bytes 131616 | tf_op jit(solution)/shard_map/ppermute | solution.py:146
  29.0 7.5 %collective-permute-start.4 = (f32[1,32896]{1,0:T(1,128)S(1)}, f32[1,32896]{1,0:T(1,128)S(1)}, u32[]{:S(2)}, u32[]{:S(2)}) collective-permute-start(f32[1,32896]{1,0:T(1,128)S(1)} %add.127), channel_id=1, source_target_pairs={{0,12},{2,14},{4,8},{6,10},{8,4},{10,6},{12,0},{14,2},{16,28},{18,... | collective-permute-start | bytes 394760 | tf_op jit(solution)/shard_map/ppermute | solution.py:146
  36.8 0.7 pad_bitcast_fusion.1.value_ref
  37.5 4.4 %shard_map.168 = f32[128,384]{1,0:T(8,128)} custom-call(f32[128,384]{1,0:T(8,128)} %pad_bitcast_fusion.1.value_ref, s32[128,384]{1,0:T(8,128)} %pad_bitcast_fusion.index_ref), custom_call_target="tpu_custom_call" | custom-call | tf_op jit(solution)/shard_map/pallas_call | solution.py:111
  42.1 0.7 copy-done.1
  42.9 1.8 %scatter_custom_fusion = f32[64,128]{1,0:T(8,128)S(1)} fusion(s32[352]{0:T(512)S(1)} %fusion.9, f32[352,128]{1,0:T(8,128)S(1)} %copy.26, f32[]{:T(128)} %constant.11.clone.1), kind=kCustom, calls=%fused_computation.31 | custom fusion | flops 45056 | bytes 32772 | tf_op jit(solution)/shard_map/scatter-add | solution.py:236
  44.7 2.4 %collective-permute-done.5 = f32[1,32896]{1,0:T(1,128)S(1)} collective-permute-done((f32[1,32896]{1,0:T(1,128)S(1)}, f32[1,32896]{1,0:T(1,128)S(1)}, u32[]{:S(2)}, u32[]{:S(2)}) %collective-permute-start.5) | collective-permute-done | bytes 131616 | tf_op jit(solution)/shard_map/ppermute | solution.py:146
  47.4 4.9 %collective-permute-done.6 = f32[1,32896]{1,0:T(1,128)S(1)} collective-permute-done((f32[1,32896]{1,0:T(1,128)S(1)}, f32[1,32896]{1,0:T(1,128)S(1)}, u32[]{:S(2)}, u32[]{:S(2)}) %collective-permute-start.6) | collective-permute-done | bytes 131616 | tf_op jit(solution)/shard_map/ppermute | solution.py:146
  52.6 1.9 %collective-permute-start.10 = (f32[1,1,4096]{2,1,0:T(1,128)S(1)}, f32[1,1,4096]{2,1,0:T(1,128)S(1)}, u32[]{:S(2)}, u32[]{:S(2)}) collective-permute-start(f32[1,1,4096]{2,1,0:T(1,128)S(1)} %constant_dynamic-slice_fusion), channel_id=1, source_target_pairs={{0,1},{1,0},{2,3},{3,2},{4,5},{5,4},{6,7},{7,6},{8,9},{9,8},{10,11... | collective-permute-start | bytes 49160 | tf_op jit(solution)/shard_map/ppermute | solution.py:265
  54.5 4.9 %collective-permute-done.7 = f32[1,32896]{1,0:T(1,128)S(1)} collective-permute-done((f32[1,32896]{1,0:T(1,128)S(1)}, f32[1,32896]{1,0:T(1,128)S(1)}, u32[]{:S(2)}, u32[]{:S(2)}) %collective-permute-start.7) | collective-permute-done | bytes 131616 | tf_op jit(solution)/shard_map/ppermute | solution.py:146
  59.5 0.7 collective-permute-start.8
  60.3 6.4 %collective-permute-done.8 = f32[1,32896]{1,0:T(1,128)S(1)} collective-permute-done((f32[1,32896]{1,0:T(1,128)S(1)}, f32[1,32896]{1,0:T(1,128)S(1)}, u32[]{:S(2)}, u32[]{:S(2)}) %collective-permute-start.8) | collective-permute-done | bytes 131616 | tf_op jit(solution)/shard_map/ppermute | solution.py:146
  67.2 0.9 %multiply_reduce_fusion = f32[]{:T(128)} fusion(f32[1,32896]{1,0:T(1,128)S(1)} %add.132, f32[1,32768]{1,0:T(1,128)S(1)} %bitcast.81), kind=kLoop, calls=%fused_computation.18 | loop fusion | flops 98303 | bytes 262148 | tf_op jit(solution)/shard_map/reduce_sum | solution.py:249
  68.0 0.7 slice_add_fusion.1
  68.8 1.9 %collective-permute-start.9 = (f32[1,2]{1,0:T(1,128)S(1)}, f32[1,2]{1,0:T(1,128)S(1)}, u32[]{:S(2)}, u32[]{:S(2)}) collective-permute-start(f32[1,2]{1,0:T(1,128)S(1)} %slice_add_fusion.1), channel_id=1, source_target_pairs={{0,1},{1,0},{2,3},{3,2},{4,5},{5,4},{6,7},{7,6},{8,9},{9,8},{10,11... | collective-permute-start | bytes 32 | tf_op jit(solution)/shard_map/ppermute | solution.py:37
  70.6 3.2 %collective-permute-done.9 = f32[1,2]{1,0:T(1,128)S(1)} collective-permute-done((f32[1,2]{1,0:T(1,128)S(1)}, f32[1,2]{1,0:T(1,128)S(1)}, u32[]{:S(2)}, u32[]{:S(2)}) %collective-permute-start.9) | collective-permute-done | bytes 40 | tf_op jit(solution)/shard_map/ppermute | solution.py:37
  75.8 0.8 %multiply_subtract_fusion = f32[1,1,32768]{2,1,0:T(1,128)} fusion(f32[1,1,32768]{2,1,0:T(1,128)S(1)} %copy-done.2, f32[1,1,32768]{2,1,0:T(1,128)S(1)} %multiply_add_fusion, f32[]{:T(128)} %bitcast.25), kind=kLoop, calls=%fused_computation.17 | loop fusion | flops 65536 | bytes 393220 | tf_op jit(solution)/shard_map/sub | solution.py:275
  (69 shorter events, 5.3 us)
Async XLA Ops:
  0.6 7.4 %copy-start.8 = (s32[32768]{0:T(1024)S(1)}, s32[32768]{0:T(1024)}, u32[]{:S(2)}) copy-start(s32[32768]{0:T(1024)} %param.31) | copy-start | bytes 393220
  1.5 8.7 %collective-permute-start = (f32[1,1,4096]{2,1,0:T(1,128)S(1)}, f32[1,1,4096]{2,1,0:T(1,128)S(1)}, u32[]{:S(2)}, u32[]{:S(2)}) collective-permute-start(f32[1,1,4096]{2,1,0:T(1,128)S(1)} %get-tuple-element.26), channel_id=1, source_target_pairs={{0,1},{1,0},{2,3},{3,2},{4,5},{5,4},{6,7},{7,6},{8,9},{9,8},{10,11... | collective-permute-start | bytes 49160 | tf_op jit(solution)/shard_map/ppermute | solution.py:180
  5.6 1.8 %copy-start.7 = (f32[1,1,2,4096]{3,2,1,0:T(2,128)S(1)}, f32[1,1,2,4096]{3,2,1,0:T(2,128)}, u32[]{:S(2)}) copy-start(f32[1,1,2,4096]{3,2,1,0:T(2,128)} %param.18) | copy-start | bytes 98308
  5.6 2.5 %copy-start.13 = (s32[6144]{0:T(1024)S(1)}, s32[6144]{0:T(1024)}, u32[]{:S(2)}) copy-start(s32[6144]{0:T(1024)} %param.28) | copy-start | bytes 73732
  7.4 0.7 copy-start.12
  8.2 0.7 copy-start.15
  8.2 0.7 copy-start.16
  8.2 0.7 copy-start.17
  12.2 1.9 %copy-start.14 = (f32[1,6144]{1,0:T(1,128)S(1)}, f32[1,6144]{1,0:T(1,128)}, u32[]{:S(2)}) copy-start(f32[1,6144]{1,0:T(1,128)} %param.20) | copy-start | bytes 73732
  12.2 2.8 %copy-start.4 = (f32[1,1,32768]{2,1,0:T(1,128)S(1)}, f32[1,1,32768]{2,1,0:T(1,128)}, u32[]{:S(2)}) copy-start(f32[1,1,32768]{2,1,0:T(1,128)} %param.17) | copy-start | bytes 393220
  12.2 2.8 %copy-start.5 = (f32[1,32768]{1,0:T(1,128)S(1)}, f32[1,32768]{1,0:T(1,128)}, u32[]{:S(2)}) copy-start(f32[1,32768]{1,0:T(1,128)} %param.24) | copy-start | bytes 393220
  12.2 2.8 %copy-start.9 = (f32[1,32768]{1,0:T(1,128)S(1)}, f32[1,32768]{1,0:T(1,128)}, u32[]{:S(2)}) copy-start(f32[1,32768]{1,0:T(1,128)} %param.21) | copy-start | bytes 393220
  14.9 4.7 %collective-permute-start.1 = (f32[1,1,4096]{2,1,0:T(1,128)S(1)}, f32[1,1,4096]{2,1,0:T(1,128)S(1)}, u32[]{:S(2)}, u32[]{:S(2)}) collective-permute-start(f32[1,1,4096]{2,1,0:T(1,128)S(1)} %get-tuple-element.9), channel_id=1, source_target_pairs={{0,254},{2,0},{4,2},{6,4},{8,6},{10,8},{12,10},{14,12},{16,14},{18... | collective-permute-start | bytes 49160 | tf_op jit(solution)/shard_map/ppermute | solution.py:16
  15.0 4.6 %copy-start.11 = (f32[4096]{0:T(1024)S(1)}, f32[4096]{0:T(1024)}, u32[]{:S(2)}) copy-start(f32[4096]{0:T(1024)} %param.25) | copy-start | bytes 49156
  16.9 2.7 %copy-start.6 = (f32[1,1,2,4096]{3,2,1,0:T(2,128)S(1)}, f32[1,1,2,4096]{3,2,1,0:T(2,128)}, u32[]{:S(2)}) copy-start(f32[1,1,2,4096]{3,2,1,0:T(2,128)} %param.16) | copy-start | bytes 98308
  16.9 2.8 %copy-start.10 = (f32[1,2,4096]{2,1,0:T(2,128)S(1)}, f32[1,2,4096]{2,1,0:T(2,128)}, u32[]{:S(2)}) copy-start(f32[1,2,4096]{2,1,0:T(2,128)} %param.22) | copy-start | bytes 98308
  21.2 2.7 %copy-start = (s32[352,128]{1,0:T(8,128)S(1)}, s32[352,128]{1,0:T(8,128)}, u32[]{:S(2)}) copy-start(s32[352,128]{1,0:T(8,128)} %add_bitcast_fusion.index_ref) | copy-start | bytes 540676
  21.2 1.5 %collective-permute-start.2 = (f32[1,32896]{1,0:T(1,128)S(1)}, f32[1,32896]{1,0:T(1,128)S(1)}, u32[]{:S(2)}, u32[]{:S(2)}) collective-permute-start(f32[1,32896]{1,0:T(1,128)S(1)} %pad_maximum_fusion.1), channel_id=1, source_target_pairs={{0,2},{2,0},{4,6},{6,4},{8,10},{10,8},{12,14},{14,12},{16,18},{18,... | collective-permute-start | bytes 394760 | tf_op jit(solution)/shard_map/ppermute | solution.py:146
  23.0 5.9 %collective-permute-start.3 = (f32[1,32896]{1,0:T(1,128)S(1)}, f32[1,32896]{1,0:T(1,128)S(1)}, u32[]{:S(2)}, u32[]{:S(2)}) collective-permute-start(f32[1,32896]{1,0:T(1,128)S(1)} %fusion.11), channel_id=1, source_target_pairs={{0,4},{2,6},{4,0},{6,2},{8,12},{10,14},{12,8},{14,10},{16,20},{18,... | collective-permute-start | bytes 394760 | tf_op jit(solution)/shard_map/ppermute | solution.py:146
  29.0 12.9 %collective-permute-start.4 = (f32[1,32896]{1,0:T(1,128)S(1)}, f32[1,32896]{1,0:T(1,128)S(1)}, u32[]{:S(2)}, u32[]{:S(2)}) collective-permute-start(f32[1,32896]{1,0:T(1,128)S(1)} %add.127), channel_id=1, source_target_pairs={{0,12},{2,14},{4,8},{6,10},{8,4},{10,6},{12,0},{14,2},{16,28},{18,... | collective-permute-start | bytes 394760 | tf_op jit(solution)/shard_map/ppermute | solution.py:146
  41.9 0.9 %copy-start.1 = (f32[128,384]{1,0:T(8,128)S(1)}, f32[128,384]{1,0:T(8,128)}, u32[]{:S(2)}) copy-start(f32[128,384]{1,0:T(8,128)} %shard_map.168) | copy-start | bytes 589828
  42.0 5.1 %collective-permute-start.5 = (f32[1,32896]{1,0:T(1,128)S(1)}, f32[1,32896]{1,0:T(1,128)S(1)}, u32[]{:S(2)}, u32[]{:S(2)}) collective-permute-start(f32[1,32896]{1,0:T(1,128)S(1)} %add.128), channel_id=1, source_target_pairs={{0,16},{2,18},{4,20},{6,22},{8,24},{10,26},{12,28},{14,30},{16,0},... | collective-permute-start | bytes 394760 | tf_op jit(solution)/shard_map/ppermute | solution.py:146
  47.2 5.1 %collective-permute-start.6 = (f32[1,32896]{1,0:T(1,128)S(1)}, f32[1,32896]{1,0:T(1,128)S(1)}, u32[]{:S(2)}, u32[]{:S(2)}) collective-permute-start(f32[1,32896]{1,0:T(1,128)S(1)} %add.129), channel_id=1, source_target_pairs={{0,32},{2,34},{4,36},{6,38},{8,40},{10,42},{12,44},{14,46},{16,48}... | collective-permute-start | bytes 394760 | tf_op jit(solution)/shard_map/ppermute | solution.py:146
  47.4 12.8 %collective-permute-start.11 = (f32[1,1,4096]{2,1,0:T(1,128)S(1)}, f32[1,1,4096]{2,1,0:T(1,128)S(1)}, u32[]{:S(2)}, u32[]{:S(2)}) collective-permute-start(f32[1,1,4096]{2,1,0:T(1,128)S(1)} %get-tuple-element.19), channel_id=1, source_target_pairs={{0,2},{2,4},{4,6},{6,8},{8,10},{10,12},{12,14},{14,16},{16,18},{18... | collective-permute-start | bytes 49160 | tf_op jit(solution)/shard_map/ppermute | solution.py:16
  52.4 6.9 %collective-permute-start.7 = (f32[1,32896]{1,0:T(1,128)S(1)}, f32[1,32896]{1,0:T(1,128)S(1)}, u32[]{:S(2)}, u32[]{:S(2)}) collective-permute-start(f32[1,32896]{1,0:T(1,128)S(1)} %add.130), channel_id=1, source_target_pairs={{0,64},{2,66},{4,68},{6,70},{8,72},{10,74},{12,76},{14,78},{16,80}... | collective-permute-start | bytes 394760 | tf_op jit(solution)/shard_map/ppermute | solution.py:146
  52.6 7.6 %collective-permute-start.10 = (f32[1,1,4096]{2,1,0:T(1,128)S(1)}, f32[1,1,4096]{2,1,0:T(1,128)S(1)}, u32[]{:S(2)}, u32[]{:S(2)}) collective-permute-start(f32[1,1,4096]{2,1,0:T(1,128)S(1)} %constant_dynamic-slice_fusion), channel_id=1, source_target_pairs={{0,1},{1,0},{2,3},{3,2},{4,5},{5,4},{6,7},{7,6},{8,9},{9,8},{10,11... | collective-permute-start | bytes 49160 | tf_op jit(solution)/shard_map/ppermute | solution.py:265
  59.5 7.2 %collective-permute-start.8 = (f32[1,32896]{1,0:T(1,128)S(1)}, f32[1,32896]{1,0:T(1,128)S(1)}, u32[]{:S(2)}, u32[]{:S(2)}) collective-permute-start(f32[1,32896]{1,0:T(1,128)S(1)} %add.131), channel_id=1, source_target_pairs={{0,192},{2,194},{4,196},{6,198},{8,200},{10,202},{12,204},{14,206}... | collective-permute-start | bytes 394760 | tf_op jit(solution)/shard_map/ppermute | solution.py:146
  60.3 6.5 %copy-start.3 = (f32[32768]{0:T(1024)S(1)}, f32[32768]{0:T(1024)}, u32[]{:S(2)}) copy-start(f32[32768]{0:T(1024)} %param.23) | copy-start | bytes 393220
  67.1 8.6 %copy-start.2 = (f32[1,1,32768]{2,1,0:T(1,128)S(1)}, f32[1,1,32768]{2,1,0:T(1,128)}, u32[]{:S(2)}) copy-start(f32[1,1,32768]{2,1,0:T(1,128)} %param.19) | copy-start | bytes 393220
  68.8 5.1 %collective-permute-start.9 = (f32[1,2]{1,0:T(1,128)S(1)}, f32[1,2]{1,0:T(1,128)S(1)}, u32[]{:S(2)}, u32[]{:S(2)}) collective-permute-start(f32[1,2]{1,0:T(1,128)S(1)} %slice_add_fusion.1), channel_id=1, source_target_pairs={{0,1},{1,0},{2,3},{3,2},{4,5},{5,4},{6,7},{7,6},{8,9},{9,8},{10,11... | collective-permute-start | bytes 32 | tf_op jit(solution)/shard_map/ppermute | solution.py:37

commit v13 on v12

--- a/solution.py
+++ b/solution.py
@@ -201,8 +201,10 @@
     dispatch_scaled = scale_dispatch[None] * dispatch_value
     level_scaled = scale_storage[None, :, 0, :] * level_value
     charge_scaled = scale_storage[None, :, 1, :] * charge_value
-    squares_local = jnp.sum(residual_nodal * residual_nodal, axis=(1, 2, 3)) + jnp.sum(
-        residual_capacity * residual_capacity, axis=(1, 2)
+    nodal_rows = residual_nodal.reshape(residual_nodal.shape[0], -1, BLOCK)
+    capacity_rows = residual_capacity.reshape(residual_capacity.shape[0], -1, BLOCK)
+    squares_local = jnp.sum(nodal_rows * nodal_rows, axis=(1, 2)) + jnp.sum(
+        capacity_rows * capacity_rows, axis=(1, 2)
     )
 
     curvature_local = (

time: 77.7 us -> 77.7 us (level)
  no operation moved by 1% of the time
where the time goes in v13:
time: 77.7 us; the launch traced here: 77.2 us
  waiting for transfers between devices  26.8 us (34%)
  starting transfers between devices  17.2 us (22%)
  other arithmetic  16.1 us (21%)
  Pallas kernels  6.34 us (8%)
  between operations  5.53 us (7%)
  local copies, waits for them, and re-layouts  5.2 us (7%)
    ppermute x7, waiting for transfers between devices, chain_with_fillers(): value = value + lax.ppermute(value, axis, pairs)  23.6 us
    ppermute x7, starting transfers between devices, chain_with_fillers(): value = value + lax.ppermute(value, axis, pairs)  9.98 us
    pallas_call x1, Pallas kernels, lane_scatter(): pl.pallas_call(lane_scatter_kernel, out_shape=jax.ShapeDtypeStruct((BLOCK...  4.43 us
    ppermute x1, starting transfers between devices, body(): other = lax.ppermute(balance, 'net', [(0, 1), (1, 0)])  3.28 us
    ppermute x1, waiting for transfers between devices, butterfly_sum(): value = value + lax.ppermute(value, axis, pairs)  3.2 us
    ppermute x1, starting transfers between devices, body(): own_terms = mine + lax.ppermute(theirs, 'net', [(0, 1), (1, 0)])  1.93 us
    pallas_call x1, Pallas kernels, lane_gather(): pl.pallas_call(lane_gather_kernel, out_shape=jax.ShapeDtypeStruct(table.s...  1.91 us
    reduce_sum x1, other arithmetic, body(): jnp.sum(dispatch_scaled * dispatch_value + DAMPING * direction_capacity *...  1.88 us
  transfers between devices with their start and end apart: 12, of which 7 were waited for; matrix products, arithmetic and copies ran while one was open for 15% of the time, Pallas kernels for 6%

profile of v13, /device:TPU:6, one launch (start us, length us, event | category | flops | bytes accessed | tf_op | source)
XLA Modules:
  0.0 77.2 jit_solution(539308753632508861)
XLA Ops:
  0.6 0.9 %fusion.13 = (f32[1,1,1,4096]{3,2,1,0:T(1,128)S(1)}, f32[1,1,4096]{2,1,0:T(1,128)S(1)}, f32[1,1,4096]{2,1,0:T(1,128)S(1)}) fusion(f32[1,1,2,4096]{3,2,1,0:T(2,128)} %param.16), kind=kLoop, calls=%fused_computation.54 | loop fusion | bytes 81920 | tf_op jit(solution)/shard_map/slice | solution.py:176
  1.5 3.3 %collective-permute-start = (f32[1,1,4096]{2,1,0:T(1,128)S(1)}, f32[1,1,4096]{2,1,0:T(1,128)S(1)}, u32[]{:S(2)}, u32[]{:S(2)}) collective-permute-start(f32[1,1,4096]{2,1,0:T(1,128)S(1)} %get-tuple-element.26), channel_id=1, source_target_pairs={{0,1},{1,0},{2,3},{3,2},{4,5},{5,4},{6,7},{7,6},{8,9},{9,8},{10,11... | collective-permute-start | bytes 49160 | tf_op jit(solution)/shard_map/ppermute | solution.py:180
  4.8 0.8 %fusion.9 = s32[352]{0:T(512)S(1)} fusion(s32[256,1]{0,1:T(1,128)} %bitcast.88, s32[48,1]{0,1:T(1,128)} %bitcast.89, s32[48,1]{0,1:T(1,128)} %bitcast.90), kind=kLoop, calls=%fused_computation.44 | loop fusion | flops 1760 | bytes 2816 | tf_op jit(solution)/shard_map/jit(_take)/jit(_where)/select_n | solution.py:121
  5.6 1.8 %multiply_reduce_fusion.1 = f32[]{:T(128)} fusion(f32[1,1,32768]{2,1,0:T(1,128)} %param.19), kind=kLoop, calls=%fused_computation.19 | loop fusion | flops 65535 | bytes 131076 | tf_op jit(solution)/shard_map/reduce_sum | solution.py:206
  8.2 0.7 add_bitcast_fusion.index_ref
  10.3 1.1 %gather_fusion = f32[352,128]{1,0:T(8,128)S(1)} fusion(f32[64,128]{1,0:T(8,128)S(1)} %fusion.5, s32[1024]{0:T(1024)S(1)} %pad_clamp_fusion), kind=kCustom, calls=%fused_computation | custom fusion | bytes 361856 | tf_op jit(solution)/shard_map/jit(_take)/gather | solution.py:121
  11.4 0.8 %broadcast_select_fusion.table_ref = f32[352,128]{1,0:T(8,128)} fusion(f32[352,128]{1,0:T(8,128)S(1)} %gather_fusion, pred[352]{0:T(512)(128)(4,1)S(1)} %compare_and_fusion), kind=kLoop, calls=%fused_computation.21 | loop fusion | flops 45056 | bytes 360800 | tf_op jit(solution)/shard_map/jit(_take)/select_n | solution.py:121
  12.2 1.9 %shard_map.167 = f32[352,128]{1,0:T(8,128)} custom-call(f32[352,128]{1,0:T(8,128)} %broadcast_select_fusion.table_ref, s32[352,128]{1,0:T(8,128)} %add_bitcast_fusion.index_ref), custom_call_target="tpu_custom_call" | custom-call | tf_op jit(solution)/shard_map/pallas_call | solution.py:71
  14.1 0.8 %fusion.12 = (f32[1,1,6144]{2,1,0:T(1,128)S(1)}, f32[1,1,6144]{2,1,0:T(1,128)S(1)}) fusion(f32[1,1,45056]{2,1,0:T(1,128)} %bitcast.75, f32[1,6144]{1,0:T(1,128)S(1)} %copy-done.14), kind=kLoop, calls=%fused_computation.53 | loop fusion | flops 18432 | bytes 122880 | tf_op jit(solution)/shard_map/neg | solution.py:228
  15.0 1.9 %fusion.4 = (f32[]{:T(128)}, f32[1,1,32768]{2,1,0:T(1,128)S(1)}, f32[1,32768]{1,0:T(1,128)S(1)}) fusion(f32[1,1,32768]{2,1,0:T(1,128)S(1)} %copy-done.4, f32[1,1,45056]{2,1,0:T(1,128)} %bitcast.76, f32[1,32768]{1,0:T(1,128)S(1)} %copy-done.9, f32[1,32768]{1,0:T(1,128)S(1)} %copy-done.5), kind=kLoop, calls=%fused_computation.20 | loop fusion | flops 294911 | bytes 786436 | tf_op jit(solution)/shard_map/reduce_sum | solution.py:212
  16.9 1.4 %multiply_reduce_fusion.3 = f32[]{:T(128)} fusion(f32[1,1,6144]{2,1,0:T(1,128)S(1)} %get-tuple-element.17, f32[1,1,45056]{2,1,0:T(1,128)} %bitcast.77), kind=kLoop, calls=%fused_computation.30 | loop fusion | flops 18431 | bytes 73732 | tf_op jit(solution)/shard_map/reduce_sum | solution.py:211
  19.7 0.7 add_reduce_fusion
  21.8 1.0 %collective-permute-done.2 = f32[1,32896]{1,0:T(1,128)S(1)} collective-permute-done((f32[1,32896]{1,0:T(1,128)S(1)}, f32[1,32896]{1,0:T(1,128)S(1)}, u32[]{:S(2)}, u32[]{:S(2)}) %collective-permute-start.2) | collective-permute-done | bytes 131616 | tf_op jit(solution)/shard_map/ppermute | solution.py:146
  23.0 0.9 %collective-permute-start.3 = (f32[1,32896]{1,0:T(1,128)S(1)}, f32[1,32896]{1,0:T(1,128)S(1)}, u32[]{:S(2)}, u32[]{:S(2)}) collective-permute-start(f32[1,32896]{1,0:T(1,128)S(1)} %fusion.11), channel_id=1, source_target_pairs={{0,4},{2,6},{4,0},{6,2},{8,12},{10,14},{12,8},{14,10},{16,20},{18,... | collective-permute-start | bytes 394760 | tf_op jit(solution)/shard_map/ppermute | solution.py:146
  24.0 0.7 pad_bitcast_fusion.index_ref
  24.7 4.1 %collective-permute-done.3 = f32[1,32896]{1,0:T(1,128)S(1)} collective-permute-done((f32[1,32896]{1,0:T(1,128)S(1)}, f32[1,32896]{1,0:T(1,128)S(1)}, u32[]{:S(2)}, u32[]{:S(2)}) %collective-permute-start.3) | collective-permute-done | bytes 131616 | tf_op jit(solution)/shard_map/ppermute | solution.py:146
  29.0 7.5 %collective-permute-start.4 = (f32[1,32896]{1,0:T(1,128)S(1)}, f32[1,32896]{1,0:T(1,128)S(1)}, u32[]{:S(2)}, u32[]{:S(2)}) collective-permute-start(f32[1,32896]{1,0:T(1,128)S(1)} %add.127), channel_id=1, source_target_pairs={{0,12},{2,14},{4,8},{6,10},{8,4},{10,6},{12,0},{14,2},{16,28},{18,... | collective-permute-start | bytes 394760 | tf_op jit(solution)/shard_map/ppermute | solution.py:146
  36.8 0.7 pad_bitcast_fusion.1.value_ref
  37.5 4.4 %shard_map.168 = f32[128,384]{1,0:T(8,128)} custom-call(f32[128,384]{1,0:T(8,128)} %pad_bitcast_fusion.1.value_ref, s32[128,384]{1,0:T(8,128)} %pad_bitcast_fusion.index_ref), custom_call_target="tpu_custom_call" | custom-call | tf_op jit(solution)/shard_map/pallas_call | solution.py:111
  42.1 0.7 copy-done.1
  42.9 1.8 %scatter_custom_fusion = f32[64,128]{1,0:T(8,128)S(1)} fusion(s32[352]{0:T(512)S(1)} %fusion.9, f32[352,128]{1,0:T(8,128)S(1)} %copy.26, f32[]{:T(128)} %constant.11.clone.1), kind=kCustom, calls=%fused_computation.31 | custom fusion | flops 45056 | bytes 32772 | tf_op jit(solution)/shard_map/scatter-add | solution.py:238
  44.7 2.4 %collective-permute-done.5 = f32[1,32896]{1,0:T(1,128)S(1)} collective-permute-done((f32[1,32896]{1,0:T(1,128)S(1)}, f32[1,32896]{1,0:T(1,128)S(1)}, u32[]{:S(2)}, u32[]{:S(2)}) %collective-permute-start.5) | collective-permute-done | bytes 131616 | tf_op jit(solution)/shard_map/ppermute | solution.py:146
  47.4 4.9 %collective-permute-done.6 = f32[1,32896]{1,0:T(1,128)S(1)} collective-permute-done((f32[1,32896]{1,0:T(1,128)S(1)}, f32[1,32896]{1,0:T(1,128)S(1)}, u32[]{:S(2)}, u32[]{:S(2)}) %collective-permute-start.6) | collective-permute-done | bytes 131616 | tf_op jit(solution)/shard_map/ppermute | solution.py:146
  52.6 1.9 %collective-permute-start.10 = (f32[1,1,4096]{2,1,0:T(1,128)S(1)}, f32[1,1,4096]{2,1,0:T(1,128)S(1)}, u32[]{:S(2)}, u32[]{:S(2)}) collective-permute-start(f32[1,1,4096]{2,1,0:T(1,128)S(1)} %constant_dynamic-slice_fusion), channel_id=1, source_target_pairs={{0,1},{1,0},{2,3},{3,2},{4,5},{5,4},{6,7},{7,6},{8,9},{9,8},{10,11... | collective-permute-start | bytes 49160 | tf_op jit(solution)/shard_map/ppermute | solution.py:267
  54.5 4.9 %collective-permute-done.7 = f32[1,32896]{1,0:T(1,128)S(1)} collective-permute-done((f32[1,32896]{1,0:T(1,128)S(1)}, f32[1,32896]{1,0:T(1,128)S(1)}, u32[]{:S(2)}, u32[]{:S(2)}) %collective-permute-start.7) | collective-permute-done | bytes 131616 | tf_op jit(solution)/shard_map/ppermute | solution.py:146
  59.5 0.7 collective-permute-start.8
  60.3 6.4 %collective-permute-done.8 = f32[1,32896]{1,0:T(1,128)S(1)} collective-permute-done((f32[1,32896]{1,0:T(1,128)S(1)}, f32[1,32896]{1,0:T(1,128)S(1)}, u32[]{:S(2)}, u32[]{:S(2)}) %collective-permute-start.8) | collective-permute-done | bytes 131616 | tf_op jit(solution)/shard_map/ppermute | solution.py:146
  67.2 0.9 %multiply_reduce_fusion = f32[]{:T(128)} fusion(f32[1,32896]{1,0:T(1,128)S(1)} %add.132, f32[1,32768]{1,0:T(1,128)S(1)} %bitcast.81), kind=kLoop, calls=%fused_computation.18 | loop fusion | flops 98303 | bytes 262148 | tf_op jit(solution)/shard_map/reduce_sum | solution.py:251
  68.0 0.7 slice_add_fusion.1
  68.8 1.9 %collective-permute-start.9 = (f32[1,2]{1,0:T(1,128)S(1)}, f32[1,2]{1,0:T(1,128)S(1)}, u32[]{:S(2)}, u32[]{:S(2)}) collective-permute-start(f32[1,2]{1,0:T(1,128)S(1)} %slice_add_fusion.1), channel_id=1, source_target_pairs={{0,1},{1,0},{2,3},{3,2},{4,5},{5,4},{6,7},{7,6},{8,9},{9,8},{10,11... | collective-permute-start | bytes 32 | tf_op jit(solution)/shard_map/ppermute | solution.py:37
  70.6 3.2 %collective-permute-done.9 = f32[1,2]{1,0:T(1,128)S(1)} collective-permute-done((f32[1,2]{1,0:T(1,128)S(1)}, f32[1,2]{1,0:T(1,128)S(1)}, u32[]{:S(2)}, u32[]{:S(2)}) %collective-permute-start.9) | collective-permute-done | bytes 40 | tf_op jit(solution)/shard_map/ppermute | solution.py:37
  75.8 0.8 %multiply_subtract_fusion = f32[1,1,32768]{2,1,0:T(1,128)} fusion(f32[1,1,32768]{2,1,0:T(1,128)S(1)} %copy-done.2, f32[1,1,32768]{2,1,0:T(1,128)S(1)} %multiply_add_fusion, f32[]{:T(128)} %bitcast.25), kind=kLoop, calls=%fused_computation.17 | loop fusion | flops 65536 | bytes 393220 | tf_op jit(solution)/shard_map/sub | solution.py:277
  (69 shorter events, 5.3 us)
Async XLA Ops:
  0.6 7.4 %copy-start.8 = (s32[32768]{0:T(1024)S(1)}, s32[32768]{0:T(1024)}, u32[]{:S(2)}) copy-start(s32[32768]{0:T(1024)} %param.31) | copy-start | bytes 393220
  1.5 8.7 %collective-permute-start = (f32[1,1,4096]{2,1,0:T(1,128)S(1)}, f32[1,1,4096]{2,1,0:T(1,128)S(1)}, u32[]{:S(2)}, u32[]{:S(2)}) collective-permute-start(f32[1,1,4096]{2,1,0:T(1,128)S(1)} %get-tuple-element.26), channel_id=1, source_target_pairs={{0,1},{1,0},{2,3},{3,2},{4,5},{5,4},{6,7},{7,6},{8,9},{9,8},{10,11... | collective-permute-start | bytes 49160 | tf_op jit(solution)/shard_map/ppermute | solution.py:180
  5.6 1.8 %copy-start.7 = (f32[1,1,2,4096]{3,2,1,0:T(2,128)S(1)}, f32[1,1,2,4096]{3,2,1,0:T(2,128)}, u32[]{:S(2)}) copy-start(f32[1,1,2,4096]{3,2,1,0:T(2,128)} %param.18) | copy-start | bytes 98308
  5.6 2.5 %copy-start.13 = (s32[6144]{0:T(1024)S(1)}, s32[6144]{0:T(1024)}, u32[]{:S(2)}) copy-start(s32[6144]{0:T(1024)} %param.28) | copy-start | bytes 73732
  7.4 0.7 copy-start.12
  8.2 0.7 copy-start.15
  8.2 0.7 copy-start.16
  8.2 0.7 copy-start.17
  12.2 1.9 %copy-start.14 = (f32[1,6144]{1,0:T(1,128)S(1)}, f32[1,6144]{1,0:T(1,128)}, u32[]{:S(2)}) copy-start(f32[1,6144]{1,0:T(1,128)} %param.20) | copy-start | bytes 73732
  12.2 2.8 %copy-start.4 = (f32[1,1,32768]{2,1,0:T(1,128)S(1)}, f32[1,1,32768]{2,1,0:T(1,128)}, u32[]{:S(2)}) copy-start(f32[1,1,32768]{2,1,0:T(1,128)} %param.17) | copy-start | bytes 393220
  12.2 2.8 %copy-start.5 = (f32[1,32768]{1,0:T(1,128)S(1)}, f32[1,32768]{1,0:T(1,128)}, u32[]{:S(2)}) copy-start(f32[1,32768]{1,0:T(1,128)} %param.24) | copy-start | bytes 393220
  12.2 2.8 %copy-start.9 = (f32[1,32768]{1,0:T(1,128)S(1)}, f32[1,32768]{1,0:T(1,128)}, u32[]{:S(2)}) copy-start(f32[1,32768]{1,0:T(1,128)} %param.21) | copy-start | bytes 393220
  14.9 4.7 %collective-permute-start.1 = (f32[1,1,4096]{2,1,0:T(1,128)S(1)}, f32[1,1,4096]{2,1,0:T(1,128)S(1)}, u32[]{:S(2)}, u32[]{:S(2)}) collective-permute-start(f32[1,1,4096]{2,1,0:T(1,128)S(1)} %get-tuple-element.9), channel_id=1, source_target_pairs={{0,254},{2,0},{4,2},{6,4},{8,6},{10,8},{12,10},{14,12},{16,14},{18... | collective-permute-start | bytes 49160 | tf_op jit(solution)/shard_map/ppermute | solution.py:16
  15.0 4.6 %copy-start.11 = (f32[4096]{0:T(1024)S(1)}, f32[4096]{0:T(1024)}, u32[]{:S(2)}) copy-start(f32[4096]{0:T(1024)} %param.25) | copy-start | bytes 49156
  16.9 2.7 %copy-start.6 = (f32[1,1,2,4096]{3,2,1,0:T(2,128)S(1)}, f32[1,1,2,4096]{3,2,1,0:T(2,128)}, u32[]{:S(2)}) copy-start(f32[1,1,2,4096]{3,2,1,0:T(2,128)} %param.16) | copy-start | bytes 98308
  16.9 2.8 %copy-start.10 = (f32[1,2,4096]{2,1,0:T(2,128)S(1)}, f32[1,2,4096]{2,1,0:T(2,128)}, u32[]{:S(2)}) copy-start(f32[1,2,4096]{2,1,0:T(2,128)} %param.22) | copy-start | bytes 98308
  21.2 2.7 %copy-start = (s32[352,128]{1,0:T(8,128)S(1)}, s32[352,128]{1,0:T(8,128)}, u32[]{:S(2)}) copy-start(s32[352,128]{1,0:T(8,128)} %add_bitcast_fusion.index_ref) | copy-start | bytes 540676
  21.2 1.5 %collective-permute-start.2 = (f32[1,32896]{1,0:T(1,128)S(1)}, f32[1,32896]{1,0:T(1,128)S(1)}, u32[]{:S(2)}, u32[]{:S(2)}) collective-permute-start(f32[1,32896]{1,0:T(1,128)S(1)} %pad_maximum_fusion.1), channel_id=1, source_target_pairs={{0,2},{2,0},{4,6},{6,4},{8,10},{10,8},{12,14},{14,12},{16,18},{18,... | collective-permute-start | bytes 394760 | tf_op jit(solution)/shard_map/ppermute | solution.py:146
  23.0 5.9 %collective-permute-start.3 = (f32[1,32896]{1,0:T(1,128)S(1)}, f32[1,32896]{1,0:T(1,128)S(1)}, u32[]{:S(2)}, u32[]{:S(2)}) collective-permute-start(f32[1,32896]{1,0:T(1,128)S(1)} %fusion.11), channel_id=1, source_target_pairs={{0,4},{2,6},{4,0},{6,2},{8,12},{10,14},{12,8},{14,10},{16,20},{18,... | collective-permute-start | bytes 394760 | tf_op jit(solution)/shard_map/ppermute | solution.py:146
  29.0 12.9 %collective-permute-start.4 = (f32[1,32896]{1,0:T(1,128)S(1)}, f32[1,32896]{1,0:T(1,128)S(1)}, u32[]{:S(2)}, u32[]{:S(2)}) collective-permute-start(f32[1,32896]{1,0:T(1,128)S(1)} %add.127), channel_id=1, source_target_pairs={{0,12},{2,14},{4,8},{6,10},{8,4},{10,6},{12,0},{14,2},{16,28},{18,... | collective-permute-start | bytes 394760 | tf_op jit(solution)/shard_map/ppermute | solution.py:146
  41.9 0.9 %copy-start.1 = (f32[128,384]{1,0:T(8,128)S(1)}, f32[128,384]{1,0:T(8,128)}, u32[]{:S(2)}) copy-start(f32[128,384]{1,0:T(8,128)} %shard_map.168) | copy-start | bytes 589828
  42.0 5.1 %collective-permute-start.5 = (f32[1,32896]{1,0:T(1,128)S(1)}, f32[1,32896]{1,0:T(1,128)S(1)}, u32[]{:S(2)}, u32[]{:S(2)}) collective-permute-start(f32[1,32896]{1,0:T(1,128)S(1)} %add.128), channel_id=1, source_target_pairs={{0,16},{2,18},{4,20},{6,22},{8,24},{10,26},{12,28},{14,30},{16,0},... | collective-permute-start | bytes 394760 | tf_op jit(solution)/shard_map/ppermute | solution.py:146
  47.2 5.1 %collective-permute-start.6 = (f32[1,32896]{1,0:T(1,128)S(1)}, f32[1,32896]{1,0:T(1,128)S(1)}, u32[]{:S(2)}, u32[]{:S(2)}) collective-permute-start(f32[1,32896]{1,0:T(1,128)S(1)} %add.129), channel_id=1, source_target_pairs={{0,32},{2,34},{4,36},{6,38},{8,40},{10,42},{12,44},{14,46},{16,48}... | collective-permute-start | bytes 394760 | tf_op jit(solution)/shard_map/ppermute | solution.py:146
  47.4 12.8 %collective-permute-start.11 = (f32[1,1,4096]{2,1,0:T(1,128)S(1)}, f32[1,1,4096]{2,1,0:T(1,128)S(1)}, u32[]{:S(2)}, u32[]{:S(2)}) collective-permute-start(f32[1,1,4096]{2,1,0:T(1,128)S(1)} %get-tuple-element.19), channel_id=1, source_target_pairs={{0,2},{2,4},{4,6},{6,8},{8,10},{10,12},{12,14},{14,16},{16,18},{18... | collective-permute-start | bytes 49160 | tf_op jit(solution)/shard_map/ppermute | solution.py:16
  52.4 6.9 %collective-permute-start.7 = (f32[1,32896]{1,0:T(1,128)S(1)}, f32[1,32896]{1,0:T(1,128)S(1)}, u32[]{:S(2)}, u32[]{:S(2)}) collective-permute-start(f32[1,32896]{1,0:T(1,128)S(1)} %add.130), channel_id=1, source_target_pairs={{0,64},{2,66},{4,68},{6,70},{8,72},{10,74},{12,76},{14,78},{16,80}... | collective-permute-start | bytes 394760 | tf_op jit(solution)/shard_map/ppermute | solution.py:146
  52.6 7.6 %collective-permute-start.10 = (f32[1,1,4096]{2,1,0:T(1,128)S(1)}, f32[1,1,4096]{2,1,0:T(1,128)S(1)}, u32[]{:S(2)}, u32[]{:S(2)}) collective-permute-start(f32[1,1,4096]{2,1,0:T(1,128)S(1)} %constant_dynamic-slice_fusion), channel_id=1, source_target_pairs={{0,1},{1,0},{2,3},{3,2},{4,5},{5,4},{6,7},{7,6},{8,9},{9,8},{10,11... | collective-permute-start | bytes 49160 | tf_op jit(solution)/shard_map/ppermute | solution.py:267
  59.5 7.2 %collective-permute-start.8 = (f32[1,32896]{1,0:T(1,128)S(1)}, f32[1,32896]{1,0:T(1,128)S(1)}, u32[]{:S(2)}, u32[]{:S(2)}) collective-permute-start(f32[1,32896]{1,0:T(1,128)S(1)} %add.131), channel_id=1, source_target_pairs={{0,192},{2,194},{4,196},{6,198},{8,200},{10,202},{12,204},{14,206}... | collective-permute-start | bytes 394760 | tf_op jit(solution)/shard_map/ppermute | solution.py:146
  60.3 6.5 %copy-start.3 = (f32[32768]{0:T(1024)S(1)}, f32[32768]{0:T(1024)}, u32[]{:S(2)}) copy-start(f32[32768]{0:T(1024)} %param.23) | copy-start | bytes 393220
  67.1 8.6 %copy-start.2 = (f32[1,1,32768]{2,1,0:T(1,128)S(1)}, f32[1,1,32768]{2,1,0:T(1,128)}, u32[]{:S(2)}) copy-start(f32[1,1,32768]{2,1,0:T(1,128)} %param.19) | copy-start | bytes 393220
  68.8 5.1 %collective-permute-start.9 = (f32[1,2]{1,0:T(1,128)S(1)}, f32[1,2]{1,0:T(1,128)S(1)}, u32[]{:S(2)}, u32[]{:S(2)}) collective-permute-start(f32[1,2]{1,0:T(1,128)S(1)} %slice_add_fusion.1), channel_id=1, source_target_pairs={{0,1},{1,0},{2,3},{3,2},{4,5},{5,4},{6,7},{7,6},{8,9},{9,8},{10,11... | collective-permute-start | bytes 32 | tf_op jit(solution)/shard_map/ppermute | solution.py:37
